TPU v7x, 32 devices: a whole 2x2x4 slice. The times are simulated.
32 devices in a mesh: shot: 4 (over x, core), gy: 4 (over z), gx: 2 (over y).
Axes of the slice: x: 2, y: 2, z: 4, core: 2. Of those that a mesh axis runs over, the one named last changes fastest.
Arguments:
- forward_start: float32 [4, 5, 128, 2048], P('shot', None, 'gy', 'gx'), may hold values from -6 to 6
- adjoint_end: float32 [4, 5, 128, 2048], P('shot', None, 'gy', 'gx'), may hold values from -6 to 6
- velocity: float32 [128, 2048], P('gy', 'gx'), may hold values from 1.5 to 3.2
- attenuation: float32 [128, 2048], P('gy', 'gx'), may hold values from 0.05 to 0.5
- wavelet: float32 [4, 3], P('shot'), may hold values from -8 to 8
- source_cell: int32 [4, 1], P('shot'), may hold values from 0 to 262143
- receiver_cells: int32 [4, 8, 128], P('shot', ('gy', 'gx')), may hold values from 0 to 32767
- observed: float32 [4, 3, 8, 128], P('shot', None, ('gy', 'gx')), may hold values from -6 to 6
- aperture: int32 [4, 8], P('shot', ('gy', 'gx')), may hold values 0 or 1
- block_slot: int32 [8, 64], P(('gy', 'gx')), may hold values from 0 to 63, each once within a row
Outputs:
- forward_end: float32 [4, 5, 128, 2048], P('shot', None, 'gy', 'gx')
- adjoint_start: float32 [4, 5, 128, 2048], P('shot', None, 'gy', 'gx')
- model_gradient: float32 [2, 8, 64], P(None, ('gy', 'gx'), 'shot')
Inputs may be any that keep to these rules, and one draw needn't show every extreme that they name: `block_slot`: each row is a permutation of the slots. `receiver_cells`: receivers may share a cell.
All inputs are finite; a program needn't handle non-finite values. No bound on the sum of `aperture` on one device may be relied on, other than what follows from the above.
Results may differ from a plain program's by a relative error of at most 0.0003.
Values sent between devices are 32-bit elements; how exact they have to be, the bound alone decides.
No kernel may reach another device: no remote copies, remote signals or barrier semaphores. Data moves between devices by JAX's collectives and lax.ppermute only.
A program may use at most 64 MiB of HBM per device.

v0:
```python
import jax
import jax.numpy as jnp
from jax import lax
from jax.sharding import PartitionSpec as P

CZ = 32
STEPS = 3
BY = 8
BX = 8
BZ = 8


coef_near = 9.0 / 8.0
coef_far = -1.0 / 24.0
stiff_scale = 0.02
relax_rate = 0.3


def padded_2(cells, sides, width):
    for axis, dim in sides:
        count = lax.axis_size(axis)
        ends = count - 1
        head = lax.slice_in_dim(cells, 0, width, axis=dim)
        tail = lax.slice_in_dim(cells, cells.shape[dim] - width, cells.shape[dim], axis=dim)
        cells = jnp.concatenate(
            [
                lax.ppermute(tail, axis, [(i, (i + 1) % count) for i in range(ends)]),
                cells,
                lax.ppermute(head, axis, [((i + 1) % count, i) for i in range(ends)]),
            ],
            axis=dim,
        )
    return cells


def forward_diff(padded, axis, count):

    def part(s):
        return lax.slice_in_dim(padded, s, s + count, axis=axis)

    return coef_near * (part(3) - part(2)) + coef_far * (part(4) - part(1))


def backward_diff(padded, axis, count):

    def part(s):
        return lax.slice_in_dim(padded, s, s + count, axis=axis)

    return coef_near * (part(2) - part(1)) + coef_far * (part(3) - part(0))


def depth_pad(field):
    return jnp.pad(field, ((0, 0), (0, 0), (2, 2)))


def wave_step(state, stiff, attenuation):
    pres, vel_y, vel_x, vel_z, memory = state
    ny, nx, nz = pres.shape
    vel_z = vel_z - forward_diff(depth_pad(pres), 2, nz)
    framed = padded_2(pres, (("gy", 0), ("gx", 1)), 2)
    vel_y = vel_y - forward_diff(framed[:, 2 : nx + 2], 0, ny)
    vel_x = vel_x - forward_diff(framed[2 : ny + 2], 1, nx)
    wide_y = padded_2(vel_y, (("gy", 0),), 2)
    wide_x = padded_2(vel_x, (("gx", 1),), 2)
    div = (
        backward_diff(wide_y, 0, ny)
        + backward_diff(wide_x, 1, nx)
        + backward_diff(depth_pad(vel_z), 2, nz)
    )
    memory = memory - relax_rate * (memory + stiff * attenuation * div)
    pres = pres - stiff * (1.0 + attenuation) * div - memory
    return ([pres, vel_y, vel_x, vel_z, memory], div)


def on_device(
    forward_start,
    adjoint_end,
    velocity,
    attenuation,
    wavelet,
    source_cell,
    receiver_cells,
    observed,
    aperture,
    block_slot,
):
    nz = CZ
    ny = velocity.shape[0]
    nx = velocity.shape[1] // nz
    velocity = velocity.reshape(ny, nx, nz)
    attenuation = attenuation.reshape(ny, nx, nz)
    stiff = stiff_scale * velocity * velocity
    index_y = lax.axis_index("gy")
    index_x = lax.axis_index("gx")
    count_x = lax.axis_size("gx")
    total_x = nx * count_x
    cell = source_cell[0, 0]
    src_y = cell // (total_x * nz) - index_y * ny
    src_x = cell // nz % total_x - index_x * nx
    src_z = cell % nz
    inside = (src_y >= 0) & (src_y < ny) & (src_x >= 0) & (src_x < nx)
    src_local = (jnp.clip(src_y, 0, ny - 1) * nx + jnp.clip(src_x, 0, nx - 1)) * nz + src_z
    recs = receiver_cells[0, 0]
    state = [forward_start[0, k].reshape(ny, nx, nz) for k in range(5)]
    divs = []
    records = []
    for step in range(STEPS):
        state, div = wave_step(state, stiff, attenuation)
        amount = jnp.where(inside, wavelet[0, step], jnp.float32(0.0))
        state[0] = state[0].reshape(-1).at[src_local].add(amount).reshape(ny, nx, nz)
        divs.append(div)
        records.append(state[0].reshape(-1)[recs])
    adj = [adjoint_end[0, k].reshape(ny, nx, nz) for k in range(5)]
    grad_v = jnp.zeros((ny, nx, nz), jnp.float32)
    grad_a = jnp.zeros((ny, nx, nz), jnp.float32)
    for step in range(STEPS - 1, -1, -1):
        adj, unused = wave_step(adj, stiff, attenuation)
        resid = records[step] - observed[0, step, 0]
        adj[0] = adj[0].reshape(-1).at[recs].add(resid).reshape(ny, nx, nz)
        div = divs[step]
        deriv_q = (relax_rate * attenuation - (1.0 + attenuation)) * div
        deriv_m = -relax_rate * attenuation * div
        grad_v = grad_v + (adj[0] * deriv_q + adj[4] * deriv_m) * (2.0 * stiff_scale * velocity)
        grad_a = grad_a + (adj[0] * (relax_rate - 1.0) - adj[4] * relax_rate) * stiff * div
    grad_scale = float(BY * BX * BZ) ** (-0.5)
    weight = aperture[0, 0].astype(jnp.float32)
    grads = jnp.stack([grad_v, grad_a]) * weight
    blocks = grads.reshape(2, ny // BY, BY, nx // BX, BX, nz // BZ, BZ)
    blocks = blocks.transpose(1, 3, 5, 0, 2, 4, 6).reshape(-1, 2, BY * BX * BZ)
    slots = block_slot[0]
    sums = jnp.sum(blocks, axis=2) * grad_scale
    ordered = jnp.zeros(sums.shape, jnp.float32).at[slots].set(sums)
    coarse = lax.psum_scatter(ordered, "shot", scatter_dimension=0, tiled=True)
    model_gradient = coarse.T[:, None, :]
    forward_end = jnp.stack(state).reshape(5, ny, nx * nz)[None]
    adjoint_start = jnp.stack(adj).reshape(5, ny, nx * nz)[None]
    return (forward_end, adjoint_start, model_gradient)


def solution(mesh):
    placed = (
        P("shot", None, "gy", "gx"),
        P("shot", None, "gy", "gx"),
        P("gy", "gx"),
        P("gy", "gx"),
        P("shot", None),
        P("shot", None),
        P("shot", ("gy", "gx"), None),
        P("shot", None, ("gy", "gx"), None),
        P("shot", ("gy", "gx")),
        P(("gy", "gx"), None),
    )
    return jax.shard_map(
        on_device,
        mesh=mesh,
        in_specs=placed,
        out_specs=(
            P("shot", None, "gy", "gx"),
            P("shot", None, "gy", "gx"),
            P(None, ("gy", "gx"), "shot"),
        ),
        check_vma=False,
    )
```

profile of v0, /device:TPU:0, one launch (start us, length us, event | category | flops | bytes accessed | tf_op | source)
XLA Modules:
  0.0 300.2 jit_solution(10151415589759265103)
XLA Ops:
  8.2 4.9 %collective-permute-start.1 = (f32[2,32,32]{2,1,0:T(8,128)S(1)}, f32[2,32,32]{2,1,0:T(8,128)S(1)}, u32[]{:S(2)}, u32[]{:S(2)}) collective-permute-start(f32[2,32,32]{2,1,0:T(8,128)S(1)} %slice.780), channel_id=1, source_target_pairs={{0,2},{2,4},{4,6},{1,3},{3,5},{5,7},{8,10},{10,12},{12,14},{9,11},... | collective-permute-start | bytes 24584 | tf_op jit(solution)/shard_map/ppermute | solution.py:27
  14.0 3.5 %collective-permute-start.25 = (f32[2,32,32]{2,1,0:T(8,128)S(1)}, f32[2,32,32]{2,1,0:T(8,128)S(1)}, u32[]{:S(2)}, u32[]{:S(2)}) collective-permute-start(f32[2,32,32]{2,1,0:T(8,128)S(1)} %slice.872), channel_id=1, source_target_pairs={{0,2},{2,4},{4,6},{1,3},{3,5},{5,7},{8,10},{10,12},{12,14},{9,11},... | collective-permute-start | bytes 24584 | tf_op jit(solution)/shard_map/ppermute | solution.py:27
  31.7 3.6 %collective-permute-start.5 = (f32[36,2,32]{2,1,0:T(2,128)S(1)}, f32[36,2,32]{2,1,0:T(2,128)S(1)}, u32[]{:S(2)}, u32[]{:S(2)}) collective-permute-start(f32[36,2,32]{2,1,0:T(2,128)S(1)} %get-tuple-element.84), channel_id=1, source_target_pairs={{0,1},{2,3},{4,5},{6,7},{8,9},{10,11},{12,13},{14,15},{16,17},{18,... | collective-permute-start | bytes 27656 | tf_op jit(solution)/shard_map/ppermute | solution.py:27
  36.8 4.5 %collective-permute-start.29 = (f32[36,2,32]{2,1,0:T(2,128)S(1)}, f32[36,2,32]{2,1,0:T(2,128)S(1)}, u32[]{:S(2)}, u32[]{:S(2)}) collective-permute-start(f32[36,2,32]{2,1,0:T(2,128)S(1)} %get-tuple-element.86), channel_id=1, source_target_pairs={{0,1},{2,3},{4,5},{6,7},{8,9},{10,11},{12,13},{14,15},{16,17},{18,... | collective-permute-start | bytes 27656 | tf_op jit(solution)/shard_map/ppermute | solution.py:27
  49.2 4.5 %collective-permute-start.30 = (f32[32,2,32]{2,1,0:T(2,128)S(1)}, f32[32,2,32]{2,1,0:T(2,128)S(1)}, u32[]{:S(2)}, u32[]{:S(2)}) collective-permute-start(f32[32,2,32]{2,1,0:T(2,128)S(1)} %get-tuple-element.139), channel_id=1, source_target_pairs={{0,1},{2,3},{4,5},{6,7},{8,9},{10,11},{12,13},{14,15},{16,17},{18,... | collective-permute-start | bytes 24584 | tf_op jit(solution)/shard_map/ppermute | solution.py:27
  55.0 5.8 %collective-permute-start.26 = (f32[2,32,32]{2,1,0:T(8,128)S(1)}, f32[2,32,32]{2,1,0:T(8,128)S(1)}, u32[]{:S(2)}, u32[]{:S(2)}) collective-permute-start(f32[2,32,32]{2,1,0:T(8,128)S(1)} %get-tuple-element.137), channel_id=1, source_target_pairs={{0,2},{2,4},{4,6},{1,3},{3,5},{5,7},{8,10},{10,12},{12,14},{9,11},... | collective-permute-start | bytes 24584 | tf_op jit(solution)/shard_map/ppermute | solution.py:27
  60.9 3.9 %collective-permute-start.2 = (f32[2,32,32]{2,1,0:T(8,128)S(1)}, f32[2,32,32]{2,1,0:T(8,128)S(1)}, u32[]{:S(2)}, u32[]{:S(2)}) collective-permute-start(f32[2,32,32]{2,1,0:T(8,128)S(1)} %get-tuple-element.125), channel_id=1, source_target_pairs={{0,2},{2,4},{4,6},{1,3},{3,5},{5,7},{8,10},{10,12},{12,14},{9,11},... | collective-permute-start | bytes 24584 | tf_op jit(solution)/shard_map/ppermute | solution.py:27
  66.1 4.5 %collective-permute-start.6 = (f32[32,2,32]{2,1,0:T(2,128)S(1)}, f32[32,2,32]{2,1,0:T(2,128)S(1)}, u32[]{:S(2)}, u32[]{:S(2)}) collective-permute-start(f32[32,2,32]{2,1,0:T(2,128)S(1)} %get-tuple-element.132), channel_id=1, source_target_pairs={{0,1},{2,3},{4,5},{6,7},{8,9},{10,11},{12,13},{14,15},{16,17},{18,... | collective-permute-start | bytes 24584 | tf_op jit(solution)/shard_map/ppermute | solution.py:27
  75.4 3.9 %collective-permute-start.9 = (f32[2,32,32]{2,1,0:T(8,128)S(1)}, f32[2,32,32]{2,1,0:T(8,128)S(1)}, u32[]{:S(2)}, u32[]{:S(2)}) collective-permute-start(f32[2,32,32]{2,1,0:T(8,128)S(1)} %slice.812), channel_id=1, source_target_pairs={{0,2},{2,4},{4,6},{1,3},{3,5},{5,7},{8,10},{10,12},{12,14},{9,11},... | collective-permute-start | bytes 24584 | tf_op jit(solution)/shard_map/ppermute | solution.py:27
  81.1 4.3 %collective-permute-done.8 = f32[2,32,32]{2,1,0:T(8,128)S(1)} collective-permute-done((f32[2,32,32]{2,1,0:T(8,128)S(1)}, f32[2,32,32]{2,1,0:T(8,128)S(1)}, u32[]{:S(2)}, u32[]{:S(2)}) %collective-permute-start.8) | collective-permute-done | bytes 8224 | tf_op jit(solution)/shard_map/ppermute | solution.py:29
  85.5 4.1 %collective-permute-start.13 = (f32[36,2,32]{2,1,0:T(2,128)S(1)}, f32[36,2,32]{2,1,0:T(2,128)S(1)}, u32[]{:S(2)}, u32[]{:S(2)}) collective-permute-start(f32[36,2,32]{2,1,0:T(2,128)S(1)} %get-tuple-element.82), channel_id=1, source_target_pairs={{0,1},{2,3},{4,5},{6,7},{8,9},{10,11},{12,13},{14,15},{16,17},{18,... | collective-permute-start | bytes 27656 | tf_op jit(solution)/shard_map/ppermute | solution.py:27
  91.3 4.2 %collective-permute-done.12 = f32[36,2,32]{2,1,0:T(2,128)S(1)} collective-permute-done((f32[36,2,32]{2,1,0:T(2,128)S(1)}, f32[36,2,32]{2,1,0:T(2,128)S(1)}, u32[]{:S(2)}, u32[]{:S(2)}) %collective-permute-start.12) | collective-permute-done | bytes 9248 | tf_op jit(solution)/shard_map/ppermute | solution.py:29
  99.0 4.5 %collective-permute-start.10 = (f32[2,32,32]{2,1,0:T(8,128)S(1)}, f32[2,32,32]{2,1,0:T(8,128)S(1)}, u32[]{:S(2)}, u32[]{:S(2)}) collective-permute-start(f32[2,32,32]{2,1,0:T(8,128)S(1)} %get-tuple-element.116), channel_id=1, source_target_pairs={{0,2},{2,4},{4,6},{1,3},{3,5},{5,7},{8,10},{10,12},{12,14},{9,11},... | collective-permute-start | bytes 24584 | tf_op jit(solution)/shard_map/ppermute | solution.py:27
  104.9 4.5 %collective-permute-start.14 = (f32[32,2,32]{2,1,0:T(2,128)S(1)}, f32[32,2,32]{2,1,0:T(2,128)S(1)}, u32[]{:S(2)}, u32[]{:S(2)}) collective-permute-start(f32[32,2,32]{2,1,0:T(2,128)S(1)} %get-tuple-element.123), channel_id=1, source_target_pairs={{0,1},{2,3},{4,5},{6,7},{8,9},{10,11},{12,13},{14,15},{16,17},{18,... | collective-permute-start | bytes 24584 | tf_op jit(solution)/shard_map/ppermute | solution.py:27
  111.0 5.3 %subtract_subtract_fusion.4 = (f32[32,32,32]{2,1,0:T(8,128)}, f32[32,32,32]{2,1,0:T(8,128)}) fusion(f32[32,32,32]{2,1,0:T(8,128)S(1)} %reshape.284, f32[32,32,32]{2,1,0:T(8,128)S(1)} %get-tuple-element.51, f32[32,32,32]{2,1,0:T(8,128)S(1)} %get-tuple-element.52, f32[32,32,32]{2,1,0:T(8,128)S(1)} %reshape_squeeze.34, ...), kind=kLoop, calls=%fused_computation.265 | loop fusion | flops 1114112 | bytes 1343488 | tf_op jit(solution)/shard_map/sub | solution.py:71
  121.6 4.3 %collective-permute-done.16 = f32[2,32,32]{2,1,0:T(8,128)S(1)} collective-permute-done((f32[2,32,32]{2,1,0:T(8,128)S(1)}, f32[2,32,32]{2,1,0:T(8,128)S(1)}, u32[]{:S(2)}, u32[]{:S(2)}) %collective-permute-start.16) | collective-permute-done | bytes 8224 | tf_op jit(solution)/shard_map/ppermute | solution.py:29
  126.0 4.2 %collective-permute-start.21 = (f32[36,2,32]{2,1,0:T(2,128)S(1)}, f32[36,2,32]{2,1,0:T(2,128)S(1)}, u32[]{:S(2)}, u32[]{:S(2)}) collective-permute-start(f32[36,2,32]{2,1,0:T(2,128)S(1)} %get-tuple-element.80), channel_id=1, source_target_pairs={{0,1},{2,3},{4,5},{6,7},{8,9},{10,11},{12,13},{14,15},{16,17},{18,... | collective-permute-start | bytes 27656 | tf_op jit(solution)/shard_map/ppermute | solution.py:27
  131.8 4.5 %collective-permute-done.20 = f32[36,2,32]{2,1,0:T(2,128)S(1)} collective-permute-done((f32[36,2,32]{2,1,0:T(2,128)S(1)}, f32[36,2,32]{2,1,0:T(2,128)S(1)}, u32[]{:S(2)}, u32[]{:S(2)}) %collective-permute-start.20) | collective-permute-done | bytes 9248 | tf_op jit(solution)/shard_map/ppermute | solution.py:29
  139.7 5.2 %collective-permute-start.18 = (f32[2,32,32]{2,1,0:T(8,128)}, f32[2,32,32]{2,1,0:T(8,128)}, u32[]{:S(2)}, u32[]{:S(2)}) collective-permute-start(f32[2,32,32]{2,1,0:T(8,128)} %get-tuple-element.107), channel_id=1, source_target_pairs={{0,2},{2,4},{4,6},{1,3},{3,5},{5,7},{8,10},{10,12},{12,14},{9,11},... | collective-permute-start | bytes 24584 | tf_op jit(solution)/shard_map/ppermute | solution.py:27
  146.8 5.8 %collective-permute-start.22 = (f32[32,2,32]{2,1,0:T(2,128)}, f32[32,2,32]{2,1,0:T(2,128)}, u32[]{:S(2)}, u32[]{:S(2)}) collective-permute-start(f32[32,2,32]{2,1,0:T(2,128)} %get-tuple-element.114), channel_id=1, source_target_pairs={{0,1},{2,3},{4,5},{6,7},{8,9},{10,11},{12,13},{14,15},{16,17},{18,... | collective-permute-start | bytes 24584 | tf_op jit(solution)/shard_map/ppermute | solution.py:27
  157.8 5.7 %subtract_subtract_fusion.3 = (f32[32,32,32]{2,1,0:T(8,128)}, f32[32,32,32]{2,1,0:T(8,128)}, f32[32,32,32]{2,1,0:T(8,128)}) fusion(f32[32,32,32]{2,1,0:T(8,128)S(1)} %reshape.287, f32[32,32,32]{2,1,0:T(8,128)S(1)} %get-tuple-element.51, f32[32,32,32]{2,1,0:T(8,128)S(1)} %get-tuple-element.52, f32[32,32,32]{2,1,0:T(8,128)} %get-tuple-element.57, ...), kind=kLoop, calls=%fused_computation.262 | loop fusion | flops 1245184 | bytes 1605632 | tf_op jit(solution)/shard_map/sub | solution.py:71
  171.5 3.6 %collective-permute-done.32 = f32[2,32,32]{2,1,0:T(8,128)S(1)} collective-permute-done((f32[2,32,32]{2,1,0:T(8,128)S(1)}, f32[2,32,32]{2,1,0:T(8,128)S(1)}, u32[]{:S(2)}, u32[]{:S(2)}) %collective-permute-start.32) | collective-permute-done | bytes 8224 | tf_op jit(solution)/shard_map/ppermute | solution.py:29
  189.5 4.5 %collective-permute-start.34 = (f32[2,32,32]{2,1,0:T(8,128)S(1)}, f32[2,32,32]{2,1,0:T(8,128)S(1)}, u32[]{:S(2)}, u32[]{:S(2)}) collective-permute-start(f32[2,32,32]{2,1,0:T(8,128)S(1)} %get-tuple-element.98), channel_id=1, source_target_pairs={{0,2},{2,4},{4,6},{1,3},{3,5},{5,7},{8,10},{10,12},{12,14},{9,11},... | collective-permute-start | bytes 24584 | tf_op jit(solution)/shard_map/ppermute | solution.py:27
  195.3 5.0 %collective-permute-start.38 = (f32[32,2,32]{2,1,0:T(2,128)S(1)}, f32[32,2,32]{2,1,0:T(2,128)S(1)}, u32[]{:S(2)}, u32[]{:S(2)}) collective-permute-start(f32[32,2,32]{2,1,0:T(2,128)S(1)} %get-tuple-element.105), channel_id=1, source_target_pairs={{0,1},{2,3},{4,5},{6,7},{8,9},{10,11},{12,13},{14,15},{16,17},{18,... | collective-permute-start | bytes 24584 | tf_op jit(solution)/shard_map/ppermute | solution.py:27
  212.7 3.6 %collective-permute-done.40 = f32[2,32,32]{2,1,0:T(8,128)S(1)} collective-permute-done((f32[2,32,32]{2,1,0:T(8,128)S(1)}, f32[2,32,32]{2,1,0:T(8,128)S(1)}, u32[]{:S(2)}, u32[]{:S(2)}) %collective-permute-start.40) | collective-permute-done | bytes 8224 | tf_op jit(solution)/shard_map/ppermute | solution.py:29
  216.3 4.2 %collective-permute-start.45 = (f32[36,2,32]{2,1,0:T(2,128)S(1)}, f32[36,2,32]{2,1,0:T(2,128)S(1)}, u32[]{:S(2)}, u32[]{:S(2)}) collective-permute-start(f32[36,2,32]{2,1,0:T(2,128)S(1)} %get-tuple-element.76), channel_id=1, source_target_pairs={{0,1},{2,3},{4,5},{6,7},{8,9},{10,11},{12,13},{14,15},{16,17},{18,... | collective-permute-start | bytes 27656 | tf_op jit(solution)/shard_map/ppermute | solution.py:27
  222.5 3.9 %collective-permute-done.44 = f32[36,2,32]{2,1,0:T(2,128)S(1)} collective-permute-done((f32[36,2,32]{2,1,0:T(2,128)S(1)}, f32[36,2,32]{2,1,0:T(2,128)S(1)}, u32[]{:S(2)}, u32[]{:S(2)}) %collective-permute-start.44) | collective-permute-done | bytes 9248 | tf_op jit(solution)/shard_map/ppermute | solution.py:29
  231.3 5.8 %collective-permute-start.46 = (f32[32,2,32]{2,1,0:T(2,128)}, f32[32,2,32]{2,1,0:T(2,128)}, u32[]{:S(2)}, u32[]{:S(2)}) collective-permute-start(f32[32,2,32]{2,1,0:T(2,128)} %get-tuple-element.94), channel_id=1, source_target_pairs={{0,1},{2,3},{4,5},{6,7},{8,9},{10,11},{12,13},{14,15},{16,17},{18,... | collective-permute-start | bytes 24584 | tf_op jit(solution)/shard_map/ppermute | solution.py:27
  239.0 5.2 %collective-permute-start.42 = (f32[2,32,32]{2,1,0:T(8,128)}, f32[2,32,32]{2,1,0:T(8,128)}, u32[]{:S(2)}, u32[]{:S(2)}) collective-permute-start(f32[2,32,32]{2,1,0:T(8,128)} %get-tuple-element.92), channel_id=1, source_target_pairs={{0,2},{2,4},{4,6},{1,3},{3,5},{5,7},{8,10},{10,12},{12,14},{9,11},... | collective-permute-start | bytes 24584 | tf_op jit(solution)/shard_map/ppermute | solution.py:27
  250.6 5.3 %subtract_subtract_fusion = (f32[32,32,32]{2,1,0:T(8,128)}, f32[32,32,32]{2,1,0:T(8,128)}) fusion(f32[32,32,32]{2,1,0:T(8,128)S(1)} %reshape.293, f32[32,32,32]{2,1,0:T(8,128)S(1)} %get-tuple-element.51, f32[32,32,32]{2,1,0:T(8,128)S(1)} %get-tuple-element.52, f32[32,32,32]{2,1,0:T(8,128)S(1)} %get-tuple-element.50, f32[32,32,32]{2,1,0:T(8,128)} %get-tuple-element.48, ...), kind=kLoop, calls=%fused_computation.253 | loop fusion | flops 1114112 | bytes 1343488 | tf_op jit(solution)/shard_map/sub | solution.py:71
  262.3 3.8 %add_multiply_fusion = (f32[32,32,32]{2,1,0:T(8,128)}, f32[32,32,32]{2,1,0:T(8,128)}) fusion(f32[32,32,32]{2,1,0:T(8,128)} %get-tuple-element.46, f32[32,32,32]{2,1,0:T(8,128)S(1)} %get-tuple-element.59, f32[32,32,32]{2,1,0:T(8,128)} %reshape.295, f32[32,32,32]{2,1,0:T(8,128)} %get-tuple-element.57, f32[32,32,32]{2,1,0:T(8,128)S(1)} %reshape.293, ...), kind=kLoop, calls=%fused_computation.250 | loop fusion | flops 1507328 | bytes 1835008 | tf_op jit(solution)/shard_map/add | solution.py:123
  276.0 16.0 %reduce-scatter.2.cloned.1.call-done = f32[16,2]{1,0:T(8,128)} async-done(((f32[64,2]{1,0:T(8,128)}), f32[16,2]{1,0:T(8,128)}) %reduce-scatter.2.cloned.1.call-update) | async-done | bytes 144 | tf_op jit(solution)/shard_map/reduce_scatter | solution.py:133
  (291 shorter events, 124.7 us)
Async XLA Ops:
  7.2 284.8 %reduce-scatter.2.cloned.1.call-start = ((), (), s32[]{:S(2)}) async-start(), calls=%async_computation.1 | async-start | bytes 40960 | tf_op jit(solution)/shard_map/reduce_scatter | solution.py:133
  8.2 23.4 %collective-permute-start.1 = (f32[2,32,32]{2,1,0:T(8,128)S(1)}, f32[2,32,32]{2,1,0:T(8,128)S(1)}, u32[]{:S(2)}, u32[]{:S(2)}) collective-permute-start(f32[2,32,32]{2,1,0:T(8,128)S(1)} %slice.780), channel_id=1, source_target_pairs={{0,2},{2,4},{4,6},{1,3},{3,5},{5,7},{8,10},{10,12},{12,14},{9,11},... | collective-permute-start | bytes 24584 | tf_op jit(solution)/shard_map/ppermute | solution.py:27
  14.0 22.6 %collective-permute-start.25 = (f32[2,32,32]{2,1,0:T(8,128)S(1)}, f32[2,32,32]{2,1,0:T(8,128)S(1)}, u32[]{:S(2)}, u32[]{:S(2)}) collective-permute-start(f32[2,32,32]{2,1,0:T(8,128)S(1)} %slice.872), channel_id=1, source_target_pairs={{0,2},{2,4},{4,6},{1,3},{3,5},{5,7},{8,10},{10,12},{12,14},{9,11},... | collective-permute-start | bytes 24584 | tf_op jit(solution)/shard_map/ppermute | solution.py:27
  17.5 14.1 %collective-permute-start = (f32[2,32,32]{2,1,0:T(8,128)S(1)}, f32[2,32,32]{2,1,0:T(8,128)S(1)}, u32[]{:S(2)}, u32[]{:S(2)}) collective-permute-start(f32[2,32,32]{2,1,0:T(8,128)S(1)} %slice.776), channel_id=1, source_target_pairs={{2,0},{4,2},{6,4},{3,1},{5,3},{7,5},{10,8},{12,10},{14,12},{11,9},... | collective-permute-start | bytes 24584 | tf_op jit(solution)/shard_map/ppermute | solution.py:29
  18.9 17.8 %collective-permute-start.24 = (f32[2,32,32]{2,1,0:T(8,128)S(1)}, f32[2,32,32]{2,1,0:T(8,128)S(1)}, u32[]{:S(2)}, u32[]{:S(2)}) collective-permute-start(f32[2,32,32]{2,1,0:T(8,128)S(1)} %slice.868), channel_id=1, source_target_pairs={{2,0},{4,2},{6,4},{3,1},{5,3},{7,5},{10,8},{12,10},{14,12},{11,9},... | collective-permute-start | bytes 24584 | tf_op jit(solution)/shard_map/ppermute | solution.py:29
  31.7 10.9 %collective-permute-start.5 = (f32[36,2,32]{2,1,0:T(2,128)S(1)}, f32[36,2,32]{2,1,0:T(2,128)S(1)}, u32[]{:S(2)}, u32[]{:S(2)}) collective-permute-start(f32[36,2,32]{2,1,0:T(2,128)S(1)} %get-tuple-element.84), channel_id=1, source_target_pairs={{0,1},{2,3},{4,5},{6,7},{8,9},{10,11},{12,13},{14,15},{16,17},{18,... | collective-permute-start | bytes 27656 | tf_op jit(solution)/shard_map/ppermute | solution.py:27
  35.3 7.4 %collective-permute-start.4 = (f32[36,2,32]{2,1,0:T(2,128)S(1)}, f32[36,2,32]{2,1,0:T(2,128)S(1)}, u32[]{:S(2)}, u32[]{:S(2)}) collective-permute-start(f32[36,2,32]{2,1,0:T(2,128)S(1)} %get-tuple-element.85), channel_id=1, source_target_pairs={{1,0},{3,2},{5,4},{7,6},{9,8},{11,10},{13,12},{15,14},{17,16},{19,... | collective-permute-start | bytes 27656 | tf_op jit(solution)/shard_map/ppermute | solution.py:29
  36.8 7.9 %collective-permute-start.29 = (f32[36,2,32]{2,1,0:T(2,128)S(1)}, f32[36,2,32]{2,1,0:T(2,128)S(1)}, u32[]{:S(2)}, u32[]{:S(2)}) collective-permute-start(f32[36,2,32]{2,1,0:T(2,128)S(1)} %get-tuple-element.86), channel_id=1, source_target_pairs={{0,1},{2,3},{4,5},{6,7},{8,9},{10,11},{12,13},{14,15},{16,17},{18,... | collective-permute-start | bytes 27656 | tf_op jit(solution)/shard_map/ppermute | solution.py:27
  43.3 29.0 %collective-permute-start.3 = (f32[2,32,32]{2,1,0:T(8,128)S(1)}, f32[2,32,32]{2,1,0:T(8,128)S(1)}, u32[]{:S(2)}, u32[]{:S(2)}) collective-permute-start(f32[2,32,32]{2,1,0:T(8,128)S(1)} %get-tuple-element.124), channel_id=1, source_target_pairs={{2,0},{4,2},{6,4},{3,1},{5,3},{7,5},{10,8},{12,10},{14,12},{11,9},... | collective-permute-start | bytes 24584 | tf_op jit(solution)/shard_map/ppermute | solution.py:29
  47.9 13.0 %collective-permute-start.31 = (f32[32,2,32]{2,1,0:T(2,128)S(1)}, f32[32,2,32]{2,1,0:T(2,128)S(1)}, u32[]{:S(2)}, u32[]{:S(2)}) collective-permute-start(f32[32,2,32]{2,1,0:T(2,128)S(1)} %get-tuple-element.138), channel_id=1, source_target_pairs={{1,0},{3,2},{5,4},{7,6},{9,8},{11,10},{13,12},{15,14},{17,16},{19,... | collective-permute-start | bytes 24584 | tf_op jit(solution)/shard_map/ppermute | solution.py:29
  49.2 15.7 %collective-permute-start.30 = (f32[32,2,32]{2,1,0:T(2,128)S(1)}, f32[32,2,32]{2,1,0:T(2,128)S(1)}, u32[]{:S(2)}, u32[]{:S(2)}) collective-permute-start(f32[32,2,32]{2,1,0:T(2,128)S(1)} %get-tuple-element.139), channel_id=1, source_target_pairs={{0,1},{2,3},{4,5},{6,7},{8,9},{10,11},{12,13},{14,15},{16,17},{18,... | collective-permute-start | bytes 24584 | tf_op jit(solution)/shard_map/ppermute | solution.py:27
  53.7 12.4 %collective-permute-start.27 = (f32[2,32,32]{2,1,0:T(8,128)S(1)}, f32[2,32,32]{2,1,0:T(8,128)S(1)}, u32[]{:S(2)}, u32[]{:S(2)}) collective-permute-start(f32[2,32,32]{2,1,0:T(8,128)S(1)} %get-tuple-element.136), channel_id=1, source_target_pairs={{2,0},{4,2},{6,4},{3,1},{5,3},{7,5},{10,8},{12,10},{14,12},{11,9},... | collective-permute-start | bytes 24584 | tf_op jit(solution)/shard_map/ppermute | solution.py:29
  55.0 15.7 %collective-permute-start.26 = (f32[2,32,32]{2,1,0:T(8,128)S(1)}, f32[2,32,32]{2,1,0:T(8,128)S(1)}, u32[]{:S(2)}, u32[]{:S(2)}) collective-permute-start(f32[2,32,32]{2,1,0:T(8,128)S(1)} %get-tuple-element.137), channel_id=1, source_target_pairs={{0,2},{2,4},{4,6},{1,3},{3,5},{5,7},{8,10},{10,12},{12,14},{9,11},... | collective-permute-start | bytes 24584 | tf_op jit(solution)/shard_map/ppermute | solution.py:27
  60.9 11.4 %collective-permute-start.2 = (f32[2,32,32]{2,1,0:T(8,128)S(1)}, f32[2,32,32]{2,1,0:T(8,128)S(1)}, u32[]{:S(2)}, u32[]{:S(2)}) collective-permute-start(f32[2,32,32]{2,1,0:T(8,128)S(1)} %get-tuple-element.125), channel_id=1, source_target_pairs={{0,2},{2,4},{4,6},{1,3},{3,5},{5,7},{8,10},{10,12},{12,14},{9,11},... | collective-permute-start | bytes 24584 | tf_op jit(solution)/shard_map/ppermute | solution.py:27
  64.8 7.5 %collective-permute-start.7 = (f32[32,2,32]{2,1,0:T(2,128)S(1)}, f32[32,2,32]{2,1,0:T(2,128)S(1)}, u32[]{:S(2)}, u32[]{:S(2)}) collective-permute-start(f32[32,2,32]{2,1,0:T(2,128)S(1)} %get-tuple-element.131), channel_id=1, source_target_pairs={{1,0},{3,2},{5,4},{7,6},{9,8},{11,10},{13,12},{15,14},{17,16},{19,... | collective-permute-start | bytes 24584 | tf_op jit(solution)/shard_map/ppermute | solution.py:29
  66.1 6.2 %collective-permute-start.6 = (f32[32,2,32]{2,1,0:T(2,128)S(1)}, f32[32,2,32]{2,1,0:T(2,128)S(1)}, u32[]{:S(2)}, u32[]{:S(2)}) collective-permute-start(f32[32,2,32]{2,1,0:T(2,128)S(1)} %get-tuple-element.132), channel_id=1, source_target_pairs={{0,1},{2,3},{4,5},{6,7},{8,9},{10,11},{12,13},{14,15},{16,17},{18,... | collective-permute-start | bytes 24584 | tf_op jit(solution)/shard_map/ppermute | solution.py:27
  97.7 12.4 %collective-permute-start.11 = (f32[2,32,32]{2,1,0:T(8,128)S(1)}, f32[2,32,32]{2,1,0:T(8,128)S(1)}, u32[]{:S(2)}, u32[]{:S(2)}) collective-permute-start(f32[2,32,32]{2,1,0:T(8,128)S(1)} %get-tuple-element.115), channel_id=1, source_target_pairs={{2,0},{4,2},{6,4},{3,1},{5,3},{7,5},{10,8},{12,10},{14,12},{11,9},... | collective-permute-start | bytes 24584 | tf_op jit(solution)/shard_map/ppermute | solution.py:29
  99.0 11.1 %collective-permute-start.10 = (f32[2,32,32]{2,1,0:T(8,128)S(1)}, f32[2,32,32]{2,1,0:T(8,128)S(1)}, u32[]{:S(2)}, u32[]{:S(2)}) collective-permute-start(f32[2,32,32]{2,1,0:T(8,128)S(1)} %get-tuple-element.116), channel_id=1, source_target_pairs={{0,2},{2,4},{4,6},{1,3},{3,5},{5,7},{8,10},{10,12},{12,14},{9,11},... | collective-permute-start | bytes 24584 | tf_op jit(solution)/shard_map/ppermute | solution.py:27
  103.6 6.5 %collective-permute-start.15 = (f32[32,2,32]{2,1,0:T(2,128)S(1)}, f32[32,2,32]{2,1,0:T(2,128)S(1)}, u32[]{:S(2)}, u32[]{:S(2)}) collective-permute-start(f32[32,2,32]{2,1,0:T(2,128)S(1)} %get-tuple-element.122), channel_id=1, source_target_pairs={{1,0},{3,2},{5,4},{7,6},{9,8},{11,10},{13,12},{15,14},{17,16},{19,... | collective-permute-start | bytes 24584 | tf_op jit(solution)/shard_map/ppermute | solution.py:29
  138.4 19.4 %collective-permute-start.19 = (f32[2,32,32]{2,1,0:T(8,128)}, f32[2,32,32]{2,1,0:T(8,128)}, u32[]{:S(2)}, u32[]{:S(2)}) collective-permute-start(f32[2,32,32]{2,1,0:T(8,128)} %get-tuple-element.106), channel_id=1, source_target_pairs={{2,0},{4,2},{6,4},{3,1},{5,3},{7,5},{10,8},{12,10},{14,12},{11,9},... | collective-permute-start | bytes 24584 | tf_op jit(solution)/shard_map/ppermute | solution.py:29
  139.7 18.1 %collective-permute-start.18 = (f32[2,32,32]{2,1,0:T(8,128)}, f32[2,32,32]{2,1,0:T(8,128)}, u32[]{:S(2)}, u32[]{:S(2)}) collective-permute-start(f32[2,32,32]{2,1,0:T(8,128)} %get-tuple-element.107), channel_id=1, source_target_pairs={{0,2},{2,4},{4,6},{1,3},{3,5},{5,7},{8,10},{10,12},{12,14},{9,11},... | collective-permute-start | bytes 24584 | tf_op jit(solution)/shard_map/ppermute | solution.py:27
  145.5 12.3 %collective-permute-start.23 = (f32[32,2,32]{2,1,0:T(2,128)}, f32[32,2,32]{2,1,0:T(2,128)}, u32[]{:S(2)}, u32[]{:S(2)}) collective-permute-start(f32[32,2,32]{2,1,0:T(2,128)} %get-tuple-element.113), channel_id=1, source_target_pairs={{1,0},{3,2},{5,4},{7,6},{9,8},{11,10},{13,12},{15,14},{17,16},{19,... | collective-permute-start | bytes 24584 | tf_op jit(solution)/shard_map/ppermute | solution.py:29
  146.8 11.0 %collective-permute-start.22 = (f32[32,2,32]{2,1,0:T(2,128)}, f32[32,2,32]{2,1,0:T(2,128)}, u32[]{:S(2)}, u32[]{:S(2)}) collective-permute-start(f32[32,2,32]{2,1,0:T(2,128)} %get-tuple-element.114), channel_id=1, source_target_pairs={{0,1},{2,3},{4,5},{6,7},{8,9},{10,11},{12,13},{14,15},{16,17},{18,... | collective-permute-start | bytes 24584 | tf_op jit(solution)/shard_map/ppermute | solution.py:27
  177.2 7.9 %collective-permute-start.37 = (f32[36,2,32]{2,1,0:T(2,128)}, f32[36,2,32]{2,1,0:T(2,128)}, u32[]{:S(2)}, u32[]{:S(2)}) collective-permute-start(f32[36,2,32]{2,1,0:T(2,128)} %get-tuple-element.78), channel_id=1, source_target_pairs={{0,1},{2,3},{4,5},{6,7},{8,9},{10,11},{12,13},{14,15},{16,17},{18,... | collective-permute-start | bytes 27656 | tf_op jit(solution)/shard_map/ppermute | solution.py:27
  188.2 12.8 %collective-permute-start.35 = (f32[2,32,32]{2,1,0:T(8,128)S(1)}, f32[2,32,32]{2,1,0:T(8,128)S(1)}, u32[]{:S(2)}, u32[]{:S(2)}) collective-permute-start(f32[2,32,32]{2,1,0:T(8,128)S(1)} %get-tuple-element.97), channel_id=1, source_target_pairs={{2,0},{4,2},{6,4},{3,1},{5,3},{7,5},{10,8},{12,10},{14,12},{11,9},... | collective-permute-start | bytes 24584 | tf_op jit(solution)/shard_map/ppermute | solution.py:29
  189.5 11.5 %collective-permute-start.34 = (f32[2,32,32]{2,1,0:T(8,128)S(1)}, f32[2,32,32]{2,1,0:T(8,128)S(1)}, u32[]{:S(2)}, u32[]{:S(2)}) collective-permute-start(f32[2,32,32]{2,1,0:T(8,128)S(1)} %get-tuple-element.98), channel_id=1, source_target_pairs={{0,2},{2,4},{4,6},{1,3},{3,5},{5,7},{8,10},{10,12},{12,14},{9,11},... | collective-permute-start | bytes 24584 | tf_op jit(solution)/shard_map/ppermute | solution.py:27
  194.0 6.9 %collective-permute-start.39 = (f32[32,2,32]{2,1,0:T(2,128)S(1)}, f32[32,2,32]{2,1,0:T(2,128)S(1)}, u32[]{:S(2)}, u32[]{:S(2)}) collective-permute-start(f32[32,2,32]{2,1,0:T(2,128)S(1)} %get-tuple-element.104), channel_id=1, source_target_pairs={{1,0},{3,2},{5,4},{7,6},{9,8},{11,10},{13,12},{15,14},{17,16},{19,... | collective-permute-start | bytes 24584 | tf_op jit(solution)/shard_map/ppermute | solution.py:29
  195.3 6.6 %collective-permute-start.38 = (f32[32,2,32]{2,1,0:T(2,128)S(1)}, f32[32,2,32]{2,1,0:T(2,128)S(1)}, u32[]{:S(2)}, u32[]{:S(2)}) collective-permute-start(f32[32,2,32]{2,1,0:T(2,128)S(1)} %get-tuple-element.105), channel_id=1, source_target_pairs={{0,1},{2,3},{4,5},{6,7},{8,9},{10,11},{12,13},{14,15},{16,17},{18,... | collective-permute-start | bytes 24584 | tf_op jit(solution)/shard_map/ppermute | solution.py:27
  230.0 20.6 %collective-permute-start.47 = (f32[32,2,32]{2,1,0:T(2,128)}, f32[32,2,32]{2,1,0:T(2,128)}, u32[]{:S(2)}, u32[]{:S(2)}) collective-permute-start(f32[32,2,32]{2,1,0:T(2,128)} %get-tuple-element.93), channel_id=1, source_target_pairs={{1,0},{3,2},{5,4},{7,6},{9,8},{11,10},{13,12},{15,14},{17,16},{19,... | collective-permute-start | bytes 24584 | tf_op jit(solution)/shard_map/ppermute | solution.py:29
  231.3 19.3 %collective-permute-start.46 = (f32[32,2,32]{2,1,0:T(2,128)}, f32[32,2,32]{2,1,0:T(2,128)}, u32[]{:S(2)}, u32[]{:S(2)}) collective-permute-start(f32[32,2,32]{2,1,0:T(2,128)} %get-tuple-element.94), channel_id=1, source_target_pairs={{0,1},{2,3},{4,5},{6,7},{8,9},{10,11},{12,13},{14,15},{16,17},{18,... | collective-permute-start | bytes 24584 | tf_op jit(solution)/shard_map/ppermute | solution.py:27
  237.7 12.9 %collective-permute-start.43 = (f32[2,32,32]{2,1,0:T(8,128)}, f32[2,32,32]{2,1,0:T(8,128)}, u32[]{:S(2)}, u32[]{:S(2)}) collective-permute-start(f32[2,32,32]{2,1,0:T(8,128)} %get-tuple-element.91), channel_id=1, source_target_pairs={{2,0},{4,2},{6,4},{3,1},{5,3},{7,5},{10,8},{12,10},{14,12},{11,9},... | collective-permute-start | bytes 24584 | tf_op jit(solution)/shard_map/ppermute | solution.py:29
  239.0 11.6 %collective-permute-start.42 = (f32[2,32,32]{2,1,0:T(8,128)}, f32[2,32,32]{2,1,0:T(8,128)}, u32[]{:S(2)}, u32[]{:S(2)}) collective-permute-start(f32[2,32,32]{2,1,0:T(8,128)} %get-tuple-element.92), channel_id=1, source_target_pairs={{0,2},{2,4},{4,6},{1,3},{3,5},{5,7},{8,10},{10,12},{12,14},{9,11},... | collective-permute-start | bytes 24584 | tf_op jit(solution)/shard_map/ppermute | solution.py:27
  (63 other events, 751.7 us)
Sparse Core Ops, SparseCore 0:
  275.4 16.5 reduce-scatter.1
where the time goes:
time: 302 us; the launch traced here: 300 us
  starting transfers between devices  132 us (44%)
  local copies, waits for them, and re-layouts  57.9 us (19%)
  waiting for transfers between devices  49.7 us (16%)
  other arithmetic  42.2 us (14%)
  between operations  18.7 us (6%)
    ppermute x24, starting transfers between devices, padded_2(): lax.ppermute(tail, axis, [(i, (i + 1) % count) for i in range(ends)])  100 us
    ppermute x24, starting transfers between devices, padded_2(): lax.ppermute(head, axis, [((i + 1) % count, i) for i in range(ends)])  31.3 us
    ppermute x24, waiting for transfers between devices, padded_2(): lax.ppermute(head, axis, [((i + 1) % count, i) for i in range(ends)])  31.2 us
    sub x6, other arithmetic, wave_step(): pres = pres - stiff * (1.0 + attenuation) * div - memory  20.9 us
    reduce_scatter x1, waiting for transfers between devices, on_device(): coarse = lax.psum_scatter(ordered, 'shot', scatter_dimension=0, tiled=True)  16 us
    unnamed x113, local copies, waits for them, and re-layouts  10.4 us
    sub x4, other arithmetic, wave_step(): vel_y = vel_y - forward_diff(framed[:, 2:nx + 2], 0, ny)  6.26 us
    another operation x6, local copies, waits for them, and re-layouts, on_device(): forward_end = jnp.stack(state).reshape(5, ny, nx * nz)[None]  6.06 us
  transfers between devices with their start and end apart: 49, of which 14 were waited for; matrix products, arithmetic and copies ran while one was open for 12% of the time, Pallas kernels for 0%

commit v1 on v0

v1 whole, which is shorter than its diff:
```python
import jax
import jax.numpy as jnp
from jax import lax
from jax.sharding import PartitionSpec as P

CZ = 32
STEPS = 3
BY = 8
BX = 8
BZ = 8
HALO = 3 * STEPS

coef_near = 9.0 / 8.0
coef_far = -1.0 / 24.0
stiff_scale = 0.02
relax_rate = 0.3


def shift(a, d, axis):
    widths = [(0, 0, 0)] * a.ndim
    widths[axis] = (-d, d, 0)
    return lax.pad(a, jnp.zeros((), a.dtype), widths)


def forward_diff(s):
    return coef_near * (s(1) - s(0)) + coef_far * (s(2) - s(-1))


def backward_diff(s):
    return coef_near * (s(0) - s(-1)) + coef_far * (s(1) - s(-2))


def exchange(cells, axis, dim, width):
    count = lax.axis_size(axis)
    ends = count - 1
    head = lax.slice_in_dim(cells, 0, width, axis=dim)
    tail = lax.slice_in_dim(cells, cells.shape[dim] - width, cells.shape[dim], axis=dim)
    below = lax.ppermute(tail, axis, [(i, i + 1) for i in range(ends)])
    above = lax.ppermute(head, axis, [(i + 1, i) for i in range(ends)])
    return below, above


def on_device(
    forward_start,
    adjoint_end,
    velocity,
    attenuation,
    wavelet,
    source_cell,
    receiver_cells,
    observed,
    aperture,
    block_slot,
):
    nz = CZ
    ny = velocity.shape[0]
    lanes = velocity.shape[1]
    nx = lanes // nz
    r = HALO
    ey = ny + 2 * r
    ex = nx + 2 * r
    el = ex * nz
    index_y = lax.axis_index("gy")
    index_x = lax.axis_index("gx")
    total_y = ny * lax.axis_size("gy")
    total_x = nx * lax.axis_size("gx")

    fields = jnp.concatenate(
        [forward_start[0], adjoint_end[0], velocity[None], attenuation[None]], axis=0
    )
    below, above = exchange(fields, "gy", 1, r)
    fields = jnp.concatenate([below, fields, above], axis=1)
    left, right = exchange(fields, "gx", 2, r * nz)
    fields = jnp.concatenate([left, fields, right], axis=2)

    vel = fields[10]
    att = fields[11]
    stiff = stiff_scale * vel * vel

    row = lax.broadcasted_iota(jnp.int32, (ey, el), 0)
    lane = lax.broadcasted_iota(jnp.int32, (ey, el), 1)
    glob_y = index_y * ny - r + row
    glob_x = index_x * nx - r + lane // nz
    inside = (glob_y >= 0) & (glob_y < total_y) & (glob_x >= 0) & (glob_x < total_x)
    depth = lane % nz
    zero = jnp.zeros((ey, el), jnp.float32)

    def zshift(a, d):
        return jnp.where((depth + d >= 0) & (depth + d < nz), shift(a, d, 1), zero)

    def wave_step(state):
        pres, vel_y, vel_x, vel_z, memory = state
        vel_y = jnp.where(inside, vel_y - forward_diff(lambda d: shift(pres, d, 0)), zero)
        vel_x = jnp.where(inside, vel_x - forward_diff(lambda d: shift(pres, d * nz, 1)), zero)
        vel_z = vel_z - forward_diff(lambda d: zshift(pres, d))
        div = (
            backward_diff(lambda d: shift(vel_y, d, 0))
            + backward_diff(lambda d: shift(vel_x, d * nz, 1))
            + backward_diff(lambda d: zshift(vel_z, d))
        )
        memory = memory - relax_rate * (memory + stiff * att * div)
        pres = jnp.where(inside, pres - stiff * (1.0 + att) * div - memory, zero)
        return [pres, vel_y, vel_x, vel_z, memory], div

    def own(a):
        return a[r : r + ny, r * nz : r * nz + lanes]

    cell = source_cell[0, 0]
    src_y = cell // (total_x * nz) - index_y * ny + r
    src_x = cell // nz % total_x - index_x * nx + r
    src_z = cell % nz
    src_here = (row == src_y) & (lane == src_x * nz + src_z)

    recs = receiver_cells[0, 0]
    rec_y = recs // (nx * nz)
    rec_x = recs // nz % nx
    rec_z = recs % nz
    own_flat = (rec_y + r) * el + (rec_x + r) * nz + rec_z

    state = [fields[k] for k in range(5)]
    divs = []
    records = []
    for step in range(STEPS):
        state, div = wave_step(state)
        state[0] = state[0] + jnp.where(src_here, wavelet[0, step], jnp.float32(0.0))
        divs.append(own(div))
        records.append(state[0].reshape(-1)[own_flat])
    forward_end = jnp.stack([own(f) for f in state])[None]

    resid = jnp.stack(records) - observed[0, :, 0]
    message = jnp.concatenate([recs.astype(jnp.float32)[None], resid], axis=0)[None]
    below, above = exchange(message, "gy", 0, 1)
    message = jnp.concatenate([below, message, above], axis=0)
    left, right = exchange(message, "gx", 0, 3)
    message = jnp.concatenate([left, message, right], axis=0)
    off_y = jnp.array([-1, 0, 1] * 3, jnp.int32)[:, None] * ny
    off_x = jnp.repeat(jnp.array([-1, 0, 1], jnp.int32), 3)[:, None] * nx
    cells = message[:, 0].astype(jnp.int32)
    at_y = cells // (nx * nz) + off_y + r
    at_x = cells // nz % nx + off_x + r
    at_z = cells % nz
    fits = (at_y >= 0) & (at_y < ey) & (at_x >= 0) & (at_x < ex)
    flat = jnp.where(fits, at_y * el + at_x * nz + at_z, ey * el).reshape(-1)
    amounts = message[:, 1:].transpose(1, 0, 2).reshape(STEPS, -1)
    inject = jnp.zeros((STEPS, ey * el), jnp.float32).at[:, flat].add(amounts, mode="drop")
    inject = inject.reshape(STEPS, ey, el)

    velocity_own = velocity
    attenuation_own = attenuation
    stiff_own = stiff_scale * velocity_own * velocity_own
    adj = [fields[5 + k] for k in range(5)]
    grad_v = jnp.zeros((ny, lanes), jnp.float32)
    grad_a = jnp.zeros((ny, lanes), jnp.float32)
    for step in range(STEPS - 1, -1, -1):
        adj, unused = wave_step(adj)
        adj[0] = adj[0] + inject[step]
        div = divs[step]
        q = own(adj[0])
        m = own(adj[4])
        deriv_q = (relax_rate * attenuation_own - (1.0 + attenuation_own)) * div
        deriv_m = -relax_rate * attenuation_own * div
        grad_v = grad_v + (q * deriv_q + m * deriv_m) * (2.0 * stiff_scale * velocity_own)
        grad_a = grad_a + (q * (relax_rate - 1.0) - m * relax_rate) * stiff_own * div
    adjoint_start = jnp.stack([own(f) for f in adj])[None]

    grad_scale = float(BY * BX * BZ) ** (-0.5)
    weight = aperture[0, 0].astype(jnp.float32)
    grads = jnp.stack([grad_v, grad_a]) * weight
    blocks = grads.reshape(2, ny // BY, BY, nx // BX, BX, nz // BZ, BZ)
    blocks = blocks.transpose(1, 3, 5, 0, 2, 4, 6).reshape(-1, 2, BY * BX * BZ)
    slots = block_slot[0]
    sums = jnp.sum(blocks, axis=2) * grad_scale
    ordered = jnp.zeros(sums.shape, jnp.float32).at[slots].set(sums)
    coarse = lax.psum_scatter(ordered, "shot", scatter_dimension=0, tiled=True)
    model_gradient = coarse.T[:, None, :]
    return (forward_end, adjoint_start, model_gradient)


def solution(mesh):
    placed = (
        P("shot", None, "gy", "gx"),
        P("shot", None, "gy", "gx"),
        P("gy", "gx"),
        P("gy", "gx"),
        P("shot", None),
        P("shot", None),
        P("shot", ("gy", "gx"), None),
        P("shot", None, ("gy", "gx"), None),
        P("shot", ("gy", "gx")),
        P(("gy", "gx"), None),
    )
    return jax.shard_map(
        on_device,
        mesh=mesh,
        in_specs=placed,
        out_specs=(
            P("shot", None, "gy", "gx"),
            P("shot", None, "gy", "gx"),
            P(None, ("gy", "gx"), "shot"),
        ),
        check_vma=False,
    )
```

time: 302 us -> 272 us (0.901)
  starting transfers between devices: 132 us -> 22 us
  local copies, waits for them, and re-layouts: 57.9 us -> 114 us
  other arithmetic: 42.2 us -> 70.4 us
    ppermute x48 -> x8, starting transfers between devices: 132 us -> 21.9 us  [the longest x4 16.6 us: exchange(): below = lax.ppermute(tail, axis, [(i, i + 1) for i in range(ends)])]
    slice x39 -> x6, local copies, waits for them, and re-layouts: 9.75 us -> 66.2 us  [the longest x1 63.2 us: on_device(): adj[0] = adj[0] + inject[step]]
    sub x13 -> x8, other arithmetic: 29.9 us -> 8.89 us  [the longest x2 4.93 us: wave_step(): memory = memory - relax_rate * (memory + stiff * att * div)]
    scatter-add x6 -> x1, other arithmetic: 4.79 us -> 25.2 us  [on_device(): jnp.zeros((STEPS, ey * el), jnp.float32).at[:, flat]]
    another operation x21 -> x2, local copies, waits for them, and re-layouts: 16.7 us -> 2.45 us  [the longest x1 1.68 us: on_device(): forward_end = jnp.stack([own(f) for f in state])[None]]
    add x1 -> x7, other arithmetic: 3.79 us -> 16 us  [the longest x2 7.02 us: on_device(): adj[0] = adj[0] + inject[step]]
    select_n x1 -> x8, other arithmetic: 0.01 us -> 8.61 us  [the longest x6 7.77 us: wave_step(): jnp.where(inside, vel_y - forward_diff(lambda d: shift(pres, d, 0)), zero)]
    reshape x13 -> x5, local copies, waits for them, and re-layouts: 9.81 us -> 3.38 us  [the longest x3 2.29 us: on_device(): records.append(state[0].reshape(-1)[own_flat])]
  transfers between devices with their start and end apart: 49 -> 9, of which waited for: 14 -> 6; matrix products, arithmetic and copies ran while one was open for 12% -> 7% of each run, Pallas kernels for 0% -> 0%
where the time goes in v1:
time: 272 us; the launch traced here: 271 us
  local copies, waits for them, and re-layouts  114 us (42%)
  other arithmetic  70.4 us (26%)
  waiting for transfers between devices  49.1 us (18%)
  starting transfers between devices  22 us (8%)
  between operations  15.9 us (6%)
    slice x1, local copies, waits for them, and re-layouts, on_device(): adj[0] = adj[0] + inject[step]  63.2 us
    scatter-add x1, other arithmetic, on_device(): jnp.zeros((STEPS, ey * el), jnp.float32).at[:, flat]  25.2 us
    reduce_scatter x1, waiting for transfers between devices, on_device(): coarse = lax.psum_scatter(ordered, 'shot', scatter_dimension=0, tiled=True)  18.5 us
    ppermute x4, starting transfers between devices, exchange(): below = lax.ppermute(tail, axis, [(i, i + 1) for i in range(ends)])  16.6 us
    ppermute x4, waiting for transfers between devices, exchange(): below = lax.ppermute(tail, axis, [(i, i + 1) for i in range(ends)])  15.8 us
    unnamed x59, local copies, waits for them, and re-layouts  15.2 us
    ppermute x4, waiting for transfers between devices, exchange(): above = lax.ppermute(head, axis, [(i + 1, i) for i in range(ends)])  14.8 us
    another operation x2, local copies, waits for them, and re-layouts, on_device(): grads = jnp.stack([grad_v, grad_a]) * weight  8.11 us
  transfers between devices with their start and end apart: 9, of which 6 were waited for; matrix products, arithmetic and copies ran while one was open for 7% of the time, Pallas kernels for 0%

profile of v1, /device:TPU:0, one launch (start us, length us, event | category | flops | bytes accessed | tf_op | source)
XLA Modules:
  0.0 271.1 jit_solution(8635909456646725362)
XLA Ops:
  10.9 5.6 %collective-permute-start = (f32[12,9,1024]{2,0,1:T(8,128)S(1)}, f32[12,9,1024]{2,0,1:T(8,128)S(1)}, u32[]{:S(2)}, u32[]{:S(2)}) collective-permute-start(f32[12,9,1024]{2,0,1:T(8,128)S(1)} %copy.20), channel_id=1, source_target_pairs={{0,2},{2,4},{4,6},{1,3},{3,5},{5,7},{8,10},{10,12},{12,14},{9,11},... | collective-permute-start | bytes 1327112 | tf_op jit(solution)/shard_map/ppermute | solution.py:38
  21.2 6.3 %collective-permute-done.1 = f32[12,9,1024]{2,0,1:T(8,128)S(1)} collective-permute-done((f32[12,9,1024]{2,0,1:T(8,128)S(1)}, f32[12,9,1024]{2,0,1:T(8,128)S(1)}, u32[]{:S(2)}, u32[]{:S(2)}) %collective-permute-start.1) | collective-permute-done | bytes 442400 | tf_op jit(solution)/shard_map/ppermute | solution.py:39
  32.5 4.6 %collective-permute-start.2 = (f32[12,50,288]{2,1,0:T(8,128)}, f32[12,50,288]{2,1,0:T(8,128)}, u32[]{:S(2)}, u32[]{:S(2)}) collective-permute-start(f32[12,50,288]{2,1,0:T(8,128)} %get-tuple-element.41), channel_id=1, source_target_pairs={{0,1},{2,3},{4,5},{6,7},{8,9},{10,11},{12,13},{14,15},{16,17},{18,... | collective-permute-start | bytes 2073608 | tf_op jit(solution)/shard_map/ppermute | solution.py:38
  42.7 14.6 %collective-permute-done.2 = f32[12,50,288]{2,1,0:T(8,128)} collective-permute-done((f32[12,50,288]{2,1,0:T(8,128)}, f32[12,50,288]{2,1,0:T(8,128)}, u32[]{:S(2)}, u32[]{:S(2)}) %collective-permute-start.2) | collective-permute-done | bytes 691232 | tf_op jit(solution)/shard_map/ppermute | solution.py:38
  57.3 5.1 %collective-permute-done.3 = f32[12,50,288]{2,1,0:T(8,128)} collective-permute-done((f32[12,50,288]{2,1,0:T(8,128)}, f32[12,50,288]{2,1,0:T(8,128)}, u32[]{:S(2)}, u32[]{:S(2)}) %collective-permute-start.3) | collective-permute-done | bytes 691232 | tf_op jit(solution)/shard_map/ppermute | solution.py:39
  62.4 5.7 %concatenate.22 = f32[12,50,1600]{2,1,0:T(8,128)} concatenate(f32[12,50,288]{2,1,0:T(8,128)} %collective-permute-done.2, f32[12,50,1024]{2,1,0:T(8,128)S(1)} %pad_maximum_fusion, f32[12,50,288]{2,1,0:T(8,128)} %collective-permute-done.3), dimensions={2} | concatenate | bytes 7680000 | tf_op jit(solution)/shard_map/concatenate | solution.py:74
  69.4 1.8 fusion.23
  71.2 1.8 fusion.14
  79.2 1.7 fusion.13
  86.0 2.0 gather_fusion.1
  90.7 5.0 %collective-permute-start.4 = (f32[1,4,128]{2,1,0:T(4,128)S(1)}, f32[1,4,128]{2,1,0:T(4,128)S(1)}, u32[]{:S(2)}, u32[]{:S(2)}) collective-permute-start(f32[1,4,128]{2,1,0:T(4,128)S(1)} %maximum_bitcast_fusion), channel_id=1, source_target_pairs={{0,2},{2,4},{4,6},{1,3},{3,5},{5,7},{8,10},{10,12},{12,14},{9,11},... | collective-permute-start | bytes 6152 | tf_op jit(solution)/shard_map/ppermute | solution.py:38
  97.3 1.8 fusion.43
  99.1 1.7 fusion.42
  100.8 1.7 fusion.41
  103.9 1.7 fusion.40
  107.7 3.4 %collective-permute-done.7 = f32[3,4,128]{2,1,0:T(4,128)S(1)} collective-permute-done((f32[3,4,128]{2,1,0:T(4,128)S(1)}, f32[3,4,128]{2,1,0:T(4,128)S(1)}, u32[]{:S(2)}, u32[]{:S(2)}) %collective-permute-start.7) | collective-permute-done | bytes 6176 | tf_op jit(solution)/shard_map/ppermute | solution.py:39
  113.0 25.2 %scatter_custom_fusion = f32[3,80000]{0,1:T(8,128)} fusion(s32[1152]{0:T(1024)S(1)} %fusion.55, f32[1152,3]{1,0:T(8,128)} %copy.24, f32[]{:T(128)} %constant.185.clone.1), kind=kCustom, calls=%fused_computation.8 | custom fusion | flops 3456 | bytes 960512 | tf_op jit(solution)/shard_map/scatter-add | solution.py:145
  138.3 63.2 %slice_reduce_fusion.1 = (f32[80000]{0:T(1024)}, f32[80000]{0:T(1024)}, f32[80000]{0:T(1024)S(1)}) fusion(f32[3,80000]{0,1:T(8,128)} %scatter_custom_fusion), kind=kLoop, calls=%fused_computation.6 | loop fusion | bytes 1920000 | tf_op jit(solution)/shard_map/slice | solution.py:156
  201.6 2.8 %select_add_fusion.5 = (f32[50,1600]{1,0:T(8,128)S(1)}, f32[50,1600]{1,0:T(8,128)}, f32[50,1600]{1,0:T(8,128)}) fusion(f32[50,1600]{1,0:T(8,128)S(1)} %squeeze.94, f32[50,1600]{1,0:T(8,128)S(1)} %get-tuple-element.31, f32[12,50,1600]{2,1,0:T(8,128)} %concatenate.22, s32[1600]{0:T(1024)S(1)} %get-tuple-element.57, s32[1600]{0:T(1024)S(1)} %get-tuple-element.58, ...), kind=kLoop, calls=%fused_computation.68 | loop fusion | flops 4160000 | bytes 3548854 | tf_op jit(solution)/shard_map/add | solution.py:156
  204.8 2.3 subtract_select_fusion.3
  207.1 1.9 squeeze.95
  209.0 4.2 %select_add_fusion.4 = (f32[50,1600]{1,0:T(8,128)S(1)}, f32[50,1600]{1,0:T(8,128)}) fusion(f32[50,1600]{1,0:T(8,128)} %squeeze.95, f32[50,1600]{1,0:T(8,128)S(1)} %get-tuple-element.31, f32[50,1600]{1,0:T(8,128)S(1)} %squeeze.94, f32[50,1600]{1,0:T(8,128)} %get-tuple-element.22, f32[50,1600]{1,0:T(8,128)} %get-tuple-element.23, ...), kind=kLoop, calls=%fused_computation.62 | loop fusion | flops 4560000 | bytes 3868854 | tf_op jit(solution)/shard_map/add | solution.py:156
  215.7 1.9 squeeze.96
  217.5 3.4 %multiply_subtract_fusion = (f32[50,1600]{1,0:T(8,128)S(1)}, f32[50,1600]{1,0:T(8,128)S(1)}) fusion(f32[50,1600]{1,0:T(8,128)} %get-tuple-element.20, f32[50,1600]{1,0:T(8,128)S(1)} %get-tuple-element.29, f32[50,1600]{1,0:T(8,128)} %add_subtract_fusion, s32[1600]{0:T(1024)S(1)} %copy-done.13, s32[1600]{0:T(1024)S(1)} %copy-done.14, ...), kind=kLoop, calls=%fused_computation.57 | loop fusion | flops 3280000 | bytes 2254400 | tf_op jit(solution)/shard_map/sub | solution.py:101
  221.0 2.3 add_multiply_fusion.1
  223.9 1.9 multiply_add_fusion
  225.8 1.7 fusion.36
  227.5 1.7 fusion.35
  230.9 3.4 %stack.74 = f32[1,4,8,4,8,4,8]{6,5,4,3,2,1,0:T(4,128)S(1)} reshape(f32[32,1024]{1,0:T(8,128)} %multiply_add_fusion) | data formatting | bytes 262144 | tf_op jit(solution)/shard_map/stack | solution.py:168
  234.2 4.7 %stack.73 = f32[1,4,8,4,8,4,8]{6,5,4,3,2,1,0:T(4,128)} reshape(f32[32,1024]{1,0:T(8,128)} %get-tuple-element.15) | data formatting | bytes 262144 | tf_op jit(solution)/shard_map/stack | solution.py:168
  239.0 3.0 %fusion.2 = f32[2,4,4,4]{3,2,1,0:T(4,128)S(1)} fusion(f32[1,4,8,4,8,4,8]{6,5,4,3,2,1,0:T(4,128)S(1)} %stack.74, f32[1,4,8,4,8,4,8]{6,5,4,3,2,1,0:T(4,128)} %stack.73, f32[]{:T(128)} %bitcast.45), kind=kLoop, calls=%fused_computation.11 | loop fusion | flops 196480 | bytes 262660 | tf_op jit(solution)/shard_map/reduce_sum | solution.py:172
  244.4 18.5 %reduce-scatter.2.cloned.1.call-done = f32[16,2]{1,0:T(8,128)} async-done(((f32[64,2]{1,0:T(8,128)}), f32[16,2]{1,0:T(8,128)}) %reduce-scatter.2.cloned.1.call-update) | async-done | bytes 144 | tf_op jit(solution)/shard_map/reduce_scatter | solution.py:174
  (116 shorter events, 48.6 us)
Async XLA Ops:
  7.2 255.7 %reduce-scatter.2.cloned.1.call-start = ((), (), s32[]{:S(2)}) async-start(), calls=%async_computation.1 | async-start | bytes 40960 | tf_op jit(solution)/shard_map/reduce_scatter | solution.py:174
  7.2 11.2 %copy-start.18 = (f32[1,3]{1,0:T(1,128)S(1)}, f32[1,3]{1,0:T(1,128)}, u32[]{:S(2)}) copy-start(f32[1,3]{1,0:T(1,128)} %param.16) | copy-start | bytes 40
  7.2 12.4 %copy-start.21 = (s32[1,1,128]{2,1,0:T(1,128)S(1)}, s32[1,1,128]{2,1,0:T(1,128)}, u32[]{:S(2)}) copy-start(s32[1,1,128]{2,1,0:T(1,128)} %param.18) | copy-start | bytes 1540
  7.2 13.5 %copy-start.22 = (s32[1,64]{1,0:T(1,128)S(1)}, s32[1,64]{1,0:T(1,128)}, u32[]{:S(2)}) copy-start(s32[1,64]{1,0:T(1,128)} %param.21) | copy-start | bytes 772
  8.9 20.4 %copy-start.7 = (f32[1,5,32,1024]{3,2,1,0:T(8,128)S(1)}, f32[1,5,32,1024]{3,2,1,0:T(8,128)}, u32[]{:S(2)}) copy-start(f32[1,5,32,1024]{3,2,1,0:T(8,128)} %param.13) | copy-start | bytes 1966084
  8.9 20.4 %copy-start.8 = (f32[32,1024]{1,0:T(8,128)S(1)}, f32[32,1024]{1,0:T(8,128)}, u32[]{:S(2)}) copy-start(f32[32,1024]{1,0:T(8,128)} %param.14) | copy-start | bytes 393220
  9.3 18.3 %collective-permute-start.1 = (f32[12,9,1024]{2,0,1:T(8,128)S(1)}, f32[12,9,1024]{2,0,1:T(8,128)S(1)}, u32[]{:S(2)}, u32[]{:S(2)}) collective-permute-start(f32[12,9,1024]{2,0,1:T(8,128)S(1)} %copy.21), channel_id=1, source_target_pairs={{2,0},{4,2},{6,4},{3,1},{5,3},{7,5},{10,8},{12,10},{14,12},{11,9},... | collective-permute-start | bytes 1327112 | tf_op jit(solution)/shard_map/ppermute | solution.py:39
  10.9 18.1 %collective-permute-start = (f32[12,9,1024]{2,0,1:T(8,128)S(1)}, f32[12,9,1024]{2,0,1:T(8,128)S(1)}, u32[]{:S(2)}, u32[]{:S(2)}) collective-permute-start(f32[12,9,1024]{2,0,1:T(8,128)S(1)} %copy.20), channel_id=1, source_target_pairs={{0,2},{2,4},{4,6},{1,3},{3,5},{5,7},{8,10},{10,12},{12,14},{9,11},... | collective-permute-start | bytes 1327112 | tf_op jit(solution)/shard_map/ppermute | solution.py:38
  32.5 24.8 %collective-permute-start.2 = (f32[12,50,288]{2,1,0:T(8,128)}, f32[12,50,288]{2,1,0:T(8,128)}, u32[]{:S(2)}, u32[]{:S(2)}) collective-permute-start(f32[12,50,288]{2,1,0:T(8,128)} %get-tuple-element.41), channel_id=1, source_target_pairs={{0,1},{2,3},{4,5},{6,7},{8,9},{10,11},{12,13},{14,15},{16,17},{18,... | collective-permute-start | bytes 2073608 | tf_op jit(solution)/shard_map/ppermute | solution.py:38
  37.1 25.3 %collective-permute-start.3 = (f32[12,50,288]{2,1,0:T(8,128)}, f32[12,50,288]{2,1,0:T(8,128)}, u32[]{:S(2)}, u32[]{:S(2)}) collective-permute-start(f32[12,50,288]{2,1,0:T(8,128)} %get-tuple-element.40), channel_id=1, source_target_pairs={{1,0},{3,2},{5,4},{7,6},{9,8},{11,10},{13,12},{15,14},{17,16},{19,... | collective-permute-start | bytes 2073608 | tf_op jit(solution)/shard_map/ppermute | solution.py:39
  42.7 26.8 %copy-start.15 = (pred[1600]{0:T(1024)(128)(4,1)S(1)}, pred[1600]{0:T(1024)(128)(4,1)}, u32[]{:S(2)}) copy-start(pred[1600]{0:T(1024)(128)(4,1)} %get-tuple-element.60) | copy-start | bytes 4804
  42.7 28.6 %copy-start.13 = (s32[1600]{0:T(1024)S(1)}, s32[1600]{0:T(1024)}, u32[]{:S(2)}) copy-start(s32[1600]{0:T(1024)} %get-tuple-element.55) | copy-start | bytes 19204
  42.7 28.6 %copy-start.14 = (s32[1600]{0:T(1024)S(1)}, s32[1600]{0:T(1024)}, u32[]{:S(2)}) copy-start(s32[1600]{0:T(1024)} %get-tuple-element.56) | copy-start | bytes 19204
  42.7 28.6 %copy-start.16 = (pred[1600]{0:T(1024)(128)(4,1)S(1)}, pred[1600]{0:T(1024)(128)(4,1)}, u32[]{:S(2)}) copy-start(pred[1600]{0:T(1024)(128)(4,1)} %get-tuple-element.59) | copy-start | bytes 4804
  68.1 4.9 %copy-start = (f32[12,50,1600]{2,1,0:T(8,128)S(1)}, f32[12,50,1600]{2,1,0:T(8,128)}, u32[]{:S(2)}) copy-start(f32[12,50,1600]{2,1,0:T(8,128)} %concatenate.22) | copy-start | bytes 11520004
  68.1 4.9 %copy-start.17 = (pred[1600]{0:T(1024)(128)(4,1)S(1)}, pred[1600]{0:T(1024)(128)(4,1)}, u32[]{:S(2)}) copy-start(pred[1600]{0:T(1024)(128)(4,1)} %iota_compare_fusion) | copy-start | bytes 4804
  77.2 3.7 %copy-start.9 = (f32[50,1600]{1,0:T(8,128)}, f32[50,1600]{1,0:T(8,128)S(1)}, u32[]{:S(2)}) copy-start(f32[50,1600]{1,0:T(8,128)S(1)} %add_subtract_fusion.2) | copy-start | bytes 960004
  77.7 3.3 %copy-start.11 = (f32[50,1600]{1,0:T(8,128)}, f32[50,1600]{1,0:T(8,128)S(1)}, u32[]{:S(2)}) copy-start(f32[50,1600]{1,0:T(8,128)S(1)} %get-tuple-element.49) | copy-start | bytes 960004
  77.7 3.3 %copy-start.12 = (f32[50,1600]{1,0:T(8,128)}, f32[50,1600]{1,0:T(8,128)S(1)}, u32[]{:S(2)}) copy-start(f32[50,1600]{1,0:T(8,128)S(1)} %get-tuple-element.48) | copy-start | bytes 960004
  79.2 1.8 copy-start.6
  79.2 10.2 %copy-start.20 = (f32[1,3,1,128]{3,2,1,0:T(1,128)S(1)}, f32[1,3,1,128]{3,2,1,0:T(1,128)}, u32[]{:S(2)}) copy-start(f32[1,3,1,128]{3,2,1,0:T(1,128)} %param.19) | copy-start | bytes 4612
  79.2 10.2 %copy-start.19 = (f32[1,128]{1,0:T(1,128)S(1)}, f32[1,128]{1,0:T(1,128)}, u32[]{:S(2)}) copy-start(f32[1,128]{1,0:T(1,128)} %convert_bitcast_fusion) | copy-start | bytes 1540
  81.0 0.8 copy-start.10
  89.4 13.0 %collective-permute-start.5 = (f32[1,4,128]{2,1,0:T(4,128)S(1)}, f32[1,4,128]{2,1,0:T(4,128)S(1)}, u32[]{:S(2)}, u32[]{:S(2)}) collective-permute-start(f32[1,4,128]{2,1,0:T(4,128)S(1)} %maximum_bitcast_fusion), channel_id=1, source_target_pairs={{2,0},{4,2},{6,4},{3,1},{5,3},{7,5},{10,8},{12,10},{14,12},{11,9},... | collective-permute-start | bytes 6152 | tf_op jit(solution)/shard_map/ppermute | solution.py:39
  90.7 11.7 %collective-permute-start.4 = (f32[1,4,128]{2,1,0:T(4,128)S(1)}, f32[1,4,128]{2,1,0:T(4,128)S(1)}, u32[]{:S(2)}, u32[]{:S(2)}) collective-permute-start(f32[1,4,128]{2,1,0:T(4,128)S(1)} %maximum_bitcast_fusion), channel_id=1, source_target_pairs={{0,2},{2,4},{4,6},{1,3},{3,5},{5,7},{8,10},{10,12},{12,14},{9,11},... | collective-permute-start | bytes 6152 | tf_op jit(solution)/shard_map/ppermute | solution.py:38
  97.3 104.4 %copy-start.1 = (f32[50,1600]{1,0:T(8,128)}, f32[50,1600]{1,0:T(8,128)S(1)}, u32[]{:S(2)}) copy-start(f32[50,1600]{1,0:T(8,128)S(1)} %get-tuple-element.33) | copy-start | bytes 960004
  102.5 4.6 %collective-permute-start.6 = (f32[3,4,128]{2,1,0:T(4,128)S(1)}, f32[3,4,128]{2,1,0:T(4,128)S(1)}, u32[]{:S(2)}, u32[]{:S(2)}) collective-permute-start(f32[3,4,128]{2,1,0:T(4,128)S(1)} %pad_maximum_fusion.2), channel_id=1, source_target_pairs={{0,1},{2,3},{4,5},{6,7},{8,9},{10,11},{12,13},{14,15},{16,17},{18,... | collective-permute-start | bytes 18440 | tf_op jit(solution)/shard_map/ppermute | solution.py:38
  105.6 5.5 %collective-permute-start.7 = (f32[3,4,128]{2,1,0:T(4,128)S(1)}, f32[3,4,128]{2,1,0:T(4,128)S(1)}, u32[]{:S(2)}, u32[]{:S(2)}) collective-permute-start(f32[3,4,128]{2,1,0:T(4,128)S(1)} %pad_maximum_fusion.2), channel_id=1, source_target_pairs={{1,0},{3,2},{5,4},{7,6},{9,8},{11,10},{13,12},{15,14},{17,16},{19,... | collective-permute-start | bytes 18440 | tf_op jit(solution)/shard_map/ppermute | solution.py:39
  207.1 7.2 %copy-start.2 = (f32[50,1600]{1,0:T(8,128)S(1)}, f32[50,1600]{1,0:T(8,128)}, u32[]{:S(2)}) copy-start(f32[50,1600]{1,0:T(8,128)} %get-tuple-element.46) | copy-start | bytes 960004
  209.0 5.3 %copy-start.3 = (f32[50,1600]{1,0:T(8,128)S(1)}, f32[50,1600]{1,0:T(8,128)}, u32[]{:S(2)}) copy-start(f32[50,1600]{1,0:T(8,128)} %get-tuple-element.47) | copy-start | bytes 960004
  213.2 7.7 %copy-start.4 = (f32[50,1600]{1,0:T(8,128)S(1)}, f32[50,1600]{1,0:T(8,128)}, u32[]{:S(2)}) copy-start(f32[50,1600]{1,0:T(8,128)} %get-tuple-element.22) | copy-start | bytes 960004
  214.3 6.6 %copy-start.5 = (f32[50,1600]{1,0:T(8,128)S(1)}, f32[50,1600]{1,0:T(8,128)}, u32[]{:S(2)}) copy-start(f32[50,1600]{1,0:T(8,128)} %get-tuple-element.20) | copy-start | bytes 960004
Sparse Core Ops, SparseCore 0:
  243.8 19.0 reduce-scatter.1

commit v2 on v1

--- a/solution.py
+++ b/solution.py
@@ -128,22 +128,13 @@
     forward_end = jnp.stack([own(f) for f in state])[None]
 
     resid = jnp.stack(records) - observed[0, :, 0]
-    message = jnp.concatenate([recs.astype(jnp.float32)[None], resid], axis=0)[None]
-    below, above = exchange(message, "gy", 0, 1)
-    message = jnp.concatenate([below, message, above], axis=0)
-    left, right = exchange(message, "gx", 0, 3)
-    message = jnp.concatenate([left, message, right], axis=0)
-    off_y = jnp.array([-1, 0, 1] * 3, jnp.int32)[:, None] * ny
-    off_x = jnp.repeat(jnp.array([-1, 0, 1], jnp.int32), 3)[:, None] * nx
-    cells = message[:, 0].astype(jnp.int32)
-    at_y = cells // (nx * nz) + off_y + r
-    at_x = cells // nz % nx + off_x + r
-    at_z = cells % nz
-    fits = (at_y >= 0) & (at_y < ey) & (at_x >= 0) & (at_x < ex)
-    flat = jnp.where(fits, at_y * el + at_x * nz + at_z, ey * el).reshape(-1)
-    amounts = message[:, 1:].transpose(1, 0, 2).reshape(STEPS, -1)
-    inject = jnp.zeros((STEPS, ey * el), jnp.float32).at[:, flat].add(amounts, mode="drop")
-    inject = inject.reshape(STEPS, ey, el)
+    inject = jnp.stack(
+        [jnp.zeros((ny * lanes,), jnp.float32).at[recs].add(resid[n]) for n in range(STEPS)]
+    ).reshape(STEPS, ny, lanes)
+    below, above = exchange(inject, "gy", 1, r)
+    inject = jnp.concatenate([below, inject, above], axis=1)
+    left, right = exchange(inject, "gx", 2, r * nz)
+    inject = jnp.concatenate([left, inject, right], axis=2)
 
     velocity_own = velocity
     attenuation_own = attenuation
@@ -171,7 +162,11 @@
     slots = block_slot[0]
     sums = jnp.sum(blocks, axis=2) * grad_scale
     ordered = jnp.zeros(sums.shape, jnp.float32).at[slots].set(sums)
-    coarse = lax.psum_scatter(ordered, "shot", scatter_dimension=0, tiled=True)
+    shots = lax.axis_size("shot")
+    parts = lax.all_to_all(
+        ordered.reshape(shots, -1, 2), "shot", split_axis=0, concat_axis=0, tiled=True
+    )
+    coarse = jnp.sum(parts, axis=0)
     model_gradient = coarse.T[:, None, :]
     return (forward_end, adjoint_start, model_gradient)
 

time: 272 us -> 160 us (0.59)
  local copies, waits for them, and re-layouts: 114 us -> 60.8 us
  other arithmetic: 70.4 us -> 32.2 us
  between operations: 15.9 us -> 2.72 us
  waiting for transfers between devices: 49.1 us -> 37.2 us
  starting transfers between devices: 22 us -> 26.1 us
    slice x1, local copies, waits for them, and re-layouts: 63.2 us -> 14.1 us  [on_device(): adj = [fields[5 + k] for k in range(5)]]
    scatter-add x1 -> x3, other arithmetic: 25.2 us -> 4.09 us  [on_device(): jnp.zeros((ny * lanes,), jnp.float32).at[recs].add(resid[n])]
    reduce_scatter x1 -> x0, waiting for transfers between devices: 18.5 us -> none  [on_device(): coarse = lax.psum_scatter(ordered, 'shot', scatter_dimension=0, tiled=True)]
    select_n x6, other arithmetic: 7.77 us -> 3.37 us  [wave_step(): jnp.where(inside, vel_y - forward_diff(lambda d: shift(pres, d, 0)), zero)]
    squeeze x3 -> x1, local copies, waits for them, and re-layouts: 3.88 us -> 0.03 us  [on_device(): adj[0] = adj[0] + inject[step]]
    unnamed x59 -> x58, local copies, waits for them, and re-layouts: 15.2 us -> 11.4 us
    all_to_all x0 -> x1, starting transfers between devices: none -> 3.2 us  [on_device(): lax.all_to_all(ordered.reshape(shots, -1, 2), 'shot', split_axis=0, conca...]
    all_to_all x0 -> x1, waiting for transfers between devices: none -> 2.99 us  [on_device(): lax.all_to_all(ordered.reshape(shots, -1, 2), 'shot', split_axis=0, conca...]
  transfers between devices with their start and end apart: 9 -> 9, of which waited for: 6 -> 8; matrix products, arithmetic and copies ran while one was open for 7% -> 7% of each run, Pallas kernels for 0% -> 0%
where the time goes in v2:
time: 160 us; the launch traced here: 159 us
  local copies, waits for them, and re-layouts  60.8 us (38%)
  waiting for transfers between devices  37.2 us (23%)
  other arithmetic  32.2 us (20%)
  starting transfers between devices  26.1 us (16%)
  between operations  2.72 us (2%)
    ppermute x4, starting transfers between devices, exchange(): below = lax.ppermute(tail, axis, [(i, i + 1) for i in range(ends)])  17.5 us
    ppermute x4, waiting for transfers between devices, exchange(): below = lax.ppermute(tail, axis, [(i, i + 1) for i in range(ends)])  17.4 us
    ppermute x4, waiting for transfers between devices, exchange(): above = lax.ppermute(head, axis, [(i + 1, i) for i in range(ends)])  16.8 us
    slice x1, local copies, waits for them, and re-layouts, on_device(): adj = [fields[5 + k] for k in range(5)]  14.1 us
    unnamed x58, local copies, waits for them, and re-layouts  11.4 us
    another operation x2, local copies, waits for them, and re-layouts, on_device(): grads = jnp.stack([grad_v, grad_a]) * weight  6.34 us
    concatenate x1, local copies, waits for them, and re-layouts, on_device(): fields = jnp.concatenate([left, fields, right], axis=2)  6.31 us
    add x3, other arithmetic, on_device(): state[0] + jnp.where(src_here, wavelet[0, step], jnp.float32(0.0))  6.04 us
  transfers between devices with their start and end apart: 9, of which 8 were waited for; matrix products, arithmetic and copies ran while one was open for 7% of the time, Pallas kernels for 0%

profile of v2, /device:TPU:0, one launch (start us, length us, event | category | flops | bytes accessed | tf_op | source)
XLA Modules:
  0.0 159.0 jit_solution(17113448642618576887)
XLA Ops:
  2.7 2.2 %copy_bitcast_fusion = (f32[5,32,1024]{2,0,1:T(8,128)S(1)}, f32[5,32,1024]{2,0,1:T(8,128)S(1)}) fusion(f32[1,5,32,1024]{3,2,1,0:T(8,128)} %param.11, f32[1,5,32,1024]{3,2,1,0:T(8,128)} %param.10), kind=kLoop, calls=%fused_computation.16 | loop fusion | bytes 2621440 | tf_op jit(solution)/shard_map/squeeze | solution.py:69
  7.5 6.4 %collective-permute-start = (f32[12,9,1024]{2,0,1:T(8,128)S(1)}, f32[12,9,1024]{2,0,1:T(8,128)}, u32[]{:S(2)}, u32[]{:S(2)}) collective-permute-start(f32[12,9,1024]{2,0,1:T(8,128)S(1)} %get-tuple-element.46), channel_id=1, source_target_pairs={{0,2},{2,4},{4,6},{1,3},{3,5},{5,7},{8,10},{10,12},{12,14},{9,11},... | collective-permute-start | bytes 1327112 | tf_op jit(solution)/shard_map/ppermute | solution.py:38
  15.3 9.1 %collective-permute-done.1 = f32[12,9,1024]{2,0,1:T(8,128)S(1)} collective-permute-done((f32[12,9,1024]{2,0,1:T(8,128)S(1)}, f32[12,9,1024]{2,0,1:T(8,128)S(1)}, u32[]{:S(2)}, u32[]{:S(2)}) %collective-permute-start.1) | collective-permute-done | bytes 442400 | tf_op jit(solution)/shard_map/ppermute | solution.py:39
  25.6 2.5 %pad_maximum_fusion = f32[12,50,1024]{2,0,1:T(8,128)S(1)} fusion(f32[12,9,1024]{2,0,1:T(8,128)} %copy-done.16, f32[1,32,1024]{2,0,1:T(1,128)S(1)} %broadcast_in_dim.43, f32[1,32,1024]{2,0,1:T(1,128)} %copy-done.14, f32[5,32,1024]{2,0,1:T(8,128)} %copy-done, f32[5,32,1024]{2,0,1:T(8,128)} %copy-done.1, f32[12,9,1024]{2,0,1:T(8,128)} %collective-permute-done), kind=kLoop, calls=%fused_computation.9 | loop fusion | flops 3072000 | bytes 4915200 | tf_op jit(solution)/shard_map/concatenate | solution.py:72
  29.9 4.5 %collective-permute-start.2 = (f32[12,50,288]{2,1,0:T(8,128)}, f32[12,50,288]{2,1,0:T(8,128)}, u32[]{:S(2)}, u32[]{:S(2)}) collective-permute-start(f32[12,50,288]{2,1,0:T(8,128)} %copy.36), channel_id=1, source_target_pairs={{0,1},{2,3},{4,5},{6,7},{8,9},{10,11},{12,13},{14,15},{16,17},{18,... | collective-permute-start | bytes 2073608 | tf_op jit(solution)/shard_map/ppermute | solution.py:38
  35.7 1.5 collective-permute-start.3
  38.6 16.0 %collective-permute-done.2 = f32[12,50,288]{2,1,0:T(8,128)} collective-permute-done((f32[12,50,288]{2,1,0:T(8,128)}, f32[12,50,288]{2,1,0:T(8,128)}, u32[]{:S(2)}, u32[]{:S(2)}) %collective-permute-start.2) | collective-permute-done | bytes 691232 | tf_op jit(solution)/shard_map/ppermute | solution.py:38
  54.6 2.5 %copy.38 = f32[12,50,288]{2,0,1:T(8,128)} copy(f32[12,50,288]{2,1,0:T(8,128)} %collective-permute-done.2) | data formatting | bytes 1382400 | tf_op jit(solution)/shard_map/ppermute | solution.py:38
  57.1 3.8 %collective-permute-done.3 = f32[12,50,288]{2,1,0:T(8,128)} collective-permute-done((f32[12,50,288]{2,1,0:T(8,128)}, f32[12,50,288]{2,1,0:T(8,128)}, u32[]{:S(2)}, u32[]{:S(2)}) %collective-permute-start.3) | collective-permute-done | bytes 691232 | tf_op jit(solution)/shard_map/ppermute | solution.py:39
  61.0 2.5 %copy.39 = f32[12,50,288]{2,0,1:T(8,128)} copy(f32[12,50,288]{2,1,0:T(8,128)} %collective-permute-done.3) | data formatting | bytes 1382400 | tf_op jit(solution)/shard_map/ppermute | solution.py:39
  63.4 6.3 %concatenate.19 = f32[12,50,1600]{2,0,1:T(8,128)} concatenate(f32[12,50,288]{2,0,1:T(8,128)} %copy.38, f32[12,50,1024]{2,0,1:T(8,128)S(1)} %pad_maximum_fusion, f32[12,50,288]{2,0,1:T(8,128)} %copy.39), dimensions={2} | concatenate | bytes 7680000 | tf_op jit(solution)/shard_map/concatenate | solution.py:74
  69.7 14.1 %fusion.69 = (f32[1,50,1600]{2,0,1:T(1,128)}, f32[1,50,1600]{2,0,1:T(1,128)}, f32[1,50,1600]{2,0,1:T(1,128)S(1)}, f32[1,50,1600]{2,0,1:T(1,128)S(1)}, f32[1,50,1...) fusion(f32[12,50,1600]{2,0,1:T(8,128)} %concatenate.19), kind=kLoop, calls=%fused_computation.182 | loop fusion | bytes 7680000 | tf_op jit(solution)/shard_map/slice | solution.py:142
  84.7 1.5 fusion.9
  86.7 1.4 fusion.14
  88.1 2.2 %fusion.10 = (f32[50,1600]{1,0:T(8,128)S(1)}, f32[50,1600]{1,0:T(8,128)S(1)}) fusion(f32[50,1600]{1,0:T(8,128)S(1)} %get-tuple-element.31, f32[]{:T(128)} %bitcast.11, pred[1600]{0:T(1024)(128)(4,1)S(1)} %iota_compare_fusion, pred[50]{0:T(512)(128)(4,1)S(1)} %get-tuple-element.83, f32[50,1600]{1,0:T(8,128)S(1)} %get-tuple-element.29, ...), kind=kLoop, calls=%fused_computation.36 | loop fusion | flops 5120000 | bytes 3230512 | tf_op jit(solution)/shard_map/add | solution.py:125
  91.0 1.5 multiply_subtract_fusion.2
  92.6 2.3 %fusion.11 = f32[50,1600]{1,0:T(8,128)S(1)} fusion(f32[50,1600]{1,0:T(8,128)S(1)} %get-tuple-element.31, f32[50,1600]{1,0:T(8,128)S(1)} %get-tuple-element.25, f32[]{:T(128)} %bitcast.12, f32[]{:T(128)} %bitcast.11, f32[50,1600]{1,0:T(8,128)S(1)} %get-tuple-element.27, pred[1600]{0:T(1024)(128)(4,1)S(1)} %iota_compare_fusion, ...), kind=kLoop, calls=%fused_computation.37 | loop fusion | flops 2960000 | bytes 2576116 | tf_op jit(solution)/shard_map/add | solution.py:125
  96.3 1.7 %fusion.44 = f32[5,32,1024]{2,1,0:T(8,128)} fusion(f32[5,32,1024]{2,1,0:T(8,128)} %fusion.45, f32[50,1600]{1,0:T(8,128)} %copy-done.11), kind=kLoop, calls=%fused_computation.121 | loop fusion | bytes 262144
  98.0 1.7 %fusion.43 = f32[5,32,1024]{2,1,0:T(8,128)} fusion(f32[5,32,1024]{2,1,0:T(8,128)} %fusion.44, f32[50,1600]{1,0:T(8,128)} %copy-done.10), kind=kLoop, calls=%fused_computation.119 | loop fusion | bytes 262144
  104.6 1.5 scatter_custom_fusion.1
  108.8 5.1 %collective-permute-start.4 = (f32[3,9,1024]{2,1,0:T(8,128)S(1)}, f32[3,9,1024]{2,1,0:T(8,128)S(1)}, u32[]{:S(2)}, u32[]{:S(2)}) collective-permute-start(f32[3,9,1024]{2,1,0:T(8,128)S(1)} %get-tuple-element.50), channel_id=1, source_target_pairs={{0,2},{2,4},{4,6},{1,3},{3,5},{5,7},{8,10},{10,12},{12,14},{9,11},... | collective-permute-start | bytes 331784 | tf_op jit(solution)/shard_map/ppermute | solution.py:38
  115.2 1.7 %fusion.42 = f32[5,32,1024]{2,1,0:T(8,128)} fusion(f32[5,32,1024]{2,1,0:T(8,128)} %fusion.43, f32[50,1600]{1,0:T(8,128)} %copy-done.9), kind=kLoop, calls=%fused_computation.117 | loop fusion | bytes 262144
  117.3 1.5 collective-permute-start.6
  120.1 1.7 %fusion.41 = f32[5,32,1024]{2,1,0:T(8,128)} fusion(f32[5,32,1024]{2,1,0:T(8,128)} %fusion.42, f32[50,1600]{1,0:T(8,128)} %get-tuple-element.24), kind=kLoop, calls=%fused_computation.115 | loop fusion | bytes 262144 | tf_op jit(solution)/shard_map/stack | solution.py:128
  123.3 3.8 %collective-permute-done.7 = f32[3,50,288]{2,1,0:T(8,128)} collective-permute-done((f32[3,50,288]{2,1,0:T(8,128)S(1)}, f32[3,50,288]{2,1,0:T(8,128)}, u32[]{:S(2)}, u32[]{:S(2)}) %collective-permute-start.7) | collective-permute-done | bytes 172832 | tf_op jit(solution)/shard_map/ppermute | solution.py:39
  127.1 1.5 concatenate.21
  128.7 3.7 %fusion.13 = (f32[50,1600]{1,0:T(8,128)S(1)}, f32[50,1600]{1,0:T(8,128)S(1)}, f32[50,1600]{1,0:T(8,128)S(1)}) fusion(f32[3,50,1600]{2,1,0:T(8,128)S(1)} %concatenate.21, f32[50,1600]{1,0:T(8,128)S(1)} %get-tuple-element.31, f32[1,50,1600]{2,0,1:T(1,128)S(1)} %get-tuple-element.34, s32[1600]{0:T(1024)S(1)} %get-tuple-element.78, ...), kind=kLoop, calls=%fused_computation.42 | loop fusion | flops 4160000 | bytes 3548854 | tf_op jit(solution)/shard_map/add | solution.py:147
  140.4 2.5 %stack.90 = f32[1,4,8,4,8,4,8]{6,5,4,3,2,1,0:T(4,128)S(1)} reshape(f32[32,1024]{1,0:T(8,128)S(1)} %multiply_add_fusion) | data formatting | bytes 262144 | tf_op jit(solution)/shard_map/stack | solution.py:159
  142.9 3.9 %stack.89 = f32[1,4,8,4,8,4,8]{6,5,4,3,2,1,0:T(4,128)} reshape(f32[32,1024]{1,0:T(8,128)S(1)} %get-tuple-element.15) | data formatting | bytes 262144 | tf_op jit(solution)/shard_map/stack | solution.py:159
  146.7 3.0 %fusion = f32[2,4,4,4]{3,2,1,0:T(4,128)S(1)} fusion(f32[1,4,8,4,8,4,8]{6,5,4,3,2,1,0:T(4,128)S(1)} %stack.90, f32[1,4,8,4,8,4,8]{6,5,4,3,2,1,0:T(4,128)} %stack.89, f32[]{:T(128)} %bitcast.43), kind=kLoop, calls=%fused_computation.8 | loop fusion | flops 196480 | bytes 262660 | tf_op jit(solution)/shard_map/reduce_sum | solution.py:163
  151.4 3.2 %all-to-all-start = ((f32[4,16,2]{1,2,0:T(2,128)}), f32[4,16,2]{1,2,0:T(2,128)S(1)}, u32[]{:S(2)}, u32[]{:S(2)}) async-start(f32[4,16,2]{1,2,0:T(2,128)} %copy.53), calls=%async_computation | async-start | bytes 8192 | tf_op jit(solution)/shard_map/all_to_all | solution.py:166
  155.4 3.0 %all-to-all-done = f32[4,16,2]{1,2,0:T(2,128)S(1)} async-done(((f32[4,16,2]{1,2,0:T(2,128)}), f32[4,16,2]{1,2,0:T(2,128)S(1)}, u32[]{:S(2)}, u32[]{:S(2)}) %all-to-all-start) | async-done | bytes 544 | tf_op jit(solution)/shard_map/all_to_all | solution.py:166
  (116 shorter events, 36.4 us)
Async XLA Ops:
  2.6 3.5 %copy-start.14 = (f32[1,32,1024]{2,0,1:T(1,128)}, f32[1,32,1024]{2,0,1:T(1,128)S(1)}, u32[]{:S(2)}) copy-start(f32[1,32,1024]{2,0,1:T(1,128)S(1)} %broadcast_in_dim.42) | copy-start | bytes 393220
  2.6 12.0 %copy-start.21 = (s32[1,1,128]{2,1,0:T(1,128)S(1)}, s32[1,1,128]{2,1,0:T(1,128)}, u32[]{:S(2)}) copy-start(s32[1,1,128]{2,1,0:T(1,128)} %param.16) | copy-start | bytes 1540
  2.7 12.0 %copy-start.19 = (f32[1,3]{1,0:T(1,128)S(1)}, f32[1,3]{1,0:T(1,128)}, u32[]{:S(2)}) copy-start(f32[1,3]{1,0:T(1,128)} %param.14) | copy-start | bytes 40
  4.8 1.0 copy-start
  4.8 1.4 copy-start.1
  6.2 18.2 %collective-permute-start.1 = (f32[12,9,1024]{2,0,1:T(8,128)S(1)}, f32[12,9,1024]{2,0,1:T(8,128)S(1)}, u32[]{:S(2)}, u32[]{:S(2)}) collective-permute-start(f32[12,9,1024]{2,0,1:T(8,128)S(1)} %get-tuple-element.47), channel_id=1, source_target_pairs={{2,0},{4,2},{6,4},{3,1},{5,3},{7,5},{10,8},{12,10},{14,12},{11,9},... | collective-permute-start | bytes 1327112 | tf_op jit(solution)/shard_map/ppermute | solution.py:39
  7.5 18.1 %collective-permute-start = (f32[12,9,1024]{2,0,1:T(8,128)S(1)}, f32[12,9,1024]{2,0,1:T(8,128)}, u32[]{:S(2)}, u32[]{:S(2)}) collective-permute-start(f32[12,9,1024]{2,0,1:T(8,128)S(1)} %get-tuple-element.46), channel_id=1, source_target_pairs={{0,2},{2,4},{4,6},{1,3},{3,5},{5,7},{8,10},{10,12},{12,14},{9,11},... | collective-permute-start | bytes 1327112 | tf_op jit(solution)/shard_map/ppermute | solution.py:38
  24.4 0.8 copy-start.16
  28.6 9.2 %copy-start.22 = (s32[1,64]{1,0:T(1,128)S(1)}, s32[1,64]{1,0:T(1,128)}, u32[]{:S(2)}) copy-start(s32[1,64]{1,0:T(1,128)} %param.19) | copy-start | bytes 772
  29.9 24.8 %collective-permute-start.2 = (f32[12,50,288]{2,1,0:T(8,128)}, f32[12,50,288]{2,1,0:T(8,128)}, u32[]{:S(2)}, u32[]{:S(2)}) collective-permute-start(f32[12,50,288]{2,1,0:T(8,128)} %copy.36), channel_id=1, source_target_pairs={{0,1},{2,3},{4,5},{6,7},{8,9},{10,11},{12,13},{14,15},{16,17},{18,... | collective-permute-start | bytes 2073608 | tf_op jit(solution)/shard_map/ppermute | solution.py:38
  35.7 25.3 %collective-permute-start.3 = (f32[12,50,288]{2,1,0:T(8,128)}, f32[12,50,288]{2,1,0:T(8,128)}, u32[]{:S(2)}, u32[]{:S(2)}) collective-permute-start(f32[12,50,288]{2,1,0:T(8,128)} %copy.37), channel_id=1, source_target_pairs={{1,0},{3,2},{5,4},{7,6},{9,8},{11,10},{13,12},{15,14},{17,16},{19,... | collective-permute-start | bytes 2073608 | tf_op jit(solution)/shard_map/ppermute | solution.py:39
  90.2 4.7 %copy-start.2 = (f32[50,1600]{1,0:T(8,128)}, f32[50,1600]{1,0:T(8,128)S(1)}, u32[]{:S(2)}) copy-start(f32[50,1600]{1,0:T(8,128)S(1)} %get-tuple-element.27) | copy-start | bytes 960004
  90.6 4.3 %copy-start.9 = (f32[50,1600]{1,0:T(8,128)}, f32[50,1600]{1,0:T(8,128)S(1)}, u32[]{:S(2)}) copy-start(f32[50,1600]{1,0:T(8,128)S(1)} %add_subtract_fusion.2) | copy-start | bytes 960004
  91.0 3.9 %copy-start.10 = (f32[50,1600]{1,0:T(8,128)}, f32[50,1600]{1,0:T(8,128)S(1)}, u32[]{:S(2)}) copy-start(f32[50,1600]{1,0:T(8,128)S(1)} %get-tuple-element.59) | copy-start | bytes 960004
  91.0 3.9 %copy-start.11 = (f32[50,1600]{1,0:T(8,128)}, f32[50,1600]{1,0:T(8,128)S(1)}, u32[]{:S(2)}) copy-start(f32[50,1600]{1,0:T(8,128)S(1)} %get-tuple-element.58) | copy-start | bytes 960004
  92.6 2.4 %copy-start.7 = (f32[50,1600]{1,0:T(8,128)}, f32[50,1600]{1,0:T(8,128)S(1)}, u32[]{:S(2)}) copy-start(f32[50,1600]{1,0:T(8,128)S(1)} %get-tuple-element.25) | copy-start | bytes 960004
  92.6 10.6 %copy-start.20 = (f32[1,3,1,128]{3,2,1,0:T(1,128)S(1)}, f32[1,3,1,128]{3,2,1,0:T(1,128)}, u32[]{:S(2)}) copy-start(f32[1,3,1,128]{3,2,1,0:T(1,128)} %param.17) | copy-start | bytes 4612
  100.8 13.1 %copy-start.12 = (f32[1,50,1600]{2,0,1:T(1,128)S(1)}, f32[1,50,1600]{2,0,1:T(1,128)}, u32[]{:S(2)}) copy-start(f32[1,50,1600]{2,0,1:T(1,128)} %get-tuple-element.32) | copy-start | bytes 960004
  102.0 12.0 %copy-start.13 = (f32[1,50,1600]{2,0,1:T(1,128)S(1)}, f32[1,50,1600]{2,0,1:T(1,128)}, u32[]{:S(2)}) copy-start(f32[1,50,1600]{2,0,1:T(1,128)} %get-tuple-element.33) | copy-start | bytes 960004
  107.5 9.4 %collective-permute-start.5 = (f32[3,9,1024]{2,1,0:T(8,128)S(1)}, f32[3,9,1024]{2,1,0:T(8,128)S(1)}, u32[]{:S(2)}, u32[]{:S(2)}) collective-permute-start(f32[3,9,1024]{2,1,0:T(8,128)S(1)} %get-tuple-element.51), channel_id=1, source_target_pairs={{2,0},{4,2},{6,4},{3,1},{5,3},{7,5},{10,8},{12,10},{14,12},{11,9},... | collective-permute-start | bytes 331784 | tf_op jit(solution)/shard_map/ppermute | solution.py:39
  108.8 8.3 %collective-permute-start.4 = (f32[3,9,1024]{2,1,0:T(8,128)S(1)}, f32[3,9,1024]{2,1,0:T(8,128)S(1)}, u32[]{:S(2)}, u32[]{:S(2)}) collective-permute-start(f32[3,9,1024]{2,1,0:T(8,128)S(1)} %get-tuple-element.50), channel_id=1, source_target_pairs={{0,2},{2,4},{4,6},{1,3},{3,5},{5,7},{8,10},{10,12},{12,14},{9,11},... | collective-permute-start | bytes 331784 | tf_op jit(solution)/shard_map/ppermute | solution.py:38
  117.3 5.3 %collective-permute-start.6 = (f32[3,50,288]{2,1,0:T(8,128)S(1)}, f32[3,50,288]{2,1,0:T(8,128)S(1)}, u32[]{:S(2)}, u32[]{:S(2)}) collective-permute-start(f32[3,50,288]{2,1,0:T(8,128)S(1)} %get-tuple-element.49), channel_id=1, source_target_pairs={{0,1},{2,3},{4,5},{6,7},{8,9},{10,11},{12,13},{14,15},{16,17},{18,... | collective-permute-start | bytes 518408 | tf_op jit(solution)/shard_map/ppermute | solution.py:38
  118.8 8.3 %collective-permute-start.7 = (f32[3,50,288]{2,1,0:T(8,128)S(1)}, f32[3,50,288]{2,1,0:T(8,128)}, u32[]{:S(2)}, u32[]{:S(2)}) collective-permute-start(f32[3,50,288]{2,1,0:T(8,128)S(1)} %get-tuple-element.48), channel_id=1, source_target_pairs={{1,0},{3,2},{5,4},{7,6},{9,8},{11,10},{13,12},{15,14},{17,16},{19,... | collective-permute-start | bytes 518408 | tf_op jit(solution)/shard_map/ppermute | solution.py:39
  122.6 0.7 copy-start.18
  128.7 3.7 %copy-start.4 = (f32[50,1600]{1,0:T(8,128)S(1)}, f32[50,1600]{1,0:T(8,128)}, u32[]{:S(2)}) copy-start(f32[50,1600]{1,0:T(8,128)} %get-tuple-element.64) | copy-start | bytes 960004
  128.7 4.1 %copy-start.5 = (f32[50,1600]{1,0:T(8,128)S(1)}, f32[50,1600]{1,0:T(8,128)}, u32[]{:S(2)}) copy-start(f32[50,1600]{1,0:T(8,128)} %get-tuple-element.56) | copy-start | bytes 960004
  128.7 4.1 %copy-start.6 = (f32[50,1600]{1,0:T(8,128)S(1)}, f32[50,1600]{1,0:T(8,128)}, u32[]{:S(2)}) copy-start(f32[50,1600]{1,0:T(8,128)} %get-tuple-element.57) | copy-start | bytes 960004
  134.1 1.6 copy-start.3
  134.1 1.6 copy-start.8
  134.1 1.6 copy-start.15
  134.1 1.6 copy-start.17
  151.4 7.0 %all-to-all-start = ((f32[4,16,2]{1,2,0:T(2,128)}), f32[4,16,2]{1,2,0:T(2,128)S(1)}, u32[]{:S(2)}, u32[]{:S(2)}) async-start(f32[4,16,2]{1,2,0:T(2,128)} %copy.53), calls=%async_computation | async-start | bytes 8192 | tf_op jit(solution)/shard_map/all_to_all | solution.py:166

commit v3 on v2

--- a/solution.py
+++ b/solution.py
@@ -38,6 +38,38 @@
     below = lax.ppermute(tail, axis, [(i, i + 1) for i in range(ends)])
     above = lax.ppermute(head, axis, [(i + 1, i) for i in range(ends)])
     return below, above
+
+
+def halo(stack, r, nz):
+    k, rows, lanes = stack.shape
+    count_y = lax.axis_size("gy")
+    count_x = lax.axis_size("gx")
+    w = r * nz
+    span_y = {-1: (0, r), 0: (0, rows), 1: (rows - r, rows)}
+    span_x = {-1: (0, w), 0: (0, lanes), 1: (lanes - w, lanes)}
+    got = {}
+    for dy in (-1, 0, 1):
+        for dx in (-1, 0, 1):
+            if dy == 0 and dx == 0:
+                continue
+            ys = span_y[dy]
+            xs = span_x[dx]
+            piece = stack[:, ys[0] : ys[1], xs[0] : xs[1]]
+            pairs = []
+            for y in range(count_y):
+                for x in range(count_x):
+                    ty, tx = y + dy, x + dx
+                    if 0 <= ty < count_y and 0 <= tx < count_x:
+                        pairs.append((y * count_x + x, ty * count_x + tx))
+            got[(-dy, -dx)] = lax.ppermute(piece, ("gy", "gx"), pairs)
+    out = []
+    for j in range(k):
+        bands = []
+        for dy in (-1, 0, 1):
+            parts = [stack[j] if (dy, dx) == (0, 0) else got[(dy, dx)][j] for dx in (-1, 0, 1)]
+            bands.append(jnp.concatenate(parts, axis=1))
+        out.append(jnp.concatenate(bands, axis=0))
+    return out
 
 
 def on_device(
@@ -65,13 +97,13 @@
     total_y = ny * lax.axis_size("gy")
     total_x = nx * lax.axis_size("gx")
 
-    fields = jnp.concatenate(
-        [forward_start[0], adjoint_end[0], velocity[None], attenuation[None]], axis=0
-    )
-    below, above = exchange(fields, "gy", 1, r)
-    fields = jnp.concatenate([below, fields, above], axis=1)
-    left, right = exchange(fields, "gx", 2, r * nz)
-    fields = jnp.concatenate([left, fields, right], axis=2)
+    fields = halo(
+        jnp.concatenate(
+            [forward_start[0], adjoint_end[0], velocity[None], attenuation[None]], axis=0
+        ),
+        r,
+        nz,
+    )
 
     vel = fields[10]
     att = fields[11]
@@ -131,10 +163,7 @@
     inject = jnp.stack(
         [jnp.zeros((ny * lanes,), jnp.float32).at[recs].add(resid[n]) for n in range(STEPS)]
     ).reshape(STEPS, ny, lanes)
-    below, above = exchange(inject, "gy", 1, r)
-    inject = jnp.concatenate([below, inject, above], axis=1)
-    left, right = exchange(inject, "gx", 2, r * nz)
-    inject = jnp.concatenate([left, inject, right], axis=2)
+    inject = halo(inject, r, nz)
 
     velocity_own = velocity
     attenuation_own = attenuation

time: 160 us -> 238 us (1.49)
  local copies, waits for them, and re-layouts: 60.8 us -> 127 us
  waiting for transfers between devices: 37.2 us -> 3.12 us
  starting transfers between devices: 26.1 us -> 49.4 us
  other arithmetic: 32.2 us -> 51.2 us
    ppermute x8 -> x16, waiting for transfers between devices: 34.2 us -> 0.41 us  [halo(): got[-dy, -dx] = lax.ppermute(piece, ('gy', 'gx'), pairs)]
    unnamed x58 -> x314, local copies, waits for them, and re-layouts: 11.4 us -> 42.1 us
    concatenate x2 -> x45, local copies, waits for them, and re-layouts: 7.84 us -> 32.8 us  [halo(): bands.append(jnp.concatenate(parts, axis=1))]
    ppermute x8 -> x16, starting transfers between devices: 22.9 us -> 46.1 us  [halo(): got[-dy, -dx] = lax.ppermute(piece, ('gy', 'gx'), pairs)]
    squeeze x1 -> x15, local copies, waits for them, and re-layouts: 0.03 us -> 16 us  [the longest x10 11.7 us: halo(): got[dy, dx][j]]
    ppermute x2 -> x0, local copies, waits for them, and re-layouts: 4.97 us -> none  [the longest x1 2.49 us: exchange(): below = lax.ppermute(tail, axis, [(i, i + 1) for i in range(ends)])]
    sub x2, other arithmetic: 2.19 us -> 7.04 us  [wave_step(): memory = memory - relax_rate * (memory + stiff * att * div)]
    add x3, other arithmetic: 6.04 us -> 9.62 us  [on_device(): state[0] + jnp.where(src_here, wavelet[0, step], jnp.float32(0.0))]
  transfers between devices with their start and end apart: 9 -> 17, of which waited for: 8 -> 2; matrix products, arithmetic and copies ran while one was open for 7% -> 31% of each run, Pallas kernels for 0% -> 0%
where the time goes in v3:
time: 238 us; the launch traced here: 235 us
  local copies, waits for them, and re-layouts  127 us (53%)
  other arithmetic  51.2 us (22%)
  starting transfers between devices  49.4 us (21%)
  between operations  4.12 us (2%)
  waiting for transfers between devices  3.12 us (1%)
    ppermute x16, starting transfers between devices, halo(): got[-dy, -dx] = lax.ppermute(piece, ('gy', 'gx'), pairs)  46.1 us
    unnamed x314, local copies, waits for them, and re-layouts  42.1 us
    concatenate x45, local copies, waits for them, and re-layouts, halo(): bands.append(jnp.concatenate(parts, axis=1))  32.8 us
    squeeze x10, local copies, waits for them, and re-layouts, halo(): got[dy, dx][j]  11.7 us
    add x3, other arithmetic, on_device(): state[0] + jnp.where(src_here, wavelet[0, step], jnp.float32(0.0))  9.62 us
    slice x6, local copies, waits for them, and re-layouts, halo(): got[dy, dx][j]  9.25 us
    sub x2, other arithmetic, wave_step(): memory = memory - relax_rate * (memory + stiff * att * div)  7.04 us
    another operation x2, local copies, waits for them, and re-layouts, on_device(): grads = jnp.stack([grad_v, grad_a]) * weight  6.32 us
  transfers between devices with their start and end apart: 17, of which 2 were waited for; matrix products, arithmetic and copies ran while one was open for 31% of the time, Pallas kernels for 0%

profile of v3, /device:TPU:0, one launch (start us, length us, event | category | flops | bytes accessed | tf_op | source)
XLA Modules:
  0.0 235.2 jit_solution(902801829473997018)
XLA Ops:
  2.6 2.1 copy_bitcast_fusion
  10.0 10.0 %collective-permute-start = (f32[12,9,288]{2,0,1:T(8,128)}, f32[12,9,288]{2,0,1:T(8,128)}, u32[]{:S(2)}, u32[]{:S(2)}) collective-permute-start(f32[12,9,288]{2,0,1:T(8,128)} %get-tuple-element.36), channel_id=1, source_target_pairs={{0,3},{2,5},{4,7},{8,11},{10,13},{12,15},{16,19},{18,21},{20,23},{... | collective-permute-start | bytes 373256 | tf_op jit(solution)/shard_map/ppermute | solution.py:64
  21.8 2.1 collective-permute-start.3
  26.7 2.1 slice_bitcast_fusion.11
  34.8 3.5 %collective-permute-start.1 = (f32[12,9,1024]{2,0,1:T(8,128)}, f32[12,9,1024]{2,0,1:T(8,128)S(1)}, u32[]{:S(2)}, u32[]{:S(2)}) collective-permute-start(f32[12,9,1024]{2,0,1:T(8,128)} %get-tuple-element.37), channel_id=1, source_target_pairs={{0,2},{1,3},{2,4},{3,5},{4,6},{5,7},{8,10},{9,11},{10,12},{11,13},... | collective-permute-start | bytes 1327112 | tf_op jit(solution)/shard_map/ppermute | solution.py:64
  38.3 1.9 fusion.69
  48.8 1.8 fusion.71
  59.4 1.9 fusion.72
  68.6 1.8 fusion.70
  82.4 1.9 slice_bitcast_fusion.37
  101.6 2.4 %fusion.9 = (f32[50,1600]{1,0:T(8,128)S(1)}, f32[50,1600]{1,0:T(8,128)S(1)}, f32[50,1600]{1,0:T(8,128)}, f32[50,1600]{1,0:T(8,128)S(1)}) fusion(f32[]{:T(128)} %bitcast.22, pred[1600]{0:T(1024)(128)(4,1)S(1)} %copy-done.107, pred[50]{0:T(512)(128)(4,1)S(1)} %copy-done.110, f32[9,1600]{1,0:T(8,128)S(1)} %concatenate.212, f32[32,1600]{1,0:T(8,128)S(1)} %concatenate.211, ...), kind=kLoop, calls=%fused_computation.30 | loop fusion | flops 5360000 | bytes 3550508 | tf_op jit(solution)/shard_map/add | solution.py:157
  108.4 1.7 maximum_subtract_fusion.5
  110.1 4.2 %fusion.10 = (f32[50,1600]{1,0:T(8,128)S(1)}, f32[50,1600]{1,0:T(8,128)S(1)}, f32[50,1600]{1,0:T(8,128)}) fusion(f32[50,1600]{1,0:T(8,128)S(1)} %get-tuple-element.29, f32[50,1600]{1,0:T(8,128)S(1)} %get-tuple-element.32, f32[]{:T(128)} %bitcast.23, pred[1600]{0:T(1024)(128)(4,1)} %iota_compare_fusion, pred[50]{0:T(512)(128)(4,1)} %get-tuple-element.208, ...), kind=kLoop, calls=%fused_computation.31 | loop fusion | flops 4800000 | bytes 3550508 | tf_op jit(solution)/shard_map/add | solution.py:157
  117.7 2.1 gather_fusion
  119.8 2.0 gather_fusion.1
  121.8 4.0 %multiply_subtract_fusion.3 = (f32[50,1600]{1,0:T(8,128)}, f32[50,1600]{1,0:T(8,128)S(1)}) fusion(f32[50,1600]{1,0:T(8,128)S(1)} %get-tuple-element.27, f32[50,1600]{1,0:T(8,128)S(1)} %get-tuple-element.30, f32[50,1600]{1,0:T(8,128)} %add_subtract_fusion.2, s32[1600]{0:T(1024)S(1)} %iota_and_fusion, s32[1600]{0:T(1024)S(1)} %copy-done.15, ...), kind=kLoop, calls=%fused_computation.62 | loop fusion | flops 3280000 | bytes 2254400 | tf_op jit(solution)/shard_map/sub | solution.py:133
  125.8 3.0 %fusion.11 = f32[50,1600]{1,0:T(8,128)} fusion(f32[50,1600]{1,0:T(8,128)S(1)} %get-tuple-element.32, f32[50,1600]{1,0:T(8,128)S(1)} %get-tuple-element.25, f32[]{:T(128)} %bitcast.24, f32[]{:T(128)} %bitcast.23, f32[50,1600]{1,0:T(8,128)S(1)} %get-tuple-element.27, f32[50,1600]{1,0:T(8,128)S(1)} %get-tuple-element.29, f32[50,1600]{1,0:T(8,128)S(1)} %copy-done.3, ...), kind=kLoop, calls=%fused_computation.32 | loop fusion | flops 1840000 | bytes 2256112 | tf_op jit(solution)/shard_map/add | solution.py:157
  147.7 9.0 %collective-permute-start.8 = (f32[3,9,288]{2,1,0:T(8,128)}, f32[3,9,288]{2,1,0:T(8,128)}, u32[]{:S(2)}, u32[]{:S(2)}) collective-permute-start(f32[3,9,288]{2,1,0:T(8,128)} %get-tuple-element.102), channel_id=1, source_target_pairs={{0,3},{2,5},{4,7},{8,11},{10,13},{12,15},{16,19},{18,21},{20,23},{... | collective-permute-start | bytes 93320 | tf_op jit(solution)/shard_map/ppermute | solution.py:64
  168.4 5.2 %collective-permute-start.11 = (f32[3,32,288]{2,1,0:T(8,128)}, f32[3,32,288]{2,1,0:T(8,128)S(1)}, u32[]{:S(2)}, u32[]{:S(2)}) collective-permute-start(f32[3,32,288]{2,1,0:T(8,128)} %get-tuple-element.106), channel_id=1, source_target_pairs={{0,1},{2,3},{4,5},{6,7},{8,9},{10,11},{12,13},{14,15},{16,17},{18,... | collective-permute-start | bytes 331784 | tf_op jit(solution)/shard_map/ppermute | solution.py:64
  175.0 2.9 %collective-permute-start.9 = (f32[3,9,1024]{2,1,0:T(8,128)}, f32[3,9,1024]{2,1,0:T(8,128)S(1)}, u32[]{:S(2)}, u32[]{:S(2)}) collective-permute-start(f32[3,9,1024]{2,1,0:T(8,128)} %get-tuple-element.103), channel_id=1, source_target_pairs={{0,2},{1,3},{2,4},{3,5},{4,6},{5,7},{8,10},{9,11},{10,12},{11,13},... | collective-permute-start | bytes 331784 | tf_op jit(solution)/shard_map/ppermute | solution.py:64
  187.8 2.7 %maximum_add_fusion = (f32[50,1600]{1,0:T(8,128)S(1)}, f32[50,1600]{1,0:T(8,128)}, f32[50,1600]{1,0:T(8,128)}) fusion(f32[9,1600]{1,0:T(8,128)S(1)} %concatenate.236, f32[32,1600]{1,0:T(8,128)S(1)} %concatenate.235, f32[9,1600]{1,0:T(8,128)S(1)} %concatenate.234, f32[50,1600]{1,0:T(8,128)S(1)} %get-tuple-element.32, s32[1600]{0:T(1024)S(1)} %get-tuple-element.203, ...), kind=kLoop, calls=%fused_computation.48 | loop fusion | flops 4640000 | bytes 3548854 | tf_op jit(solution)/shard_map/add | solution.py:176
  191.4 1.7 concatenate.239
  196.2 2.4 %maximum_add_fusion.1 = (f32[50,1600]{1,0:T(8,128)S(1)}, f32[50,1600]{1,0:T(8,128)S(1)}) fusion(f32[9,1600]{1,0:T(8,128)} %concatenate.240, f32[32,1600]{1,0:T(8,128)} %concatenate.239, f32[9,1600]{1,0:T(8,128)} %concatenate.238, f32[50,1600]{1,0:T(8,128)S(1)} %get-tuple-element.32, f32[9,1600]{1,0:T(8,128)} %copy-done.21, f32[32,1600]{1,0:T(8,128)S(1)} %concatenate.235, ...), kind=kLoop, calls=%fused_computation.49 | loop fusion | flops 5040000 | bytes 3868854 | tf_op jit(solution)/shard_map/add | solution.py:176
  201.1 1.8 concatenate.243
  206.0 3.1 %multiply_subtract_fusion = (f32[50,1600]{1,0:T(8,128)S(1)}, f32[50,1600]{1,0:T(8,128)S(1)}) fusion(f32[50,1600]{1,0:T(8,128)S(1)} %get-tuple-element.20, f32[50,1600]{1,0:T(8,128)S(1)} %get-tuple-element.30, f32[50,1600]{1,0:T(8,128)} %add_subtract_fusion, s32[1600]{0:T(1024)S(1)} %iota_and_fusion, s32[1600]{0:T(1024)S(1)} %copy-done.15, ...), kind=kLoop, calls=%fused_computation.50 | loop fusion | flops 3280000 | bytes 2254400 | tf_op jit(solution)/shard_map/sub | solution.py:133
  209.2 2.2 add_multiply_fusion.1
  211.4 2.0 multiply_add_fusion
  216.5 2.5 %stack.89 = f32[1,4,8,4,8,4,8]{6,5,4,3,2,1,0:T(4,128)S(1)} reshape(f32[32,1024]{1,0:T(8,128)S(1)} %copy-done.33) | data formatting | bytes 262144 | tf_op jit(solution)/shard_map/stack | solution.py:188
  219.0 3.8 %stack.90 = f32[1,4,8,4,8,4,8]{6,5,4,3,2,1,0:T(4,128)} reshape(f32[32,1024]{1,0:T(8,128)S(1)} %copy-done.34) | data formatting | bytes 262144 | tf_op jit(solution)/shard_map/stack | solution.py:188
  222.9 3.0 %fusion = f32[2,4,4,4]{3,2,1,0:T(4,128)S(1)} fusion(f32[1,4,8,4,8,4,8]{6,5,4,3,2,1,0:T(4,128)} %stack.90, f32[1,4,8,4,8,4,8]{6,5,4,3,2,1,0:T(4,128)S(1)} %stack.89, f32[]{:T(128)} %bitcast.87), kind=kLoop, calls=%fused_computation.8 | loop fusion | flops 196480 | bytes 262660 | tf_op jit(solution)/shard_map/reduce_sum | solution.py:192
  227.7 3.2 %all-to-all-start = ((f32[4,16,2]{1,2,0:T(2,128)}), f32[4,16,2]{1,2,0:T(2,128)S(1)}, u32[]{:S(2)}, u32[]{:S(2)}) async-start(f32[4,16,2]{1,2,0:T(2,128)} %copy.29), calls=%async_computation | async-start | bytes 8192 | tf_op jit(solution)/shard_map/all_to_all | solution.py:195
  231.9 2.7 %all-to-all-done = f32[4,16,2]{1,2,0:T(2,128)S(1)} async-done(((f32[4,16,2]{1,2,0:T(2,128)}), f32[4,16,2]{1,2,0:T(2,128)S(1)}, u32[]{:S(2)}, u32[]{:S(2)}) %all-to-all-start) | async-done | bytes 544 | tf_op jit(solution)/shard_map/all_to_all | solution.py:195
  (452 shorter events, 134.5 us)
Async XLA Ops:
  6.0 28.8 %collective-permute-start.2 = (f32[12,9,288]{2,0,1:T(8,128)}, f32[12,9,288]{2,0,1:T(8,128)}, u32[]{:S(2)}, u32[]{:S(2)}) collective-permute-start(f32[12,9,288]{2,0,1:T(8,128)} %get-tuple-element.33), channel_id=1, source_target_pairs={{1,2},{3,4},{5,6},{9,10},{11,12},{13,14},{17,18},{19,20},{21,22},{... | collective-permute-start | bytes 373256 | tf_op jit(solution)/shard_map/ppermute | solution.py:64
  7.4 40.2 %collective-permute-start.7 = (f32[12,9,288]{2,0,1:T(8,128)}, f32[12,9,288]{2,0,1:T(8,128)}, u32[]{:S(2)}, u32[]{:S(2)}) collective-permute-start(f32[12,9,288]{2,0,1:T(8,128)} %get-tuple-element.34), channel_id=1, source_target_pairs={{3,0},{5,2},{7,4},{11,8},{13,10},{15,12},{19,16},{21,18},{23,20},{... | collective-permute-start | bytes 373256 | tf_op jit(solution)/shard_map/ppermute | solution.py:64
  8.7 49.3 %collective-permute-start.5 = (f32[12,9,288]{2,0,1:T(8,128)}, f32[12,9,288]{2,0,1:T(8,128)}, u32[]{:S(2)}, u32[]{:S(2)}) collective-permute-start(f32[12,9,288]{2,0,1:T(8,128)} %get-tuple-element.35), channel_id=1, source_target_pairs={{2,1},{4,3},{6,5},{10,9},{12,11},{14,13},{18,17},{20,19},{22,21},{... | collective-permute-start | bytes 373256 | tf_op jit(solution)/shard_map/ppermute | solution.py:64
  10.0 58.6 %collective-permute-start = (f32[12,9,288]{2,0,1:T(8,128)}, f32[12,9,288]{2,0,1:T(8,128)}, u32[]{:S(2)}, u32[]{:S(2)}) collective-permute-start(f32[12,9,288]{2,0,1:T(8,128)} %get-tuple-element.36), channel_id=1, source_target_pairs={{0,3},{2,5},{4,7},{8,11},{10,13},{12,15},{16,19},{18,21},{20,23},{... | collective-permute-start | bytes 373256 | tf_op jit(solution)/shard_map/ppermute | solution.py:64
  21.8 60.6 %collective-permute-start.3 = (f32[12,32,288]{2,1,0:T(8,128)}, f32[12,32,288]{2,1,0:T(8,128)}, u32[]{:S(2)}, u32[]{:S(2)}) collective-permute-start(f32[12,32,288]{2,1,0:T(8,128)} %copy.25), channel_id=1, source_target_pairs={{0,1},{2,3},{4,5},{6,7},{8,9},{10,11},{12,13},{14,15},{16,17},{18,... | collective-permute-start | bytes 1327112 | tf_op jit(solution)/shard_map/ppermute | solution.py:64
  32.6 37.8 %copy-start.100 = (pred[50]{0:T(512)(128)(4,1)}, pred[50]{0:T(512)(128)(4,1)S(1)}, u32[]{:S(2)}) copy-start(pred[50]{0:T(512)(128)(4,1)S(1)} %get-tuple-element.207) | copy-start | bytes 154
  34.8 42.9 %collective-permute-start.1 = (f32[12,9,1024]{2,0,1:T(8,128)}, f32[12,9,1024]{2,0,1:T(8,128)S(1)}, u32[]{:S(2)}, u32[]{:S(2)}) collective-permute-start(f32[12,9,1024]{2,0,1:T(8,128)} %get-tuple-element.37), channel_id=1, source_target_pairs={{0,2},{1,3},{2,4},{3,5},{4,6},{5,7},{8,10},{9,11},{10,12},{11,13},... | collective-permute-start | bytes 1327112 | tf_op jit(solution)/shard_map/ppermute | solution.py:64
  47.6 31.3 %collective-permute-start.6 = (f32[12,9,1024]{2,0,1:T(8,128)S(1)}, f32[12,9,1024]{2,0,1:T(8,128)S(1)}, u32[]{:S(2)}, u32[]{:S(2)}) collective-permute-start(f32[12,9,1024]{2,0,1:T(8,128)S(1)} %get-tuple-element.38), channel_id=1, source_target_pairs={{2,0},{3,1},{4,2},{5,3},{6,4},{7,5},{10,8},{11,9},{12,10},{13,11},... | collective-permute-start | bytes 1327112 | tf_op jit(solution)/shard_map/ppermute | solution.py:64
  57.9 26.4 %collective-permute-start.4 = (f32[12,32,288]{2,1,0:T(8,128)S(1)}, f32[12,32,288]{2,1,0:T(8,128)S(1)}, u32[]{:S(2)}, u32[]{:S(2)}) collective-permute-start(f32[12,32,288]{2,1,0:T(8,128)S(1)} %copy.26), channel_id=1, source_target_pairs={{1,0},{3,2},{5,4},{7,6},{9,8},{11,10},{13,12},{15,14},{17,16},{19,... | collective-permute-start | bytes 1327112 | tf_op jit(solution)/shard_map/ppermute | solution.py:64
  138.2 21.9 %copy-start.75 = (f32[1,9,288]{2,1,0:T(8,128)S(1)}, f32[1,9,288]{2,1,0:T(8,128)}, u32[]{:S(2)}) copy-start(f32[1,9,288]{2,1,0:T(8,128)} %copy.218) | copy-start | bytes 31108
  138.2 21.9 %copy-start.77 = (f32[1,9,288]{2,1,0:T(8,128)S(1)}, f32[1,9,288]{2,1,0:T(8,128)}, u32[]{:S(2)}) copy-start(f32[1,9,288]{2,1,0:T(8,128)} %copy.219) | copy-start | bytes 31108
  138.3 22.7 %copy-start.76 = (f32[1,9,288]{2,1,0:T(8,128)S(1)}, f32[1,9,288]{2,1,0:T(8,128)}, u32[]{:S(2)}) copy-start(f32[1,9,288]{2,1,0:T(8,128)} %copy.214) | copy-start | bytes 31108
  138.3 22.6 %copy-start.78 = (f32[1,9,288]{2,1,0:T(8,128)S(1)}, f32[1,9,288]{2,1,0:T(8,128)}, u32[]{:S(2)}) copy-start(f32[1,9,288]{2,1,0:T(8,128)} %copy.215) | copy-start | bytes 31108
  138.3 23.4 %copy-start.25 = (f32[32,1024]{1,0:T(8,128)S(1)}, f32[32,1024]{1,0:T(8,128)}, u32[]{:S(2)}) copy-start(f32[32,1024]{1,0:T(8,128)} %get-tuple-element.41) | copy-start | bytes 393220
  138.3 23.4 %copy-start.50 = (f32[32,288]{1,0:T(8,128)S(1)}, f32[32,288]{1,0:T(8,128)}, u32[]{:S(2)}) copy-start(f32[32,288]{1,0:T(8,128)} %get-tuple-element.75) | copy-start | bytes 110596
  138.3 23.3 %copy-start.52 = (f32[32,288]{1,0:T(8,128)S(1)}, f32[32,288]{1,0:T(8,128)}, u32[]{:S(2)}) copy-start(f32[32,288]{1,0:T(8,128)} %get-tuple-element.63) | copy-start | bytes 110596
  139.1 22.7 %copy-start.24 = (f32[32,1024]{1,0:T(8,128)S(1)}, f32[32,1024]{1,0:T(8,128)}, u32[]{:S(2)}) copy-start(f32[32,1024]{1,0:T(8,128)} %get-tuple-element.42) | copy-start | bytes 393220
  139.1 22.7 %copy-start.49 = (f32[32,288]{1,0:T(8,128)S(1)}, f32[32,288]{1,0:T(8,128)}, u32[]{:S(2)}) copy-start(f32[32,288]{1,0:T(8,128)} %get-tuple-element.78) | copy-start | bytes 110596
  139.1 22.7 %copy-start.51 = (f32[32,288]{1,0:T(8,128)S(1)}, f32[32,288]{1,0:T(8,128)}, u32[]{:S(2)}) copy-start(f32[32,288]{1,0:T(8,128)} %get-tuple-element.66) | copy-start | bytes 110596
  139.9 22.1 %copy-start.104 = (pred[50]{0:T(512)(128)(4,1)S(1)}, pred[50]{0:T(512)(128)(4,1)}, u32[]{:S(2)}) copy-start(pred[50]{0:T(512)(128)(4,1)} %copy-done.100) | copy-start | bytes 154
  143.8 24.5 %collective-permute-start.10 = (f32[3,9,288]{2,1,0:T(8,128)}, f32[3,9,288]{2,1,0:T(8,128)}, u32[]{:S(2)}, u32[]{:S(2)}) collective-permute-start(f32[3,9,288]{2,1,0:T(8,128)} %get-tuple-element.99), channel_id=1, source_target_pairs={{1,2},{3,4},{5,6},{9,10},{11,12},{13,14},{17,18},{19,20},{21,22},{... | collective-permute-start | bytes 93320 | tf_op jit(solution)/shard_map/ppermute | solution.py:64
  145.1 29.8 %collective-permute-start.15 = (f32[3,9,288]{2,1,0:T(8,128)}, f32[3,9,288]{2,1,0:T(8,128)}, u32[]{:S(2)}, u32[]{:S(2)}) collective-permute-start(f32[3,9,288]{2,1,0:T(8,128)} %get-tuple-element.100), channel_id=1, source_target_pairs={{3,0},{5,2},{7,4},{11,8},{13,10},{15,12},{19,16},{21,18},{23,20},{... | collective-permute-start | bytes 93320 | tf_op jit(solution)/shard_map/ppermute | solution.py:64
  146.4 32.8 %collective-permute-start.13 = (f32[3,9,288]{2,1,0:T(8,128)}, f32[3,9,288]{2,1,0:T(8,128)}, u32[]{:S(2)}, u32[]{:S(2)}) collective-permute-start(f32[3,9,288]{2,1,0:T(8,128)} %get-tuple-element.101), channel_id=1, source_target_pairs={{2,1},{4,3},{6,5},{10,9},{12,11},{14,13},{18,17},{20,19},{22,21},{... | collective-permute-start | bytes 93320 | tf_op jit(solution)/shard_map/ppermute | solution.py:64
  147.7 34.5 %collective-permute-start.8 = (f32[3,9,288]{2,1,0:T(8,128)}, f32[3,9,288]{2,1,0:T(8,128)}, u32[]{:S(2)}, u32[]{:S(2)}) collective-permute-start(f32[3,9,288]{2,1,0:T(8,128)} %get-tuple-element.102), channel_id=1, source_target_pairs={{0,3},{2,5},{4,7},{8,11},{10,13},{12,15},{16,19},{18,21},{20,23},{... | collective-permute-start | bytes 93320 | tf_op jit(solution)/shard_map/ppermute | solution.py:64
  156.7 27.5 %collective-permute-start.12 = (f32[3,32,288]{2,1,0:T(8,128)}, f32[3,32,288]{2,1,0:T(8,128)}, u32[]{:S(2)}, u32[]{:S(2)}) collective-permute-start(f32[3,32,288]{2,1,0:T(8,128)} %get-tuple-element.105), channel_id=1, source_target_pairs={{1,0},{3,2},{5,4},{7,6},{9,8},{11,10},{13,12},{15,14},{17,16},{19,... | collective-permute-start | bytes 331784 | tf_op jit(solution)/shard_map/ppermute | solution.py:64
  163.4 24.4 %copy-start.11 = (f32[9,1600]{1,0:T(8,128)S(1)}, f32[9,1600]{1,0:T(8,128)}, u32[]{:S(2)}) copy-start(f32[9,1600]{1,0:T(8,128)} %copy-done.10) | copy-start | bytes 172804
  163.4 24.4 %copy-start.13 = (f32[9,1600]{1,0:T(8,128)S(1)}, f32[9,1600]{1,0:T(8,128)}, u32[]{:S(2)}) copy-start(f32[9,1600]{1,0:T(8,128)} %copy-done.12) | copy-start | bytes 172804
  163.4 24.4 %copy-start.44 = (pred[1600]{0:T(1024)(128)(4,1)S(1)}, pred[1600]{0:T(1024)(128)(4,1)}, u32[]{:S(2)}) copy-start(pred[1600]{0:T(1024)(128)(4,1)} %get-tuple-element.205) | copy-start | bytes 4804
  168.4 17.4 %collective-permute-start.11 = (f32[3,32,288]{2,1,0:T(8,128)}, f32[3,32,288]{2,1,0:T(8,128)S(1)}, u32[]{:S(2)}, u32[]{:S(2)}) collective-permute-start(f32[3,32,288]{2,1,0:T(8,128)} %get-tuple-element.106), channel_id=1, source_target_pairs={{0,1},{2,3},{4,5},{6,7},{8,9},{10,11},{12,13},{14,15},{16,17},{18,... | collective-permute-start | bytes 331784 | tf_op jit(solution)/shard_map/ppermute | solution.py:64
  175.0 8.6 %collective-permute-start.9 = (f32[3,9,1024]{2,1,0:T(8,128)}, f32[3,9,1024]{2,1,0:T(8,128)S(1)}, u32[]{:S(2)}, u32[]{:S(2)}) collective-permute-start(f32[3,9,1024]{2,1,0:T(8,128)} %get-tuple-element.103), channel_id=1, source_target_pairs={{0,2},{1,3},{2,4},{3,5},{4,6},{5,7},{8,10},{9,11},{10,12},{11,13},... | collective-permute-start | bytes 331784 | tf_op jit(solution)/shard_map/ppermute | solution.py:64
  179.2 7.8 %collective-permute-start.14 = (f32[3,9,1024]{2,1,0:T(8,128)}, f32[3,9,1024]{2,1,0:T(8,128)S(1)}, u32[]{:S(2)}, u32[]{:S(2)}) collective-permute-start(f32[3,9,1024]{2,1,0:T(8,128)} %get-tuple-element.104), channel_id=1, source_target_pairs={{2,0},{3,1},{4,2},{5,3},{6,4},{7,5},{10,8},{11,9},{12,10},{13,11},... | collective-permute-start | bytes 331784 | tf_op jit(solution)/shard_map/ppermute | solution.py:64
  227.7 7.0 %all-to-all-start = ((f32[4,16,2]{1,2,0:T(2,128)}), f32[4,16,2]{1,2,0:T(2,128)S(1)}, u32[]{:S(2)}, u32[]{:S(2)}) async-start(f32[4,16,2]{1,2,0:T(2,128)} %copy.29), calls=%async_computation | async-start | bytes 8192 | tf_op jit(solution)/shard_map/all_to_all | solution.py:195
  (101 other events, 636.6 us)

commit v4 on v0

v4 whole, which is shorter than its diff:
```python
import jax
import jax.numpy as jnp
from jax import lax
from jax.experimental import pallas as pl
from jax.experimental.pallas import tpu as pltpu
from jax.sharding import PartitionSpec as P

CZ = 32
STEPS = 3
BY = 8
BX = 8
BZ = 8
HALO = 3 * STEPS

coef_near = 9.0 / 8.0
coef_far = -1.0 / 24.0
stiff_scale = 0.02
relax_rate = 0.3


def round_up(value, unit):
    return (value + unit - 1) // unit * unit


class Frame:
    def __init__(self, ny, lanes):
        self.ny = ny
        self.lanes = lanes
        self.oy = round_up(HALO, 8)
        self.ox = round_up(HALO * CZ, 128)
        self.ey = 2 * self.oy + ny
        self.el = 2 * self.ox + lanes


def send_pieces(stack, frame):
    ny, lanes, ox = frame.ny, frame.lanes, frame.ox
    lo_rows = stack[:, :HALO]
    hi_rows = stack[:, ny - HALO :]
    count_y = lax.axis_size("gy")
    count_x = lax.axis_size("gx")

    def move(piece, dy, dx):
        pairs = []
        for y in range(count_y):
            for x in range(count_x):
                ty, tx = y + dy, x + dx
                if 0 <= ty < count_y and 0 <= tx < count_x:
                    pairs.append((y * count_x + x, ty * count_x + tx))
        return lax.ppermute(piece, ("gy", "gx"), pairs)

    return (
        move(hi_rows, 1, 0),
        move(lo_rows, -1, 0),
        move(stack[:, :, lanes - ox :], 0, 1),
        move(stack[:, :, :ox], 0, -1),
        move(hi_rows[:, :, lanes - ox :], 1, 1),
        move(hi_rows[:, :, :ox], 1, -1),
        move(lo_rows[:, :, lanes - ox :], -1, 1),
        move(lo_rows[:, :, :ox], -1, -1),
    )


def assemble(dst, own, pieces, j, frame):
    ny, lanes, oy, ox, el = frame.ny, frame.lanes, frame.oy, frame.ox, frame.el
    below, above, left, right, b_l, b_r, a_l, a_r = pieces
    lo = slice(oy - HALO, oy)
    mid = slice(oy, oy + ny)
    hi = slice(oy + ny, oy + ny + HALO)
    west = slice(0, ox)
    centre = slice(ox, ox + lanes)
    east = slice(ox + lanes, el)
    dst[...] = jnp.zeros(dst.shape, dst.dtype)
    dst[mid, centre] = own[j]
    dst[lo, centre] = below[j]
    dst[hi, centre] = above[j]
    dst[mid, west] = left[j]
    dst[mid, east] = right[j]
    dst[lo, west] = b_l[j]
    dst[lo, east] = b_r[j]
    dst[hi, west] = a_l[j]
    dst[hi, east] = a_r[j]


def stepper(frame, bounds_ref):
    ey, el = frame.ey, frame.el
    row = lax.broadcasted_iota(jnp.int32, (ey, el), 0)
    lane = lax.broadcasted_iota(jnp.int32, (ey, el), 1)
    inside = (
        (row >= bounds_ref[0])
        & (row < bounds_ref[1])
        & (lane >= bounds_ref[2])
        & (lane < bounds_ref[3])
    )
    depth = lane % CZ
    zero = jnp.zeros((ey, el), jnp.float32)
    z_ok = {d: (depth + d >= 0) & (depth + d < CZ) for d in (-2, -1, 1, 2)}

    def rows(a, d):
        return a if d == 0 else pltpu.roll(a, (-d) % ey, 0)

    def lanes(a, d):
        return a if d == 0 else pltpu.roll(a, (-d) % el, 1)

    def deep(a, d):
        return a if d == 0 else jnp.where(z_ok[d], lanes(a, d), zero)

    def forward_diff(s):
        return coef_near * (s(1) - s(0)) + coef_far * (s(2) - s(-1))

    def backward_diff(s):
        return coef_near * (s(0) - s(-1)) + coef_far * (s(1) - s(-2))

    def wave_step(state, stiff, att):
        pres, vel_y, vel_x, vel_z, memory = state
        vel_y = jnp.where(inside, vel_y - forward_diff(lambda d: rows(pres, d)), zero)
        vel_x = jnp.where(inside, vel_x - forward_diff(lambda d: lanes(pres, d * CZ)), zero)
        vel_z = vel_z - forward_diff(lambda d: deep(pres, d))
        div = (
            backward_diff(lambda d: rows(vel_y, d))
            + backward_diff(lambda d: lanes(vel_x, d * CZ))
            + backward_diff(lambda d: deep(vel_z, d))
        )
        memory = memory - relax_rate * (memory + stiff * att * div)
        pres = jnp.where(inside, pres - stiff * (1.0 + att) * div - memory, zero)
        return [pres, vel_y, vel_x, vel_z, memory], div

    return wave_step, row, lane


def forward_kernel(frame, bounds_ref, source_ref, wave_ref, own_ref, *rest):
    pieces = rest[:8]
    end_ref, div_ref, pres_ref, ext = rest[8:]
    for e, j in enumerate((0, 1, 2, 3, 4, 10, 11)):
        assemble(ext.at[e], own_ref, pieces, j, frame)
    wave_step, row, lane = stepper(frame, bounds_ref)
    source = (row == source_ref[0]) & (lane == source_ref[1])
    vel = ext[5]
    att = ext[6]
    stiff = stiff_scale * vel * vel
    state = [ext[k] for k in range(5)]
    mid = slice(frame.oy, frame.oy + frame.ny)
    centre = slice(frame.ox, frame.ox + frame.lanes)
    for step in range(STEPS):
        state, div = wave_step(state, stiff, att)
        state[0] = state[0] + jnp.where(source, wave_ref[step], jnp.float32(0.0))
        div_ref[step] = div[mid, centre]
        pres_ref[step] = state[0][mid, centre]
    for k in range(5):
        end_ref[0, k] = state[k][mid, centre]


def adjoint_kernel(frame, bounds_ref, own_ref, *rest):
    pieces = rest[:8]
    inject_own = rest[8]
    inject_pieces = rest[9:17]
    div_ref, start_ref, grad_ref, ext = rest[17:]
    for e, j in enumerate((5, 6, 7, 8, 9, 10, 11)):
        assemble(ext.at[e], own_ref, pieces, j, frame)
    for n in range(STEPS):
        assemble(ext.at[7 + n], inject_own, inject_pieces, n, frame)
    wave_step, row, lane = stepper(frame, bounds_ref)
    vel = ext[5]
    att = ext[6]
    stiff = stiff_scale * vel * vel
    mid = slice(frame.oy, frame.oy + frame.ny)
    centre = slice(frame.ox, frame.ox + frame.lanes)
    velocity = vel[mid, centre]
    attenuation = att[mid, centre]
    stiff_own = stiff[mid, centre]
    adj = [ext[k] for k in range(5)]
    grad_v = jnp.zeros((frame.ny, frame.lanes), jnp.float32)
    grad_a = jnp.zeros((frame.ny, frame.lanes), jnp.float32)
    for step in range(STEPS - 1, -1, -1):
        adj, unused = wave_step(adj, stiff, att)
        adj[0] = adj[0] + ext[7 + step]
        div = div_ref[step]
        q = adj[0][mid, centre]
        m = adj[4][mid, centre]
        deriv_q = (relax_rate * attenuation - (1.0 + attenuation)) * div
        deriv_m = -relax_rate * attenuation * div
        grad_v = grad_v + (q * deriv_q + m * deriv_m) * (2.0 * stiff_scale * velocity)
        grad_a = grad_a + (q * (relax_rate - 1.0) - m * relax_rate) * stiff_own * div
    for k in range(5):
        start_ref[0, k] = adj[k][mid, centre]
    for c, g in enumerate((grad_v, grad_a)):
        grad_ref[c] = g.reshape(frame.ny // BY, BY, frame.lanes).sum(axis=1)


def vmem():
    return pl.BlockSpec(memory_space=pltpu.VMEM)


def smem():
    return pl.BlockSpec(memory_space=pltpu.SMEM)


def on_device(
    forward_start,
    adjoint_end,
    velocity,
    attenuation,
    wavelet,
    source_cell,
    receiver_cells,
    observed,
    aperture,
    block_slot,
):
    nz = CZ
    ny = velocity.shape[0]
    lanes = velocity.shape[1]
    nx = lanes // nz
    frame = Frame(ny, lanes)
    index_y = lax.axis_index("gy")
    index_x = lax.axis_index("gx")
    total_y = ny * lax.axis_size("gy")
    total_x = nx * lax.axis_size("gx")

    row_lo = frame.oy - index_y * ny
    lane_lo = frame.ox - index_x * lanes
    bounds = jnp.stack([row_lo, row_lo + total_y, lane_lo, lane_lo + total_x * nz]).astype(jnp.int32)

    cell = source_cell[0, 0]
    src_row = cell // (total_x * nz) + row_lo
    src_lane = cell % (total_x * nz) + lane_lo
    source = jnp.stack([src_row, src_lane]).astype(jnp.int32)

    stack = jnp.concatenate(
        [forward_start[0], adjoint_end[0], velocity[None], attenuation[None]], axis=0
    )
    pieces = send_pieces(stack, frame)

    ext_shape = (frame.ey, frame.el)
    forward_end, divs, pres = pl.pallas_call(
        lambda *refs: forward_kernel(frame, *refs),
        out_shape=(
            jax.ShapeDtypeStruct((1, 5, ny, lanes), jnp.float32),
            jax.ShapeDtypeStruct((STEPS, ny, lanes), jnp.float32),
            jax.ShapeDtypeStruct((STEPS, ny, lanes), jnp.float32),
        ),
        in_specs=[smem(), smem(), smem()] + [vmem()] * 9,
        out_specs=(vmem(), vmem(), vmem()),
        scratch_shapes=[pltpu.VMEM((7,) + ext_shape, jnp.float32)],
        compiler_params=pltpu.CompilerParams(vmem_limit_bytes=48 * 1024 * 1024),
    )(bounds, source, wavelet[0], stack, *pieces)

    recs = receiver_cells[0, 0]
    records = pres.reshape(STEPS, ny * lanes)[:, recs]
    resid = records - observed[0, :, 0]
    inject = jnp.stack(
        [jnp.zeros((ny * lanes,), jnp.float32).at[recs].add(resid[n]) for n in range(STEPS)]
    ).reshape(STEPS, ny, lanes)
    inject_pieces = send_pieces(inject, frame)

    adjoint_start, row_sums = pl.pallas_call(
        lambda *refs: adjoint_kernel(frame, *refs),
        out_shape=(
            jax.ShapeDtypeStruct((1, 5, ny, lanes), jnp.float32),
            jax.ShapeDtypeStruct((2, ny // BY, lanes), jnp.float32),
        ),
        in_specs=[smem()] + [vmem()] * 19,
        out_specs=(vmem(), vmem()),
        scratch_shapes=[pltpu.VMEM((10,) + ext_shape, jnp.float32)],
        compiler_params=pltpu.CompilerParams(vmem_limit_bytes=48 * 1024 * 1024),
    )(bounds, stack, *pieces, inject, *inject_pieces, divs)

    grad_scale = float(BY * BX * BZ) ** (-0.5)
    weight = aperture[0, 0].astype(jnp.float32)
    blocks = row_sums.reshape(2, ny // BY, nx // BX, BX, nz // BZ, BZ).sum(axis=(3, 5))
    sums = blocks.transpose(1, 2, 3, 0).reshape(-1, 2) * (grad_scale * weight)
    slots = block_slot[0]
    ordered = jnp.zeros(sums.shape, jnp.float32).at[slots].set(sums)
    shots = lax.axis_size("shot")
    parts = lax.all_to_all(
        ordered.reshape(shots, -1, 2), "shot", split_axis=0, concat_axis=0, tiled=True
    )
    coarse = jnp.sum(parts, axis=0)
    model_gradient = coarse.T[:, None, :]
    return (forward_end, adjoint_start, model_gradient)


def solution(mesh):
    placed = (
        P("shot", None, "gy", "gx"),
        P("shot", None, "gy", "gx"),
        P("gy", "gx"),
        P("gy", "gx"),
        P("shot", None),
        P("shot", None),
        P("shot", ("gy", "gx"), None),
        P("shot", None, ("gy", "gx"), None),
        P("shot", ("gy", "gx")),
        P(("gy", "gx"), None),
    )
    return jax.shard_map(
        on_device,
        mesh=mesh,
        in_specs=placed,
        out_specs=(
            P("shot", None, "gy", "gx"),
            P("shot", None, "gy", "gx"),
            P(None, ("gy", "gx"), "shot"),
        ),
        check_vma=False,
    )
```

time: 302 us -> 125 us (0.41)
  starting transfers between devices: 132 us -> 42.1 us
  other arithmetic: 42.2 us -> 7.59 us
  waiting for transfers between devices: 49.7 us -> 19.2 us
  local copies, waits for them, and re-layouts: 57.9 us -> 32 us
  between operations: 18.7 us -> 2.35 us
  Pallas kernels: 0 us -> 13.9 us
  blocking collectives: 0 us -> 6.34 us
    ppermute x48 -> x16, starting transfers between devices: 132 us -> 42.1 us  [move(): return lax.ppermute(piece, ('gy', 'gx'), pairs)]
    sub x13 -> x1, other arithmetic: 29.9 us -> 0.01 us  [on_device(): resid = records - observed[0, :, 0]]
    another operation x23 -> x4, local copies, waits for them, and re-layouts: 21.1 us -> 4.76 us  [on_device(): jnp.stack([jnp.zeros((ny * lanes,), jnp.float32).at[recs].add(resid[n]) f...]
    reduce_scatter x1 -> x0, waiting for transfers between devices: 16 us -> none  [on_device(): coarse = lax.psum_scatter(ordered, 'shot', scatter_dimension=0, tiled=True)]
    ppermute x48 -> x16, waiting for transfers between devices: 33.7 us -> 19.2 us  [move(): return lax.ppermute(piece, ('gy', 'gx'), pairs)]
    pallas_call x0 -> x2, Pallas kernels: none -> 13.9 us  [the longest x1 7.11 us: on_device(): pl.pallas_call(lambda *refs: adjoint_kernel(frame, *refs), out_shape=(jax...]
    all_to_all x0 -> x1, blocking collectives: none -> 6.34 us  [on_device(): lax.all_to_all(ordered.reshape(shots, -1, 2), 'shot', split_axis=0, conca...]
    unnamed x113 -> x27, local copies, waits for them, and re-layouts: 10.4 us -> 4.29 us
  transfers between devices with their start and end apart: 49 -> 16, of which waited for: 14 -> 3; matrix products, arithmetic and copies ran while one was open for 12% -> 3% of each run, Pallas kernels for 0% -> 0%
where the time goes in v4:
time: 125 us; the launch traced here: 124 us
  starting transfers between devices  42.1 us (34%)
  local copies, waits for them, and re-layouts  32 us (26%)
  waiting for transfers between devices  19.2 us (15%)
  Pallas kernels  13.9 us (11%)
  other arithmetic  7.59 us (6%)
  blocking collectives  6.34 us (5%)
  between operations  2.35 us (2%)
    ppermute x16, starting transfers between devices, move(): return lax.ppermute(piece, ('gy', 'gx'), pairs)  42.1 us
    ppermute x16, waiting for transfers between devices, move(): return lax.ppermute(piece, ('gy', 'gx'), pairs)  19.2 us
    reshape x1, local copies, waits for them, and re-layouts, on_device(): records = pres.reshape(STEPS, ny * lanes)[:, recs]  9.44 us
    pallas_call x1, Pallas kernels, on_device(): pl.pallas_call(lambda *refs: adjoint_kernel(frame, *refs), out_shape=(jax...  7.11 us
    pallas_call x1, Pallas kernels, on_device(): pl.pallas_call(lambda *refs: forward_kernel(frame, *refs), out_shape=(jax...  6.83 us
    gather x1, local copies, waits for them, and re-layouts, on_device(): records = pres.reshape(STEPS, ny * lanes)[:, recs]  6.42 us
    all_to_all x1, blocking collectives, on_device(): lax.all_to_all(ordered.reshape(shots, -1, 2), 'shot', split_axis=0, conca...  6.34 us
    scatter-add x3, other arithmetic, on_device(): jnp.zeros((ny * lanes,), jnp.float32).at[recs].add(resid[n])  5.04 us
  transfers between devices with their start and end apart: 16, of which 3 were waited for; matrix products, arithmetic and copies ran while one was open for 3% of the time, Pallas kernels for 0%

profile of v4, /device:TPU:0, one launch (start us, length us, event | category | flops | bytes accessed | tf_op | source)
XLA Modules:
  0.0 123.6 jit_solution(8837187598283337852)
XLA Ops:
  0.6 1.6 %pad_maximum_fusion.refs_3_.refs_1_ = f32[12,32,1024]{2,1,0:T(8,128)S(1)} fusion(f32[1,32,1024]{2,1,0:T(8,128)} %bitcast.43, f32[1,32,1024]{2,1,0:T(8,128)} %bitcast.44, f32[5,32,1024]{2,1,0:T(8,128)} %bitcast.41, f32[5,32,1024]{2,1,0:T(8,128)} %bitcast.42), kind=kLoop, calls=%fused_computation.5 | loop fusion | flops 1179648 | bytes 3145728 | tf_op jit(solution)/shard_map/concatenate | solution.py:228
  2.4 1.2 copy.21
  3.6 5.0 %collective-permute-start = (f32[12,9,1024]{2,0,1:T(8,128)}, f32[12,9,1024]{2,0,1:T(8,128)S(1)}, u32[]{:S(2)}, u32[]{:S(2)}) collective-permute-start(f32[12,9,1024]{2,0,1:T(8,128)} %copy.21), channel_id=1, source_target_pairs={{0,2},{1,3},{2,4},{3,5},{4,6},{5,7},{8,10},{9,11},{10,12},{11,13},... | collective-permute-start | bytes 1327112 | tf_op jit(solution)/shard_map/ppermute | solution.py:49
  8.5 1.1 copy.22
  9.6 1.3 %collective-permute-start.1 = (f32[12,9,1024]{2,0,1:T(8,128)}, f32[12,9,1024]{2,0,1:T(8,128)S(1)}, u32[]{:S(2)}, u32[]{:S(2)}) collective-permute-start(f32[12,9,1024]{2,0,1:T(8,128)} %copy.22), channel_id=1, source_target_pairs={{2,0},{3,1},{4,2},{5,3},{6,4},{7,5},{10,8},{11,9},{12,10},{13,11},... | collective-permute-start | bytes 1327112 | tf_op jit(solution)/shard_map/ppermute | solution.py:49
  10.9 1.2 fusion.11
  12.1 3.6 %collective-permute-start.2 = (f32[12,32,384]{2,1,0:T(8,128)}, f32[12,32,384]{2,1,0:T(8,128)S(1)}, u32[]{:S(2)}, u32[]{:S(2)}) collective-permute-start(f32[12,32,384]{2,1,0:T(8,128)} %get-tuple-element.30), channel_id=1, source_target_pairs={{0,1},{2,3},{4,5},{6,7},{8,9},{10,11},{12,13},{14,15},{16,17},{18,... | collective-permute-start | bytes 1769480 | tf_op jit(solution)/shard_map/ppermute | solution.py:49
  15.6 1.3 %collective-permute-start.3 = (f32[12,32,384]{2,1,0:T(8,128)}, f32[12,32,384]{2,1,0:T(8,128)S(1)}, u32[]{:S(2)}, u32[]{:S(2)}) collective-permute-start(f32[12,32,384]{2,1,0:T(8,128)} %get-tuple-element.29), channel_id=1, source_target_pairs={{1,0},{3,2},{5,4},{7,6},{9,8},{11,10},{13,12},{15,14},{17,16},{19,... | collective-permute-start | bytes 1769480 | tf_op jit(solution)/shard_map/ppermute | solution.py:49
  17.0 1.0 fusion.10
  18.0 6.8 %collective-permute-start.4 = (f32[12,9,384]{2,1,0:T(8,128)S(1)}, f32[12,9,384]{2,1,0:T(8,128)S(1)}, u32[]{:S(2)}, u32[]{:S(2)}) collective-permute-start(f32[12,9,384]{2,1,0:T(8,128)S(1)} %get-tuple-element.28), channel_id=1, source_target_pairs={{0,3},{2,5},{4,7},{8,11},{10,13},{12,15},{16,19},{18,21},{20,23},{... | collective-permute-start | bytes 497672 | tf_op jit(solution)/shard_map/ppermute | solution.py:49
  25.5 4.4 %collective-permute-done.4.refs_8_.refs_6_ = f32[12,9,384]{2,1,0:T(8,128)S(1)} collective-permute-done((f32[12,9,384]{2,1,0:T(8,128)S(1)}, f32[12,9,384]{2,1,0:T(8,128)S(1)}, u32[]{:S(2)}, u32[]{:S(2)}) %collective-permute-start.4) | collective-permute-done | bytes 165920 | tf_op jit(solution)/shard_map/ppermute | solution.py:49
  30.6 1.4 %collective-permute-start.6 = (f32[12,9,384]{2,1,0:T(8,128)}, f32[12,9,384]{2,1,0:T(8,128)}, u32[]{:S(2)}, u32[]{:S(2)}) collective-permute-start(f32[12,9,384]{2,1,0:T(8,128)} %get-tuple-element.26), channel_id=1, source_target_pairs={{2,1},{4,3},{6,5},{10,9},{12,11},{14,13},{18,17},{20,19},{22,21},{... | collective-permute-start | bytes 497672 | tf_op jit(solution)/shard_map/ppermute | solution.py:49
  32.0 1.3 %collective-permute-start.7 = (f32[12,9,384]{2,1,0:T(8,128)}, f32[12,9,384]{2,1,0:T(8,128)}, u32[]{:S(2)}, u32[]{:S(2)}) collective-permute-start(f32[12,9,384]{2,1,0:T(8,128)} %get-tuple-element.25), channel_id=1, source_target_pairs={{3,0},{5,2},{7,4},{11,8},{13,10},{15,12},{19,16},{21,18},{23,20},{... | collective-permute-start | bytes 497672 | tf_op jit(solution)/shard_map/ppermute | solution.py:49
  34.9 8.7 %collective-permute-done.7.refs_11_.refs_9_ = f32[12,9,384]{2,1,0:T(8,128)} collective-permute-done((f32[12,9,384]{2,1,0:T(8,128)}, f32[12,9,384]{2,1,0:T(8,128)}, u32[]{:S(2)}, u32[]{:S(2)}) %collective-permute-start.7) | collective-permute-done | bytes 165920 | tf_op jit(solution)/shard_map/ppermute | solution.py:49
  43.6 6.8 %shard_map.121 = (f32[1,5,32,1024]{3,2,1,0:T(8,128)}, f32[3,32,1024]{2,1,0:T(8,128)S(1)}, f32[3,32,1024]{2,1,0:T(8,128)S(1)}) custom-call(s32[4]{0:T(128)S(1)} %pad_add_fusion.refs_0_, s32[2]{0:T(128)S(1)} %pad_add_fusion.1.refs_1_, f32[3]{0:T(128)S(1)} %bitcast.39, f32[12,32,1024]{2,1,0:T(8,128)} %copy-done.6, f32[12,9,1024]{2,1,0:T(8,128)S(1)} %copy.23.refs_4_.refs_2_, ...), custom_call_target="tpu_custom_call" | custom-call | tf_op jit(solution)/shard_map/pallas_call | solution.py:234
  51.9 9.4 %copy.33 = f32[3,32,1024]{0,2,1:T(8,128)} copy(f32[3,32,1024]{2,1,0:T(8,128)} %copy-done.4) | data formatting | bytes 786432 | tf_op jit(solution)/shard_map/reshape | solution.py:248
  61.3 6.4 %gather_fusion = f32[128,3]{1,0:T(8,128)S(1)} fusion(f32[3,32768]{0,1:T(8,128)} %bitcast.40, s32[1024]{0:T(1024)S(1)} %pad_clamp_fusion), kind=kCustom, calls=%fused_computation | custom fusion | bytes 3584 | tf_op jit(solution)/shard_map/gather | solution.py:248
  68.0 1.3 %scatter_custom_fusion = f32[32768]{0:T(1024)S(1)} fusion(s32[128]{0:T(128)S(1)} %fusion.8, f32[128]{0:T(128)S(1)} %get-tuple-element.24, f32[]{:T(128)} %constant.56.clone.1), kind=kCustom, calls=%fused_computation.14 | custom fusion | flops 128 | bytes 131076 | tf_op jit(solution)/shard_map/scatter-add | solution.py:251
  70.9 1.9 %scatter_custom_fusion.1 = f32[32768]{0:T(1024)} fusion(s32[128]{0:T(128)S(1)} %fusion.8, f32[128]{0:T(128)S(1)} %get-tuple-element.23, f32[]{:T(128)} %constant.56.clone.1), kind=kCustom, calls=%fused_computation.12 | custom fusion | flops 128 | bytes 131076 | tf_op jit(solution)/shard_map/scatter-add | solution.py:251
  72.7 1.6 %stack.45 = f32[1,32,1024]{2,1,0:T(8,128)} reshape(f32[32768]{0:T(1024)} %scatter_custom_fusion.1) | data formatting | bytes 262144 | tf_op jit(solution)/shard_map/stack | solution.py:250
  74.3 1.9 %scatter_custom_fusion.2 = f32[32768]{0:T(1024)} fusion(s32[128]{0:T(128)S(1)} %fusion.8, f32[128]{0:T(128)S(1)} %get-tuple-element.22, f32[]{:T(128)} %constant.56.clone.1), kind=kCustom, calls=%fused_computation.10 | custom fusion | flops 128 | bytes 131076 | tf_op jit(solution)/shard_map/scatter-add | solution.py:251
  76.2 1.6 %stack.46 = f32[1,32,1024]{2,1,0:T(8,128)} reshape(f32[32768]{0:T(1024)} %scatter_custom_fusion.2) | data formatting | bytes 262144 | tf_op jit(solution)/shard_map/stack | solution.py:250
  77.8 1.0 constant_dynamic-update-slice_fusion.1
  79.8 4.1 %collective-permute-start.12 = (f32[3,9,384]{2,1,0:T(8,128)S(1)}, f32[3,9,384]{2,1,0:T(8,128)S(1)}, u32[]{:S(2)}, u32[]{:S(2)}) collective-permute-start(f32[3,9,384]{2,1,0:T(8,128)S(1)} %get-tuple-element.36), channel_id=1, source_target_pairs={{0,3},{2,5},{4,7},{8,11},{10,13},{12,15},{16,19},{18,21},{20,23},{... | collective-permute-start | bytes 124424 | tf_op jit(solution)/shard_map/ppermute | solution.py:49
  85.2 9.9 %collective-permute-start.8 = (f32[3,9,1024]{2,1,0:T(8,128)S(1)}, f32[3,9,1024]{2,1,0:T(8,128)S(1)}, u32[]{:S(2)}, u32[]{:S(2)}) collective-permute-start(f32[3,9,1024]{2,1,0:T(8,128)S(1)} %get-tuple-element.40), channel_id=1, source_target_pairs={{0,2},{1,3},{2,4},{3,5},{4,6},{5,7},{8,10},{9,11},{10,12},{11,13},... | collective-permute-start | bytes 331784 | tf_op jit(solution)/shard_map/ppermute | solution.py:49
  95.2 1.3 %collective-permute-start.9 = (f32[3,9,1024]{2,1,0:T(8,128)S(1)}, f32[3,9,1024]{2,1,0:T(8,128)S(1)}, u32[]{:S(2)}, u32[]{:S(2)}) collective-permute-start(f32[3,9,1024]{2,1,0:T(8,128)S(1)} %get-tuple-element.39), channel_id=1, source_target_pairs={{2,0},{3,1},{4,2},{5,3},{6,4},{7,5},{10,8},{11,9},{12,10},{13,11},... | collective-permute-start | bytes 331784 | tf_op jit(solution)/shard_map/ppermute | solution.py:49
  96.5 1.4 %collective-permute-start.10 = (f32[3,32,384]{2,1,0:T(8,128)S(1)}, f32[3,32,384]{2,1,0:T(8,128)S(1)}, u32[]{:S(2)}, u32[]{:S(2)}) collective-permute-start(f32[3,32,384]{2,1,0:T(8,128)S(1)} %get-tuple-element.38), channel_id=1, source_target_pairs={{0,1},{2,3},{4,5},{6,7},{8,9},{10,11},{12,13},{14,15},{16,17},{18,... | collective-permute-start | bytes 442376 | tf_op jit(solution)/shard_map/ppermute | solution.py:49
  97.9 1.3 %collective-permute-start.11 = (f32[3,32,384]{2,1,0:T(8,128)S(1)}, f32[3,32,384]{2,1,0:T(8,128)S(1)}, u32[]{:S(2)}, u32[]{:S(2)}) collective-permute-start(f32[3,32,384]{2,1,0:T(8,128)S(1)} %get-tuple-element.37), channel_id=1, source_target_pairs={{1,0},{3,2},{5,4},{7,6},{9,8},{11,10},{13,12},{15,14},{17,16},{19,... | collective-permute-start | bytes 442376 | tf_op jit(solution)/shard_map/ppermute | solution.py:49
  99.2 1.5 %collective-permute-start.15 = (f32[3,9,384]{2,1,0:T(8,128)S(1)}, f32[3,9,384]{2,1,0:T(8,128)S(1)}, u32[]{:S(2)}, u32[]{:S(2)}) collective-permute-start(f32[3,9,384]{2,1,0:T(8,128)S(1)} %get-tuple-element.33), channel_id=1, source_target_pairs={{3,0},{5,2},{7,4},{11,8},{13,10},{15,12},{19,16},{21,18},{23,20},{... | collective-permute-start | bytes 124424 | tf_op jit(solution)/shard_map/ppermute | solution.py:49
  101.4 6.2 %collective-permute-done.15.refs_18_ = f32[3,9,384]{2,1,0:T(8,128)S(1)} collective-permute-done((f32[3,9,384]{2,1,0:T(8,128)S(1)}, f32[3,9,384]{2,1,0:T(8,128)S(1)}, u32[]{:S(2)}, u32[]{:S(2)}) %collective-permute-start.15) | collective-permute-done | bytes 41504 | tf_op jit(solution)/shard_map/ppermute | solution.py:49
  107.6 7.1 %shard_map.122 = (f32[1,5,32,1024]{3,2,1,0:T(8,128)}, f32[2,4,1024]{2,1,0:T(4,128)S(1)}) custom-call(s32[4]{0:T(128)S(1)} %pad_add_fusion.refs_0_, f32[12,32,1024]{2,1,0:T(8,128)} %copy-done.6, f32[12,9,1024]{2,1,0:T(8,128)S(1)} %copy.23.refs_4_.refs_2_, f32[12,9,1024]{2,1,0:T(8,128)S(1)} %copy.24.refs_5_.refs_3_, ...), custom_call_target="tpu_custom_call" | custom-call | tf_op jit(solution)/shard_map/pallas_call | solution.py:255
  116.6 6.3 %all_to_all.5 = f32[4,16,2]{1,2,0:T(2,128)S(1)} all-to-all(f32[4,16,2]{1,2,0:T(2,128)S(1)} %copy.31), channel_id=1, replica_groups=mesh['shot'=4,'gy'=4,'gx'=2] {'shot'}, dimensions={0} | all-to-all | bytes 1024 | tf_op jit(solution)/shard_map/all_to_all | solution.py:274
  (64 shorter events, 10.6 us)
Async XLA Ops:
  2.2 14.7 %copy-start.6 = (f32[12,32,1024]{2,1,0:T(8,128)}, f32[12,32,1024]{2,1,0:T(8,128)S(1)}, u32[]{:S(2)}) copy-start(f32[12,32,1024]{2,1,0:T(8,128)S(1)} %pad_maximum_fusion.refs_3_.refs_1_) | copy-start | bytes 4718596
  3.6 27.0 %collective-permute-start = (f32[12,9,1024]{2,0,1:T(8,128)}, f32[12,9,1024]{2,0,1:T(8,128)S(1)}, u32[]{:S(2)}, u32[]{:S(2)}) collective-permute-start(f32[12,9,1024]{2,0,1:T(8,128)} %copy.21), channel_id=1, source_target_pairs={{0,2},{1,3},{2,4},{3,5},{4,6},{5,7},{8,10},{9,11},{10,12},{11,13},... | collective-permute-start | bytes 1327112 | tf_op jit(solution)/shard_map/ppermute | solution.py:49
  9.6 22.4 %collective-permute-start.1 = (f32[12,9,1024]{2,0,1:T(8,128)}, f32[12,9,1024]{2,0,1:T(8,128)S(1)}, u32[]{:S(2)}, u32[]{:S(2)}) collective-permute-start(f32[12,9,1024]{2,0,1:T(8,128)} %copy.22), channel_id=1, source_target_pairs={{2,0},{3,1},{4,2},{5,3},{6,4},{7,5},{10,8},{11,9},{12,10},{13,11},... | collective-permute-start | bytes 1327112 | tf_op jit(solution)/shard_map/ppermute | solution.py:49
  12.1 12.7 %copy-start.10 = (s32[1,1,128]{2,1,0:T(1,128)S(1)}, s32[1,1,128]{2,1,0:T(1,128)}, u32[]{:S(2)}) copy-start(s32[1,1,128]{2,1,0:T(1,128)} %param.16) | copy-start | bytes 1540
  12.1 21.3 %copy-start.9 = (f32[1,3,1,128]{3,2,1,0:T(1,128)S(1)}, f32[1,3,1,128]{3,2,1,0:T(1,128)}, u32[]{:S(2)}) copy-start(f32[1,3,1,128]{3,2,1,0:T(1,128)} %param.17) | copy-start | bytes 4612
  12.1 31.5 %collective-permute-start.2 = (f32[12,32,384]{2,1,0:T(8,128)}, f32[12,32,384]{2,1,0:T(8,128)S(1)}, u32[]{:S(2)}, u32[]{:S(2)}) collective-permute-start(f32[12,32,384]{2,1,0:T(8,128)} %get-tuple-element.30), channel_id=1, source_target_pairs={{0,1},{2,3},{4,5},{6,7},{8,9},{10,11},{12,13},{14,15},{16,17},{18,... | collective-permute-start | bytes 1769480 | tf_op jit(solution)/shard_map/ppermute | solution.py:49
  15.6 27.9 %collective-permute-start.3 = (f32[12,32,384]{2,1,0:T(8,128)}, f32[12,32,384]{2,1,0:T(8,128)S(1)}, u32[]{:S(2)}, u32[]{:S(2)}) collective-permute-start(f32[12,32,384]{2,1,0:T(8,128)} %get-tuple-element.29), channel_id=1, source_target_pairs={{1,0},{3,2},{5,4},{7,6},{9,8},{11,10},{13,12},{15,14},{17,16},{19,... | collective-permute-start | bytes 1769480 | tf_op jit(solution)/shard_map/ppermute | solution.py:49
  18.0 25.6 %copy-start.5 = (f32[1,3]{1,0:T(1,128)S(1)}, f32[1,3]{1,0:T(1,128)}, u32[]{:S(2)}) copy-start(f32[1,3]{1,0:T(1,128)} %param.14) | copy-start | bytes 40
  18.0 12.0 %collective-permute-start.4 = (f32[12,9,384]{2,1,0:T(8,128)S(1)}, f32[12,9,384]{2,1,0:T(8,128)S(1)}, u32[]{:S(2)}, u32[]{:S(2)}) collective-permute-start(f32[12,9,384]{2,1,0:T(8,128)S(1)} %get-tuple-element.28), channel_id=1, source_target_pairs={{0,3},{2,5},{4,7},{8,11},{10,13},{12,15},{16,19},{18,21},{20,23},{... | collective-permute-start | bytes 497672 | tf_op jit(solution)/shard_map/ppermute | solution.py:49
  29.9 4.9 %collective-permute-start.5 = (f32[12,9,384]{2,1,0:T(8,128)}, f32[12,9,384]{2,1,0:T(8,128)S(1)}, u32[]{:S(2)}, u32[]{:S(2)}) collective-permute-start(f32[12,9,384]{2,1,0:T(8,128)} %get-tuple-element.27), channel_id=1, source_target_pairs={{1,2},{3,4},{5,6},{9,10},{11,12},{13,14},{17,18},{19,20},{21,22},{... | collective-permute-start | bytes 497672 | tf_op jit(solution)/shard_map/ppermute | solution.py:49
  30.6 4.3 %collective-permute-start.6 = (f32[12,9,384]{2,1,0:T(8,128)}, f32[12,9,384]{2,1,0:T(8,128)}, u32[]{:S(2)}, u32[]{:S(2)}) collective-permute-start(f32[12,9,384]{2,1,0:T(8,128)} %get-tuple-element.26), channel_id=1, source_target_pairs={{2,1},{4,3},{6,5},{10,9},{12,11},{14,13},{18,17},{20,19},{22,21},{... | collective-permute-start | bytes 497672 | tf_op jit(solution)/shard_map/ppermute | solution.py:49
  32.0 1.3 %copy-start.7 = (f32[12,9,1024]{2,0,1:T(8,128)}, f32[12,9,1024]{2,0,1:T(8,128)S(1)}, u32[]{:S(2)}) copy-start(f32[12,9,1024]{2,0,1:T(8,128)S(1)} %collective-permute-done.1) | copy-start | bytes 1327108
  32.0 11.5 %collective-permute-start.7 = (f32[12,9,384]{2,1,0:T(8,128)}, f32[12,9,384]{2,1,0:T(8,128)}, u32[]{:S(2)}, u32[]{:S(2)}) collective-permute-start(f32[12,9,384]{2,1,0:T(8,128)} %get-tuple-element.25), channel_id=1, source_target_pairs={{3,0},{5,2},{7,4},{11,8},{13,10},{15,12},{19,16},{21,18},{23,20},{... | collective-permute-start | bytes 497672 | tf_op jit(solution)/shard_map/ppermute | solution.py:49
  33.5 1.1 copy-start.8
  34.9 15.5 %copy-start = (f32[12,9,384]{2,1,0:T(8,128)}, f32[12,9,384]{2,1,0:T(8,128)S(1)}, u32[]{:S(2)}) copy-start(f32[12,9,384]{2,1,0:T(8,128)S(1)} %collective-permute-done.5.refs_9_.refs_7_) | copy-start | bytes 497668
  50.4 0.7 copy-start.2
  51.1 0.7 copy-start.4
  72.7 28.0 %copy-start.11 = (s32[1,64]{1,0:T(1,128)S(1)}, s32[1,64]{1,0:T(1,128)}, u32[]{:S(2)}) copy-start(s32[1,64]{1,0:T(1,128)} %param.19) | copy-start | bytes 772
  77.8 29.8 %copy-start.1 = (f32[12,9,384]{2,1,0:T(8,128)S(1)}, f32[12,9,384]{2,1,0:T(8,128)}, u32[]{:S(2)}) copy-start(f32[12,9,384]{2,1,0:T(8,128)} %copy-done) | copy-start | bytes 497668
  77.8 29.8 %copy-start.3 = (f32[3,32,1024]{2,1,0:T(8,128)S(1)}, f32[3,32,1024]{2,1,0:T(8,128)}, u32[]{:S(2)}) copy-start(f32[3,32,1024]{2,1,0:T(8,128)} %copy-done.2) | copy-start | bytes 1179652
  79.8 16.7 %collective-permute-start.12 = (f32[3,9,384]{2,1,0:T(8,128)S(1)}, f32[3,9,384]{2,1,0:T(8,128)S(1)}, u32[]{:S(2)}, u32[]{:S(2)}) collective-permute-start(f32[3,9,384]{2,1,0:T(8,128)S(1)} %get-tuple-element.36), channel_id=1, source_target_pairs={{0,3},{2,5},{4,7},{8,11},{10,13},{12,15},{16,19},{18,21},{20,23},{... | collective-permute-start | bytes 124424 | tf_op jit(solution)/shard_map/ppermute | solution.py:49
  83.9 14.1 %collective-permute-start.13 = (f32[3,9,384]{2,1,0:T(8,128)S(1)}, f32[3,9,384]{2,1,0:T(8,128)S(1)}, u32[]{:S(2)}, u32[]{:S(2)}) collective-permute-start(f32[3,9,384]{2,1,0:T(8,128)S(1)} %get-tuple-element.35), channel_id=1, source_target_pairs={{1,2},{3,4},{5,6},{9,10},{11,12},{13,14},{17,18},{19,20},{21,22},{... | collective-permute-start | bytes 124424 | tf_op jit(solution)/shard_map/ppermute | solution.py:49
  84.5 14.7 %collective-permute-start.14 = (f32[3,9,384]{2,1,0:T(8,128)S(1)}, f32[3,9,384]{2,1,0:T(8,128)S(1)}, u32[]{:S(2)}, u32[]{:S(2)}) collective-permute-start(f32[3,9,384]{2,1,0:T(8,128)S(1)} %get-tuple-element.34), channel_id=1, source_target_pairs={{2,1},{4,3},{6,5},{10,9},{12,11},{14,13},{18,17},{20,19},{22,21},{... | collective-permute-start | bytes 124424 | tf_op jit(solution)/shard_map/ppermute | solution.py:49
  85.2 22.3 %collective-permute-start.8 = (f32[3,9,1024]{2,1,0:T(8,128)S(1)}, f32[3,9,1024]{2,1,0:T(8,128)S(1)}, u32[]{:S(2)}, u32[]{:S(2)}) collective-permute-start(f32[3,9,1024]{2,1,0:T(8,128)S(1)} %get-tuple-element.40), channel_id=1, source_target_pairs={{0,2},{1,3},{2,4},{3,5},{4,6},{5,7},{8,10},{9,11},{10,12},{11,13},... | collective-permute-start | bytes 331784 | tf_op jit(solution)/shard_map/ppermute | solution.py:49
  95.2 12.4 %collective-permute-start.9 = (f32[3,9,1024]{2,1,0:T(8,128)S(1)}, f32[3,9,1024]{2,1,0:T(8,128)S(1)}, u32[]{:S(2)}, u32[]{:S(2)}) collective-permute-start(f32[3,9,1024]{2,1,0:T(8,128)S(1)} %get-tuple-element.39), channel_id=1, source_target_pairs={{2,0},{3,1},{4,2},{5,3},{6,4},{7,5},{10,8},{11,9},{12,10},{13,11},... | collective-permute-start | bytes 331784 | tf_op jit(solution)/shard_map/ppermute | solution.py:49
  96.5 11.1 %collective-permute-start.10 = (f32[3,32,384]{2,1,0:T(8,128)S(1)}, f32[3,32,384]{2,1,0:T(8,128)S(1)}, u32[]{:S(2)}, u32[]{:S(2)}) collective-permute-start(f32[3,32,384]{2,1,0:T(8,128)S(1)} %get-tuple-element.38), channel_id=1, source_target_pairs={{0,1},{2,3},{4,5},{6,7},{8,9},{10,11},{12,13},{14,15},{16,17},{18,... | collective-permute-start | bytes 442376 | tf_op jit(solution)/shard_map/ppermute | solution.py:49
  97.9 9.7 %collective-permute-start.11 = (f32[3,32,384]{2,1,0:T(8,128)S(1)}, f32[3,32,384]{2,1,0:T(8,128)S(1)}, u32[]{:S(2)}, u32[]{:S(2)}) collective-permute-start(f32[3,32,384]{2,1,0:T(8,128)S(1)} %get-tuple-element.37), channel_id=1, source_target_pairs={{1,0},{3,2},{5,4},{7,6},{9,8},{11,10},{13,12},{15,14},{17,16},{19,... | collective-permute-start | bytes 442376 | tf_op jit(solution)/shard_map/ppermute | solution.py:49
  99.2 8.3 %collective-permute-start.15 = (f32[3,9,384]{2,1,0:T(8,128)S(1)}, f32[3,9,384]{2,1,0:T(8,128)S(1)}, u32[]{:S(2)}, u32[]{:S(2)}) collective-permute-start(f32[3,9,384]{2,1,0:T(8,128)S(1)} %get-tuple-element.33), channel_id=1, source_target_pairs={{3,0},{5,2},{7,4},{11,8},{13,10},{15,12},{19,16},{21,18},{23,20},{... | collective-permute-start | bytes 124424 | tf_op jit(solution)/shard_map/ppermute | solution.py:49

commit v5 on v4

--- a/solution.py
+++ b/solution.py
@@ -129,7 +129,7 @@
 
 def forward_kernel(frame, bounds_ref, source_ref, wave_ref, own_ref, *rest):
     pieces = rest[:8]
-    end_ref, div_ref, pres_ref, ext = rest[8:]
+    gauge_ref, end_ref, div_ref, inject_ref, ext = rest[8:]
     for e, j in enumerate((0, 1, 2, 3, 4, 10, 11)):
         assemble(ext.at[e], own_ref, pieces, j, frame)
     wave_step, row, lane = stepper(frame, bounds_ref)
@@ -144,7 +144,7 @@
         state, div = wave_step(state, stiff, att)
         state[0] = state[0] + jnp.where(source, wave_ref[step], jnp.float32(0.0))
         div_ref[step] = div[mid, centre]
-        pres_ref[step] = state[0][mid, centre]
+        inject_ref[step] = gauge_ref[0] * state[0][mid, centre] - gauge_ref[1 + step]
     for k in range(5):
         end_ref[0, k] = state[k][mid, centre]
 
@@ -231,25 +231,24 @@
     pieces = send_pieces(stack, frame)
 
     ext_shape = (frame.ey, frame.el)
-    forward_end, divs, pres = pl.pallas_call(
+    recs = receiver_cells[0, 0]
+    gauge = jnp.stack(
+        [jnp.zeros((ny * lanes,), jnp.float32).at[recs].add(1.0)]
+        + [jnp.zeros((ny * lanes,), jnp.float32).at[recs].add(observed[0, n, 0]) for n in range(STEPS)]
+    ).reshape(1 + STEPS, ny, lanes)
+
+    forward_end, divs, inject = pl.pallas_call(
         lambda *refs: forward_kernel(frame, *refs),
         out_shape=(
             jax.ShapeDtypeStruct((1, 5, ny, lanes), jnp.float32),
             jax.ShapeDtypeStruct((STEPS, ny, lanes), jnp.float32),
             jax.ShapeDtypeStruct((STEPS, ny, lanes), jnp.float32),
         ),
-        in_specs=[smem(), smem(), smem()] + [vmem()] * 9,
+        in_specs=[smem(), smem(), smem()] + [vmem()] * 10,
         out_specs=(vmem(), vmem(), vmem()),
         scratch_shapes=[pltpu.VMEM((7,) + ext_shape, jnp.float32)],
         compiler_params=pltpu.CompilerParams(vmem_limit_bytes=48 * 1024 * 1024),
-    )(bounds, source, wavelet[0], stack, *pieces)
-
-    recs = receiver_cells[0, 0]
-    records = pres.reshape(STEPS, ny * lanes)[:, recs]
-    resid = records - observed[0, :, 0]
-    inject = jnp.stack(
-        [jnp.zeros((ny * lanes,), jnp.float32).at[recs].add(resid[n]) for n in range(STEPS)]
-    ).reshape(STEPS, ny, lanes)
+    )(bounds, source, wavelet[0], stack, *pieces, gauge)
     inject_pieces = send_pieces(inject, frame)
 
     adjoint_start, row_sums = pl.pallas_call(

time: 125 us -> 106 us (0.85)
  local copies, waits for them, and re-layouts: 32 us -> 13.8 us
  waiting for transfers between devices: 19.2 us -> 9.45 us
  starting transfers between devices: 42.1 us -> 47.8 us
  other arithmetic: 7.59 us -> 12.2 us
    ppermute x16, waiting for transfers between devices: 19.2 us -> 9.45 us  [move(): return lax.ppermute(piece, ('gy', 'gx'), pairs)]
    reshape x1 -> x0, local copies, waits for them, and re-layouts: 9.44 us -> none  [on_device(): records = pres.reshape(STEPS, ny * lanes)[:, recs]]
    gather x1 -> x0, local copies, waits for them, and re-layouts: 6.42 us -> none  [on_device(): records = pres.reshape(STEPS, ny * lanes)[:, recs]]
    ppermute x16, starting transfers between devices: 42.1 us -> 47.8 us  [move(): return lax.ppermute(piece, ('gy', 'gx'), pairs)]
    unnamed x27 -> x10, local copies, waits for them, and re-layouts: 4.29 us -> 0.02 us
    scatter-add x3 -> x4, other arithmetic: 5.04 us -> 7.98 us  [the longest x3 5.99 us: on_device(): jnp.zeros((ny * lanes,), jnp.float32).at[recs].add(observed[0, n, 0])]
    another operation x4, local copies, waits for them, and re-layouts: 4.76 us -> 6.32 us  [on_device(): jnp.stack([jnp.zeros((ny * lanes,), jnp.float32).at[recs].add(1.0)] + [jn...]
  transfers between devices with their start and end apart: 16 -> 16, of which waited for: 3 -> 2; matrix products, arithmetic and copies ran while one was open for 3% -> 20% of each run, Pallas kernels for 0% -> 0%
where the time goes in v5:
time: 106 us; the launch traced here: 105 us
  starting transfers between devices  47.8 us (45%)
  local copies, waits for them, and re-layouts  13.8 us (13%)
  Pallas kernels  13.6 us (13%)
  other arithmetic  12.2 us (12%)
  waiting for transfers between devices  9.45 us (9%)
  blocking collectives  6.34 us (6%)
  between operations  2.34 us (2%)
    ppermute x16, starting transfers between devices, move(): return lax.ppermute(piece, ('gy', 'gx'), pairs)  47.8 us
    ppermute x16, waiting for transfers between devices, move(): return lax.ppermute(piece, ('gy', 'gx'), pairs)  9.45 us
    pallas_call x1, Pallas kernels, on_device(): pl.pallas_call(lambda *refs: adjoint_kernel(frame, *refs), out_shape=(jax...  6.87 us
    pallas_call x1, Pallas kernels, on_device(): pl.pallas_call(lambda *refs: forward_kernel(frame, *refs), out_shape=(jax...  6.69 us
    all_to_all x1, blocking collectives, on_device(): lax.all_to_all(ordered.reshape(shots, -1, 2), 'shot', split_axis=0, conca...  6.34 us
    another operation x4, local copies, waits for them, and re-layouts, on_device(): jnp.stack([jnp.zeros((ny * lanes,), jnp.float32).at[recs].add(1.0)] + [jn...  6.32 us
    scatter-add x3, other arithmetic, on_device(): jnp.zeros((ny * lanes,), jnp.float32).at[recs].add(observed[0, n, 0])  5.99 us
  transfers between devices with their start and end apart: 16, of which 2 were waited for; matrix products, arithmetic and copies ran while one was open for 20% of the time, Pallas kernels for 0%

profile of v5, /device:TPU:0, one launch (start us, length us, event | category | flops | bytes accessed | tf_op | source)
XLA Modules:
  0.0 105.4 jit_solution(17909552136741983067)
XLA Ops:
  0.6 1.6 %pad_maximum_fusion.refs_3_.refs_1_ = f32[12,32,1024]{2,1,0:T(8,128)S(1)} fusion(f32[1,32,1024]{2,1,0:T(8,128)} %bitcast.43, f32[1,32,1024]{2,1,0:T(8,128)} %bitcast.44, f32[5,32,1024]{2,1,0:T(8,128)} %bitcast.41, f32[5,32,1024]{2,1,0:T(8,128)} %bitcast.42), kind=kLoop, calls=%fused_computation.5 | loop fusion | flops 1179648 | bytes 3145728 | tf_op jit(solution)/shard_map/concatenate | solution.py:228
  2.7 5.0 %collective-permute-start = (f32[12,9,1024]{2,0,1:T(8,128)S(1)}, f32[12,9,1024]{2,0,1:T(8,128)S(1)}, u32[]{:S(2)}, u32[]{:S(2)}) collective-permute-start(f32[12,9,1024]{2,0,1:T(8,128)S(1)} %copy.17), channel_id=1, source_target_pairs={{0,2},{1,3},{2,4},{3,5},{4,6},{5,7},{8,10},{9,11},{10,12},{11,13},... | collective-permute-start | bytes 1327112 | tf_op jit(solution)/shard_map/ppermute | solution.py:49
  7.6 1.1 %copy.18 = f32[12,9,1024]{2,0,1:T(8,128)} copy(f32[12,9,1024]{2,1,0:T(8,128)S(1)} %get-tuple-element.28) | data formatting | bytes 884736 | tf_op jit(solution)/shard_map/slice | solution.py:37
  8.7 1.3 %collective-permute-start.1 = (f32[12,9,1024]{2,0,1:T(8,128)}, f32[12,9,1024]{2,0,1:T(8,128)}, u32[]{:S(2)}, u32[]{:S(2)}) collective-permute-start(f32[12,9,1024]{2,0,1:T(8,128)} %copy.18), channel_id=1, source_target_pairs={{2,0},{3,1},{4,2},{5,3},{6,4},{7,5},{10,8},{11,9},{12,10},{13,11},... | collective-permute-start | bytes 1327112 | tf_op jit(solution)/shard_map/ppermute | solution.py:49
  10.0 1.0 fusion.13
  11.0 3.6 %collective-permute-start.2 = (f32[12,32,384]{2,1,0:T(8,128)}, f32[12,32,384]{2,1,0:T(8,128)S(1)}, u32[]{:S(2)}, u32[]{:S(2)}) collective-permute-start(f32[12,32,384]{2,1,0:T(8,128)} %get-tuple-element.27), channel_id=1, source_target_pairs={{0,1},{2,3},{4,5},{6,7},{8,9},{10,11},{12,13},{14,15},{16,17},{18,... | collective-permute-start | bytes 1769480 | tf_op jit(solution)/shard_map/ppermute | solution.py:49
  14.6 1.3 %collective-permute-start.3 = (f32[12,32,384]{2,1,0:T(8,128)S(1)}, f32[12,32,384]{2,1,0:T(8,128)S(1)}, u32[]{:S(2)}, u32[]{:S(2)}) collective-permute-start(f32[12,32,384]{2,1,0:T(8,128)S(1)} %get-tuple-element.26), channel_id=1, source_target_pairs={{1,0},{3,2},{5,4},{7,6},{9,8},{11,10},{13,12},{15,14},{17,16},{19,... | collective-permute-start | bytes 1769480 | tf_op jit(solution)/shard_map/ppermute | solution.py:49
  15.9 1.0 fusion.12
  16.9 6.7 %collective-permute-start.4 = (f32[12,9,384]{2,1,0:T(8,128)S(1)}, f32[12,9,384]{2,1,0:T(8,128)S(1)}, u32[]{:S(2)}, u32[]{:S(2)}) collective-permute-start(f32[12,9,384]{2,1,0:T(8,128)S(1)} %get-tuple-element.25), channel_id=1, source_target_pairs={{0,3},{2,5},{4,7},{8,11},{10,13},{12,15},{16,19},{18,21},{20,23},{... | collective-permute-start | bytes 497672 | tf_op jit(solution)/shard_map/ppermute | solution.py:49
  25.5 3.2 %collective-permute-done.4.refs_8_.refs_6_ = f32[12,9,384]{2,1,0:T(8,128)S(1)} collective-permute-done((f32[12,9,384]{2,1,0:T(8,128)S(1)}, f32[12,9,384]{2,1,0:T(8,128)S(1)}, u32[]{:S(2)}, u32[]{:S(2)}) %collective-permute-start.4) | collective-permute-done | bytes 165920 | tf_op jit(solution)/shard_map/ppermute | solution.py:49
  30.1 1.3 %collective-permute-start.7 = (f32[12,9,384]{2,1,0:T(8,128)}, f32[12,9,384]{2,1,0:T(8,128)S(1)}, u32[]{:S(2)}, u32[]{:S(2)}) collective-permute-start(f32[12,9,384]{2,1,0:T(8,128)} %get-tuple-element.22), channel_id=1, source_target_pairs={{3,0},{5,2},{7,4},{11,8},{13,10},{15,12},{19,16},{21,18},{23,20},{... | collective-permute-start | bytes 497672 | tf_op jit(solution)/shard_map/ppermute | solution.py:49
  31.5 2.0 %scatter_custom_fusion.3 = f32[32768]{0:T(1024)} fusion(s32[128]{0:T(128)} %fusion.10, f32[128]{0:T(128)} %get-tuple-element.39, f32[]{:T(128)} %constant.57.clone.1), kind=kCustom, calls=%fused_computation.7 | custom fusion | flops 128 | bytes 131584 | tf_op jit(solution)/shard_map/scatter-add | solution.py:237
  33.5 1.6 %stack.50 = f32[1,32,1024]{2,1,0:T(8,128)} reshape(f32[32768]{0:T(1024)} %scatter_custom_fusion.3) | data formatting | bytes 262144 | tf_op jit(solution)/shard_map/stack | solution.py:235
  35.0 2.0 %scatter_custom_fusion.2 = f32[32768]{0:T(1024)} fusion(s32[128]{0:T(128)} %fusion.10, f32[128]{0:T(128)S(1)} %get-tuple-element.40, f32[]{:T(128)} %constant.57.clone.1), kind=kCustom, calls=%fused_computation.9 | custom fusion | flops 128 | bytes 131584 | tf_op jit(solution)/shard_map/scatter-add | solution.py:237
  37.0 1.6 %stack.49 = f32[1,32,1024]{2,1,0:T(8,128)} reshape(f32[32768]{0:T(1024)} %scatter_custom_fusion.2) | data formatting | bytes 262144 | tf_op jit(solution)/shard_map/stack | solution.py:235
  38.6 2.0 %scatter_custom_fusion.1 = f32[32768]{0:T(1024)} fusion(s32[128]{0:T(128)} %fusion.10, f32[128]{0:T(128)S(1)} %get-tuple-element.38, f32[]{:T(128)} %constant.57.clone.1), kind=kCustom, calls=%fused_computation.11 | custom fusion | flops 128 | bytes 131584 | tf_op jit(solution)/shard_map/scatter-add | solution.py:237
  40.6 1.6 %stack.48 = f32[1,32,1024]{2,1,0:T(8,128)} reshape(f32[32768]{0:T(1024)} %scatter_custom_fusion.1) | data formatting | bytes 262144 | tf_op jit(solution)/shard_map/stack | solution.py:235
  42.2 2.0 %scatter_custom_fusion = f32[32768]{0:T(1024)} fusion(s32[128]{0:T(128)} %fusion.10, f32[128]{0:T(128)S(1)} %broadcast.46, f32[]{:T(128)} %constant.57.clone.1), kind=kCustom, calls=%fused_computation.13 | custom fusion | flops 128 | bytes 131584 | tf_op jit(solution)/shard_map/scatter-add | solution.py:236
  44.2 1.6 %stack.47 = f32[1,32,1024]{2,1,0:T(8,128)} reshape(f32[32768]{0:T(1024)} %scatter_custom_fusion) | data formatting | bytes 262144 | tf_op jit(solution)/shard_map/stack | solution.py:235
  45.8 1.1 %pad_maximum_fusion.1.refs_12_ = f32[4,32,1024]{2,1,0:T(8,128)S(1)} fusion(f32[1,32,1024]{2,1,0:T(8,128)} %stack.50, f32[1,32,1024]{2,1,0:T(8,128)} %stack.49, f32[1,32,1024]{2,1,0:T(8,128)} %stack.48, f32[1,32,1024]{2,1,0:T(8,128)} %stack.47), kind=kLoop, calls=%fused_computation.6 | loop fusion | flops 393216 | bytes 1048576 | tf_op jit(solution)/shard_map/stack | solution.py:235
  47.2 1.3 %copy.20.refs_5_.refs_3_ = f32[12,9,1024]{2,1,0:T(8,128)S(1)} copy(f32[12,9,1024]{2,0,1:T(8,128)} %collective-permute-done.1) | data formatting | bytes 884736 | tf_op jit(solution)/shard_map/ppermute | solution.py:49
  48.6 6.7 %shard_map.121 = (f32[1,5,32,1024]{3,2,1,0:T(8,128)}, f32[3,32,1024]{2,1,0:T(8,128)S(1)}, f32[3,32,1024]{2,1,0:T(8,128)S(1)}) custom-call(s32[4]{0:T(128)S(1)} %pad_add_fusion.refs_0_, s32[2]{0:T(128)S(1)} %pad_add_fusion.1.refs_1_, f32[3]{0:T(128)S(1)} %bitcast.40, f32[12,32,1024]{2,1,0:T(8,128)} %copy-done.1, f32[12,9,1024]{2,1,0:T(8,128)S(1)} %copy.19.refs_4_.refs_2_, ...), custom_call_target="tpu_custom_call" | custom-call | tf_op jit(solution)/shard_map/pallas_call | solution.py:240
  55.4 8.6 %collective-permute-start.12 = (f32[3,9,384]{2,1,0:T(8,128)S(1)}, f32[3,9,384]{2,1,0:T(8,128)S(1)}, u32[]{:S(2)}, u32[]{:S(2)}) collective-permute-start(f32[3,9,384]{2,1,0:T(8,128)S(1)} %get-tuple-element.33), channel_id=1, source_target_pairs={{0,3},{2,5},{4,7},{8,11},{10,13},{12,15},{16,19},{18,21},{20,23},{... | collective-permute-start | bytes 124424 | tf_op jit(solution)/shard_map/ppermute | solution.py:49
  65.4 11.1 %collective-permute-start.8 = (f32[3,9,1024]{2,1,0:T(8,128)S(1)}, f32[3,9,1024]{2,1,0:T(8,128)S(1)}, u32[]{:S(2)}, u32[]{:S(2)}) collective-permute-start(f32[3,9,1024]{2,1,0:T(8,128)S(1)} %get-tuple-element.37), channel_id=1, source_target_pairs={{0,2},{1,3},{2,4},{3,5},{4,6},{5,7},{8,10},{9,11},{10,12},{11,13},... | collective-permute-start | bytes 331784 | tf_op jit(solution)/shard_map/ppermute | solution.py:49
  76.5 1.3 %collective-permute-start.9 = (f32[3,9,1024]{2,1,0:T(8,128)S(1)}, f32[3,9,1024]{2,1,0:T(8,128)S(1)}, u32[]{:S(2)}, u32[]{:S(2)}) collective-permute-start(f32[3,9,1024]{2,1,0:T(8,128)S(1)} %get-tuple-element.36), channel_id=1, source_target_pairs={{2,0},{3,1},{4,2},{5,3},{6,4},{7,5},{10,8},{11,9},{12,10},{13,11},... | collective-permute-start | bytes 331784 | tf_op jit(solution)/shard_map/ppermute | solution.py:49
  77.8 2.2 %collective-permute-start.10 = (f32[3,32,384]{2,1,0:T(8,128)S(1)}, f32[3,32,384]{2,1,0:T(8,128)S(1)}, u32[]{:S(2)}, u32[]{:S(2)}) collective-permute-start(f32[3,32,384]{2,1,0:T(8,128)S(1)} %get-tuple-element.35), channel_id=1, source_target_pairs={{0,1},{2,3},{4,5},{6,7},{8,9},{10,11},{12,13},{14,15},{16,17},{18,... | collective-permute-start | bytes 442376 | tf_op jit(solution)/shard_map/ppermute | solution.py:49
  80.1 1.3 %collective-permute-start.11 = (f32[3,32,384]{2,1,0:T(8,128)S(1)}, f32[3,32,384]{2,1,0:T(8,128)S(1)}, u32[]{:S(2)}, u32[]{:S(2)}) collective-permute-start(f32[3,32,384]{2,1,0:T(8,128)S(1)} %get-tuple-element.34), channel_id=1, source_target_pairs={{1,0},{3,2},{5,4},{7,6},{9,8},{11,10},{13,12},{15,14},{17,16},{19,... | collective-permute-start | bytes 442376 | tf_op jit(solution)/shard_map/ppermute | solution.py:49
  81.4 1.5 %collective-permute-start.15 = (f32[3,9,384]{2,1,0:T(8,128)S(1)}, f32[3,9,384]{2,1,0:T(8,128)S(1)}, u32[]{:S(2)}, u32[]{:S(2)}) collective-permute-start(f32[3,9,384]{2,1,0:T(8,128)S(1)} %get-tuple-element.30), channel_id=1, source_target_pairs={{3,0},{5,2},{7,4},{11,8},{13,10},{15,12},{19,16},{21,18},{23,20},{... | collective-permute-start | bytes 124424 | tf_op jit(solution)/shard_map/ppermute | solution.py:49
  83.5 6.2 %collective-permute-done.15.refs_18_ = f32[3,9,384]{2,1,0:T(8,128)S(1)} collective-permute-done((f32[3,9,384]{2,1,0:T(8,128)S(1)}, f32[3,9,384]{2,1,0:T(8,128)S(1)}, u32[]{:S(2)}, u32[]{:S(2)}) %collective-permute-start.15) | collective-permute-done | bytes 41504 | tf_op jit(solution)/shard_map/ppermute | solution.py:49
  89.7 6.9 %shard_map.122 = (f32[1,5,32,1024]{3,2,1,0:T(8,128)}, f32[2,4,1024]{2,1,0:T(4,128)S(1)}) custom-call(s32[4]{0:T(128)S(1)} %pad_add_fusion.refs_0_, f32[12,32,1024]{2,1,0:T(8,128)} %copy-done.1, f32[12,9,1024]{2,1,0:T(8,128)S(1)} %copy.19.refs_4_.refs_2_, f32[12,9,1024]{2,1,0:T(8,128)S(1)} %copy.20.refs_5_.refs_3_, ...), custom_call_target="tpu_custom_call" | custom-call | tf_op jit(solution)/shard_map/pallas_call | solution.py:254
  97.7 0.8 scatter_custom_fusion.4
  98.5 6.3 %all_to_all.5 = f32[4,16,2]{1,2,0:T(2,128)S(1)} all-to-all(f32[4,16,2]{1,2,0:T(2,128)S(1)} %copy.25), channel_id=1, replica_groups=mesh['shot'=4,'gy'=4,'gx'=2] {'shot'}, dimensions={0} | all-to-all | bytes 1024 | tf_op jit(solution)/shard_map/all_to_all | solution.py:273
  (46 shorter events, 6.5 us)
Async XLA Ops:
  2.2 13.6 %copy-start.1 = (f32[12,32,1024]{2,1,0:T(8,128)}, f32[12,32,1024]{2,1,0:T(8,128)S(1)}, u32[]{:S(2)}) copy-start(f32[12,32,1024]{2,1,0:T(8,128)S(1)} %pad_maximum_fusion.refs_3_.refs_1_) | copy-start | bytes 4718596
  2.7 26.7 %collective-permute-start = (f32[12,9,1024]{2,0,1:T(8,128)S(1)}, f32[12,9,1024]{2,0,1:T(8,128)S(1)}, u32[]{:S(2)}, u32[]{:S(2)}) collective-permute-start(f32[12,9,1024]{2,0,1:T(8,128)S(1)} %copy.17), channel_id=1, source_target_pairs={{0,2},{1,3},{2,4},{3,5},{4,6},{5,7},{8,10},{9,11},{10,12},{11,13},... | collective-permute-start | bytes 1327112 | tf_op jit(solution)/shard_map/ppermute | solution.py:49
  8.7 21.4 %collective-permute-start.1 = (f32[12,9,1024]{2,0,1:T(8,128)}, f32[12,9,1024]{2,0,1:T(8,128)}, u32[]{:S(2)}, u32[]{:S(2)}) collective-permute-start(f32[12,9,1024]{2,0,1:T(8,128)} %copy.18), channel_id=1, source_target_pairs={{2,0},{3,1},{4,2},{5,3},{6,4},{7,5},{10,8},{11,9},{12,10},{13,11},... | collective-permute-start | bytes 1327112 | tf_op jit(solution)/shard_map/ppermute | solution.py:49
  11.0 12.6 %copy-start.2 = (f32[1,3,1,128]{3,2,1,0:T(1,128)S(1)}, f32[1,3,1,128]{3,2,1,0:T(1,128)}, u32[]{:S(2)}) copy-start(f32[1,3,1,128]{3,2,1,0:T(1,128)} %param.17) | copy-start | bytes 4612
  11.0 13.2 %copy-start.3 = (s32[1,1,128]{2,1,0:T(1,128)S(1)}, s32[1,1,128]{2,1,0:T(1,128)}, u32[]{:S(2)}) copy-start(s32[1,1,128]{2,1,0:T(1,128)} %param.16) | copy-start | bytes 1540
  11.0 37.6 %collective-permute-start.2 = (f32[12,32,384]{2,1,0:T(8,128)}, f32[12,32,384]{2,1,0:T(8,128)S(1)}, u32[]{:S(2)}, u32[]{:S(2)}) collective-permute-start(f32[12,32,384]{2,1,0:T(8,128)} %get-tuple-element.27), channel_id=1, source_target_pairs={{0,1},{2,3},{4,5},{6,7},{8,9},{10,11},{12,13},{14,15},{16,17},{18,... | collective-permute-start | bytes 1769480 | tf_op jit(solution)/shard_map/ppermute | solution.py:49
  14.6 34.0 %collective-permute-start.3 = (f32[12,32,384]{2,1,0:T(8,128)S(1)}, f32[12,32,384]{2,1,0:T(8,128)S(1)}, u32[]{:S(2)}, u32[]{:S(2)}) collective-permute-start(f32[12,32,384]{2,1,0:T(8,128)S(1)} %get-tuple-element.26), channel_id=1, source_target_pairs={{1,0},{3,2},{5,4},{7,6},{9,8},{11,10},{13,12},{15,14},{17,16},{19,... | collective-permute-start | bytes 1769480 | tf_op jit(solution)/shard_map/ppermute | solution.py:49
  16.9 11.8 %collective-permute-start.4 = (f32[12,9,384]{2,1,0:T(8,128)S(1)}, f32[12,9,384]{2,1,0:T(8,128)S(1)}, u32[]{:S(2)}, u32[]{:S(2)}) collective-permute-start(f32[12,9,384]{2,1,0:T(8,128)S(1)} %get-tuple-element.25), channel_id=1, source_target_pairs={{0,3},{2,5},{4,7},{8,11},{10,13},{12,15},{16,19},{18,21},{20,23},{... | collective-permute-start | bytes 497672 | tf_op jit(solution)/shard_map/ppermute | solution.py:49
  28.7 19.9 %collective-permute-start.5 = (f32[12,9,384]{2,1,0:T(8,128)}, f32[12,9,384]{2,1,0:T(8,128)S(1)}, u32[]{:S(2)}, u32[]{:S(2)}) collective-permute-start(f32[12,9,384]{2,1,0:T(8,128)} %get-tuple-element.24), channel_id=1, source_target_pairs={{1,2},{3,4},{5,6},{9,10},{11,12},{13,14},{17,18},{19,20},{21,22},{... | collective-permute-start | bytes 497672 | tf_op jit(solution)/shard_map/ppermute | solution.py:49
  29.4 19.2 %collective-permute-start.6 = (f32[12,9,384]{2,1,0:T(8,128)}, f32[12,9,384]{2,1,0:T(8,128)S(1)}, u32[]{:S(2)}, u32[]{:S(2)}) collective-permute-start(f32[12,9,384]{2,1,0:T(8,128)} %get-tuple-element.23), channel_id=1, source_target_pairs={{2,1},{4,3},{6,5},{10,9},{12,11},{14,13},{18,17},{20,19},{22,21},{... | collective-permute-start | bytes 497672 | tf_op jit(solution)/shard_map/ppermute | solution.py:49
  30.1 18.5 %collective-permute-start.7 = (f32[12,9,384]{2,1,0:T(8,128)}, f32[12,9,384]{2,1,0:T(8,128)S(1)}, u32[]{:S(2)}, u32[]{:S(2)}) collective-permute-start(f32[12,9,384]{2,1,0:T(8,128)} %get-tuple-element.22), channel_id=1, source_target_pairs={{3,0},{5,2},{7,4},{11,8},{13,10},{15,12},{19,16},{21,18},{23,20},{... | collective-permute-start | bytes 497672 | tf_op jit(solution)/shard_map/ppermute | solution.py:49
  46.9 1.7 %copy-start = (f32[1,3]{1,0:T(1,128)S(1)}, f32[1,3]{1,0:T(1,128)}, u32[]{:S(2)}) copy-start(f32[1,3]{1,0:T(1,128)} %param.14) | copy-start | bytes 40
  55.3 27.5 %copy-start.4 = (s32[1,64]{1,0:T(1,128)S(1)}, s32[1,64]{1,0:T(1,128)}, u32[]{:S(2)}) copy-start(s32[1,64]{1,0:T(1,128)} %param.19) | copy-start | bytes 772
  55.4 22.4 %collective-permute-start.12 = (f32[3,9,384]{2,1,0:T(8,128)S(1)}, f32[3,9,384]{2,1,0:T(8,128)S(1)}, u32[]{:S(2)}, u32[]{:S(2)}) collective-permute-start(f32[3,9,384]{2,1,0:T(8,128)S(1)} %get-tuple-element.33), channel_id=1, source_target_pairs={{0,3},{2,5},{4,7},{8,11},{10,13},{12,15},{16,19},{18,21},{20,23},{... | collective-permute-start | bytes 124424 | tf_op jit(solution)/shard_map/ppermute | solution.py:49
  64.0 16.1 %collective-permute-start.13 = (f32[3,9,384]{2,1,0:T(8,128)S(1)}, f32[3,9,384]{2,1,0:T(8,128)S(1)}, u32[]{:S(2)}, u32[]{:S(2)}) collective-permute-start(f32[3,9,384]{2,1,0:T(8,128)S(1)} %get-tuple-element.32), channel_id=1, source_target_pairs={{1,2},{3,4},{5,6},{9,10},{11,12},{13,14},{17,18},{19,20},{21,22},{... | collective-permute-start | bytes 124424 | tf_op jit(solution)/shard_map/ppermute | solution.py:49
  64.7 16.7 %collective-permute-start.14 = (f32[3,9,384]{2,1,0:T(8,128)S(1)}, f32[3,9,384]{2,1,0:T(8,128)S(1)}, u32[]{:S(2)}, u32[]{:S(2)}) collective-permute-start(f32[3,9,384]{2,1,0:T(8,128)S(1)} %get-tuple-element.31), channel_id=1, source_target_pairs={{2,1},{4,3},{6,5},{10,9},{12,11},{14,13},{18,17},{20,19},{22,21},{... | collective-permute-start | bytes 124424 | tf_op jit(solution)/shard_map/ppermute | solution.py:49
  65.4 24.3 %collective-permute-start.8 = (f32[3,9,1024]{2,1,0:T(8,128)S(1)}, f32[3,9,1024]{2,1,0:T(8,128)S(1)}, u32[]{:S(2)}, u32[]{:S(2)}) collective-permute-start(f32[3,9,1024]{2,1,0:T(8,128)S(1)} %get-tuple-element.37), channel_id=1, source_target_pairs={{0,2},{1,3},{2,4},{3,5},{4,6},{5,7},{8,10},{9,11},{10,12},{11,13},... | collective-permute-start | bytes 331784 | tf_op jit(solution)/shard_map/ppermute | solution.py:49
  76.5 13.2 %collective-permute-start.9 = (f32[3,9,1024]{2,1,0:T(8,128)S(1)}, f32[3,9,1024]{2,1,0:T(8,128)S(1)}, u32[]{:S(2)}, u32[]{:S(2)}) collective-permute-start(f32[3,9,1024]{2,1,0:T(8,128)S(1)} %get-tuple-element.36), channel_id=1, source_target_pairs={{2,0},{3,1},{4,2},{5,3},{6,4},{7,5},{10,8},{11,9},{12,10},{13,11},... | collective-permute-start | bytes 331784 | tf_op jit(solution)/shard_map/ppermute | solution.py:49
  77.8 11.9 %collective-permute-start.10 = (f32[3,32,384]{2,1,0:T(8,128)S(1)}, f32[3,32,384]{2,1,0:T(8,128)S(1)}, u32[]{:S(2)}, u32[]{:S(2)}) collective-permute-start(f32[3,32,384]{2,1,0:T(8,128)S(1)} %get-tuple-element.35), channel_id=1, source_target_pairs={{0,1},{2,3},{4,5},{6,7},{8,9},{10,11},{12,13},{14,15},{16,17},{18,... | collective-permute-start | bytes 442376 | tf_op jit(solution)/shard_map/ppermute | solution.py:49
  80.1 9.7 %collective-permute-start.11 = (f32[3,32,384]{2,1,0:T(8,128)S(1)}, f32[3,32,384]{2,1,0:T(8,128)S(1)}, u32[]{:S(2)}, u32[]{:S(2)}) collective-permute-start(f32[3,32,384]{2,1,0:T(8,128)S(1)} %get-tuple-element.34), channel_id=1, source_target_pairs={{1,0},{3,2},{5,4},{7,6},{9,8},{11,10},{13,12},{15,14},{17,16},{19,... | collective-permute-start | bytes 442376 | tf_op jit(solution)/shard_map/ppermute | solution.py:49
  81.4 8.3 %collective-permute-start.15 = (f32[3,9,384]{2,1,0:T(8,128)S(1)}, f32[3,9,384]{2,1,0:T(8,128)S(1)}, u32[]{:S(2)}, u32[]{:S(2)}) collective-permute-start(f32[3,9,384]{2,1,0:T(8,128)S(1)} %get-tuple-element.30), channel_id=1, source_target_pairs={{3,0},{5,2},{7,4},{11,8},{13,10},{15,12},{19,16},{21,18},{23,20},{... | collective-permute-start | bytes 124424 | tf_op jit(solution)/shard_map/ppermute | solution.py:49

commit v6 on v4

--- a/solution.py
+++ b/solution.py
@@ -10,7 +10,7 @@
 BY = 8
 BX = 8
 BZ = 8
-HALO = 3 * STEPS
+HALO = 3 * STEPS + 3 * (STEPS - 1)
 
 coef_near = 9.0 / 8.0
 coef_far = -1.0 / 24.0
@@ -127,53 +127,37 @@
     return wave_step, row, lane
 
 
-def forward_kernel(frame, bounds_ref, source_ref, wave_ref, own_ref, *rest):
+def window_kernel(frame, bounds_ref, source_ref, wave_ref, own_ref, *rest):
     pieces = rest[:8]
-    end_ref, div_ref, pres_ref, ext = rest[8:]
-    for e, j in enumerate((0, 1, 2, 3, 4, 10, 11)):
-        assemble(ext.at[e], own_ref, pieces, j, frame)
+    end_ref, start_ref, grad_ref, ext, inject, divs = rest[8:]
+    for j in range(16):
+        assemble(ext.at[j], own_ref, pieces, j, frame)
     wave_step, row, lane = stepper(frame, bounds_ref)
     source = (row == source_ref[0]) & (lane == source_ref[1])
-    vel = ext[5]
-    att = ext[6]
+    vel = ext[10]
+    att = ext[11]
     stiff = stiff_scale * vel * vel
-    state = [ext[k] for k in range(5)]
     mid = slice(frame.oy, frame.oy + frame.ny)
     centre = slice(frame.ox, frame.ox + frame.lanes)
+    state = [ext[k] for k in range(5)]
     for step in range(STEPS):
         state, div = wave_step(state, stiff, att)
         state[0] = state[0] + jnp.where(source, wave_ref[step], jnp.float32(0.0))
-        div_ref[step] = div[mid, centre]
-        pres_ref[step] = state[0][mid, centre]
+        divs[step] = div[mid, centre]
+        inject[step] = ext[12] * state[0] - ext[13 + step]
     for k in range(5):
         end_ref[0, k] = state[k][mid, centre]
 
-
-def adjoint_kernel(frame, bounds_ref, own_ref, *rest):
-    pieces = rest[:8]
-    inject_own = rest[8]
-    inject_pieces = rest[9:17]
-    div_ref, start_ref, grad_ref, ext = rest[17:]
-    for e, j in enumerate((5, 6, 7, 8, 9, 10, 11)):
-        assemble(ext.at[e], own_ref, pieces, j, frame)
-    for n in range(STEPS):
-        assemble(ext.at[7 + n], inject_own, inject_pieces, n, frame)
-    wave_step, row, lane = stepper(frame, bounds_ref)
-    vel = ext[5]
-    att = ext[6]
-    stiff = stiff_scale * vel * vel
-    mid = slice(frame.oy, frame.oy + frame.ny)
-    centre = slice(frame.ox, frame.ox + frame.lanes)
     velocity = vel[mid, centre]
     attenuation = att[mid, centre]
     stiff_own = stiff[mid, centre]
-    adj = [ext[k] for k in range(5)]
+    adj = [ext[5 + k] for k in range(5)]
     grad_v = jnp.zeros((frame.ny, frame.lanes), jnp.float32)
     grad_a = jnp.zeros((frame.ny, frame.lanes), jnp.float32)
     for step in range(STEPS - 1, -1, -1):
         adj, unused = wave_step(adj, stiff, att)
-        adj[0] = adj[0] + ext[7 + step]
-        div = div_ref[step]
+        adj[0] = adj[0] + inject[step]
+        div = divs[step]
         q = adj[0][mid, centre]
         m = adj[4][mid, centre]
         deriv_q = (relax_rate * attenuation - (1.0 + attenuation)) * div
@@ -225,44 +209,39 @@
     src_lane = cell % (total_x * nz) + lane_lo
     source = jnp.stack([src_row, src_lane]).astype(jnp.int32)
 
+    recs = receiver_cells[0, 0]
+    at_row = (recs // lanes)[:, None] == lax.broadcasted_iota(jnp.int32, (recs.shape[0], ny), 1)
+    at_lane = (recs % lanes)[:, None] == lax.broadcasted_iota(jnp.int32, (recs.shape[0], lanes), 1)
+    weights = jnp.concatenate([jnp.ones((1, recs.shape[0]), jnp.float32), observed[0, :, 0]], axis=0)
+    gauge = jnp.einsum(
+        "nky,kl->nyl",
+        weights[:, :, None] * at_row.astype(jnp.float32)[None],
+        at_lane.astype(jnp.float32),
+        precision=lax.Precision.HIGHEST,
+    )
+
     stack = jnp.concatenate(
-        [forward_start[0], adjoint_end[0], velocity[None], attenuation[None]], axis=0
+        [forward_start[0], adjoint_end[0], velocity[None], attenuation[None], gauge], axis=0
     )
     pieces = send_pieces(stack, frame)
 
     ext_shape = (frame.ey, frame.el)
-    forward_end, divs, pres = pl.pallas_call(
-        lambda *refs: forward_kernel(frame, *refs),
+    forward_end, adjoint_start, row_sums = pl.pallas_call(
+        lambda *refs: window_kernel(frame, *refs),
         out_shape=(
             jax.ShapeDtypeStruct((1, 5, ny, lanes), jnp.float32),
-            jax.ShapeDtypeStruct((STEPS, ny, lanes), jnp.float32),
-            jax.ShapeDtypeStruct((STEPS, ny, lanes), jnp.float32),
+            jax.ShapeDtypeStruct((1, 5, ny, lanes), jnp.float32),
+            jax.ShapeDtypeStruct((2, ny // BY, lanes), jnp.float32),
         ),
         in_specs=[smem(), smem(), smem()] + [vmem()] * 9,
         out_specs=(vmem(), vmem(), vmem()),
-        scratch_shapes=[pltpu.VMEM((7,) + ext_shape, jnp.float32)],
+        scratch_shapes=[
+            pltpu.VMEM((16,) + ext_shape, jnp.float32),
+            pltpu.VMEM((STEPS,) + ext_shape, jnp.float32),
+            pltpu.VMEM((STEPS, ny, lanes), jnp.float32),
+        ],
         compiler_params=pltpu.CompilerParams(vmem_limit_bytes=48 * 1024 * 1024),
     )(bounds, source, wavelet[0], stack, *pieces)
-
-    recs = receiver_cells[0, 0]
-    records = pres.reshape(STEPS, ny * lanes)[:, recs]
-    resid = records - observed[0, :, 0]
-    inject = jnp.stack(
-        [jnp.zeros((ny * lanes,), jnp.float32).at[recs].add(resid[n]) for n in range(STEPS)]
-    ).reshape(STEPS, ny, lanes)
-    inject_pieces = send_pieces(inject, frame)
-
-    adjoint_start, row_sums = pl.pallas_call(
-        lambda *refs: adjoint_kernel(frame, *refs),
-        out_shape=(
-            jax.ShapeDtypeStruct((1, 5, ny, lanes), jnp.float32),
-            jax.ShapeDtypeStruct((2, ny // BY, lanes), jnp.float32),
-        ),
-        in_specs=[smem()] + [vmem()] * 19,
-        out_specs=(vmem(), vmem()),
-        scratch_shapes=[pltpu.VMEM((10,) + ext_shape, jnp.float32)],
-        compiler_params=pltpu.CompilerParams(vmem_limit_bytes=48 * 1024 * 1024),
-    )(bounds, stack, *pieces, inject, *inject_pieces, divs)
 
     grad_scale = float(BY * BX * BZ) ** (-0.5)
     weight = aperture[0, 0].astype(jnp.float32)

time: 125 us -> 92.3 us (0.74)
  the two profiles are of different devices: /device:TPU:0 before, /device:TPU:16 now
where the time goes in v6:
time: 92.3 us; the launch traced here: 91.9 us
  waiting for transfers between devices  28.8 us (31%)
  starting transfers between devices  25.6 us (28%)
  Pallas kernels  14.6 us (16%)
  local copies, waits for them, and re-layouts  12.3 us (13%)
  blocking collectives  6.32 us (7%)
  between operations  2.25 us (2%)
  other arithmetic  1.65 us (2%)
    ppermute x8, waiting for transfers between devices, move(): return lax.ppermute(piece, ('gy', 'gx'), pairs)  28.8 us
    ppermute x8, starting transfers between devices, move(): return lax.ppermute(piece, ('gy', 'gx'), pairs)  25.6 us
    pallas_call x1, Pallas kernels, on_device(): pl.pallas_call(lambda *refs: window_kernel(frame, *refs), out_shape=(jax....  14.6 us
    all_to_all x1, blocking collectives, on_device(): lax.all_to_all(ordered.reshape(shots, -1, 2), 'shot', split_axis=0, conca...  6.32 us
    unnamed x21, local copies, waits for them, and re-layouts  3.96 us
    ppermute x2, local copies, waits for them, and re-layouts, move(): return lax.ppermute(piece, ('gy', 'gx'), pairs)  2.44 us
  transfers between devices with their start and end apart: 8, of which 3 were waited for; matrix products, arithmetic and copies ran while one was open for 6% of the time, Pallas kernels for 0%

profile of v6, /device:TPU:16, one launch (start us, length us, event | category | flops | bytes accessed | tf_op | source)
XLA Modules:
  0.0 91.9 jit_solution(5574741830659669154)
XLA Ops:
  0.7 0.7 and_select_fusion.1
  1.4 1.1 %bitcast_dynamic-update-slice_fusion.1 = f32[16,32,1024]{2,1,0:T(8,128)S(1)} fusion(f32[1,5,32,1024]{3,2,1,0:T(8,128)} %param.10), kind=kLoop, calls=%fused_computation.3 | loop fusion | bytes 1310720
  2.5 0.7 copy.30
  3.2 1.1 %bitcast_dynamic-update-slice_fusion = f32[16,32,1024]{2,1,0:T(8,128)S(1)} fusion(f32[16,32,1024]{2,1,0:T(8,128)S(1)} %bitcast_dynamic-update-slice_fusion.1, f32[1,5,32,1024]{3,2,1,0:T(8,128)} %param.11), kind=kLoop, calls=%fused_computation.2 | loop fusion | bytes 1310720
  4.4 0.5 convolution_dynamic-update-slice_fusion.refs_3_
  4.9 0.2 fusion.12
  5.1 0.6 copy.17
  5.7 3.5 %collective-permute-start = (f32[16,15,1024]{2,0,1:T(8,128)S(1)}, f32[16,15,1024]{2,0,1:T(8,128)S(1)}, u32[]{:S(2)}, u32[]{:S(2)}) collective-permute-start(f32[16,15,1024]{2,0,1:T(8,128)S(1)} %copy.17), channel_id=1, source_target_pairs={{0,2},{1,3},{2,4},{3,5},{4,6},{5,7},{8,10},{9,11},{10,12},{11,13},... | collective-permute-start | bytes 2949128 | tf_op jit(solution)/shard_map/ppermute | solution.py:49
  9.2 0.6 copy.18
  9.8 2.4 %collective-permute-start.1 = (f32[16,15,1024]{2,0,1:T(8,128)S(1)}, f32[16,15,1024]{2,0,1:T(8,128)S(1)}, u32[]{:S(2)}, u32[]{:S(2)}) collective-permute-start(f32[16,15,1024]{2,0,1:T(8,128)S(1)} %copy.18), channel_id=1, source_target_pairs={{2,0},{3,1},{4,2},{5,3},{6,4},{7,5},{10,8},{11,9},{12,10},{13,11},... | collective-permute-start | bytes 2949128 | tf_op jit(solution)/shard_map/ppermute | solution.py:49
  12.1 1.6 %fusion.11 = (f32[16,32,512]{2,1,0:T(8,128)}, f32[16,32,512]{2,1,0:T(8,128)}) fusion(f32[16,32,1024]{2,1,0:T(8,128)S(1)} %convolution_dynamic-update-slice_fusion.refs_3_), kind=kLoop, calls=%fused_computation.29 | loop fusion | bytes 4194304 | tf_op jit(solution)/shard_map/slice | solution.py:55
  13.7 3.5 %collective-permute-start.2 = (f32[16,32,512]{2,1,0:T(8,128)}, f32[16,32,512]{2,1,0:T(8,128)S(1)}, u32[]{:S(2)}, u32[]{:S(2)}) collective-permute-start(f32[16,32,512]{2,1,0:T(8,128)} %get-tuple-element.23), channel_id=1, source_target_pairs={{0,1},{2,3},{4,5},{6,7},{8,9},{10,11},{12,13},{14,15},{16,17},{18,... | collective-permute-start | bytes 3145736 | tf_op jit(solution)/shard_map/ppermute | solution.py:49
  17.2 1.3 %collective-permute-start.3 = (f32[16,32,512]{2,1,0:T(8,128)}, f32[16,32,512]{2,1,0:T(8,128)}, u32[]{:S(2)}, u32[]{:S(2)}) collective-permute-start(f32[16,32,512]{2,1,0:T(8,128)} %get-tuple-element.22), channel_id=1, source_target_pairs={{1,0},{3,2},{5,4},{7,6},{9,8},{11,10},{13,12},{15,14},{17,16},{19,... | collective-permute-start | bytes 3145736 | tf_op jit(solution)/shard_map/ppermute | solution.py:49
  18.5 1.2 %fusion.10 = (f32[16,15,512]{2,1,0:T(8,128)}, f32[16,15,512]{2,1,0:T(8,128)}, f32[16,15,512]{2,1,0:T(8,128)}, f32[16,15,512]{2,1,0:T(8,128)S(1)}) fusion(f32[16,32,1024]{2,1,0:T(8,128)S(1)} %convolution_dynamic-update-slice_fusion.refs_3_), kind=kLoop, calls=%fused_computation.28 | loop fusion | bytes 3932160 | tf_op jit(solution)/shard_map/slice | solution.py:59
  19.7 6.7 %collective-permute-start.4 = (f32[16,15,512]{2,1,0:T(8,128)S(1)}, f32[16,15,512]{2,1,0:T(8,128)S(1)}, u32[]{:S(2)}, u32[]{:S(2)}) collective-permute-start(f32[16,15,512]{2,1,0:T(8,128)S(1)} %get-tuple-element.21), channel_id=1, source_target_pairs={{0,3},{2,5},{4,7},{8,11},{10,13},{12,15},{16,19},{18,21},{20,23},{... | collective-permute-start | bytes 1474568 | tf_op jit(solution)/shard_map/ppermute | solution.py:49
  26.5 15.0 %collective-permute-done.4.refs_8_ = f32[16,15,512]{2,1,0:T(8,128)S(1)} collective-permute-done((f32[16,15,512]{2,1,0:T(8,128)S(1)}, f32[16,15,512]{2,1,0:T(8,128)S(1)}, u32[]{:S(2)}, u32[]{:S(2)}) %collective-permute-start.4) | collective-permute-done | bytes 491552 | tf_op jit(solution)/shard_map/ppermute | solution.py:49
  41.5 1.3 %collective-permute-start.5 = (f32[16,15,512]{2,1,0:T(8,128)}, f32[16,15,512]{2,1,0:T(8,128)S(1)}, u32[]{:S(2)}, u32[]{:S(2)}) collective-permute-start(f32[16,15,512]{2,1,0:T(8,128)} %get-tuple-element.20), channel_id=1, source_target_pairs={{1,2},{3,4},{5,6},{9,10},{11,12},{13,14},{17,18},{19,20},{21,22},{... | collective-permute-start | bytes 1474568 | tf_op jit(solution)/shard_map/ppermute | solution.py:49
  42.8 5.5 %collective-permute-start.6 = (f32[16,15,512]{2,1,0:T(8,128)}, f32[16,15,512]{2,1,0:T(8,128)S(1)}, u32[]{:S(2)}, u32[]{:S(2)}) collective-permute-start(f32[16,15,512]{2,1,0:T(8,128)} %get-tuple-element.19), channel_id=1, source_target_pairs={{2,1},{4,3},{6,5},{10,9},{12,11},{14,13},{18,17},{20,19},{22,21},{... | collective-permute-start | bytes 1474568 | tf_op jit(solution)/shard_map/ppermute | solution.py:49
  48.3 1.0 %copy-done.3 = f32[16,15,1024]{2,0,1:T(8,128)} copy-done((f32[16,15,1024]{2,0,1:T(8,128)}, f32[16,15,1024]{2,0,1:T(8,128)S(1)}, u32[]{:S(2)}) %copy-start.3) | copy-done | bytes 983064
  49.3 1.5 %collective-permute-start.7 = (f32[16,15,512]{2,1,0:T(8,128)}, f32[16,15,512]{2,1,0:T(8,128)S(1)}, u32[]{:S(2)}, u32[]{:S(2)}) collective-permute-start(f32[16,15,512]{2,1,0:T(8,128)} %get-tuple-element.18), channel_id=1, source_target_pairs={{3,0},{5,2},{7,4},{11,8},{13,10},{15,12},{19,16},{21,18},{23,20},{... | collective-permute-start | bytes 1474568 | tf_op jit(solution)/shard_map/ppermute | solution.py:49
  52.2 1.9 %copy.19.refs_4_ = f32[16,15,1024]{2,1,0:T(8,128)S(1)} copy(f32[16,15,1024]{2,0,1:T(8,128)} %copy-done.2) | data formatting | bytes 1966080 | tf_op jit(solution)/shard_map/ppermute | solution.py:49
  54.1 0.6 copy.20.refs_5_
  54.7 6.5 %collective-permute-done.5.refs_9_ = f32[16,15,512]{2,1,0:T(8,128)S(1)} collective-permute-done((f32[16,15,512]{2,1,0:T(8,128)}, f32[16,15,512]{2,1,0:T(8,128)S(1)}, u32[]{:S(2)}, u32[]{:S(2)}) %collective-permute-start.5) | collective-permute-done | bytes 491552 | tf_op jit(solution)/shard_map/ppermute | solution.py:49
  61.2 7.3 %collective-permute-done.7.refs_11_ = f32[16,15,512]{2,1,0:T(8,128)S(1)} collective-permute-done((f32[16,15,512]{2,1,0:T(8,128)}, f32[16,15,512]{2,1,0:T(8,128)S(1)}, u32[]{:S(2)}, u32[]{:S(2)}) %collective-permute-start.7) | collective-permute-done | bytes 491552 | tf_op jit(solution)/shard_map/ppermute | solution.py:49
  68.5 14.6 %shard_map.121 = (f32[1,5,32,1024]{3,2,1,0:T(8,128)}, f32[1,5,32,1024]{3,2,1,0:T(8,128)}, f32[2,4,1024]{2,1,0:T(4,128)S(1)}) custom-call(s32[4]{0:T(128)S(1)} %pad_add_fusion.refs_0_, s32[2]{0:T(128)S(1)} %pad_add_fusion.1.refs_1_, f32[3]{0:T(128)S(1)} %bitcast.55, f32[16,32,1024]{2,1,0:T(8,128)} %copy-done.1, f32[16,15,1024]{2,1,0:T(8,128)S(1)} %copy.19.refs_4_, ...), custom_call_target="tpu_custom_call" | custom-call | tf_op jit(solution)/shard_map/pallas_call | solution.py:229
  83.0 0.6 reshape.113
  83.7 0.2 reduce_sum.18
  83.9 0.2 copy.25
  84.1 0.8 scatter_custom_fusion
  84.9 0.1 copy.23
  85.0 6.3 %all_to_all.5 = f32[4,16,2]{1,2,0:T(2,128)S(1)} all-to-all(f32[4,16,2]{1,2,0:T(2,128)S(1)} %copy.23), channel_id=1, replica_groups=mesh['shot'=4,'gy'=4,'gx'=2] {'shot'}, dimensions={0} | all-to-all | bytes 1024 | tf_op jit(solution)/shard_map/all_to_all | solution.py:253
  91.3 0.6 reduce_sum.19
  (28 shorter events, 0.2 us)
Async XLA Ops:
  0.6 3.7 %copy-start.5 = (f32[32,1024]{1,0:T(8,128)S(1)}, f32[32,1024]{1,0:T(8,128)}, u32[]{:S(2)}) copy-start(f32[32,1024]{1,0:T(8,128)} %param.12) | copy-start | bytes 393220
  0.6 3.7 %copy-start.6 = (f32[32,1024]{1,0:T(8,128)S(1)}, f32[32,1024]{1,0:T(8,128)}, u32[]{:S(2)}) copy-start(f32[32,1024]{1,0:T(8,128)} %param.13) | copy-start | bytes 393220
  4.9 13.6 %copy-start.1 = (f32[16,32,1024]{2,1,0:T(8,128)}, f32[16,32,1024]{2,1,0:T(8,128)S(1)}, u32[]{:S(2)}) copy-start(f32[16,32,1024]{2,1,0:T(8,128)S(1)} %convolution_dynamic-update-slice_fusion.refs_3_) | copy-start | bytes 6291460
  5.7 37.1 %collective-permute-start = (f32[16,15,1024]{2,0,1:T(8,128)S(1)}, f32[16,15,1024]{2,0,1:T(8,128)S(1)}, u32[]{:S(2)}, u32[]{:S(2)}) collective-permute-start(f32[16,15,1024]{2,0,1:T(8,128)S(1)} %copy.17), channel_id=1, source_target_pairs={{0,2},{1,3},{2,4},{3,5},{4,6},{5,7},{8,10},{9,11},{10,12},{11,13},... | collective-permute-start | bytes 2949128 | tf_op jit(solution)/shard_map/ppermute | solution.py:49
  9.8 38.5 %collective-permute-start.1 = (f32[16,15,1024]{2,0,1:T(8,128)S(1)}, f32[16,15,1024]{2,0,1:T(8,128)S(1)}, u32[]{:S(2)}, u32[]{:S(2)}) collective-permute-start(f32[16,15,1024]{2,0,1:T(8,128)S(1)} %copy.18), channel_id=1, source_target_pairs={{2,0},{3,1},{4,2},{5,3},{6,4},{7,5},{10,8},{11,9},{12,10},{13,11},... | collective-permute-start | bytes 2949128 | tf_op jit(solution)/shard_map/ppermute | solution.py:49
  13.7 54.8 %collective-permute-start.2 = (f32[16,32,512]{2,1,0:T(8,128)}, f32[16,32,512]{2,1,0:T(8,128)S(1)}, u32[]{:S(2)}, u32[]{:S(2)}) collective-permute-start(f32[16,32,512]{2,1,0:T(8,128)} %get-tuple-element.23), channel_id=1, source_target_pairs={{0,1},{2,3},{4,5},{6,7},{8,9},{10,11},{12,13},{14,15},{16,17},{18,... | collective-permute-start | bytes 3145736 | tf_op jit(solution)/shard_map/ppermute | solution.py:49
  17.2 35.1 %copy-start.7 = (s32[1,64]{1,0:T(1,128)S(1)}, s32[1,64]{1,0:T(1,128)}, u32[]{:S(2)}) copy-start(s32[1,64]{1,0:T(1,128)} %param.19) | copy-start | bytes 772
  17.2 51.3 %collective-permute-start.3 = (f32[16,32,512]{2,1,0:T(8,128)}, f32[16,32,512]{2,1,0:T(8,128)}, u32[]{:S(2)}, u32[]{:S(2)}) collective-permute-start(f32[16,32,512]{2,1,0:T(8,128)} %get-tuple-element.22), channel_id=1, source_target_pairs={{1,0},{3,2},{5,4},{7,6},{9,8},{11,10},{13,12},{15,14},{17,16},{19,... | collective-permute-start | bytes 3145736 | tf_op jit(solution)/shard_map/ppermute | solution.py:49
  19.7 48.8 %copy-start = (f32[1,3]{1,0:T(1,128)S(1)}, f32[1,3]{1,0:T(1,128)}, u32[]{:S(2)}) copy-start(f32[1,3]{1,0:T(1,128)} %param.14) | copy-start | bytes 40
  19.7 21.7 %collective-permute-start.4 = (f32[16,15,512]{2,1,0:T(8,128)S(1)}, f32[16,15,512]{2,1,0:T(8,128)S(1)}, u32[]{:S(2)}, u32[]{:S(2)}) collective-permute-start(f32[16,15,512]{2,1,0:T(8,128)S(1)} %get-tuple-element.21), channel_id=1, source_target_pairs={{0,3},{2,5},{4,7},{8,11},{10,13},{12,15},{16,19},{18,21},{20,23},{... | collective-permute-start | bytes 1474568 | tf_op jit(solution)/shard_map/ppermute | solution.py:49
  41.5 19.8 %collective-permute-start.5 = (f32[16,15,512]{2,1,0:T(8,128)}, f32[16,15,512]{2,1,0:T(8,128)S(1)}, u32[]{:S(2)}, u32[]{:S(2)}) collective-permute-start(f32[16,15,512]{2,1,0:T(8,128)} %get-tuple-element.20), channel_id=1, source_target_pairs={{1,2},{3,4},{5,6},{9,10},{11,12},{13,14},{17,18},{19,20},{21,22},{... | collective-permute-start | bytes 1474568 | tf_op jit(solution)/shard_map/ppermute | solution.py:49
  42.8 5.5 %copy-start.2 = (f32[16,15,1024]{2,0,1:T(8,128)}, f32[16,15,1024]{2,0,1:T(8,128)S(1)}, u32[]{:S(2)}) copy-start(f32[16,15,1024]{2,0,1:T(8,128)S(1)} %collective-permute-done) | copy-start | bytes 2949124
  42.8 18.5 %collective-permute-start.6 = (f32[16,15,512]{2,1,0:T(8,128)}, f32[16,15,512]{2,1,0:T(8,128)S(1)}, u32[]{:S(2)}, u32[]{:S(2)}) collective-permute-start(f32[16,15,512]{2,1,0:T(8,128)} %get-tuple-element.19), channel_id=1, source_target_pairs={{2,1},{4,3},{6,5},{10,9},{12,11},{14,13},{18,17},{20,19},{22,21},{... | collective-permute-start | bytes 1474568 | tf_op jit(solution)/shard_map/ppermute | solution.py:49
  48.3 1.0 %copy-start.3 = (f32[16,15,1024]{2,0,1:T(8,128)}, f32[16,15,1024]{2,0,1:T(8,128)S(1)}, u32[]{:S(2)}) copy-start(f32[16,15,1024]{2,0,1:T(8,128)S(1)} %collective-permute-done.1) | copy-start | bytes 2949124
  49.3 19.2 %collective-permute-start.7 = (f32[16,15,512]{2,1,0:T(8,128)}, f32[16,15,512]{2,1,0:T(8,128)S(1)}, u32[]{:S(2)}, u32[]{:S(2)}) collective-permute-start(f32[16,15,512]{2,1,0:T(8,128)} %get-tuple-element.18), channel_id=1, source_target_pairs={{3,0},{5,2},{7,4},{11,8},{13,10},{15,12},{19,16},{21,18},{23,20},{... | collective-permute-start | bytes 1474568 | tf_op jit(solution)/shard_map/ppermute | solution.py:49
  52.1 2.0 %copy-start.4 = (f32[16,15,1024]{2,0,1:T(8,128)S(1)}, f32[16,15,1024]{2,0,1:T(8,128)}, u32[]{:S(2)}) copy-start(f32[16,15,1024]{2,0,1:T(8,128)} %copy-done.3) | copy-start | bytes 2949124

commit v7 on v4

--- a/solution.py
+++ b/solution.py
@@ -10,7 +10,7 @@
 BY = 8
 BX = 8
 BZ = 8
-HALO = 3 * STEPS
+HALO = 3 * STEPS + 3 * (STEPS - 1)
 
 coef_near = 9.0 / 8.0
 coef_far = -1.0 / 24.0
@@ -32,10 +32,14 @@
         self.el = 2 * self.ox + lanes
 
 
-def send_pieces(stack, frame):
-    ny, lanes, ox = frame.ny, frame.lanes, frame.ox
-    lo_rows = stack[:, :HALO]
-    hi_rows = stack[:, ny - HALO :]
+def lane_halo(halo):
+    return round_up(halo * CZ, 128)
+
+
+def send_pieces(stack, frame, halo):
+    ny, lanes, ox = frame.ny, frame.lanes, lane_halo(halo)
+    lo_rows = stack[:, :halo]
+    hi_rows = stack[:, ny - halo :]
     count_y = lax.axis_size("gy")
     count_x = lax.axis_size("gx")
 
@@ -60,15 +64,16 @@
     )
 
 
-def assemble(dst, own, pieces, j, frame):
-    ny, lanes, oy, ox, el = frame.ny, frame.lanes, frame.oy, frame.ox, frame.el
+def assemble(dst, own, pieces, j, frame, halo):
+    ny, lanes, oy, ox = frame.ny, frame.lanes, frame.oy, frame.ox
+    w = lane_halo(halo)
     below, above, left, right, b_l, b_r, a_l, a_r = pieces
-    lo = slice(oy - HALO, oy)
+    lo = slice(oy - halo, oy)
     mid = slice(oy, oy + ny)
-    hi = slice(oy + ny, oy + ny + HALO)
-    west = slice(0, ox)
+    hi = slice(oy + ny, oy + ny + halo)
+    west = slice(ox - w, ox)
     centre = slice(ox, ox + lanes)
-    east = slice(ox + lanes, el)
+    east = slice(ox + lanes, ox + lanes + w)
     dst[...] = jnp.zeros(dst.shape, dst.dtype)
     dst[mid, centre] = own[j]
     dst[lo, centre] = below[j]
@@ -130,37 +135,37 @@
 def forward_kernel(frame, bounds_ref, source_ref, wave_ref, own_ref, *rest):
     pieces = rest[:8]
     end_ref, div_ref, pres_ref, ext = rest[8:]
-    for e, j in enumerate((0, 1, 2, 3, 4, 10, 11)):
-        assemble(ext.at[e], own_ref, pieces, j, frame)
+    for j in range(7):
+        assemble(ext.at[j], own_ref, pieces, j, frame, HALO)
     wave_step, row, lane = stepper(frame, bounds_ref)
     source = (row == source_ref[0]) & (lane == source_ref[1])
     vel = ext[5]
     att = ext[6]
     stiff = stiff_scale * vel * vel
-    state = [ext[k] for k in range(5)]
     mid = slice(frame.oy, frame.oy + frame.ny)
     centre = slice(frame.ox, frame.ox + frame.lanes)
+    state = [ext[k] for k in range(5)]
     for step in range(STEPS):
         state, div = wave_step(state, stiff, att)
         state[0] = state[0] + jnp.where(source, wave_ref[step], jnp.float32(0.0))
         div_ref[step] = div[mid, centre]
-        pres_ref[step] = state[0][mid, centre]
+        pres_ref[step] = state[0]
     for k in range(5):
         end_ref[0, k] = state[k][mid, centre]
 
 
-def adjoint_kernel(frame, bounds_ref, own_ref, *rest):
-    pieces = rest[:8]
-    inject_own = rest[8]
-    inject_pieces = rest[9:17]
-    div_ref, start_ref, grad_ref, ext = rest[17:]
-    for e, j in enumerate((5, 6, 7, 8, 9, 10, 11)):
-        assemble(ext.at[e], own_ref, pieces, j, frame)
-    for n in range(STEPS):
-        assemble(ext.at[7 + n], inject_own, inject_pieces, n, frame)
+def adjoint_kernel(frame, bounds_ref, model_ref, model_pieces_ref, *rest):
+    model_pieces = (model_pieces_ref,) + rest[:7]
+    own_ref = rest[7]
+    pieces = rest[8:16]
+    first_ref, pres_ref, div_ref, start_ref, grad_ref, ext, field = rest[16:]
+    for e in range(2):
+        assemble(field.at[e], model_ref, model_pieces, 5 + e, frame, HALO)
+    for j in range(8):
+        assemble(ext.at[j], own_ref, pieces, j, frame, 3 * STEPS)
     wave_step, row, lane = stepper(frame, bounds_ref)
-    vel = ext[5]
-    att = ext[6]
+    vel = field[0]
+    att = field[1]
     stiff = stiff_scale * vel * vel
     mid = slice(frame.oy, frame.oy + frame.ny)
     centre = slice(frame.ox, frame.ox + frame.lanes)
@@ -172,15 +177,21 @@
     grad_a = jnp.zeros((frame.ny, frame.lanes), jnp.float32)
     for step in range(STEPS - 1, -1, -1):
         adj, unused = wave_step(adj, stiff, att)
-        adj[0] = adj[0] + ext[7 + step]
+        if step == 0:
+            q = adj[0][mid, centre] + (
+                ext[5][mid, centre] * pres_ref[0][mid, centre] - first_ref[...]
+            )
+        else:
+            adj[0] = adj[0] + (ext[5] * pres_ref[step] - ext[5 + step])
+            q = adj[0][mid, centre]
         div = div_ref[step]
-        q = adj[0][mid, centre]
         m = adj[4][mid, centre]
         deriv_q = (relax_rate * attenuation - (1.0 + attenuation)) * div
         deriv_m = -relax_rate * attenuation * div
         grad_v = grad_v + (q * deriv_q + m * deriv_m) * (2.0 * stiff_scale * velocity)
         grad_a = grad_a + (q * (relax_rate - 1.0) - m * relax_rate) * stiff_own * div
-    for k in range(5):
+    start_ref[0, 0] = q
+    for k in range(1, 5):
         start_ref[0, k] = adj[k][mid, centre]
     for c, g in enumerate((grad_v, grad_a)):
         grad_ref[c] = g.reshape(frame.ny // BY, BY, frame.lanes).sum(axis=1)
@@ -225,10 +236,21 @@
     src_lane = cell % (total_x * nz) + lane_lo
     source = jnp.stack([src_row, src_lane]).astype(jnp.int32)
 
-    stack = jnp.concatenate(
-        [forward_start[0], adjoint_end[0], velocity[None], attenuation[None]], axis=0
-    )
-    pieces = send_pieces(stack, frame)
+    recs = receiver_cells[0, 0]
+    at_row = (recs // lanes)[:, None] == lax.broadcasted_iota(jnp.int32, (recs.shape[0], ny), 1)
+    at_lane = (recs % lanes)[:, None] == lax.broadcasted_iota(jnp.int32, (recs.shape[0], lanes), 1)
+    weights = jnp.concatenate([jnp.ones((1, recs.shape[0]), jnp.float32), observed[0, :, 0]], axis=0)
+    gauge = jnp.einsum(
+        "nky,kl->nyl",
+        weights[:, :, None] * at_row.astype(jnp.float32)[None],
+        at_lane.astype(jnp.float32),
+        precision=lax.Precision.HIGHEST,
+    )
+
+    model = jnp.concatenate([forward_start[0], velocity[None], attenuation[None]], axis=0)
+    model_pieces = send_pieces(model, frame, HALO)
+    late = jnp.concatenate([adjoint_end[0], gauge[:1], gauge[2:]], axis=0)
+    late_pieces = send_pieces(late, frame, 3 * STEPS)
 
     ext_shape = (frame.ey, frame.el)
     forward_end, divs, pres = pl.pallas_call(
@@ -236,21 +258,13 @@
         out_shape=(
             jax.ShapeDtypeStruct((1, 5, ny, lanes), jnp.float32),
             jax.ShapeDtypeStruct((STEPS, ny, lanes), jnp.float32),
-            jax.ShapeDtypeStruct((STEPS, ny, lanes), jnp.float32),
+            jax.ShapeDtypeStruct((STEPS,) + ext_shape, jnp.float32),
         ),
         in_specs=[smem(), smem(), smem()] + [vmem()] * 9,
         out_specs=(vmem(), vmem(), vmem()),
         scratch_shapes=[pltpu.VMEM((7,) + ext_shape, jnp.float32)],
         compiler_params=pltpu.CompilerParams(vmem_limit_bytes=48 * 1024 * 1024),
-    )(bounds, source, wavelet[0], stack, *pieces)
-
-    recs = receiver_cells[0, 0]
-    records = pres.reshape(STEPS, ny * lanes)[:, recs]
-    resid = records - observed[0, :, 0]
-    inject = jnp.stack(
-        [jnp.zeros((ny * lanes,), jnp.float32).at[recs].add(resid[n]) for n in range(STEPS)]
-    ).reshape(STEPS, ny, lanes)
-    inject_pieces = send_pieces(inject, frame)
+    )(bounds, source, wavelet[0], model, *model_pieces)
 
     adjoint_start, row_sums = pl.pallas_call(
         lambda *refs: adjoint_kernel(frame, *refs),
@@ -258,11 +272,14 @@
             jax.ShapeDtypeStruct((1, 5, ny, lanes), jnp.float32),
             jax.ShapeDtypeStruct((2, ny // BY, lanes), jnp.float32),
         ),
-        in_specs=[smem()] + [vmem()] * 19,
+        in_specs=[smem()] + [vmem()] * 21,
         out_specs=(vmem(), vmem()),
-        scratch_shapes=[pltpu.VMEM((10,) + ext_shape, jnp.float32)],
+        scratch_shapes=[
+            pltpu.VMEM((8,) + ext_shape, jnp.float32),
+            pltpu.VMEM((2,) + ext_shape, jnp.float32),
+        ],
         compiler_params=pltpu.CompilerParams(vmem_limit_bytes=48 * 1024 * 1024),
-    )(bounds, stack, *pieces, inject, *inject_pieces, divs)
+    )(bounds, model, *model_pieces, late, *late_pieces, gauge[1], pres, divs)
 
     grad_scale = float(BY * BX * BZ) ** (-0.5)
     weight = aperture[0, 0].astype(jnp.float32)

time: 125 us -> 104 us (0.83)
  local copies, waits for them, and re-layouts: 32 us -> 10.9 us
  waiting for transfers between devices: 19.2 us -> 35.2 us
  starting transfers between devices: 42.1 us -> 28.1 us
  other arithmetic: 7.59 us -> 2.34 us
  Pallas kernels: 13.9 us -> 17.3 us
    ppermute x16, waiting for transfers between devices: 19.2 us -> 35.2 us  [move(): return lax.ppermute(piece, ('gy', 'gx'), pairs)]
    ppermute x16, starting transfers between devices: 42.1 us -> 28.1 us  [move(): return lax.ppermute(piece, ('gy', 'gx'), pairs)]
    reshape x1 -> x0, local copies, waits for them, and re-layouts: 9.44 us -> none  [on_device(): records = pres.reshape(STEPS, ny * lanes)[:, recs]]
    gather x1 -> x0, local copies, waits for them, and re-layouts: 6.42 us -> none  [on_device(): records = pres.reshape(STEPS, ny * lanes)[:, recs]]
    scatter-add x3 -> x0, other arithmetic: 5.04 us -> none  [on_device(): jnp.zeros((ny * lanes,), jnp.float32).at[recs].add(resid[n])]
    another operation x4 -> x0, local copies, waits for them, and re-layouts: 4.76 us -> none  [on_device(): jnp.stack([jnp.zeros((ny * lanes,), jnp.float32).at[recs].add(resid[n]) f...]
    pallas_call x1, Pallas kernels: 6.83 us -> 9.23 us  [on_device(): pl.pallas_call(lambda *refs: forward_kernel(frame, *refs), out_shape=(jax...]
    unnamed x27 -> x31, local copies, waits for them, and re-layouts: 4.29 us -> 2.58 us
  transfers between devices with their start and end apart: 16 -> 16, of which waited for: 3 -> 3; matrix products, arithmetic and copies ran while one was open for 3% -> 6% of each run, Pallas kernels for 0% -> 9%
where the time goes in v7:
time: 104 us; the launch traced here: 103 us
  waiting for transfers between devices  35.2 us (34%)
  starting transfers between devices  28.1 us (27%)
  Pallas kernels  17.3 us (17%)
  local copies, waits for them, and re-layouts  10.9 us (10%)
  blocking collectives  6.34 us (6%)
  between operations  2.41 us (2%)
  other arithmetic  2.34 us (2%)
    ppermute x16, waiting for transfers between devices, move(): return lax.ppermute(piece, ('gy', 'gx'), pairs)  35.2 us
    ppermute x16, starting transfers between devices, move(): return lax.ppermute(piece, ('gy', 'gx'), pairs)  28.1 us
    pallas_call x1, Pallas kernels, on_device(): pl.pallas_call(lambda *refs: forward_kernel(frame, *refs), out_shape=(jax...  9.23 us
    pallas_call x1, Pallas kernels, on_device(): pl.pallas_call(lambda *refs: adjoint_kernel(frame, *refs), out_shape=(jax...  8.1 us
    all_to_all x1, blocking collectives, on_device(): lax.all_to_all(ordered.reshape(shots, -1, 2), 'shot', split_axis=0, conca...  6.34 us
    unnamed x31, local copies, waits for them, and re-layouts  2.58 us
    slice x2, local copies, waits for them, and re-layouts, send_pieces(): lo_rows = stack[:, :halo]  2.21 us
  transfers between devices with their start and end apart: 16, of which 3 were waited for; matrix products, arithmetic and copies ran while one was open for 6% of the time, Pallas kernels for 9%

profile of v7, /device:TPU:0, one launch (start us, length us, event | category | flops | bytes accessed | tf_op | source)
XLA Modules:
  0.0 103.2 jit_solution(15459828100213444030)
XLA Ops:
  0.6 1.3 %pad_maximum_fusion.1.refs_3_.refs_1_ = f32[7,32,1024]{2,1,0:T(8,128)S(1)} fusion(f32[1,32,1024]{2,1,0:T(8,128)} %bitcast.56, f32[1,32,1024]{2,1,0:T(8,128)} %bitcast.57, f32[5,32,1024]{2,1,0:T(8,128)} %bitcast.54), kind=kLoop, calls=%fused_computation.2 | loop fusion | flops 458752 | bytes 1835008 | tf_op jit(solution)/shard_map/concatenate | solution.py:250
  2.0 1.1 %fusion.16 = (f32[7,15,1024]{2,1,0:T(8,128)}, f32[7,15,1024]{2,1,0:T(8,128)}) fusion(f32[7,32,1024]{2,1,0:T(8,128)S(1)} %pad_maximum_fusion.1.refs_3_.refs_1_), kind=kLoop, calls=%fused_computation.32 | loop fusion | bytes 1720320 | tf_op jit(solution)/shard_map/slice | solution.py:41
  3.1 5.1 %collective-permute-start = (f32[7,15,1024]{2,1,0:T(8,128)}, f32[7,15,1024]{2,1,0:T(8,128)S(1)}, u32[]{:S(2)}, u32[]{:S(2)}) collective-permute-start(f32[7,15,1024]{2,1,0:T(8,128)} %get-tuple-element.37), channel_id=1, source_target_pairs={{0,2},{1,3},{2,4},{3,5},{4,6},{5,7},{8,10},{9,11},{10,12},{11,13},... | collective-permute-start | bytes 1290248 | tf_op jit(solution)/shard_map/ppermute | solution.py:53
  8.2 0.8 fusion.14
  9.0 4.4 %collective-permute-start.4 = (f32[7,15,512]{2,1,0:T(8,128)S(1)}, f32[7,15,512]{2,1,0:T(8,128)S(1)}, u32[]{:S(2)}, u32[]{:S(2)}) collective-permute-start(f32[7,15,512]{2,1,0:T(8,128)S(1)} %get-tuple-element.33), channel_id=1, source_target_pairs={{0,3},{2,5},{4,7},{8,11},{10,13},{12,15},{16,19},{18,21},{20,23},{... | collective-permute-start | bytes 645128 | tf_op jit(solution)/shard_map/ppermute | solution.py:53
  14.1 0.7 slice_bitcast_fusion
  14.8 0.9 fusion.11
  15.7 1.3 %collective-permute-start.12 = (f32[8,9,384]{2,1,0:T(8,128)S(1)}, f32[8,9,384]{2,1,0:T(8,128)S(1)}, u32[]{:S(2)}, u32[]{:S(2)}) collective-permute-start(f32[8,9,384]{2,1,0:T(8,128)S(1)} %get-tuple-element.25), channel_id=1, source_target_pairs={{0,3},{2,5},{4,7},{8,11},{10,13},{12,15},{16,19},{18,21},{20,23},{... | collective-permute-start | bytes 331784 | tf_op jit(solution)/shard_map/ppermute | solution.py:53
  17.0 0.7 collective-permute-start.13
  17.6 0.7 collective-permute-start.14
  18.3 1.0 %fusion.15 = (f32[7,32,512]{2,1,0:T(8,128)}, f32[7,32,512]{2,1,0:T(8,128)}) fusion(f32[7,32,1024]{2,1,0:T(8,128)S(1)} %pad_maximum_fusion.1.refs_3_.refs_1_), kind=kLoop, calls=%fused_computation.31 | loop fusion | bytes 1835008 | tf_op jit(solution)/shard_map/slice | solution.py:59
  19.4 12.1 %collective-permute-done.12.refs_15_ = f32[8,9,384]{2,1,0:T(8,128)S(1)} collective-permute-done((f32[8,9,384]{2,1,0:T(8,128)S(1)}, f32[8,9,384]{2,1,0:T(8,128)S(1)}, u32[]{:S(2)}, u32[]{:S(2)}) %collective-permute-start.12) | collective-permute-done | bytes 110624 | tf_op jit(solution)/shard_map/ppermute | solution.py:53
  32.1 1.3 %collective-permute-start.1 = (f32[7,15,1024]{2,1,0:T(8,128)}, f32[7,15,1024]{2,1,0:T(8,128)S(1)}, u32[]{:S(2)}, u32[]{:S(2)}) collective-permute-start(f32[7,15,1024]{2,1,0:T(8,128)} %get-tuple-element.36), channel_id=1, source_target_pairs={{2,0},{3,1},{4,2},{5,3},{6,4},{7,5},{10,8},{11,9},{12,10},{13,11},... | collective-permute-start | bytes 1290248 | tf_op jit(solution)/shard_map/ppermute | solution.py:53
  34.1 1.3 %collective-permute-start.2 = (f32[7,32,512]{2,1,0:T(8,128)}, f32[7,32,512]{2,1,0:T(8,128)S(1)}, u32[]{:S(2)}, u32[]{:S(2)}) collective-permute-start(f32[7,32,512]{2,1,0:T(8,128)} %get-tuple-element.35), channel_id=1, source_target_pairs={{0,1},{2,3},{4,5},{6,7},{8,9},{10,11},{12,13},{14,15},{16,17},{18,... | collective-permute-start | bytes 1376264 | tf_op jit(solution)/shard_map/ppermute | solution.py:53
  35.4 0.7 collective-permute-start.5
  36.2 0.7 collective-permute-start.6
  36.8 1.1 %fusion.13 = (f32[8,9,1024]{2,1,0:T(8,128)}, f32[8,9,1024]{2,1,0:T(8,128)}) fusion(f32[8,32,1024]{2,1,0:T(8,128)S(1)} %pad_maximum_fusion.refs_10_), kind=kLoop, calls=%fused_computation.29 | loop fusion | bytes 1179648 | tf_op jit(solution)/shard_map/slice | solution.py:41
  37.9 1.3 %collective-permute-start.3 = (f32[7,32,512]{2,1,0:T(8,128)}, f32[7,32,512]{2,1,0:T(8,128)S(1)}, u32[]{:S(2)}, u32[]{:S(2)}) collective-permute-start(f32[7,32,512]{2,1,0:T(8,128)} %get-tuple-element.34), channel_id=1, source_target_pairs={{1,0},{3,2},{5,4},{7,6},{9,8},{11,10},{13,12},{15,14},{17,16},{19,... | collective-permute-start | bytes 1376264 | tf_op jit(solution)/shard_map/ppermute | solution.py:53
  39.2 1.3 %collective-permute-start.7 = (f32[7,15,512]{2,1,0:T(8,128)}, f32[7,15,512]{2,1,0:T(8,128)}, u32[]{:S(2)}, u32[]{:S(2)}) collective-permute-start(f32[7,15,512]{2,1,0:T(8,128)} %get-tuple-element.30), channel_id=1, source_target_pairs={{3,0},{5,2},{7,4},{11,8},{13,10},{15,12},{19,16},{21,18},{23,20},{... | collective-permute-start | bytes 645128 | tf_op jit(solution)/shard_map/ppermute | solution.py:53
  40.5 1.0 fusion.12
  42.2 18.0 %collective-permute-done.7.refs_11_.refs_9_ = f32[7,15,512]{2,1,0:T(8,128)} collective-permute-done((f32[7,15,512]{2,1,0:T(8,128)}, f32[7,15,512]{2,1,0:T(8,128)}, u32[]{:S(2)}, u32[]{:S(2)}) %collective-permute-start.7) | collective-permute-done | bytes 215072 | tf_op jit(solution)/shard_map/ppermute | solution.py:53
  60.2 2.0 %collective-permute-start.10 = (f32[8,32,384]{2,1,0:T(8,128)}, f32[8,32,384]{2,1,0:T(8,128)}, u32[]{:S(2)}, u32[]{:S(2)}) collective-permute-start(f32[8,32,384]{2,1,0:T(8,128)} %get-tuple-element.27), channel_id=1, source_target_pairs={{0,1},{2,3},{4,5},{6,7},{8,9},{10,11},{12,13},{14,15},{16,17},{18,... | collective-permute-start | bytes 1179656 | tf_op jit(solution)/shard_map/ppermute | solution.py:53
  62.2 1.3 %collective-permute-start.11 = (f32[8,32,384]{2,1,0:T(8,128)}, f32[8,32,384]{2,1,0:T(8,128)}, u32[]{:S(2)}, u32[]{:S(2)}) collective-permute-start(f32[8,32,384]{2,1,0:T(8,128)} %get-tuple-element.26), channel_id=1, source_target_pairs={{1,0},{3,2},{5,4},{7,6},{9,8},{11,10},{13,12},{15,14},{17,16},{19,... | collective-permute-start | bytes 1179656 | tf_op jit(solution)/shard_map/ppermute | solution.py:53
  64.2 3.4 %collective-permute-start.8 = (f32[8,9,1024]{2,1,0:T(8,128)}, f32[8,9,1024]{2,1,0:T(8,128)S(1)}, u32[]{:S(2)}, u32[]{:S(2)}) collective-permute-start(f32[8,9,1024]{2,1,0:T(8,128)} %get-tuple-element.29), channel_id=1, source_target_pairs={{0,2},{1,3},{2,4},{3,5},{4,6},{5,7},{8,10},{9,11},{10,12},{11,13},... | collective-permute-start | bytes 884744 | tf_op jit(solution)/shard_map/ppermute | solution.py:53
  67.7 1.3 %collective-permute-start.9 = (f32[8,9,1024]{2,1,0:T(8,128)}, f32[8,9,1024]{2,1,0:T(8,128)S(1)}, u32[]{:S(2)}, u32[]{:S(2)}) collective-permute-start(f32[8,9,1024]{2,1,0:T(8,128)} %get-tuple-element.28), channel_id=1, source_target_pairs={{2,0},{3,1},{4,2},{5,3},{6,4},{7,5},{10,8},{11,9},{12,10},{13,11},... | collective-permute-start | bytes 884744 | tf_op jit(solution)/shard_map/ppermute | solution.py:53
  69.0 1.5 %collective-permute-start.15 = (f32[8,9,384]{2,1,0:T(8,128)}, f32[8,9,384]{2,1,0:T(8,128)S(1)}, u32[]{:S(2)}, u32[]{:S(2)}) collective-permute-start(f32[8,9,384]{2,1,0:T(8,128)} %get-tuple-element.22), channel_id=1, source_target_pairs={{3,0},{5,2},{7,4},{11,8},{13,10},{15,12},{19,16},{21,18},{23,20},{... | collective-permute-start | bytes 331784 | tf_op jit(solution)/shard_map/ppermute | solution.py:53
  70.6 9.2 %shard_map.121 = (f32[1,5,32,1024]{3,2,1,0:T(8,128)}, f32[3,32,1024]{2,1,0:T(8,128)S(1)}, f32[3,64,2048]{2,1,0:T(8,128)S(1)}) custom-call(s32[4]{0:T(128)S(1)} %pad_add_fusion.refs_0_, s32[2]{0:T(128)S(1)} %pad_add_fusion.1.refs_1_, f32[3]{0:T(128)S(1)} %bitcast.53, f32[7,32,1024]{2,1,0:T(8,128)S(1)} %pad_maximum_fusion.1.refs_3_.refs_1_, ...), custom_call_target="tpu_custom_call" | custom-call | tf_op jit(solution)/shard_map/pallas_call | solution.py:256
  79.8 1.2 %copy-done.1 = f32[3,64,2048]{2,1,0:T(8,128)} copy-done((f32[3,64,2048]{2,1,0:T(8,128)}, f32[3,64,2048]{2,1,0:T(8,128)S(1)}, u32[]{:S(2)}) %copy-start.1) | copy-done | bytes 1572888
  81.0 5.1 %collective-permute-done.15.refs_18_ = f32[8,9,384]{2,1,0:T(8,128)S(1)} collective-permute-done((f32[8,9,384]{2,1,0:T(8,128)}, f32[8,9,384]{2,1,0:T(8,128)S(1)}, u32[]{:S(2)}, u32[]{:S(2)}) %collective-permute-start.15) | collective-permute-done | bytes 110624 | tf_op jit(solution)/shard_map/ppermute | solution.py:53
  86.2 8.1 %shard_map.122 = (f32[1,5,32,1024]{3,2,1,0:T(8,128)}, f32[2,4,1024]{2,1,0:T(4,128)S(1)}) custom-call(s32[4]{0:T(128)S(1)} %pad_add_fusion.refs_0_, f32[7,32,1024]{2,1,0:T(8,128)} %copy-done, f32[7,15,1024]{2,1,0:T(8,128)S(1)} %collective-permute-done.refs_4_.refs_2_, f32[7,15,1024]{2,1,0:T(8,128)S(1)} %collective-permute-done.1.refs_5_.refs_3_, ...), custom_call_target="tpu_custom_call" | custom-call | tf_op jit(solution)/shard_map/pallas_call | solution.py:269
  95.4 0.8 scatter_custom_fusion
  96.3 6.3 %all_to_all.5 = f32[4,16,2]{1,2,0:T(2,128)S(1)} all-to-all(f32[4,16,2]{1,2,0:T(2,128)S(1)} %copy.19), channel_id=1, replica_groups=mesh['shot'=4,'gy'=4,'gx'=2] {'shot'}, dimensions={0} | all-to-all | bytes 1024 | tf_op jit(solution)/shard_map/all_to_all | solution.py:291
  (58 shorter events, 3.9 us)
Async XLA Ops:
  2.0 68.6 %copy-start = (f32[7,32,1024]{2,1,0:T(8,128)}, f32[7,32,1024]{2,1,0:T(8,128)S(1)}, u32[]{:S(2)}) copy-start(f32[7,32,1024]{2,1,0:T(8,128)S(1)} %pad_maximum_fusion.1.refs_3_.refs_1_) | copy-start | bytes 2752516
  2.0 11.5 %copy-start.13 = (s32[1,1,128]{2,1,0:T(1,128)S(1)}, s32[1,1,128]{2,1,0:T(1,128)}, u32[]{:S(2)}) copy-start(s32[1,1,128]{2,1,0:T(1,128)} %param.16) | copy-start | bytes 1540
  2.0 11.5 %copy-start.12 = (f32[1,3,1,128]{3,2,1,0:T(1,128)S(1)}, f32[1,3,1,128]{3,2,1,0:T(1,128)}, u32[]{:S(2)}) copy-start(f32[1,3,1,128]{3,2,1,0:T(1,128)} %param.17) | copy-start | bytes 4612
  3.1 11.6 %copy-start.11 = (f32[1,5,32,1024]{3,2,1,0:T(8,128)S(1)}, f32[1,5,32,1024]{3,2,1,0:T(8,128)}, u32[]{:S(2)}) copy-start(f32[1,5,32,1024]{3,2,1,0:T(8,128)} %param.11) | copy-start | bytes 1966084
  3.1 59.1 %collective-permute-start = (f32[7,15,1024]{2,1,0:T(8,128)}, f32[7,15,1024]{2,1,0:T(8,128)S(1)}, u32[]{:S(2)}, u32[]{:S(2)}) collective-permute-start(f32[7,15,1024]{2,1,0:T(8,128)} %get-tuple-element.37), channel_id=1, source_target_pairs={{0,2},{1,3},{2,4},{3,5},{4,6},{5,7},{8,10},{9,11},{10,12},{11,13},... | collective-permute-start | bytes 1290248 | tf_op jit(solution)/shard_map/ppermute | solution.py:53
  9.0 27.1 %collective-permute-start.4 = (f32[7,15,512]{2,1,0:T(8,128)S(1)}, f32[7,15,512]{2,1,0:T(8,128)S(1)}, u32[]{:S(2)}, u32[]{:S(2)}) collective-permute-start(f32[7,15,512]{2,1,0:T(8,128)S(1)} %get-tuple-element.33), channel_id=1, source_target_pairs={{0,3},{2,5},{4,7},{8,11},{10,13},{12,15},{16,19},{18,21},{20,23},{... | collective-permute-start | bytes 645128 | tf_op jit(solution)/shard_map/ppermute | solution.py:53
  14.8 25.7 %copy-start.10 = (f32[8,32,1024]{2,1,0:T(8,128)}, f32[8,32,1024]{2,1,0:T(8,128)S(1)}, u32[]{:S(2)}) copy-start(f32[8,32,1024]{2,1,0:T(8,128)S(1)} %pad_maximum_fusion.refs_10_) | copy-start | bytes 3145732
  15.7 15.8 %collective-permute-start.12 = (f32[8,9,384]{2,1,0:T(8,128)S(1)}, f32[8,9,384]{2,1,0:T(8,128)S(1)}, u32[]{:S(2)}, u32[]{:S(2)}) collective-permute-start(f32[8,9,384]{2,1,0:T(8,128)S(1)} %get-tuple-element.25), channel_id=1, source_target_pairs={{0,3},{2,5},{4,7},{8,11},{10,13},{12,15},{16,19},{18,21},{20,23},{... | collective-permute-start | bytes 331784 | tf_op jit(solution)/shard_map/ppermute | solution.py:53
  17.0 16.5 %collective-permute-start.13 = (f32[8,9,384]{2,1,0:T(8,128)S(1)}, f32[8,9,384]{2,1,0:T(8,128)S(1)}, u32[]{:S(2)}, u32[]{:S(2)}) collective-permute-start(f32[8,9,384]{2,1,0:T(8,128)S(1)} %get-tuple-element.24), channel_id=1, source_target_pairs={{1,2},{3,4},{5,6},{9,10},{11,12},{13,14},{17,18},{19,20},{21,22},{... | collective-permute-start | bytes 331784 | tf_op jit(solution)/shard_map/ppermute | solution.py:53
  17.6 17.8 %collective-permute-start.14 = (f32[8,9,384]{2,1,0:T(8,128)S(1)}, f32[8,9,384]{2,1,0:T(8,128)S(1)}, u32[]{:S(2)}, u32[]{:S(2)}) collective-permute-start(f32[8,9,384]{2,1,0:T(8,128)S(1)} %get-tuple-element.23), channel_id=1, source_target_pairs={{2,1},{4,3},{6,5},{10,9},{12,11},{14,13},{18,17},{20,19},{22,21},{... | collective-permute-start | bytes 331784 | tf_op jit(solution)/shard_map/ppermute | solution.py:53
  31.5 0.7 copy-start.3
  32.1 32.1 %collective-permute-start.1 = (f32[7,15,1024]{2,1,0:T(8,128)}, f32[7,15,1024]{2,1,0:T(8,128)S(1)}, u32[]{:S(2)}, u32[]{:S(2)}) collective-permute-start(f32[7,15,1024]{2,1,0:T(8,128)} %get-tuple-element.36), channel_id=1, source_target_pairs={{2,0},{3,1},{4,2},{5,3},{6,4},{7,5},{10,8},{11,9},{12,10},{13,11},... | collective-permute-start | bytes 1290248 | tf_op jit(solution)/shard_map/ppermute | solution.py:53
  33.4 0.7 copy-start.5
  34.1 33.6 %collective-permute-start.2 = (f32[7,32,512]{2,1,0:T(8,128)}, f32[7,32,512]{2,1,0:T(8,128)S(1)}, u32[]{:S(2)}, u32[]{:S(2)}) collective-permute-start(f32[7,32,512]{2,1,0:T(8,128)} %get-tuple-element.35), channel_id=1, source_target_pairs={{0,1},{2,3},{4,5},{6,7},{8,9},{10,11},{12,13},{14,15},{16,17},{18,... | collective-permute-start | bytes 1376264 | tf_op jit(solution)/shard_map/ppermute | solution.py:53
  35.4 2.5 %copy-start.7 = (f32[8,9,384]{2,1,0:T(8,128)}, f32[8,9,384]{2,1,0:T(8,128)S(1)}, u32[]{:S(2)}) copy-start(f32[8,9,384]{2,1,0:T(8,128)S(1)} %collective-permute-done.14.refs_17_) | copy-start | bytes 331780
  35.4 2.5 %collective-permute-start.5 = (f32[7,15,512]{2,1,0:T(8,128)S(1)}, f32[7,15,512]{2,1,0:T(8,128)S(1)}, u32[]{:S(2)}, u32[]{:S(2)}) collective-permute-start(f32[7,15,512]{2,1,0:T(8,128)S(1)} %get-tuple-element.32), channel_id=1, source_target_pairs={{1,2},{3,4},{5,6},{9,10},{11,12},{13,14},{17,18},{19,20},{21,22},{... | collective-permute-start | bytes 645128 | tf_op jit(solution)/shard_map/ppermute | solution.py:53
  36.1 32.8 %copy-start.14 = (s32[1,64]{1,0:T(1,128)S(1)}, s32[1,64]{1,0:T(1,128)}, u32[]{:S(2)}) copy-start(s32[1,64]{1,0:T(1,128)} %param.19) | copy-start | bytes 772
  36.1 34.4 %copy-start.9 = (f32[1,3]{1,0:T(1,128)S(1)}, f32[1,3]{1,0:T(1,128)}, u32[]{:S(2)}) copy-start(f32[1,3]{1,0:T(1,128)} %param.14) | copy-start | bytes 40
  36.2 3.0 %collective-permute-start.6 = (f32[7,15,512]{2,1,0:T(8,128)S(1)}, f32[7,15,512]{2,1,0:T(8,128)S(1)}, u32[]{:S(2)}, u32[]{:S(2)}) collective-permute-start(f32[7,15,512]{2,1,0:T(8,128)S(1)} %get-tuple-element.31), channel_id=1, source_target_pairs={{2,1},{4,3},{6,5},{10,9},{12,11},{14,13},{18,17},{20,19},{22,21},{... | collective-permute-start | bytes 645128 | tf_op jit(solution)/shard_map/ppermute | solution.py:53
  37.9 31.1 %collective-permute-start.3 = (f32[7,32,512]{2,1,0:T(8,128)}, f32[7,32,512]{2,1,0:T(8,128)S(1)}, u32[]{:S(2)}, u32[]{:S(2)}) collective-permute-start(f32[7,32,512]{2,1,0:T(8,128)} %get-tuple-element.34), channel_id=1, source_target_pairs={{1,0},{3,2},{5,4},{7,6},{9,8},{11,10},{13,12},{15,14},{17,16},{19,... | collective-permute-start | bytes 1376264 | tf_op jit(solution)/shard_map/ppermute | solution.py:53
  39.2 21.0 %collective-permute-start.7 = (f32[7,15,512]{2,1,0:T(8,128)}, f32[7,15,512]{2,1,0:T(8,128)}, u32[]{:S(2)}, u32[]{:S(2)}) collective-permute-start(f32[7,15,512]{2,1,0:T(8,128)} %get-tuple-element.30), channel_id=1, source_target_pairs={{3,0},{5,2},{7,4},{11,8},{13,10},{15,12},{19,16},{21,18},{23,20},{... | collective-permute-start | bytes 645128 | tf_op jit(solution)/shard_map/ppermute | solution.py:53
  60.2 26.0 %collective-permute-start.10 = (f32[8,32,384]{2,1,0:T(8,128)}, f32[8,32,384]{2,1,0:T(8,128)}, u32[]{:S(2)}, u32[]{:S(2)}) collective-permute-start(f32[8,32,384]{2,1,0:T(8,128)} %get-tuple-element.27), channel_id=1, source_target_pairs={{0,1},{2,3},{4,5},{6,7},{8,9},{10,11},{12,13},{14,15},{16,17},{18,... | collective-permute-start | bytes 1179656 | tf_op jit(solution)/shard_map/ppermute | solution.py:53
  62.2 24.0 %collective-permute-start.11 = (f32[8,32,384]{2,1,0:T(8,128)}, f32[8,32,384]{2,1,0:T(8,128)}, u32[]{:S(2)}, u32[]{:S(2)}) collective-permute-start(f32[8,32,384]{2,1,0:T(8,128)} %get-tuple-element.26), channel_id=1, source_target_pairs={{1,0},{3,2},{5,4},{7,6},{9,8},{11,10},{13,12},{15,14},{17,16},{19,... | collective-permute-start | bytes 1179656 | tf_op jit(solution)/shard_map/ppermute | solution.py:53
  64.2 21.9 %collective-permute-start.8 = (f32[8,9,1024]{2,1,0:T(8,128)}, f32[8,9,1024]{2,1,0:T(8,128)S(1)}, u32[]{:S(2)}, u32[]{:S(2)}) collective-permute-start(f32[8,9,1024]{2,1,0:T(8,128)} %get-tuple-element.29), channel_id=1, source_target_pairs={{0,2},{1,3},{2,4},{3,5},{4,6},{5,7},{8,10},{9,11},{10,12},{11,13},... | collective-permute-start | bytes 884744 | tf_op jit(solution)/shard_map/ppermute | solution.py:53
  67.7 18.5 %collective-permute-start.9 = (f32[8,9,1024]{2,1,0:T(8,128)}, f32[8,9,1024]{2,1,0:T(8,128)S(1)}, u32[]{:S(2)}, u32[]{:S(2)}) collective-permute-start(f32[8,9,1024]{2,1,0:T(8,128)} %get-tuple-element.28), channel_id=1, source_target_pairs={{2,0},{3,1},{4,2},{5,3},{6,4},{7,5},{10,8},{11,9},{12,10},{13,11},... | collective-permute-start | bytes 884744 | tf_op jit(solution)/shard_map/ppermute | solution.py:53
  69.0 17.2 %collective-permute-start.15 = (f32[8,9,384]{2,1,0:T(8,128)}, f32[8,9,384]{2,1,0:T(8,128)S(1)}, u32[]{:S(2)}, u32[]{:S(2)}) collective-permute-start(f32[8,9,384]{2,1,0:T(8,128)} %get-tuple-element.22), channel_id=1, source_target_pairs={{3,0},{5,2},{7,4},{11,8},{13,10},{15,12},{19,16},{21,18},{23,20},{... | collective-permute-start | bytes 331784 | tf_op jit(solution)/shard_map/ppermute | solution.py:53
  70.6 15.6 %copy-start.2 = (f32[32,1024]{1,0:T(8,128)S(1)}, f32[32,1024]{1,0:T(8,128)}, u32[]{:S(2)}) copy-start(f32[32,1024]{1,0:T(8,128)} %get-tuple-element.38.refs_19_) | copy-start | bytes 393220
  70.6 15.6 %copy-start.4 = (f32[8,9,384]{2,1,0:T(8,128)S(1)}, f32[8,9,384]{2,1,0:T(8,128)}, u32[]{:S(2)}) copy-start(f32[8,9,384]{2,1,0:T(8,128)} %copy-done.3) | copy-start | bytes 331780
  70.6 15.6 %copy-start.6 = (f32[8,9,384]{2,1,0:T(8,128)S(1)}, f32[8,9,384]{2,1,0:T(8,128)}, u32[]{:S(2)}) copy-start(f32[8,9,384]{2,1,0:T(8,128)} %copy-done.5) | copy-start | bytes 331780
  70.6 15.6 %copy-start.8 = (f32[8,9,384]{2,1,0:T(8,128)S(1)}, f32[8,9,384]{2,1,0:T(8,128)}, u32[]{:S(2)}) copy-start(f32[8,9,384]{2,1,0:T(8,128)} %copy-done.7) | copy-start | bytes 331780
  79.8 1.2 %copy-start.1 = (f32[3,64,2048]{2,1,0:T(8,128)}, f32[3,64,2048]{2,1,0:T(8,128)S(1)}, u32[]{:S(2)}) copy-start(f32[3,64,2048]{2,1,0:T(8,128)S(1)} %get-tuple-element.9.refs_20_) | copy-start | bytes 4718596

commit v8 on v7

--- a/solution.py
+++ b/solution.py
@@ -250,6 +250,7 @@
     model = jnp.concatenate([forward_start[0], velocity[None], attenuation[None]], axis=0)
     model_pieces = send_pieces(model, frame, HALO)
     late = jnp.concatenate([adjoint_end[0], gauge[:1], gauge[2:]], axis=0)
+    late, model_pieces = lax.optimization_barrier((late, model_pieces))
     late_pieces = send_pieces(late, frame, 3 * STEPS)
 
     ext_shape = (frame.ey, frame.el)

time: 104 us -> 100 us (0.962)
  the two profiles are of different devices: /device:TPU:0 before, /device:TPU:12 now
where the time goes in v8:
time: 100 us; the launch traced here: 99.6 us
  starting transfers between devices  40.3 us (40%)
  waiting for transfers between devices  22.3 us (22%)
  Pallas kernels  17.1 us (17%)
  local copies, waits for them, and re-layouts  8.38 us (8%)
  blocking collectives  6.34 us (6%)
  other arithmetic  2.37 us (2%)
  between operations  2.32 us (2%)
    ppermute x16, starting transfers between devices, move(): return lax.ppermute(piece, ('gy', 'gx'), pairs)  40.3 us
    ppermute x16, waiting for transfers between devices, move(): return lax.ppermute(piece, ('gy', 'gx'), pairs)  22.3 us
    pallas_call x1, Pallas kernels, on_device(): pl.pallas_call(lambda *refs: forward_kernel(frame, *refs), out_shape=(jax...  8.78 us
    pallas_call x1, Pallas kernels, on_device(): pl.pallas_call(lambda *refs: adjoint_kernel(frame, *refs), out_shape=(jax...  8.32 us
    all_to_all x1, blocking collectives, on_device(): lax.all_to_all(ordered.reshape(shots, -1, 2), 'shot', split_axis=0, conca...  6.34 us
    unnamed x27, local copies, waits for them, and re-layouts  2.85 us
  transfers between devices with their start and end apart: 16, of which 5 were waited for; matrix products, arithmetic and copies ran while one was open for 3% of the time, Pallas kernels for 9%

profile of v8, /device:TPU:12, one launch (start us, length us, event | category | flops | bytes accessed | tf_op | source)
XLA Modules:
  0.0 99.6 jit_solution(706165621621292655)
XLA Ops:
  0.6 1.3 %pad_maximum_fusion.1.refs_3_.refs_1_ = f32[7,32,1024]{2,1,0:T(8,128)S(1)} fusion(f32[1,32,1024]{2,1,0:T(8,128)} %bitcast.56, f32[1,32,1024]{2,1,0:T(8,128)} %bitcast.57, f32[5,32,1024]{2,1,0:T(8,128)} %bitcast.54), kind=kLoop, calls=%fused_computation.2 | loop fusion | flops 458752 | bytes 1835008 | tf_op jit(solution)/shard_map/concatenate | solution.py:250
  2.0 3.5 %collective-permute-start = (f32[7,15,1024]{2,1,0:T(8,128)S(1)}, f32[7,15,1024]{2,1,0:T(8,128)S(1)}, u32[]{:S(2)}, u32[]{:S(2)}) collective-permute-start(f32[7,15,1024]{2,1,0:T(8,128)S(1)} %get-tuple-element.55), channel_id=1, source_target_pairs={{0,2},{1,3},{2,4},{3,5},{4,6},{5,7},{8,10},{9,11},{10,12},{11,13},... | collective-permute-start | bytes 1290248 | tf_op jit(solution)/shard_map/ppermute | solution.py:53
  5.6 2.4 %collective-permute-start.1 = (f32[7,15,1024]{2,1,0:T(8,128)S(1)}, f32[7,15,1024]{2,1,0:T(8,128)S(1)}, u32[]{:S(2)}, u32[]{:S(2)}) collective-permute-start(f32[7,15,1024]{2,1,0:T(8,128)S(1)} %get-tuple-element.54), channel_id=1, source_target_pairs={{2,0},{3,1},{4,2},{5,3},{6,4},{7,5},{10,8},{11,9},{12,10},{13,11},... | collective-permute-start | bytes 1290248 | tf_op jit(solution)/shard_map/ppermute | solution.py:53
  8.0 1.4 %collective-permute-start.2 = (f32[7,32,512]{2,1,0:T(8,128)S(1)}, f32[7,32,512]{2,1,0:T(8,128)S(1)}, u32[]{:S(2)}, u32[]{:S(2)}) collective-permute-start(f32[7,32,512]{2,1,0:T(8,128)S(1)} %get-tuple-element.53), channel_id=1, source_target_pairs={{0,1},{2,3},{4,5},{6,7},{8,9},{10,11},{12,13},{14,15},{16,17},{18,... | collective-permute-start | bytes 1376264 | tf_op jit(solution)/shard_map/ppermute | solution.py:53
  9.6 1.3 %collective-permute-start.4 = (f32[7,15,512]{2,1,0:T(8,128)S(1)}, f32[7,15,512]{2,1,0:T(8,128)S(1)}, u32[]{:S(2)}, u32[]{:S(2)}) collective-permute-start(f32[7,15,512]{2,1,0:T(8,128)S(1)} %get-tuple-element.51), channel_id=1, source_target_pairs={{0,3},{2,5},{4,7},{8,11},{10,13},{12,15},{16,19},{18,21},{20,23},{... | collective-permute-start | bytes 645128 | tf_op jit(solution)/shard_map/ppermute | solution.py:53
  10.9 6.6 %collective-permute-start.5 = (f32[7,15,512]{2,1,0:T(8,128)S(1)}, f32[7,15,512]{2,1,0:T(8,128)S(1)}, u32[]{:S(2)}, u32[]{:S(2)}) collective-permute-start(f32[7,15,512]{2,1,0:T(8,128)S(1)} %get-tuple-element.50), channel_id=1, source_target_pairs={{1,2},{3,4},{5,6},{9,10},{11,12},{13,14},{17,18},{19,20},{21,22},{... | collective-permute-start | bytes 645128 | tf_op jit(solution)/shard_map/ppermute | solution.py:53
  17.6 3.6 %collective-permute-done.4.refs_8_.refs_6_ = f32[7,15,512]{2,1,0:T(8,128)S(1)} collective-permute-done((f32[7,15,512]{2,1,0:T(8,128)S(1)}, f32[7,15,512]{2,1,0:T(8,128)S(1)}, u32[]{:S(2)}, u32[]{:S(2)}) %collective-permute-start.4) | collective-permute-done | bytes 215072 | tf_op jit(solution)/shard_map/ppermute | solution.py:53
  21.2 1.5 %collective-permute-start.3 = (f32[7,32,512]{2,1,0:T(8,128)S(1)}, f32[7,32,512]{2,1,0:T(8,128)S(1)}, u32[]{:S(2)}, u32[]{:S(2)}) collective-permute-start(f32[7,32,512]{2,1,0:T(8,128)S(1)} %get-tuple-element.52), channel_id=1, source_target_pairs={{1,0},{3,2},{5,4},{7,6},{9,8},{11,10},{13,12},{15,14},{17,16},{19,... | collective-permute-start | bytes 1376264 | tf_op jit(solution)/shard_map/ppermute | solution.py:53
  22.7 1.3 %collective-permute-start.6 = (f32[7,15,512]{2,1,0:T(8,128)S(1)}, f32[7,15,512]{2,1,0:T(8,128)S(1)}, u32[]{:S(2)}, u32[]{:S(2)}) collective-permute-start(f32[7,15,512]{2,1,0:T(8,128)S(1)} %get-tuple-element.49), channel_id=1, source_target_pairs={{2,1},{4,3},{6,5},{10,9},{12,11},{14,13},{18,17},{20,19},{22,21},{... | collective-permute-start | bytes 645128 | tf_op jit(solution)/shard_map/ppermute | solution.py:53
  24.5 7.2 %collective-permute-done.6.refs_10_.refs_8_ = f32[7,15,512]{2,1,0:T(8,128)S(1)} collective-permute-done((f32[7,15,512]{2,1,0:T(8,128)S(1)}, f32[7,15,512]{2,1,0:T(8,128)S(1)}, u32[]{:S(2)}, u32[]{:S(2)}) %collective-permute-start.6) | collective-permute-done | bytes 215072 | tf_op jit(solution)/shard_map/ppermute | solution.py:53
  31.7 1.3 %collective-permute-start.7 = (f32[7,15,512]{2,1,0:T(8,128)S(1)}, f32[7,15,512]{2,1,0:T(8,128)S(1)}, u32[]{:S(2)}, u32[]{:S(2)}) collective-permute-start(f32[7,15,512]{2,1,0:T(8,128)S(1)} %get-tuple-element.48), channel_id=1, source_target_pairs={{3,0},{5,2},{7,4},{11,8},{13,10},{15,12},{19,16},{21,18},{23,20},{... | collective-permute-start | bytes 645128 | tf_op jit(solution)/shard_map/ppermute | solution.py:53
  33.8 2.7 %collective-permute-done.7.refs_11_.refs_9_ = f32[7,15,512]{2,1,0:T(8,128)S(1)} collective-permute-done((f32[7,15,512]{2,1,0:T(8,128)S(1)}, f32[7,15,512]{2,1,0:T(8,128)S(1)}, u32[]{:S(2)}, u32[]{:S(2)}) %collective-permute-start.7) | collective-permute-done | bytes 215072 | tf_op jit(solution)/shard_map/ppermute | solution.py:53
  36.5 1.1 %fusion.13 = (f32[8,9,1024]{2,1,0:T(8,128)}, f32[8,9,1024]{2,1,0:T(8,128)}) fusion(f32[8,32,1024]{2,1,0:T(8,128)S(1)} %pad_maximum_fusion.refs_10_), kind=kLoop, calls=%fused_computation.29 | loop fusion | bytes 1179648 | tf_op jit(solution)/shard_map/slice | solution.py:41
  37.6 0.9 fusion.11
  38.4 1.3 %collective-permute-start.12 = (f32[8,9,384]{2,1,0:T(8,128)S(1)}, f32[8,9,384]{2,1,0:T(8,128)S(1)}, u32[]{:S(2)}, u32[]{:S(2)}) collective-permute-start(f32[8,9,384]{2,1,0:T(8,128)S(1)} %get-tuple-element.43), channel_id=1, source_target_pairs={{0,3},{2,5},{4,7},{8,11},{10,13},{12,15},{16,19},{18,21},{20,23},{... | collective-permute-start | bytes 331784 | tf_op jit(solution)/shard_map/ppermute | solution.py:53
  39.7 1.0 fusion.12
  40.7 3.5 %collective-permute-start.8 = (f32[8,9,1024]{2,1,0:T(8,128)}, f32[8,9,1024]{2,1,0:T(8,128)}, u32[]{:S(2)}, u32[]{:S(2)}) collective-permute-start(f32[8,9,1024]{2,1,0:T(8,128)} %get-tuple-element.47), channel_id=1, source_target_pairs={{0,2},{1,3},{2,4},{3,5},{4,6},{5,7},{8,10},{9,11},{10,12},{11,13},... | collective-permute-start | bytes 884744 | tf_op jit(solution)/shard_map/ppermute | solution.py:53
  44.2 3.1 %collective-permute-start.9 = (f32[8,9,1024]{2,1,0:T(8,128)}, f32[8,9,1024]{2,1,0:T(8,128)}, u32[]{:S(2)}, u32[]{:S(2)}) collective-permute-start(f32[8,9,1024]{2,1,0:T(8,128)} %get-tuple-element.46), channel_id=1, source_target_pairs={{2,0},{3,1},{4,2},{5,3},{6,4},{7,5},{10,8},{11,9},{12,10},{13,11},... | collective-permute-start | bytes 884744 | tf_op jit(solution)/shard_map/ppermute | solution.py:53
  47.3 1.3 %collective-permute-start.10 = (f32[8,32,384]{2,1,0:T(8,128)}, f32[8,32,384]{2,1,0:T(8,128)}, u32[]{:S(2)}, u32[]{:S(2)}) collective-permute-start(f32[8,32,384]{2,1,0:T(8,128)} %get-tuple-element.45), channel_id=1, source_target_pairs={{0,1},{2,3},{4,5},{6,7},{8,9},{10,11},{12,13},{14,15},{16,17},{18,... | collective-permute-start | bytes 1179656 | tf_op jit(solution)/shard_map/ppermute | solution.py:53
  48.6 7.1 %collective-permute-start.11 = (f32[8,32,384]{2,1,0:T(8,128)}, f32[8,32,384]{2,1,0:T(8,128)}, u32[]{:S(2)}, u32[]{:S(2)}) collective-permute-start(f32[8,32,384]{2,1,0:T(8,128)} %get-tuple-element.44), channel_id=1, source_target_pairs={{1,0},{3,2},{5,4},{7,6},{9,8},{11,10},{13,12},{15,14},{17,16},{19,... | collective-permute-start | bytes 1179656 | tf_op jit(solution)/shard_map/ppermute | solution.py:53
  55.7 0.7 copy-done.5
  56.4 2.0 %collective-permute-start.13 = (f32[8,9,384]{2,1,0:T(8,128)}, f32[8,9,384]{2,1,0:T(8,128)}, u32[]{:S(2)}, u32[]{:S(2)}) collective-permute-start(f32[8,9,384]{2,1,0:T(8,128)} %get-tuple-element.42), channel_id=1, source_target_pairs={{1,2},{3,4},{5,6},{9,10},{11,12},{13,14},{17,18},{19,20},{21,22},{... | collective-permute-start | bytes 331784 | tf_op jit(solution)/shard_map/ppermute | solution.py:53
  59.7 1.5 %collective-permute-done.13.refs_16_ = f32[8,9,384]{2,1,0:T(8,128)} collective-permute-done((f32[8,9,384]{2,1,0:T(8,128)}, f32[8,9,384]{2,1,0:T(8,128)}, u32[]{:S(2)}, u32[]{:S(2)}) %collective-permute-start.13) | collective-permute-done | bytes 110624 | tf_op jit(solution)/shard_map/ppermute | solution.py:53
  61.2 1.3 %collective-permute-start.14 = (f32[8,9,384]{2,1,0:T(8,128)}, f32[8,9,384]{2,1,0:T(8,128)S(1)}, u32[]{:S(2)}, u32[]{:S(2)}) collective-permute-start(f32[8,9,384]{2,1,0:T(8,128)} %get-tuple-element.41), channel_id=1, source_target_pairs={{2,1},{4,3},{6,5},{10,9},{12,11},{14,13},{18,17},{20,19},{22,21},{... | collective-permute-start | bytes 331784 | tf_op jit(solution)/shard_map/ppermute | solution.py:53
  62.6 7.3 %collective-permute-done.14.refs_17_ = f32[8,9,384]{2,1,0:T(8,128)S(1)} collective-permute-done((f32[8,9,384]{2,1,0:T(8,128)}, f32[8,9,384]{2,1,0:T(8,128)S(1)}, u32[]{:S(2)}, u32[]{:S(2)}) %collective-permute-start.14) | collective-permute-done | bytes 110624 | tf_op jit(solution)/shard_map/ppermute | solution.py:53
  69.9 1.5 %collective-permute-start.15 = (f32[8,9,384]{2,1,0:T(8,128)}, f32[8,9,384]{2,1,0:T(8,128)S(1)}, u32[]{:S(2)}, u32[]{:S(2)}) collective-permute-start(f32[8,9,384]{2,1,0:T(8,128)} %get-tuple-element.40), channel_id=1, source_target_pairs={{3,0},{5,2},{7,4},{11,8},{13,10},{15,12},{19,16},{21,18},{23,20},{... | collective-permute-start | bytes 331784 | tf_op jit(solution)/shard_map/ppermute | solution.py:53
  71.4 0.9 copy-done.3
  72.4 8.8 %shard_map.121 = (f32[1,5,32,1024]{3,2,1,0:T(8,128)}, f32[3,32,1024]{2,1,0:T(8,128)S(1)}, f32[3,64,2048]{2,1,0:T(8,128)S(1)}) custom-call(s32[4]{0:T(128)S(1)} %pad_add_fusion.refs_0_, s32[2]{0:T(128)S(1)} %pad_add_fusion.1.refs_1_, f32[3]{0:T(128)S(1)} %bitcast.53, f32[7,32,1024]{2,1,0:T(8,128)S(1)} %pad_maximum_fusion.1.refs_3_.refs_1_, ...), custom_call_target="tpu_custom_call" | custom-call | tf_op jit(solution)/shard_map/pallas_call | solution.py:257
  81.2 1.2 %copy-done.1 = f32[3,64,2048]{2,1,0:T(8,128)} copy-done((f32[3,64,2048]{2,1,0:T(8,128)}, f32[3,64,2048]{2,1,0:T(8,128)S(1)}, u32[]{:S(2)}) %copy-start.1) | copy-done | bytes 1572888
  82.4 8.3 %shard_map.122 = (f32[1,5,32,1024]{3,2,1,0:T(8,128)}, f32[2,4,1024]{2,1,0:T(4,128)S(1)}) custom-call(s32[4]{0:T(128)S(1)} %pad_add_fusion.refs_0_, f32[7,32,1024]{2,1,0:T(8,128)} %copy-done, f32[7,15,1024]{2,1,0:T(8,128)S(1)} %collective-permute-done.refs_4_.refs_2_, f32[7,15,1024]{2,1,0:T(8,128)S(1)} %collective-permute-done.1.refs_5_.refs_3_, ...), custom_call_target="tpu_custom_call" | custom-call | tf_op jit(solution)/shard_map/pallas_call | solution.py:270
  91.8 0.8 scatter_custom_fusion
  92.7 6.3 %all_to_all.5 = f32[4,16,2]{1,2,0:T(2,128)S(1)} all-to-all(f32[4,16,2]{1,2,0:T(2,128)S(1)} %copy.19), channel_id=1, replica_groups=mesh['shot'=4,'gy'=4,'gx'=2] {'shot'}, dimensions={0} | all-to-all | bytes 1024 | tf_op jit(solution)/shard_map/all_to_all | solution.py:292
  (54 shorter events, 3.5 us)
Async XLA Ops:
  1.9 69.5 %copy-start = (f32[7,32,1024]{2,1,0:T(8,128)}, f32[7,32,1024]{2,1,0:T(8,128)S(1)}, u32[]{:S(2)}) copy-start(f32[7,32,1024]{2,1,0:T(8,128)S(1)} %pad_maximum_fusion.1.refs_3_.refs_1_) | copy-start | bytes 2752516
  2.0 34.5 %collective-permute-start = (f32[7,15,1024]{2,1,0:T(8,128)S(1)}, f32[7,15,1024]{2,1,0:T(8,128)S(1)}, u32[]{:S(2)}, u32[]{:S(2)}) collective-permute-start(f32[7,15,1024]{2,1,0:T(8,128)S(1)} %get-tuple-element.55), channel_id=1, source_target_pairs={{0,2},{1,3},{2,4},{3,5},{4,6},{5,7},{8,10},{9,11},{10,12},{11,13},... | collective-permute-start | bytes 1290248 | tf_op jit(solution)/shard_map/ppermute | solution.py:53
  5.5 11.9 %copy-start.11 = (s32[1,1,128]{2,1,0:T(1,128)S(1)}, s32[1,1,128]{2,1,0:T(1,128)}, u32[]{:S(2)}) copy-start(s32[1,1,128]{2,1,0:T(1,128)} %param.16) | copy-start | bytes 1540
  5.5 12.0 %copy-start.10 = (f32[1,3,1,128]{3,2,1,0:T(1,128)S(1)}, f32[1,3,1,128]{3,2,1,0:T(1,128)}, u32[]{:S(2)}) copy-start(f32[1,3,1,128]{3,2,1,0:T(1,128)} %param.17) | copy-start | bytes 4612
  5.6 30.9 %collective-permute-start.1 = (f32[7,15,1024]{2,1,0:T(8,128)S(1)}, f32[7,15,1024]{2,1,0:T(8,128)S(1)}, u32[]{:S(2)}, u32[]{:S(2)}) collective-permute-start(f32[7,15,1024]{2,1,0:T(8,128)S(1)} %get-tuple-element.54), channel_id=1, source_target_pairs={{2,0},{3,1},{4,2},{5,3},{6,4},{7,5},{10,8},{11,9},{12,10},{13,11},... | collective-permute-start | bytes 1290248 | tf_op jit(solution)/shard_map/ppermute | solution.py:53
  8.0 25.7 %copy-start.9 = (f32[1,5,32,1024]{3,2,1,0:T(8,128)S(1)}, f32[1,5,32,1024]{3,2,1,0:T(8,128)}, u32[]{:S(2)}) copy-start(f32[1,5,32,1024]{3,2,1,0:T(8,128)} %param.11) | copy-start | bytes 1966084
  8.0 28.5 %collective-permute-start.2 = (f32[7,32,512]{2,1,0:T(8,128)S(1)}, f32[7,32,512]{2,1,0:T(8,128)S(1)}, u32[]{:S(2)}, u32[]{:S(2)}) collective-permute-start(f32[7,32,512]{2,1,0:T(8,128)S(1)} %get-tuple-element.53), channel_id=1, source_target_pairs={{0,1},{2,3},{4,5},{6,7},{8,9},{10,11},{12,13},{14,15},{16,17},{18,... | collective-permute-start | bytes 1376264 | tf_op jit(solution)/shard_map/ppermute | solution.py:53
  9.6 11.6 %collective-permute-start.4 = (f32[7,15,512]{2,1,0:T(8,128)S(1)}, f32[7,15,512]{2,1,0:T(8,128)S(1)}, u32[]{:S(2)}, u32[]{:S(2)}) collective-permute-start(f32[7,15,512]{2,1,0:T(8,128)S(1)} %get-tuple-element.51), channel_id=1, source_target_pairs={{0,3},{2,5},{4,7},{8,11},{10,13},{12,15},{16,19},{18,21},{20,23},{... | collective-permute-start | bytes 645128 | tf_op jit(solution)/shard_map/ppermute | solution.py:53
  10.9 11.8 %collective-permute-start.5 = (f32[7,15,512]{2,1,0:T(8,128)S(1)}, f32[7,15,512]{2,1,0:T(8,128)S(1)}, u32[]{:S(2)}, u32[]{:S(2)}) collective-permute-start(f32[7,15,512]{2,1,0:T(8,128)S(1)} %get-tuple-element.50), channel_id=1, source_target_pairs={{1,2},{3,4},{5,6},{9,10},{11,12},{13,14},{17,18},{19,20},{21,22},{... | collective-permute-start | bytes 645128 | tf_op jit(solution)/shard_map/ppermute | solution.py:53
  21.2 15.4 %collective-permute-start.3 = (f32[7,32,512]{2,1,0:T(8,128)S(1)}, f32[7,32,512]{2,1,0:T(8,128)S(1)}, u32[]{:S(2)}, u32[]{:S(2)}) collective-permute-start(f32[7,32,512]{2,1,0:T(8,128)S(1)} %get-tuple-element.52), channel_id=1, source_target_pairs={{1,0},{3,2},{5,4},{7,6},{9,8},{11,10},{13,12},{15,14},{17,16},{19,... | collective-permute-start | bytes 1376264 | tf_op jit(solution)/shard_map/ppermute | solution.py:53
  22.7 9.0 %collective-permute-start.6 = (f32[7,15,512]{2,1,0:T(8,128)S(1)}, f32[7,15,512]{2,1,0:T(8,128)S(1)}, u32[]{:S(2)}, u32[]{:S(2)}) collective-permute-start(f32[7,15,512]{2,1,0:T(8,128)S(1)} %get-tuple-element.49), channel_id=1, source_target_pairs={{2,1},{4,3},{6,5},{10,9},{12,11},{14,13},{18,17},{20,19},{22,21},{... | collective-permute-start | bytes 645128 | tf_op jit(solution)/shard_map/ppermute | solution.py:53
  31.7 4.8 %collective-permute-start.7 = (f32[7,15,512]{2,1,0:T(8,128)S(1)}, f32[7,15,512]{2,1,0:T(8,128)S(1)}, u32[]{:S(2)}, u32[]{:S(2)}) collective-permute-start(f32[7,15,512]{2,1,0:T(8,128)S(1)} %get-tuple-element.48), channel_id=1, source_target_pairs={{3,0},{5,2},{7,4},{11,8},{13,10},{15,12},{19,16},{21,18},{23,20},{... | collective-permute-start | bytes 645128 | tf_op jit(solution)/shard_map/ppermute | solution.py:53
  33.8 5.9 %copy-start.8 = (f32[8,32,1024]{2,1,0:T(8,128)}, f32[8,32,1024]{2,1,0:T(8,128)S(1)}, u32[]{:S(2)}) copy-start(f32[8,32,1024]{2,1,0:T(8,128)S(1)} %pad_maximum_fusion.refs_10_) | copy-start | bytes 3145732
  36.5 1.9 %copy-start.2 = (f32[7,15,512]{2,1,0:T(8,128)}, f32[7,15,512]{2,1,0:T(8,128)S(1)}, u32[]{:S(2)}) copy-start(f32[7,15,512]{2,1,0:T(8,128)S(1)} %collective-permute-done.7.refs_11_.refs_9_) | copy-start | bytes 645124
  37.6 20.8 %copy-start.12 = (s32[1,64]{1,0:T(1,128)S(1)}, s32[1,64]{1,0:T(1,128)}, u32[]{:S(2)}) copy-start(s32[1,64]{1,0:T(1,128)} %param.19) | copy-start | bytes 772
  37.6 33.8 %copy-start.7 = (f32[1,3]{1,0:T(1,128)S(1)}, f32[1,3]{1,0:T(1,128)}, u32[]{:S(2)}) copy-start(f32[1,3]{1,0:T(1,128)} %param.14) | copy-start | bytes 40
  38.4 17.3 %collective-permute-start.12 = (f32[8,9,384]{2,1,0:T(8,128)S(1)}, f32[8,9,384]{2,1,0:T(8,128)S(1)}, u32[]{:S(2)}, u32[]{:S(2)}) collective-permute-start(f32[8,9,384]{2,1,0:T(8,128)S(1)} %get-tuple-element.43), channel_id=1, source_target_pairs={{0,3},{2,5},{4,7},{8,11},{10,13},{12,15},{16,19},{18,21},{20,23},{... | collective-permute-start | bytes 331784 | tf_op jit(solution)/shard_map/ppermute | solution.py:53
  40.7 41.6 %collective-permute-start.8 = (f32[8,9,1024]{2,1,0:T(8,128)}, f32[8,9,1024]{2,1,0:T(8,128)}, u32[]{:S(2)}, u32[]{:S(2)}) collective-permute-start(f32[8,9,1024]{2,1,0:T(8,128)} %get-tuple-element.47), channel_id=1, source_target_pairs={{0,2},{1,3},{2,4},{3,5},{4,6},{5,7},{8,10},{9,11},{10,12},{11,13},... | collective-permute-start | bytes 884744 | tf_op jit(solution)/shard_map/ppermute | solution.py:53
  44.2 38.2 %collective-permute-start.9 = (f32[8,9,1024]{2,1,0:T(8,128)}, f32[8,9,1024]{2,1,0:T(8,128)}, u32[]{:S(2)}, u32[]{:S(2)}) collective-permute-start(f32[8,9,1024]{2,1,0:T(8,128)} %get-tuple-element.46), channel_id=1, source_target_pairs={{2,0},{3,1},{4,2},{5,3},{6,4},{7,5},{10,8},{11,9},{12,10},{13,11},... | collective-permute-start | bytes 884744 | tf_op jit(solution)/shard_map/ppermute | solution.py:53
  47.3 35.0 %collective-permute-start.10 = (f32[8,32,384]{2,1,0:T(8,128)}, f32[8,32,384]{2,1,0:T(8,128)}, u32[]{:S(2)}, u32[]{:S(2)}) collective-permute-start(f32[8,32,384]{2,1,0:T(8,128)} %get-tuple-element.45), channel_id=1, source_target_pairs={{0,1},{2,3},{4,5},{6,7},{8,9},{10,11},{12,13},{14,15},{16,17},{18,... | collective-permute-start | bytes 1179656 | tf_op jit(solution)/shard_map/ppermute | solution.py:53
  48.6 33.7 %collective-permute-start.11 = (f32[8,32,384]{2,1,0:T(8,128)}, f32[8,32,384]{2,1,0:T(8,128)}, u32[]{:S(2)}, u32[]{:S(2)}) collective-permute-start(f32[8,32,384]{2,1,0:T(8,128)} %get-tuple-element.44), channel_id=1, source_target_pairs={{1,0},{3,2},{5,4},{7,6},{9,8},{11,10},{13,12},{15,14},{17,16},{19,... | collective-permute-start | bytes 1179656 | tf_op jit(solution)/shard_map/ppermute | solution.py:53
  55.7 0.7 copy-start.5
  56.4 4.8 %collective-permute-start.13 = (f32[8,9,384]{2,1,0:T(8,128)}, f32[8,9,384]{2,1,0:T(8,128)}, u32[]{:S(2)}, u32[]{:S(2)}) collective-permute-start(f32[8,9,384]{2,1,0:T(8,128)} %get-tuple-element.42), channel_id=1, source_target_pairs={{1,2},{3,4},{5,6},{9,10},{11,12},{13,14},{17,18},{19,20},{21,22},{... | collective-permute-start | bytes 331784 | tf_op jit(solution)/shard_map/ppermute | solution.py:53
  61.2 8.7 %collective-permute-start.14 = (f32[8,9,384]{2,1,0:T(8,128)}, f32[8,9,384]{2,1,0:T(8,128)S(1)}, u32[]{:S(2)}, u32[]{:S(2)}) collective-permute-start(f32[8,9,384]{2,1,0:T(8,128)} %get-tuple-element.41), channel_id=1, source_target_pairs={{2,1},{4,3},{6,5},{10,9},{12,11},{14,13},{18,17},{20,19},{22,21},{... | collective-permute-start | bytes 331784 | tf_op jit(solution)/shard_map/ppermute | solution.py:53
  69.9 12.5 %collective-permute-start.15 = (f32[8,9,384]{2,1,0:T(8,128)}, f32[8,9,384]{2,1,0:T(8,128)S(1)}, u32[]{:S(2)}, u32[]{:S(2)}) collective-permute-start(f32[8,9,384]{2,1,0:T(8,128)} %get-tuple-element.40), channel_id=1, source_target_pairs={{3,0},{5,2},{7,4},{11,8},{13,10},{15,12},{19,16},{21,18},{23,20},{... | collective-permute-start | bytes 331784 | tf_op jit(solution)/shard_map/ppermute | solution.py:53
  71.4 0.9 copy-start.3
  72.4 10.0 %copy-start.4 = (f32[32,1024]{1,0:T(8,128)S(1)}, f32[32,1024]{1,0:T(8,128)}, u32[]{:S(2)}) copy-start(f32[32,1024]{1,0:T(8,128)} %get-tuple-element.56.refs_19_) | copy-start | bytes 393220
  72.4 10.0 %copy-start.6 = (f32[8,9,384]{2,1,0:T(8,128)S(1)}, f32[8,9,384]{2,1,0:T(8,128)}, u32[]{:S(2)}) copy-start(f32[8,9,384]{2,1,0:T(8,128)} %copy-done.5) | copy-start | bytes 331780
  81.2 1.2 %copy-start.1 = (f32[3,64,2048]{2,1,0:T(8,128)}, f32[3,64,2048]{2,1,0:T(8,128)S(1)}, u32[]{:S(2)}) copy-start(f32[3,64,2048]{2,1,0:T(8,128)S(1)} %get-tuple-element.27.refs_20_) | copy-start | bytes 4718596

commit v9 on v6

--- a/solution.py
+++ b/solution.py
@@ -32,10 +32,60 @@
         self.el = 2 * self.ox + lanes
 
 
-def send_pieces(stack, frame):
-    ny, lanes, ox = frame.ny, frame.lanes, frame.ox
-    lo_rows = stack[:, :HALO]
-    hi_rows = stack[:, ny - HALO :]
+NEEDS = (
+    (15, 15), (14, 12), (12, 14), (12, 12), (12, 12),
+    (9, 9), (8, 6), (6, 8), (6, 6), (6, 6),
+    (12, 12), (12, 12),
+    (6, 6), (0, 0), (3, 3), (6, 6),
+)
+
+
+class Packing:
+    def __init__(self, frame):
+        self.rows = [h for h, w in NEEDS]
+        self.lanes = [round_up(w * CZ, 128) for h, w in NEEDS]
+        self.row_at = [sum(self.rows[:j]) for j in range(len(NEEDS))]
+        self.lane_at = [sum(self.lanes[:j]) for j in range(len(NEEDS))]
+        self.total_rows = sum(self.rows)
+        self.total_lanes = sum(self.lanes)
+        self.corner = frame.ox
+
+
+def pack_kernel(frame, packing, fwd_ref, adj_ref, vel_ref, att_ref, gauge_ref, *outs):
+    up, down, east, west, up_east, up_west, down_east, down_west = outs
+    ny, lanes, cw = frame.ny, frame.lanes, packing.corner
+
+    def field(j):
+        if j < 5:
+            return fwd_ref.at[0, j]
+        if j < 10:
+            return adj_ref.at[0, j - 5]
+        if j == 10:
+            return vel_ref
+        if j == 11:
+            return att_ref
+        return gauge_ref.at[j - 12]
+
+    for j in range(len(NEEDS)):
+        h, w = packing.rows[j], packing.lanes[j]
+        if h == 0:
+            continue
+        src = field(j)
+        r = slice(packing.row_at[j], packing.row_at[j] + h)
+        c = slice(packing.lane_at[j], packing.lane_at[j] + w)
+        top = slice(ny - h, ny)
+        bottom = slice(0, h)
+        up[r, :] = src[top, :]
+        down[r, :] = src[bottom, :]
+        east[:, c] = src[:, lanes - w : lanes]
+        west[:, c] = src[:, 0:w]
+        up_east[r, :] = src[top, lanes - cw : lanes]
+        up_west[r, :] = src[top, 0:cw]
+        down_east[r, :] = src[bottom, lanes - cw : lanes]
+        down_west[r, :] = src[bottom, 0:cw]
+
+
+def send_pieces(packed):
     count_y = lax.axis_size("gy")
     count_x = lax.axis_size("gx")
 
@@ -48,37 +98,34 @@
                     pairs.append((y * count_x + x, ty * count_x + tx))
         return lax.ppermute(piece, ("gy", "gx"), pairs)
 
-    return (
-        move(hi_rows, 1, 0),
-        move(lo_rows, -1, 0),
-        move(stack[:, :, lanes - ox :], 0, 1),
-        move(stack[:, :, :ox], 0, -1),
-        move(hi_rows[:, :, lanes - ox :], 1, 1),
-        move(hi_rows[:, :, :ox], 1, -1),
-        move(lo_rows[:, :, lanes - ox :], -1, 1),
-        move(lo_rows[:, :, :ox], -1, -1),
-    )
-
-
-def assemble(dst, own, pieces, j, frame):
-    ny, lanes, oy, ox, el = frame.ny, frame.lanes, frame.oy, frame.ox, frame.el
+    steps = ((1, 0), (-1, 0), (0, 1), (0, -1), (1, 1), (1, -1), (-1, 1), (-1, -1))
+    return tuple(move(p, dy, dx) for p, (dy, dx) in zip(packed, steps))
+
+
+def assemble(dst, own, pieces, j, frame, packing):
+    ny, lanes, oy, ox, cw = frame.ny, frame.lanes, frame.oy, frame.ox, packing.corner
     below, above, left, right, b_l, b_r, a_l, a_r = pieces
-    lo = slice(oy - HALO, oy)
+    h, w = packing.rows[j], packing.lanes[j]
+    dst[...] = jnp.zeros(dst.shape, dst.dtype)
     mid = slice(oy, oy + ny)
-    hi = slice(oy + ny, oy + ny + HALO)
-    west = slice(0, ox)
     centre = slice(ox, ox + lanes)
-    east = slice(ox + lanes, el)
-    dst[...] = jnp.zeros(dst.shape, dst.dtype)
-    dst[mid, centre] = own[j]
-    dst[lo, centre] = below[j]
-    dst[hi, centre] = above[j]
-    dst[mid, west] = left[j]
-    dst[mid, east] = right[j]
-    dst[lo, west] = b_l[j]
-    dst[lo, east] = b_r[j]
-    dst[hi, west] = a_l[j]
-    dst[hi, east] = a_r[j]
+    dst[mid, centre] = own[...]
+    if h == 0:
+        return
+    r = slice(packing.row_at[j], packing.row_at[j] + h)
+    c = slice(packing.lane_at[j], packing.lane_at[j] + w)
+    lo = slice(oy - h, oy)
+    hi = slice(oy + ny, oy + ny + h)
+    west = slice(ox - w, ox)
+    east = slice(ox + lanes, ox + lanes + w)
+    dst[lo, centre] = below[r, :]
+    dst[hi, centre] = above[r, :]
+    dst[mid, west] = left[:, c]
+    dst[mid, east] = right[:, c]
+    dst[lo, west] = b_l[r, cw - w : cw]
+    dst[lo, east] = b_r[r, 0:w]
+    dst[hi, west] = a_l[r, cw - w : cw]
+    dst[hi, east] = a_r[r, 0:w]
 
 
 def stepper(frame, bounds_ref):
@@ -127,11 +174,18 @@
     return wave_step, row, lane
 
 
-def window_kernel(frame, bounds_ref, source_ref, wave_ref, own_ref, *rest):
-    pieces = rest[:8]
-    end_ref, start_ref, grad_ref, ext, inject, divs = rest[8:]
+def window_kernel(frame, packing, bounds_ref, source_ref, wave_ref, *rest):
+    fwd_ref, adj_ref, vel_ref, att_ref, gauge_ref = rest[:5]
+    pieces = rest[5:13]
+    end_ref, start_ref, grad_ref, ext, inject, divs = rest[13:]
+    owns = (
+        [fwd_ref.at[0, k] for k in range(5)]
+        + [adj_ref.at[0, k] for k in range(5)]
+        + [vel_ref, att_ref]
+        + [gauge_ref.at[k] for k in range(4)]
+    )
     for j in range(16):
-        assemble(ext.at[j], own_ref, pieces, j, frame)
+        assemble(ext.at[j], owns[j], pieces, j, frame, packing)
     wave_step, row, lane = stepper(frame, bounds_ref)
     source = (row == source_ref[0]) & (lane == source_ref[1])
     vel = ext[10]
@@ -220,20 +274,31 @@
         precision=lax.Precision.HIGHEST,
     )
 
-    stack = jnp.concatenate(
-        [forward_start[0], adjoint_end[0], velocity[None], attenuation[None], gauge], axis=0
-    )
-    pieces = send_pieces(stack, frame)
+    packing = Packing(frame)
+    packed = pl.pallas_call(
+        lambda *refs: pack_kernel(frame, packing, *refs),
+        out_shape=tuple(
+            jax.ShapeDtypeStruct(shape, jnp.float32)
+            for shape in (
+                [(packing.total_rows, lanes)] * 2
+                + [(ny, packing.total_lanes)] * 2
+                + [(packing.total_rows, packing.corner)] * 4
+            )
+        ),
+        in_specs=[vmem()] * 5,
+        out_specs=tuple([vmem()] * 8),
+    )(forward_start, adjoint_end, velocity, attenuation, gauge)
+    pieces = send_pieces(packed)
 
     ext_shape = (frame.ey, frame.el)
     forward_end, adjoint_start, row_sums = pl.pallas_call(
-        lambda *refs: window_kernel(frame, *refs),
+        lambda *refs: window_kernel(frame, packing, *refs),
         out_shape=(
             jax.ShapeDtypeStruct((1, 5, ny, lanes), jnp.float32),
             jax.ShapeDtypeStruct((1, 5, ny, lanes), jnp.float32),
             jax.ShapeDtypeStruct((2, ny // BY, lanes), jnp.float32),
         ),
-        in_specs=[smem(), smem(), smem()] + [vmem()] * 9,
+        in_specs=[smem(), smem(), smem()] + [vmem()] * 13,
         out_specs=(vmem(), vmem(), vmem()),
         scratch_shapes=[
             pltpu.VMEM((16,) + ext_shape, jnp.float32),
@@ -241,7 +306,7 @@
             pltpu.VMEM((STEPS, ny, lanes), jnp.float32),
         ],
         compiler_params=pltpu.CompilerParams(vmem_limit_bytes=48 * 1024 * 1024),
-    )(bounds, source, wavelet[0], stack, *pieces)
+    )(bounds, source, wavelet[0], forward_start, adjoint_end, velocity, attenuation, gauge, *pieces)
 
     grad_scale = float(BY * BX * BZ) ** (-0.5)
     weight = aperture[0, 0].astype(jnp.float32)

time: 92.3 us -> 77.4 us (0.84)
  the two profiles are of different devices: /device:TPU:16 before, /device:TPU:0 now
where the time goes in v9:
time: 77.4 us; the launch traced here: 76.9 us
  starting transfers between devices  26.1 us (34%)
  Pallas kernels  17.4 us (22%)
  waiting for transfers between devices  15.7 us (20%)
  blocking collectives  6.34 us (8%)
  local copies, waits for them, and re-layouts  6.29 us (8%)
  between operations  2.14 us (3%)
  other arithmetic  1.61 us (2%)
  matrix products  1.29 us (2%)
    ppermute x8, starting transfers between devices, move(): return lax.ppermute(piece, ('gy', 'gx'), pairs)  26.1 us
    ppermute x8, waiting for transfers between devices, move(): return lax.ppermute(piece, ('gy', 'gx'), pairs)  15.7 us
    pallas_call x1, Pallas kernels, on_device(): pl.pallas_call(lambda *refs: window_kernel(frame, packing, *refs), out_sh...  13.8 us
    all_to_all x1, blocking collectives, on_device(): lax.all_to_all(ordered.reshape(shots, -1, 2), 'shot', split_axis=0, conca...  6.34 us
    unnamed x25, local copies, waits for them, and re-layouts  4.58 us
    pallas_call x1, Pallas kernels, on_device(): pl.pallas_call(lambda *refs: pack_kernel(frame, packing, *refs), out_shap...  3.62 us
  transfers between devices with their start and end apart: 8, of which 1 were waited for; matrix products, arithmetic and copies ran while one was open for 0% of the time, Pallas kernels for 0%

profile of v9, /device:TPU:0, one launch (start us, length us, event | category | flops | bytes accessed | tf_op | source)
XLA Modules:
  0.0 76.9 jit_solution(1267126131215405455)
XLA Ops:
  0.6 0.7 and_select_fusion.1
  1.3 0.7 copy-done.10
  2.0 1.3 %fusion.1.refs_4_.refs_7_ = f32[4,32,1024]{2,1,0:T(8,128)} fusion(s32[128]{0:T(128)S(1)} %get-tuple-element.35, f32[128,32]{0,1:T(8,128)S(1)} %fusion.9, f32[4,128]{1,0:T(4,128)S(1)} %concatenate.3), kind=kOutput, calls=%fused_computation.3 | convolution fusion | flops 201474048 | bytes 543232 | tf_op jit(solution)/shard_map/nky,kl->nyl/dot_general | solution.py:270
  3.3 0.0 copy-start.4
  3.3 3.6 %shard_map.121 = (f32[139,1024]{1,0:T(8,128)}, f32[139,1024]{1,0:T(8,128)}, f32[32,4992]{1,0:T(8,128)}, f32[32,4992]{1,0:T(8,128)}, f32[139,512]{1,0:T(8,128)}, ...) custom-call(f32[1,5,32,1024]{3,2,1,0:T(8,128)} %refs_3_.3, f32[1,5,32,1024]{3,2,1,0:T(8,128)} %refs_4_.1, ...), custom_call_target="tpu_custom_call" | custom-call | tf_op jit(solution)/shard_map/pallas_call | solution.py:278
  6.9 5.9 %collective-permute-start.4 = (f32[139,512]{1,0:T(8,128)}, f32[139,512]{1,0:T(8,128)S(1)}, u32[]{:S(2)}, u32[]{:S(2)}) collective-permute-start(f32[139,512]{1,0:T(8,128)} %get-tuple-element.18), channel_id=1, source_target_pairs={{0,3},{2,5},{4,7},{8,11},{10,13},{12,15},{16,19},{18,21},{20,23},{... | collective-permute-start | bytes 854024 | tf_op jit(solution)/shard_map/ppermute | solution.py:99
  12.8 0.7 collective-permute-start.5
  13.5 6.2 %collective-permute-start.2 = (f32[32,4992]{1,0:T(8,128)}, f32[32,4992]{1,0:T(8,128)S(1)}, u32[]{:S(2)}, u32[]{:S(2)}) collective-permute-start(f32[32,4992]{1,0:T(8,128)} %get-tuple-element.16), channel_id=1, source_target_pairs={{0,1},{2,3},{4,5},{6,7},{8,9},{10,11},{12,13},{14,15},{16,17},{18,... | collective-permute-start | bytes 1916936 | tf_op jit(solution)/shard_map/ppermute | solution.py:99
  19.7 1.3 %collective-permute-start.3 = (f32[32,4992]{1,0:T(8,128)}, f32[32,4992]{1,0:T(8,128)S(1)}, u32[]{:S(2)}, u32[]{:S(2)}) collective-permute-start(f32[32,4992]{1,0:T(8,128)} %get-tuple-element.17), channel_id=1, source_target_pairs={{1,0},{3,2},{5,4},{7,6},{9,8},{11,10},{13,12},{15,14},{17,16},{19,... | collective-permute-start | bytes 1916936 | tf_op jit(solution)/shard_map/ppermute | solution.py:99
  21.0 1.4 %collective-permute-start.6 = (f32[139,512]{1,0:T(8,128)}, f32[139,512]{1,0:T(8,128)}, u32[]{:S(2)}, u32[]{:S(2)}) collective-permute-start(f32[139,512]{1,0:T(8,128)} %get-tuple-element.20), channel_id=1, source_target_pairs={{2,1},{4,3},{6,5},{10,9},{12,11},{14,13},{18,17},{20,19},{22,21},{... | collective-permute-start | bytes 854024 | tf_op jit(solution)/shard_map/ppermute | solution.py:99
  22.4 0.0 collective-permute-done.4.refs_12_
  22.4 0.7 copy-done.5
  23.1 8.1 %collective-permute-start = (f32[139,1024]{1,0:T(8,128)}, f32[139,1024]{1,0:T(8,128)}, u32[]{:S(2)}, u32[]{:S(2)}) collective-permute-start(f32[139,1024]{1,0:T(8,128)} %get-tuple-element.14), channel_id=1, source_target_pairs={{0,2},{1,3},{2,4},{3,5},{4,6},{5,7},{8,10},{9,11},{10,12},{11,13},... | collective-permute-start | bytes 1708040 | tf_op jit(solution)/shard_map/ppermute | solution.py:99
  31.2 0.0 collective-permute-done.5.refs_13_
  31.2 0.7 copy-done.7
  31.9 1.3 %collective-permute-start.1 = (f32[139,1024]{1,0:T(8,128)}, f32[139,1024]{1,0:T(8,128)}, u32[]{:S(2)}, u32[]{:S(2)}) collective-permute-start(f32[139,1024]{1,0:T(8,128)} %get-tuple-element.15), channel_id=1, source_target_pairs={{2,0},{3,1},{4,2},{5,3},{6,4},{7,5},{10,8},{11,9},{12,10},{13,11},... | collective-permute-start | bytes 1708040 | tf_op jit(solution)/shard_map/ppermute | solution.py:99
  34.6 0.1 pad_add_fusion.1.refs_1_
  34.6 1.3 %collective-permute-start.7 = (f32[139,512]{1,0:T(8,128)}, f32[139,512]{1,0:T(8,128)S(1)}, u32[]{:S(2)}, u32[]{:S(2)}) collective-permute-start(f32[139,512]{1,0:T(8,128)} %get-tuple-element.21), channel_id=1, source_target_pairs={{3,0},{5,2},{7,4},{11,8},{13,10},{15,12},{19,16},{21,18},{23,20},{... | collective-permute-start | bytes 854024 | tf_op jit(solution)/shard_map/ppermute | solution.py:99
  35.9 0.0 copy-start.11
  35.9 0.1 pad_add_fusion.refs_0_
  36.0 0.6 copy-done.11
  36.6 15.7 %collective-permute-done.7.refs_15_ = f32[139,512]{1,0:T(8,128)S(1)} collective-permute-done((f32[139,512]{1,0:T(8,128)}, f32[139,512]{1,0:T(8,128)S(1)}, u32[]{:S(2)}, u32[]{:S(2)}) %collective-permute-start.7) | collective-permute-done | bytes 284704 | tf_op jit(solution)/shard_map/ppermute | solution.py:99
  52.3 1.0 %copy-done.6 = f32[139,512]{1,0:T(8,128)S(1)} copy-done((f32[139,512]{1,0:T(8,128)S(1)}, f32[139,512]{1,0:T(8,128)}, u32[]{:S(2)}) %copy-start.6) | copy-done | bytes 284696
  53.3 1.0 %copy-done.8 = f32[139,512]{1,0:T(8,128)S(1)} copy-done((f32[139,512]{1,0:T(8,128)S(1)}, f32[139,512]{1,0:T(8,128)}, u32[]{:S(2)}) %copy-start.8) | copy-done | bytes 284696
  54.3 13.8 %shard_map.122 = (f32[1,5,32,1024]{3,2,1,0:T(8,128)}, f32[1,5,32,1024]{3,2,1,0:T(8,128)}, f32[2,4,1024]{2,1,0:T(4,128)S(1)}) custom-call(s32[4]{0:T(128)S(1)} %pad_add_fusion.refs_0_, s32[2]{0:T(128)S(1)} %pad_add_fusion.1.refs_1_, f32[3]{0:T(128)S(1)} %bitcast.47, f32[1,5,32,1024]{3,2,1,0:T(8,128)S(1)} %copy-done.1, f32[1,5,32,1024]{3,2,1,0:T(8,128)S(1)} %copy-done.2, ...), custom_call_target="tpu_custom_call" | custom-call | tf_op jit(solution)/shard_map/pallas_call | solution.py:294
  68.1 0.6 reshape.113
  68.7 0.2 reduce_sum.18
  68.9 0.2 copy.21
  69.1 0.8 scatter_custom_fusion
  69.9 0.1 copy.19
  70.0 6.3 %all_to_all.5 = f32[4,16,2]{1,2,0:T(2,128)S(1)} all-to-all(f32[4,16,2]{1,2,0:T(2,128)S(1)} %copy.19), channel_id=1, replica_groups=mesh['shot'=4,'gy'=4,'gx'=2] {'shot'}, dimensions={0} | all-to-all | bytes 1024 | tf_op jit(solution)/shard_map/all_to_all | solution.py:318
  76.3 0.6 reduce_sum.19
  (26 shorter events, 0.1 us)
Async XLA Ops:
  1.3 0.7 copy-start.10
  3.3 49.0 %copy-start = (f32[4,32,1024]{2,1,0:T(8,128)S(1)}, f32[4,32,1024]{2,1,0:T(8,128)}, u32[]{:S(2)}) copy-start(f32[4,32,1024]{2,1,0:T(8,128)} %fusion.1.refs_4_.refs_7_) | copy-start | bytes 1572868
  3.3 49.0 %copy-start.1 = (f32[1,5,32,1024]{3,2,1,0:T(8,128)S(1)}, f32[1,5,32,1024]{3,2,1,0:T(8,128)}, u32[]{:S(2)}) copy-start(f32[1,5,32,1024]{3,2,1,0:T(8,128)} %refs_3_.3) | copy-start | bytes 1966084
  3.3 49.0 %copy-start.2 = (f32[1,5,32,1024]{3,2,1,0:T(8,128)S(1)}, f32[1,5,32,1024]{3,2,1,0:T(8,128)}, u32[]{:S(2)}) copy-start(f32[1,5,32,1024]{3,2,1,0:T(8,128)} %refs_4_.1) | copy-start | bytes 1966084
  3.3 49.0 %copy-start.3 = (f32[32,1024]{1,0:T(8,128)S(1)}, f32[32,1024]{1,0:T(8,128)}, u32[]{:S(2)}) copy-start(f32[32,1024]{1,0:T(8,128)} %refs_5_.1) | copy-start | bytes 393220
  3.3 49.0 %copy-start.4 = (f32[32,1024]{1,0:T(8,128)S(1)}, f32[32,1024]{1,0:T(8,128)}, u32[]{:S(2)}) copy-start(f32[32,1024]{1,0:T(8,128)} %refs_6_.1) | copy-start | bytes 393220
  6.9 15.5 %collective-permute-start.4 = (f32[139,512]{1,0:T(8,128)}, f32[139,512]{1,0:T(8,128)S(1)}, u32[]{:S(2)}, u32[]{:S(2)}) collective-permute-start(f32[139,512]{1,0:T(8,128)} %get-tuple-element.18), channel_id=1, source_target_pairs={{0,3},{2,5},{4,7},{8,11},{10,13},{12,15},{16,19},{18,21},{20,23},{... | collective-permute-start | bytes 854024 | tf_op jit(solution)/shard_map/ppermute | solution.py:99
  12.8 18.4 %collective-permute-start.5 = (f32[139,512]{1,0:T(8,128)}, f32[139,512]{1,0:T(8,128)S(1)}, u32[]{:S(2)}, u32[]{:S(2)}) collective-permute-start(f32[139,512]{1,0:T(8,128)} %get-tuple-element.19), channel_id=1, source_target_pairs={{1,2},{3,4},{5,6},{9,10},{11,12},{13,14},{17,18},{19,20},{21,22},{... | collective-permute-start | bytes 854024 | tf_op jit(solution)/shard_map/ppermute | solution.py:99
  13.5 38.7 %collective-permute-start.2 = (f32[32,4992]{1,0:T(8,128)}, f32[32,4992]{1,0:T(8,128)S(1)}, u32[]{:S(2)}, u32[]{:S(2)}) collective-permute-start(f32[32,4992]{1,0:T(8,128)} %get-tuple-element.16), channel_id=1, source_target_pairs={{0,1},{2,3},{4,5},{6,7},{8,9},{10,11},{12,13},{14,15},{16,17},{18,... | collective-permute-start | bytes 1916936 | tf_op jit(solution)/shard_map/ppermute | solution.py:99
  19.7 32.5 %collective-permute-start.3 = (f32[32,4992]{1,0:T(8,128)}, f32[32,4992]{1,0:T(8,128)S(1)}, u32[]{:S(2)}, u32[]{:S(2)}) collective-permute-start(f32[32,4992]{1,0:T(8,128)} %get-tuple-element.17), channel_id=1, source_target_pairs={{1,0},{3,2},{5,4},{7,6},{9,8},{11,10},{13,12},{15,14},{17,16},{19,... | collective-permute-start | bytes 1916936 | tf_op jit(solution)/shard_map/ppermute | solution.py:99
  21.0 13.6 %collective-permute-start.6 = (f32[139,512]{1,0:T(8,128)}, f32[139,512]{1,0:T(8,128)}, u32[]{:S(2)}, u32[]{:S(2)}) collective-permute-start(f32[139,512]{1,0:T(8,128)} %get-tuple-element.20), channel_id=1, source_target_pairs={{2,1},{4,3},{6,5},{10,9},{12,11},{14,13},{18,17},{20,19},{22,21},{... | collective-permute-start | bytes 854024 | tf_op jit(solution)/shard_map/ppermute | solution.py:99
  22.4 0.7 copy-start.5
  23.1 29.1 %collective-permute-start = (f32[139,1024]{1,0:T(8,128)}, f32[139,1024]{1,0:T(8,128)}, u32[]{:S(2)}, u32[]{:S(2)}) collective-permute-start(f32[139,1024]{1,0:T(8,128)} %get-tuple-element.14), channel_id=1, source_target_pairs={{0,2},{1,3},{2,4},{3,5},{4,6},{5,7},{8,10},{9,11},{10,12},{11,13},... | collective-permute-start | bytes 1708040 | tf_op jit(solution)/shard_map/ppermute | solution.py:99
  31.2 0.7 copy-start.7
  31.9 20.3 %collective-permute-start.1 = (f32[139,1024]{1,0:T(8,128)}, f32[139,1024]{1,0:T(8,128)}, u32[]{:S(2)}, u32[]{:S(2)}) collective-permute-start(f32[139,1024]{1,0:T(8,128)} %get-tuple-element.15), channel_id=1, source_target_pairs={{2,0},{3,1},{4,2},{5,3},{6,4},{7,5},{10,8},{11,9},{12,10},{13,11},... | collective-permute-start | bytes 1708040 | tf_op jit(solution)/shard_map/ppermute | solution.py:99
  34.6 17.6 %collective-permute-start.7 = (f32[139,512]{1,0:T(8,128)}, f32[139,512]{1,0:T(8,128)S(1)}, u32[]{:S(2)}, u32[]{:S(2)}) collective-permute-start(f32[139,512]{1,0:T(8,128)} %get-tuple-element.21), channel_id=1, source_target_pairs={{3,0},{5,2},{7,4},{11,8},{13,10},{15,12},{19,16},{21,18},{23,20},{... | collective-permute-start | bytes 854024 | tf_op jit(solution)/shard_map/ppermute | solution.py:99
  35.9 0.7 copy-start.11
  36.6 15.7 %copy-start.9 = (f32[1,3]{1,0:T(1,128)S(1)}, f32[1,3]{1,0:T(1,128)}, u32[]{:S(2)}) copy-start(f32[1,3]{1,0:T(1,128)} %param.14) | copy-start | bytes 40
  52.3 1.0 %copy-start.6 = (f32[139,512]{1,0:T(8,128)S(1)}, f32[139,512]{1,0:T(8,128)}, u32[]{:S(2)}) copy-start(f32[139,512]{1,0:T(8,128)} %copy-done.5) | copy-start | bytes 854020
  53.3 1.0 %copy-start.8 = (f32[139,512]{1,0:T(8,128)S(1)}, f32[139,512]{1,0:T(8,128)}, u32[]{:S(2)}) copy-start(f32[139,512]{1,0:T(8,128)} %copy-done.7) | copy-start | bytes 854020

commit v10 on v9

--- a/solution.py
+++ b/solution.py
@@ -106,7 +106,6 @@
     ny, lanes, oy, ox, cw = frame.ny, frame.lanes, frame.oy, frame.ox, packing.corner
     below, above, left, right, b_l, b_r, a_l, a_r = pieces
     h, w = packing.rows[j], packing.lanes[j]
-    dst[...] = jnp.zeros(dst.shape, dst.dtype)
     mid = slice(oy, oy + ny)
     centre = slice(ox, ox + lanes)
     dst[mid, centre] = own[...]

time: 77.4 us -> 77.4 us (level)
  no operation moved by 1% of the time
where the time goes in v10:
time: 77.4 us; the launch traced here: 76.9 us
  starting transfers between devices  26.1 us (34%)
  Pallas kernels  17.5 us (23%)
  waiting for transfers between devices  15.7 us (20%)
  blocking collectives  6.34 us (8%)
  local copies, waits for them, and re-layouts  6.29 us (8%)
  between operations  2.14 us (3%)
  other arithmetic  1.61 us (2%)
  matrix products  1.29 us (2%)
    ppermute x8, starting transfers between devices, move(): return lax.ppermute(piece, ('gy', 'gx'), pairs)  26.1 us
    ppermute x8, waiting for transfers between devices, move(): return lax.ppermute(piece, ('gy', 'gx'), pairs)  15.7 us
    pallas_call x1, Pallas kernels, on_device(): pl.pallas_call(lambda *refs: window_kernel(frame, packing, *refs), out_sh...  13.8 us
    all_to_all x1, blocking collectives, on_device(): lax.all_to_all(ordered.reshape(shots, -1, 2), 'shot', split_axis=0, conca...  6.34 us
    unnamed x25, local copies, waits for them, and re-layouts  4.58 us
    pallas_call x1, Pallas kernels, on_device(): pl.pallas_call(lambda *refs: pack_kernel(frame, packing, *refs), out_shap...  3.62 us
  transfers between devices with their start and end apart: 8, of which 1 were waited for; matrix products, arithmetic and copies ran while one was open for 0% of the time, Pallas kernels for 0%

profile of v10, /device:TPU:0, one launch (start us, length us, event | category | flops | bytes accessed | tf_op | source)
XLA Modules:
  0.0 76.9 jit_solution(4305130527667785053)
XLA Ops:
  0.6 0.7 and_select_fusion.1
  1.3 0.7 copy-done.10
  2.0 1.3 %fusion.1.refs_4_.refs_7_ = f32[4,32,1024]{2,1,0:T(8,128)} fusion(s32[128]{0:T(128)S(1)} %get-tuple-element.35, f32[128,32]{0,1:T(8,128)S(1)} %fusion.9, f32[4,128]{1,0:T(4,128)S(1)} %concatenate.3), kind=kOutput, calls=%fused_computation.3 | convolution fusion | flops 201474048 | bytes 543232 | tf_op jit(solution)/shard_map/nky,kl->nyl/dot_general | solution.py:269
  3.3 0.0 copy-start.4
  3.3 3.6 %shard_map.121 = (f32[139,1024]{1,0:T(8,128)}, f32[139,1024]{1,0:T(8,128)}, f32[32,4992]{1,0:T(8,128)}, f32[32,4992]{1,0:T(8,128)}, f32[139,512]{1,0:T(8,128)}, ...) custom-call(f32[1,5,32,1024]{3,2,1,0:T(8,128)} %refs_3_.3, f32[1,5,32,1024]{3,2,1,0:T(8,128)} %refs_4_.1, ...), custom_call_target="tpu_custom_call" | custom-call | tf_op jit(solution)/shard_map/pallas_call | solution.py:277
  6.9 5.9 %collective-permute-start.4 = (f32[139,512]{1,0:T(8,128)}, f32[139,512]{1,0:T(8,128)S(1)}, u32[]{:S(2)}, u32[]{:S(2)}) collective-permute-start(f32[139,512]{1,0:T(8,128)} %get-tuple-element.18), channel_id=1, source_target_pairs={{0,3},{2,5},{4,7},{8,11},{10,13},{12,15},{16,19},{18,21},{20,23},{... | collective-permute-start | bytes 854024 | tf_op jit(solution)/shard_map/ppermute | solution.py:99
  12.8 0.7 collective-permute-start.5
  13.5 6.2 %collective-permute-start.2 = (f32[32,4992]{1,0:T(8,128)}, f32[32,4992]{1,0:T(8,128)S(1)}, u32[]{:S(2)}, u32[]{:S(2)}) collective-permute-start(f32[32,4992]{1,0:T(8,128)} %get-tuple-element.16), channel_id=1, source_target_pairs={{0,1},{2,3},{4,5},{6,7},{8,9},{10,11},{12,13},{14,15},{16,17},{18,... | collective-permute-start | bytes 1916936 | tf_op jit(solution)/shard_map/ppermute | solution.py:99
  19.7 1.3 %collective-permute-start.3 = (f32[32,4992]{1,0:T(8,128)}, f32[32,4992]{1,0:T(8,128)S(1)}, u32[]{:S(2)}, u32[]{:S(2)}) collective-permute-start(f32[32,4992]{1,0:T(8,128)} %get-tuple-element.17), channel_id=1, source_target_pairs={{1,0},{3,2},{5,4},{7,6},{9,8},{11,10},{13,12},{15,14},{17,16},{19,... | collective-permute-start | bytes 1916936 | tf_op jit(solution)/shard_map/ppermute | solution.py:99
  21.0 1.4 %collective-permute-start.6 = (f32[139,512]{1,0:T(8,128)}, f32[139,512]{1,0:T(8,128)}, u32[]{:S(2)}, u32[]{:S(2)}) collective-permute-start(f32[139,512]{1,0:T(8,128)} %get-tuple-element.20), channel_id=1, source_target_pairs={{2,1},{4,3},{6,5},{10,9},{12,11},{14,13},{18,17},{20,19},{22,21},{... | collective-permute-start | bytes 854024 | tf_op jit(solution)/shard_map/ppermute | solution.py:99
  22.4 0.0 collective-permute-done.4.refs_12_
  22.4 0.7 copy-done.5
  23.1 8.1 %collective-permute-start = (f32[139,1024]{1,0:T(8,128)}, f32[139,1024]{1,0:T(8,128)}, u32[]{:S(2)}, u32[]{:S(2)}) collective-permute-start(f32[139,1024]{1,0:T(8,128)} %get-tuple-element.14), channel_id=1, source_target_pairs={{0,2},{1,3},{2,4},{3,5},{4,6},{5,7},{8,10},{9,11},{10,12},{11,13},... | collective-permute-start | bytes 1708040 | tf_op jit(solution)/shard_map/ppermute | solution.py:99
  31.2 0.0 collective-permute-done.5.refs_13_
  31.2 0.7 copy-done.7
  31.9 1.3 %collective-permute-start.1 = (f32[139,1024]{1,0:T(8,128)}, f32[139,1024]{1,0:T(8,128)}, u32[]{:S(2)}, u32[]{:S(2)}) collective-permute-start(f32[139,1024]{1,0:T(8,128)} %get-tuple-element.15), channel_id=1, source_target_pairs={{2,0},{3,1},{4,2},{5,3},{6,4},{7,5},{10,8},{11,9},{12,10},{13,11},... | collective-permute-start | bytes 1708040 | tf_op jit(solution)/shard_map/ppermute | solution.py:99
  34.6 0.1 pad_add_fusion.1.refs_1_
  34.6 1.3 %collective-permute-start.7 = (f32[139,512]{1,0:T(8,128)}, f32[139,512]{1,0:T(8,128)S(1)}, u32[]{:S(2)}, u32[]{:S(2)}) collective-permute-start(f32[139,512]{1,0:T(8,128)} %get-tuple-element.21), channel_id=1, source_target_pairs={{3,0},{5,2},{7,4},{11,8},{13,10},{15,12},{19,16},{21,18},{23,20},{... | collective-permute-start | bytes 854024 | tf_op jit(solution)/shard_map/ppermute | solution.py:99
  35.9 0.0 copy-start.11
  35.9 0.1 pad_add_fusion.refs_0_
  36.0 0.6 copy-done.11
  36.6 15.7 %collective-permute-done.7.refs_15_ = f32[139,512]{1,0:T(8,128)S(1)} collective-permute-done((f32[139,512]{1,0:T(8,128)}, f32[139,512]{1,0:T(8,128)S(1)}, u32[]{:S(2)}, u32[]{:S(2)}) %collective-permute-start.7) | collective-permute-done | bytes 284704 | tf_op jit(solution)/shard_map/ppermute | solution.py:99
  52.3 1.0 %copy-done.6 = f32[139,512]{1,0:T(8,128)S(1)} copy-done((f32[139,512]{1,0:T(8,128)S(1)}, f32[139,512]{1,0:T(8,128)}, u32[]{:S(2)}) %copy-start.6) | copy-done | bytes 284696
  53.3 1.0 %copy-done.8 = f32[139,512]{1,0:T(8,128)S(1)} copy-done((f32[139,512]{1,0:T(8,128)S(1)}, f32[139,512]{1,0:T(8,128)}, u32[]{:S(2)}) %copy-start.8) | copy-done | bytes 284696
  54.3 13.8 %shard_map.122 = (f32[1,5,32,1024]{3,2,1,0:T(8,128)}, f32[1,5,32,1024]{3,2,1,0:T(8,128)}, f32[2,4,1024]{2,1,0:T(4,128)S(1)}) custom-call(s32[4]{0:T(128)S(1)} %pad_add_fusion.refs_0_, s32[2]{0:T(128)S(1)} %pad_add_fusion.1.refs_1_, f32[3]{0:T(128)S(1)} %bitcast.47, f32[1,5,32,1024]{3,2,1,0:T(8,128)S(1)} %copy-done.1, f32[1,5,32,1024]{3,2,1,0:T(8,128)S(1)} %copy-done.2, ...), custom_call_target="tpu_custom_call" | custom-call | tf_op jit(solution)/shard_map/pallas_call | solution.py:293
  68.1 0.6 reshape.113
  68.8 0.2 reduce_sum.18
  69.0 0.2 copy.21
  69.2 0.8 scatter_custom_fusion
  69.9 0.1 copy.19
  70.0 6.3 %all_to_all.5 = f32[4,16,2]{1,2,0:T(2,128)S(1)} all-to-all(f32[4,16,2]{1,2,0:T(2,128)S(1)} %copy.19), channel_id=1, replica_groups=mesh['shot'=4,'gy'=4,'gx'=2] {'shot'}, dimensions={0} | all-to-all | bytes 1024 | tf_op jit(solution)/shard_map/all_to_all | solution.py:317
  76.4 0.6 reduce_sum.19
  (26 shorter events, 0.1 us)
Async XLA Ops:
  1.3 0.7 copy-start.10
  3.3 49.0 %copy-start = (f32[4,32,1024]{2,1,0:T(8,128)S(1)}, f32[4,32,1024]{2,1,0:T(8,128)}, u32[]{:S(2)}) copy-start(f32[4,32,1024]{2,1,0:T(8,128)} %fusion.1.refs_4_.refs_7_) | copy-start | bytes 1572868
  3.3 49.0 %copy-start.1 = (f32[1,5,32,1024]{3,2,1,0:T(8,128)S(1)}, f32[1,5,32,1024]{3,2,1,0:T(8,128)}, u32[]{:S(2)}) copy-start(f32[1,5,32,1024]{3,2,1,0:T(8,128)} %refs_3_.3) | copy-start | bytes 1966084
  3.3 49.0 %copy-start.2 = (f32[1,5,32,1024]{3,2,1,0:T(8,128)S(1)}, f32[1,5,32,1024]{3,2,1,0:T(8,128)}, u32[]{:S(2)}) copy-start(f32[1,5,32,1024]{3,2,1,0:T(8,128)} %refs_4_.1) | copy-start | bytes 1966084
  3.3 49.0 %copy-start.3 = (f32[32,1024]{1,0:T(8,128)S(1)}, f32[32,1024]{1,0:T(8,128)}, u32[]{:S(2)}) copy-start(f32[32,1024]{1,0:T(8,128)} %refs_5_.1) | copy-start | bytes 393220
  3.3 49.0 %copy-start.4 = (f32[32,1024]{1,0:T(8,128)S(1)}, f32[32,1024]{1,0:T(8,128)}, u32[]{:S(2)}) copy-start(f32[32,1024]{1,0:T(8,128)} %refs_6_.1) | copy-start | bytes 393220
  6.9 15.5 %collective-permute-start.4 = (f32[139,512]{1,0:T(8,128)}, f32[139,512]{1,0:T(8,128)S(1)}, u32[]{:S(2)}, u32[]{:S(2)}) collective-permute-start(f32[139,512]{1,0:T(8,128)} %get-tuple-element.18), channel_id=1, source_target_pairs={{0,3},{2,5},{4,7},{8,11},{10,13},{12,15},{16,19},{18,21},{20,23},{... | collective-permute-start | bytes 854024 | tf_op jit(solution)/shard_map/ppermute | solution.py:99
  12.8 18.4 %collective-permute-start.5 = (f32[139,512]{1,0:T(8,128)}, f32[139,512]{1,0:T(8,128)S(1)}, u32[]{:S(2)}, u32[]{:S(2)}) collective-permute-start(f32[139,512]{1,0:T(8,128)} %get-tuple-element.19), channel_id=1, source_target_pairs={{1,2},{3,4},{5,6},{9,10},{11,12},{13,14},{17,18},{19,20},{21,22},{... | collective-permute-start | bytes 854024 | tf_op jit(solution)/shard_map/ppermute | solution.py:99
  13.5 38.7 %collective-permute-start.2 = (f32[32,4992]{1,0:T(8,128)}, f32[32,4992]{1,0:T(8,128)S(1)}, u32[]{:S(2)}, u32[]{:S(2)}) collective-permute-start(f32[32,4992]{1,0:T(8,128)} %get-tuple-element.16), channel_id=1, source_target_pairs={{0,1},{2,3},{4,5},{6,7},{8,9},{10,11},{12,13},{14,15},{16,17},{18,... | collective-permute-start | bytes 1916936 | tf_op jit(solution)/shard_map/ppermute | solution.py:99
  19.7 32.5 %collective-permute-start.3 = (f32[32,4992]{1,0:T(8,128)}, f32[32,4992]{1,0:T(8,128)S(1)}, u32[]{:S(2)}, u32[]{:S(2)}) collective-permute-start(f32[32,4992]{1,0:T(8,128)} %get-tuple-element.17), channel_id=1, source_target_pairs={{1,0},{3,2},{5,4},{7,6},{9,8},{11,10},{13,12},{15,14},{17,16},{19,... | collective-permute-start | bytes 1916936 | tf_op jit(solution)/shard_map/ppermute | solution.py:99
  21.0 13.6 %collective-permute-start.6 = (f32[139,512]{1,0:T(8,128)}, f32[139,512]{1,0:T(8,128)}, u32[]{:S(2)}, u32[]{:S(2)}) collective-permute-start(f32[139,512]{1,0:T(8,128)} %get-tuple-element.20), channel_id=1, source_target_pairs={{2,1},{4,3},{6,5},{10,9},{12,11},{14,13},{18,17},{20,19},{22,21},{... | collective-permute-start | bytes 854024 | tf_op jit(solution)/shard_map/ppermute | solution.py:99
  22.4 0.7 copy-start.5
  23.1 29.1 %collective-permute-start = (f32[139,1024]{1,0:T(8,128)}, f32[139,1024]{1,0:T(8,128)}, u32[]{:S(2)}, u32[]{:S(2)}) collective-permute-start(f32[139,1024]{1,0:T(8,128)} %get-tuple-element.14), channel_id=1, source_target_pairs={{0,2},{1,3},{2,4},{3,5},{4,6},{5,7},{8,10},{9,11},{10,12},{11,13},... | collective-permute-start | bytes 1708040 | tf_op jit(solution)/shard_map/ppermute | solution.py:99
  31.2 0.7 copy-start.7
  31.9 20.3 %collective-permute-start.1 = (f32[139,1024]{1,0:T(8,128)}, f32[139,1024]{1,0:T(8,128)}, u32[]{:S(2)}, u32[]{:S(2)}) collective-permute-start(f32[139,1024]{1,0:T(8,128)} %get-tuple-element.15), channel_id=1, source_target_pairs={{2,0},{3,1},{4,2},{5,3},{6,4},{7,5},{10,8},{11,9},{12,10},{13,11},... | collective-permute-start | bytes 1708040 | tf_op jit(solution)/shard_map/ppermute | solution.py:99
  34.6 17.6 %collective-permute-start.7 = (f32[139,512]{1,0:T(8,128)}, f32[139,512]{1,0:T(8,128)S(1)}, u32[]{:S(2)}, u32[]{:S(2)}) collective-permute-start(f32[139,512]{1,0:T(8,128)} %get-tuple-element.21), channel_id=1, source_target_pairs={{3,0},{5,2},{7,4},{11,8},{13,10},{15,12},{19,16},{21,18},{23,20},{... | collective-permute-start | bytes 854024 | tf_op jit(solution)/shard_map/ppermute | solution.py:99
  35.9 0.7 copy-start.11
  36.6 15.7 %copy-start.9 = (f32[1,3]{1,0:T(1,128)S(1)}, f32[1,3]{1,0:T(1,128)}, u32[]{:S(2)}) copy-start(f32[1,3]{1,0:T(1,128)} %param.14) | copy-start | bytes 40
  52.3 1.0 %copy-start.6 = (f32[139,512]{1,0:T(8,128)S(1)}, f32[139,512]{1,0:T(8,128)}, u32[]{:S(2)}) copy-start(f32[139,512]{1,0:T(8,128)} %copy-done.5) | copy-start | bytes 854020
  53.3 1.0 %copy-start.8 = (f32[139,512]{1,0:T(8,128)S(1)}, f32[139,512]{1,0:T(8,128)}, u32[]{:S(2)}) copy-start(f32[139,512]{1,0:T(8,128)} %copy-done.7) | copy-start | bytes 854020

commit v11 on v10

--- a/solution.py
+++ b/solution.py
@@ -127,10 +127,19 @@
     dst[hi, east] = a_r[r, 0:w]
 
 
-def stepper(frame, bounds_ref):
-    ey, el = frame.ey, frame.el
-    row = lax.broadcasted_iota(jnp.int32, (ey, el), 0)
-    lane = lax.broadcasted_iota(jnp.int32, (ey, el), 1)
+def window(frame, depth):
+    r0 = max(0, (frame.oy - depth) // 8 * 8)
+    r1 = min(frame.ey, round_up(frame.oy + frame.ny + depth, 8))
+    l0 = max(0, (frame.ox - depth * CZ) // 128 * 128)
+    l1 = min(frame.el, round_up(frame.ox + frame.lanes + depth * CZ, 128))
+    return r0, r1, l0, l1
+
+
+def stepper(frame, bounds_ref, win):
+    r0, r1, l0, l1 = win
+    ey, el = r1 - r0, l1 - l0
+    row = lax.broadcasted_iota(jnp.int32, (ey, el), 0) + r0
+    lane = lax.broadcasted_iota(jnp.int32, (ey, el), 1) + l0
     inside = (
         (row >= bounds_ref[0])
         & (row < bounds_ref[1])
@@ -185,40 +194,56 @@
     )
     for j in range(16):
         assemble(ext.at[j], owns[j], pieces, j, frame, packing)
-    wave_step, row, lane = stepper(frame, bounds_ref)
-    source = (row == source_ref[0]) & (lane == source_ref[1])
-    vel = ext[10]
-    att = ext[11]
-    stiff = stiff_scale * vel * vel
-    mid = slice(frame.oy, frame.oy + frame.ny)
-    centre = slice(frame.ox, frame.ox + frame.lanes)
+    vel_all = ext[10]
+    att_all = ext[11]
+    stiff_all = stiff_scale * vel_all * vel_all
+
+    def cut(a, inner, outer):
+        return a[inner[0] - outer[0] : inner[1] - outer[0], inner[2] - outer[2] : inner[3] - outer[2]]
+
+    full = (0, frame.ey, 0, frame.el)
+    tile = (frame.oy, frame.oy + frame.ny, frame.ox, frame.ox + frame.lanes)
+
     state = [ext[k] for k in range(5)]
+    where = full
     for step in range(STEPS):
-        state, div = wave_step(state, stiff, att)
+        win = window(frame, 3 * (STEPS - step) + 3 * (STEPS - 1))
+        state = [cut(a, win, where) for a in state]
+        where = win
+        wave_step, row, lane = stepper(frame, bounds_ref, win)
+        source = (row == source_ref[0]) & (lane == source_ref[1])
+        state, div = wave_step(state, cut(stiff_all, win, full), cut(att_all, win, full))
         state[0] = state[0] + jnp.where(source, wave_ref[step], jnp.float32(0.0))
-        divs[step] = div[mid, centre]
-        inject[step] = ext[12] * state[0] - ext[13 + step]
+        divs[step] = cut(div, tile, win)
+        inject[step, win[0] : win[1], win[2] : win[3]] = (
+            cut(ext[12], win, full) * state[0] - cut(ext[13 + step], win, full)
+        )
     for k in range(5):
-        end_ref[0, k] = state[k][mid, centre]
-
-    velocity = vel[mid, centre]
-    attenuation = att[mid, centre]
-    stiff_own = stiff[mid, centre]
+        end_ref[0, k] = cut(state[k], tile, where)
+
+    velocity = cut(vel_all, tile, full)
+    attenuation = cut(att_all, tile, full)
+    stiff_own = cut(stiff_all, tile, full)
     adj = [ext[5 + k] for k in range(5)]
+    where = full
     grad_v = jnp.zeros((frame.ny, frame.lanes), jnp.float32)
     grad_a = jnp.zeros((frame.ny, frame.lanes), jnp.float32)
     for step in range(STEPS - 1, -1, -1):
-        adj, unused = wave_step(adj, stiff, att)
-        adj[0] = adj[0] + inject[step]
+        win = window(frame, 3 * (step + 1))
+        adj = [cut(a, win, where) for a in adj]
+        where = win
+        wave_step, row, lane = stepper(frame, bounds_ref, win)
+        adj, unused = wave_step(adj, cut(stiff_all, win, full), cut(att_all, win, full))
+        adj[0] = adj[0] + inject[step, win[0] : win[1], win[2] : win[3]]
         div = divs[step]
-        q = adj[0][mid, centre]
-        m = adj[4][mid, centre]
+        q = cut(adj[0], tile, win)
+        m = cut(adj[4], tile, win)
         deriv_q = (relax_rate * attenuation - (1.0 + attenuation)) * div
         deriv_m = -relax_rate * attenuation * div
         grad_v = grad_v + (q * deriv_q + m * deriv_m) * (2.0 * stiff_scale * velocity)
         grad_a = grad_a + (q * (relax_rate - 1.0) - m * relax_rate) * stiff_own * div
     for k in range(5):
-        start_ref[0, k] = adj[k][mid, centre]
+        start_ref[0, k] = cut(adj[k], tile, where)
     for c, g in enumerate((grad_v, grad_a)):
         grad_ref[c] = g.reshape(frame.ny // BY, BY, frame.lanes).sum(axis=1)
 

time: 77.4 us -> 75.4 us (0.974)
  Pallas kernels: 17.5 us -> 15.5 us
    pallas_call x1, Pallas kernels: 13.8 us -> 11.8 us  [on_device(): pl.pallas_call(lambda *refs: window_kernel(frame, packing, *refs), out_sh...]
where the time goes in v11:
time: 75.4 us; the launch traced here: 74.9 us
  starting transfers between devices  26.1 us (35%)
  waiting for transfers between devices  15.7 us (21%)
  Pallas kernels  15.5 us (21%)
  blocking collectives  6.34 us (8%)
  local copies, waits for them, and re-layouts  6.29 us (8%)
  between operations  2.14 us (3%)
  other arithmetic  1.61 us (2%)
  matrix products  1.29 us (2%)
    ppermute x8, starting transfers between devices, move(): return lax.ppermute(piece, ('gy', 'gx'), pairs)  26.1 us
    ppermute x8, waiting for transfers between devices, move(): return lax.ppermute(piece, ('gy', 'gx'), pairs)  15.7 us
    pallas_call x1, Pallas kernels, on_device(): pl.pallas_call(lambda *refs: window_kernel(frame, packing, *refs), out_sh...  11.8 us
    all_to_all x1, blocking collectives, on_device(): lax.all_to_all(ordered.reshape(shots, -1, 2), 'shot', split_axis=0, conca...  6.34 us
    unnamed x25, local copies, waits for them, and re-layouts  4.58 us
    pallas_call x1, Pallas kernels, on_device(): pl.pallas_call(lambda *refs: pack_kernel(frame, packing, *refs), out_shap...  3.62 us
  transfers between devices with their start and end apart: 8, of which 1 were waited for; matrix products, arithmetic and copies ran while one was open for 0% of the time, Pallas kernels for 0%

profile of v11, /device:TPU:0, one launch (start us, length us, event | category | flops | bytes accessed | tf_op | source)
XLA Modules:
  0.0 74.9 jit_solution(4990274338212782721)
XLA Ops:
  0.6 0.7 and_select_fusion.1
  1.3 0.7 copy-done.10
  2.0 1.3 %fusion.1.refs_4_.refs_7_ = f32[4,32,1024]{2,1,0:T(8,128)} fusion(s32[128]{0:T(128)S(1)} %get-tuple-element.35, f32[128,32]{0,1:T(8,128)S(1)} %fusion.9, f32[4,128]{1,0:T(4,128)S(1)} %concatenate.3), kind=kOutput, calls=%fused_computation.3 | convolution fusion | flops 201474048 | bytes 543232 | tf_op jit(solution)/shard_map/nky,kl->nyl/dot_general | solution.py:294
  3.3 0.0 copy-start.4
  3.3 3.6 %shard_map.121 = (f32[139,1024]{1,0:T(8,128)}, f32[139,1024]{1,0:T(8,128)}, f32[32,4992]{1,0:T(8,128)}, f32[32,4992]{1,0:T(8,128)}, f32[139,512]{1,0:T(8,128)}, ...) custom-call(f32[1,5,32,1024]{3,2,1,0:T(8,128)} %refs_3_.3, f32[1,5,32,1024]{3,2,1,0:T(8,128)} %refs_4_.1, ...), custom_call_target="tpu_custom_call" | custom-call | tf_op jit(solution)/shard_map/pallas_call | solution.py:302
  6.9 5.9 %collective-permute-start.4 = (f32[139,512]{1,0:T(8,128)}, f32[139,512]{1,0:T(8,128)S(1)}, u32[]{:S(2)}, u32[]{:S(2)}) collective-permute-start(f32[139,512]{1,0:T(8,128)} %get-tuple-element.18), channel_id=1, source_target_pairs={{0,3},{2,5},{4,7},{8,11},{10,13},{12,15},{16,19},{18,21},{20,23},{... | collective-permute-start | bytes 854024 | tf_op jit(solution)/shard_map/ppermute | solution.py:99
  12.8 0.7 collective-permute-start.5
  13.5 6.2 %collective-permute-start.2 = (f32[32,4992]{1,0:T(8,128)}, f32[32,4992]{1,0:T(8,128)S(1)}, u32[]{:S(2)}, u32[]{:S(2)}) collective-permute-start(f32[32,4992]{1,0:T(8,128)} %get-tuple-element.16), channel_id=1, source_target_pairs={{0,1},{2,3},{4,5},{6,7},{8,9},{10,11},{12,13},{14,15},{16,17},{18,... | collective-permute-start | bytes 1916936 | tf_op jit(solution)/shard_map/ppermute | solution.py:99
  19.7 1.3 %collective-permute-start.3 = (f32[32,4992]{1,0:T(8,128)}, f32[32,4992]{1,0:T(8,128)S(1)}, u32[]{:S(2)}, u32[]{:S(2)}) collective-permute-start(f32[32,4992]{1,0:T(8,128)} %get-tuple-element.17), channel_id=1, source_target_pairs={{1,0},{3,2},{5,4},{7,6},{9,8},{11,10},{13,12},{15,14},{17,16},{19,... | collective-permute-start | bytes 1916936 | tf_op jit(solution)/shard_map/ppermute | solution.py:99
  21.0 1.4 %collective-permute-start.6 = (f32[139,512]{1,0:T(8,128)}, f32[139,512]{1,0:T(8,128)}, u32[]{:S(2)}, u32[]{:S(2)}) collective-permute-start(f32[139,512]{1,0:T(8,128)} %get-tuple-element.20), channel_id=1, source_target_pairs={{2,1},{4,3},{6,5},{10,9},{12,11},{14,13},{18,17},{20,19},{22,21},{... | collective-permute-start | bytes 854024 | tf_op jit(solution)/shard_map/ppermute | solution.py:99
  22.4 0.0 collective-permute-done.4.refs_12_
  22.4 0.7 copy-done.5
  23.1 8.1 %collective-permute-start = (f32[139,1024]{1,0:T(8,128)}, f32[139,1024]{1,0:T(8,128)}, u32[]{:S(2)}, u32[]{:S(2)}) collective-permute-start(f32[139,1024]{1,0:T(8,128)} %get-tuple-element.14), channel_id=1, source_target_pairs={{0,2},{1,3},{2,4},{3,5},{4,6},{5,7},{8,10},{9,11},{10,12},{11,13},... | collective-permute-start | bytes 1708040 | tf_op jit(solution)/shard_map/ppermute | solution.py:99
  31.2 0.0 collective-permute-done.5.refs_13_
  31.2 0.7 copy-done.7
  31.9 1.3 %collective-permute-start.1 = (f32[139,1024]{1,0:T(8,128)}, f32[139,1024]{1,0:T(8,128)}, u32[]{:S(2)}, u32[]{:S(2)}) collective-permute-start(f32[139,1024]{1,0:T(8,128)} %get-tuple-element.15), channel_id=1, source_target_pairs={{2,0},{3,1},{4,2},{5,3},{6,4},{7,5},{10,8},{11,9},{12,10},{13,11},... | collective-permute-start | bytes 1708040 | tf_op jit(solution)/shard_map/ppermute | solution.py:99
  34.6 0.1 pad_add_fusion.1.refs_1_
  34.6 1.3 %collective-permute-start.7 = (f32[139,512]{1,0:T(8,128)}, f32[139,512]{1,0:T(8,128)S(1)}, u32[]{:S(2)}, u32[]{:S(2)}) collective-permute-start(f32[139,512]{1,0:T(8,128)} %get-tuple-element.21), channel_id=1, source_target_pairs={{3,0},{5,2},{7,4},{11,8},{13,10},{15,12},{19,16},{21,18},{23,20},{... | collective-permute-start | bytes 854024 | tf_op jit(solution)/shard_map/ppermute | solution.py:99
  35.9 0.0 copy-start.11
  35.9 0.1 pad_add_fusion.refs_0_
  36.0 0.6 copy-done.11
  36.6 15.7 %collective-permute-done.7.refs_15_ = f32[139,512]{1,0:T(8,128)S(1)} collective-permute-done((f32[139,512]{1,0:T(8,128)}, f32[139,512]{1,0:T(8,128)S(1)}, u32[]{:S(2)}, u32[]{:S(2)}) %collective-permute-start.7) | collective-permute-done | bytes 284704 | tf_op jit(solution)/shard_map/ppermute | solution.py:99
  52.3 1.0 %copy-done.6 = f32[139,512]{1,0:T(8,128)S(1)} copy-done((f32[139,512]{1,0:T(8,128)S(1)}, f32[139,512]{1,0:T(8,128)}, u32[]{:S(2)}) %copy-start.6) | copy-done | bytes 284696
  53.3 1.0 %copy-done.8 = f32[139,512]{1,0:T(8,128)S(1)} copy-done((f32[139,512]{1,0:T(8,128)S(1)}, f32[139,512]{1,0:T(8,128)}, u32[]{:S(2)}) %copy-start.8) | copy-done | bytes 284696
  54.3 11.8 %shard_map.122 = (f32[1,5,32,1024]{3,2,1,0:T(8,128)}, f32[1,5,32,1024]{3,2,1,0:T(8,128)}, f32[2,4,1024]{2,1,0:T(4,128)S(1)}) custom-call(s32[4]{0:T(128)S(1)} %pad_add_fusion.refs_0_, s32[2]{0:T(128)S(1)} %pad_add_fusion.1.refs_1_, f32[3]{0:T(128)S(1)} %bitcast.47, f32[1,5,32,1024]{3,2,1,0:T(8,128)S(1)} %copy-done.1, f32[1,5,32,1024]{3,2,1,0:T(8,128)S(1)} %copy-done.2, ...), custom_call_target="tpu_custom_call" | custom-call | tf_op jit(solution)/shard_map/pallas_call | solution.py:318
  66.1 0.6 reshape.113
  66.8 0.2 reduce_sum.18
  67.0 0.2 copy.21
  67.2 0.8 %scatter_custom_fusion = f32[64,2]{1,0:T(8,128)S(1)} fusion(s32[64]{0:T(128)S(1)} %fusion.10, f32[64,2]{1,0:T(8,128)S(1)} %bitcast.49, f32[]{:T(128)} %constant.78.clone.1), kind=kCustom, calls=%fused_computation.9 | custom fusion | bytes 516 | tf_op jit(solution)/shard_map/scatter | solution.py:340
  67.9 0.1 copy.19
  68.0 6.3 %all_to_all.5 = f32[4,16,2]{1,2,0:T(2,128)S(1)} all-to-all(f32[4,16,2]{1,2,0:T(2,128)S(1)} %copy.19), channel_id=1, replica_groups=mesh['shot'=4,'gy'=4,'gx'=2] {'shot'}, dimensions={0} | all-to-all | bytes 1024 | tf_op jit(solution)/shard_map/all_to_all | solution.py:342
  74.4 0.6 reduce_sum.19
  (26 shorter events, 0.1 us)
Async XLA Ops:
  1.3 0.7 copy-start.10
  3.3 49.0 %copy-start = (f32[4,32,1024]{2,1,0:T(8,128)S(1)}, f32[4,32,1024]{2,1,0:T(8,128)}, u32[]{:S(2)}) copy-start(f32[4,32,1024]{2,1,0:T(8,128)} %fusion.1.refs_4_.refs_7_) | copy-start | bytes 1572868
  3.3 49.0 %copy-start.1 = (f32[1,5,32,1024]{3,2,1,0:T(8,128)S(1)}, f32[1,5,32,1024]{3,2,1,0:T(8,128)}, u32[]{:S(2)}) copy-start(f32[1,5,32,1024]{3,2,1,0:T(8,128)} %refs_3_.3) | copy-start | bytes 1966084
  3.3 49.0 %copy-start.2 = (f32[1,5,32,1024]{3,2,1,0:T(8,128)S(1)}, f32[1,5,32,1024]{3,2,1,0:T(8,128)}, u32[]{:S(2)}) copy-start(f32[1,5,32,1024]{3,2,1,0:T(8,128)} %refs_4_.1) | copy-start | bytes 1966084
  3.3 49.0 %copy-start.3 = (f32[32,1024]{1,0:T(8,128)S(1)}, f32[32,1024]{1,0:T(8,128)}, u32[]{:S(2)}) copy-start(f32[32,1024]{1,0:T(8,128)} %refs_5_.1) | copy-start | bytes 393220
  3.3 49.0 %copy-start.4 = (f32[32,1024]{1,0:T(8,128)S(1)}, f32[32,1024]{1,0:T(8,128)}, u32[]{:S(2)}) copy-start(f32[32,1024]{1,0:T(8,128)} %refs_6_.1) | copy-start | bytes 393220
  6.9 15.5 %collective-permute-start.4 = (f32[139,512]{1,0:T(8,128)}, f32[139,512]{1,0:T(8,128)S(1)}, u32[]{:S(2)}, u32[]{:S(2)}) collective-permute-start(f32[139,512]{1,0:T(8,128)} %get-tuple-element.18), channel_id=1, source_target_pairs={{0,3},{2,5},{4,7},{8,11},{10,13},{12,15},{16,19},{18,21},{20,23},{... | collective-permute-start | bytes 854024 | tf_op jit(solution)/shard_map/ppermute | solution.py:99
  12.8 18.4 %collective-permute-start.5 = (f32[139,512]{1,0:T(8,128)}, f32[139,512]{1,0:T(8,128)S(1)}, u32[]{:S(2)}, u32[]{:S(2)}) collective-permute-start(f32[139,512]{1,0:T(8,128)} %get-tuple-element.19), channel_id=1, source_target_pairs={{1,2},{3,4},{5,6},{9,10},{11,12},{13,14},{17,18},{19,20},{21,22},{... | collective-permute-start | bytes 854024 | tf_op jit(solution)/shard_map/ppermute | solution.py:99
  13.5 38.7 %collective-permute-start.2 = (f32[32,4992]{1,0:T(8,128)}, f32[32,4992]{1,0:T(8,128)S(1)}, u32[]{:S(2)}, u32[]{:S(2)}) collective-permute-start(f32[32,4992]{1,0:T(8,128)} %get-tuple-element.16), channel_id=1, source_target_pairs={{0,1},{2,3},{4,5},{6,7},{8,9},{10,11},{12,13},{14,15},{16,17},{18,... | collective-permute-start | bytes 1916936 | tf_op jit(solution)/shard_map/ppermute | solution.py:99
  19.7 32.5 %collective-permute-start.3 = (f32[32,4992]{1,0:T(8,128)}, f32[32,4992]{1,0:T(8,128)S(1)}, u32[]{:S(2)}, u32[]{:S(2)}) collective-permute-start(f32[32,4992]{1,0:T(8,128)} %get-tuple-element.17), channel_id=1, source_target_pairs={{1,0},{3,2},{5,4},{7,6},{9,8},{11,10},{13,12},{15,14},{17,16},{19,... | collective-permute-start | bytes 1916936 | tf_op jit(solution)/shard_map/ppermute | solution.py:99
  21.0 13.6 %collective-permute-start.6 = (f32[139,512]{1,0:T(8,128)}, f32[139,512]{1,0:T(8,128)}, u32[]{:S(2)}, u32[]{:S(2)}) collective-permute-start(f32[139,512]{1,0:T(8,128)} %get-tuple-element.20), channel_id=1, source_target_pairs={{2,1},{4,3},{6,5},{10,9},{12,11},{14,13},{18,17},{20,19},{22,21},{... | collective-permute-start | bytes 854024 | tf_op jit(solution)/shard_map/ppermute | solution.py:99
  22.4 0.7 copy-start.5
  23.1 29.1 %collective-permute-start = (f32[139,1024]{1,0:T(8,128)}, f32[139,1024]{1,0:T(8,128)}, u32[]{:S(2)}, u32[]{:S(2)}) collective-permute-start(f32[139,1024]{1,0:T(8,128)} %get-tuple-element.14), channel_id=1, source_target_pairs={{0,2},{1,3},{2,4},{3,5},{4,6},{5,7},{8,10},{9,11},{10,12},{11,13},... | collective-permute-start | bytes 1708040 | tf_op jit(solution)/shard_map/ppermute | solution.py:99
  31.2 0.7 copy-start.7
  31.9 20.3 %collective-permute-start.1 = (f32[139,1024]{1,0:T(8,128)}, f32[139,1024]{1,0:T(8,128)}, u32[]{:S(2)}, u32[]{:S(2)}) collective-permute-start(f32[139,1024]{1,0:T(8,128)} %get-tuple-element.15), channel_id=1, source_target_pairs={{2,0},{3,1},{4,2},{5,3},{6,4},{7,5},{10,8},{11,9},{12,10},{13,11},... | collective-permute-start | bytes 1708040 | tf_op jit(solution)/shard_map/ppermute | solution.py:99
  34.6 17.6 %collective-permute-start.7 = (f32[139,512]{1,0:T(8,128)}, f32[139,512]{1,0:T(8,128)S(1)}, u32[]{:S(2)}, u32[]{:S(2)}) collective-permute-start(f32[139,512]{1,0:T(8,128)} %get-tuple-element.21), channel_id=1, source_target_pairs={{3,0},{5,2},{7,4},{11,8},{13,10},{15,12},{19,16},{21,18},{23,20},{... | collective-permute-start | bytes 854024 | tf_op jit(solution)/shard_map/ppermute | solution.py:99
  35.9 0.7 copy-start.11
  36.6 15.7 %copy-start.9 = (f32[1,3]{1,0:T(1,128)S(1)}, f32[1,3]{1,0:T(1,128)}, u32[]{:S(2)}) copy-start(f32[1,3]{1,0:T(1,128)} %param.14) | copy-start | bytes 40
  52.3 1.0 %copy-start.6 = (f32[139,512]{1,0:T(8,128)S(1)}, f32[139,512]{1,0:T(8,128)}, u32[]{:S(2)}) copy-start(f32[139,512]{1,0:T(8,128)} %copy-done.5) | copy-start | bytes 854020
  53.3 1.0 %copy-start.8 = (f32[139,512]{1,0:T(8,128)S(1)}, f32[139,512]{1,0:T(8,128)}, u32[]{:S(2)}) copy-start(f32[139,512]{1,0:T(8,128)} %copy-done.7) | copy-start | bytes 854020

commit v12 on v11

--- a/solution.py
+++ b/solution.py
@@ -339,10 +339,17 @@
     slots = block_slot[0]
     ordered = jnp.zeros(sums.shape, jnp.float32).at[slots].set(sums)
     shots = lax.axis_size("shot")
-    parts = lax.all_to_all(
-        ordered.reshape(shots, -1, 2), "shot", split_axis=0, concat_axis=0, tiled=True
-    )
-    coarse = jnp.sum(parts, axis=0)
+    me = lax.axis_index("shot")
+    held = ordered.reshape(shots, -1, 2)
+    span = shots // 2
+    while span >= 1:
+        halves = held.reshape(2, -1, held.shape[1], 2)
+        bit = (me // span) % 2 == 1
+        mine = jnp.where(bit, halves[1], halves[0])
+        other = jnp.where(bit, halves[0], halves[1])
+        held = mine + lax.ppermute(other, "shot", [(i, i ^ span) for i in range(shots)])
+        span //= 2
+    coarse = held[0]
     model_gradient = coarse.T[:, None, :]
     return (forward_end, adjoint_start, model_gradient)
 

time: 75.4 us -> 73.9 us (0.980)
  blocking collectives: 6.34 us -> 0 us
  waiting for transfers between devices: 15.7 us -> 18.8 us
  starting transfers between devices: 26.1 us -> 27.8 us
    all_to_all x1 -> x0, blocking collectives: 6.34 us -> none  [on_device(): lax.all_to_all(ordered.reshape(shots, -1, 2), 'shot', split_axis=0, conca...]
    ppermute x0 -> x2, waiting for transfers between devices: none -> 3.14 us  [on_device(): lax.ppermute(other, 'shot', [(i, i ^ span) for i in range(shots)])]
    ppermute x0 -> x2, starting transfers between devices: none -> 1.56 us  [on_device(): lax.ppermute(other, 'shot', [(i, i ^ span) for i in range(shots)])]
  transfers between devices with their start and end apart: 8 -> 10, of which waited for: 1 -> 3; matrix products, arithmetic and copies ran while one was open for 0% -> 0% of each run, Pallas kernels for 0% -> 0%
where the time goes in v12:
time: 73.9 us; the launch traced here: 73.5 us
  starting transfers between devices  27.8 us (38%)
  waiting for transfers between devices  18.8 us (25%)
  Pallas kernels  15.4 us (21%)
  local copies, waits for them, and re-layouts  6.4 us (9%)
  between operations  2.18 us (3%)
  other arithmetic  1.62 us (2%)
  matrix products  1.28 us (2%)
    ppermute x8, starting transfers between devices, move(): return lax.ppermute(piece, ('gy', 'gx'), pairs)  26.3 us
    ppermute x8, waiting for transfers between devices, move(): return lax.ppermute(piece, ('gy', 'gx'), pairs)  15.6 us
    pallas_call x1, Pallas kernels, on_device(): pl.pallas_call(lambda *refs: window_kernel(frame, packing, *refs), out_sh...  11.8 us
    unnamed x25, local copies, waits for them, and re-layouts  4.61 us
    pallas_call x1, Pallas kernels, on_device(): pl.pallas_call(lambda *refs: pack_kernel(frame, packing, *refs), out_shap...  3.6 us
    ppermute x2, waiting for transfers between devices, on_device(): lax.ppermute(other, 'shot', [(i, i ^ span) for i in range(shots)])  3.14 us
    ppermute x2, starting transfers between devices, on_device(): lax.ppermute(other, 'shot', [(i, i ^ span) for i in range(shots)])  1.56 us
  transfers between devices with their start and end apart: 10, of which 3 were waited for; matrix products, arithmetic and copies ran while one was open for 0% of the time, Pallas kernels for 0%

profile of v12, /device:TPU:0, one launch (start us, length us, event | category | flops | bytes accessed | tf_op | source)
XLA Modules:
  0.0 73.5 jit_solution(1988591371516835543)
XLA Ops:
  0.6 0.7 and_select_fusion.1
  1.3 0.7 copy-done.10
  2.0 1.3 %fusion.1.refs_4_.refs_7_ = f32[4,32,1024]{2,1,0:T(8,128)} fusion(s32[128]{0:T(128)S(1)} %get-tuple-element.34, f32[128,32]{0,1:T(8,128)S(1)} %fusion.9, f32[4,128]{1,0:T(4,128)S(1)} %concatenate.3), kind=kOutput, calls=%fused_computation.3 | convolution fusion | flops 201474048 | bytes 543232 | tf_op jit(solution)/shard_map/nky,kl->nyl/dot_general | solution.py:294
  3.3 3.6 %shard_map.121 = (f32[139,1024]{1,0:T(8,128)}, f32[139,1024]{1,0:T(8,128)}, f32[32,4992]{1,0:T(8,128)}, f32[32,4992]{1,0:T(8,128)}, f32[139,512]{1,0:T(8,128)}, ...) custom-call(f32[1,5,32,1024]{3,2,1,0:T(8,128)} %refs_3_.3, f32[1,5,32,1024]{3,2,1,0:T(8,128)} %refs_4_.1, ...), custom_call_target="tpu_custom_call" | custom-call | tf_op jit(solution)/shard_map/pallas_call | solution.py:302
  6.9 6.0 %collective-permute-start.4 = (f32[139,512]{1,0:T(8,128)}, f32[139,512]{1,0:T(8,128)S(1)}, u32[]{:S(2)}, u32[]{:S(2)}) collective-permute-start(f32[139,512]{1,0:T(8,128)} %get-tuple-element.18), channel_id=1, source_target_pairs={{0,3},{2,5},{4,7},{8,11},{10,13},{12,15},{16,19},{18,21},{20,23},{... | collective-permute-start | bytes 854024 | tf_op jit(solution)/shard_map/ppermute | solution.py:99
  12.9 0.7 collective-permute-start.5
  13.6 6.2 %collective-permute-start.2 = (f32[32,4992]{1,0:T(8,128)}, f32[32,4992]{1,0:T(8,128)S(1)}, u32[]{:S(2)}, u32[]{:S(2)}) collective-permute-start(f32[32,4992]{1,0:T(8,128)} %get-tuple-element.16), channel_id=1, source_target_pairs={{0,1},{2,3},{4,5},{6,7},{8,9},{10,11},{12,13},{14,15},{16,17},{18,... | collective-permute-start | bytes 1916936 | tf_op jit(solution)/shard_map/ppermute | solution.py:99
  19.8 1.3 %collective-permute-start.3 = (f32[32,4992]{1,0:T(8,128)}, f32[32,4992]{1,0:T(8,128)S(1)}, u32[]{:S(2)}, u32[]{:S(2)}) collective-permute-start(f32[32,4992]{1,0:T(8,128)} %get-tuple-element.17), channel_id=1, source_target_pairs={{1,0},{3,2},{5,4},{7,6},{9,8},{11,10},{13,12},{15,14},{17,16},{19,... | collective-permute-start | bytes 1916936 | tf_op jit(solution)/shard_map/ppermute | solution.py:99
  21.1 1.4 %collective-permute-start.6 = (f32[139,512]{1,0:T(8,128)}, f32[139,512]{1,0:T(8,128)}, u32[]{:S(2)}, u32[]{:S(2)}) collective-permute-start(f32[139,512]{1,0:T(8,128)} %get-tuple-element.20), channel_id=1, source_target_pairs={{2,1},{4,3},{6,5},{10,9},{12,11},{14,13},{18,17},{20,19},{22,21},{... | collective-permute-start | bytes 854024 | tf_op jit(solution)/shard_map/ppermute | solution.py:99
  22.5 0.7 copy-done.5
  23.2 8.1 %collective-permute-start = (f32[139,1024]{1,0:T(8,128)}, f32[139,1024]{1,0:T(8,128)}, u32[]{:S(2)}, u32[]{:S(2)}) collective-permute-start(f32[139,1024]{1,0:T(8,128)} %get-tuple-element.14), channel_id=1, source_target_pairs={{0,2},{1,3},{2,4},{3,5},{4,6},{5,7},{8,10},{9,11},{10,12},{11,13},... | collective-permute-start | bytes 1708040 | tf_op jit(solution)/shard_map/ppermute | solution.py:99
  31.3 0.7 copy-done.7
  32.1 1.3 %collective-permute-start.1 = (f32[139,1024]{1,0:T(8,128)}, f32[139,1024]{1,0:T(8,128)}, u32[]{:S(2)}, u32[]{:S(2)}) collective-permute-start(f32[139,1024]{1,0:T(8,128)} %get-tuple-element.15), channel_id=1, source_target_pairs={{2,0},{3,1},{4,2},{5,3},{6,4},{7,5},{10,8},{11,9},{12,10},{13,11},... | collective-permute-start | bytes 1708040 | tf_op jit(solution)/shard_map/ppermute | solution.py:99
  34.7 0.1 pad_add_fusion.1.refs_1_
  34.8 1.3 %collective-permute-start.7 = (f32[139,512]{1,0:T(8,128)}, f32[139,512]{1,0:T(8,128)S(1)}, u32[]{:S(2)}, u32[]{:S(2)}) collective-permute-start(f32[139,512]{1,0:T(8,128)} %get-tuple-element.21), channel_id=1, source_target_pairs={{3,0},{5,2},{7,4},{11,8},{13,10},{15,12},{19,16},{21,18},{23,20},{... | collective-permute-start | bytes 854024 | tf_op jit(solution)/shard_map/ppermute | solution.py:99
  36.1 0.1 pad_add_fusion.refs_0_
  36.2 0.6 copy-done.11
  36.8 15.6 %collective-permute-done.7.refs_15_ = f32[139,512]{1,0:T(8,128)S(1)} collective-permute-done((f32[139,512]{1,0:T(8,128)}, f32[139,512]{1,0:T(8,128)S(1)}, u32[]{:S(2)}, u32[]{:S(2)}) %collective-permute-start.7) | collective-permute-done | bytes 284704 | tf_op jit(solution)/shard_map/ppermute | solution.py:99
  52.5 1.0 %copy-done.6 = f32[139,512]{1,0:T(8,128)S(1)} copy-done((f32[139,512]{1,0:T(8,128)S(1)}, f32[139,512]{1,0:T(8,128)}, u32[]{:S(2)}) %copy-start.6) | copy-done | bytes 284696
  53.4 1.0 %copy-done.8 = f32[139,512]{1,0:T(8,128)S(1)} copy-done((f32[139,512]{1,0:T(8,128)S(1)}, f32[139,512]{1,0:T(8,128)}, u32[]{:S(2)}) %copy-start.8) | copy-done | bytes 284696
  54.4 11.8 %shard_map.122 = (f32[1,5,32,1024]{3,2,1,0:T(8,128)}, f32[1,5,32,1024]{3,2,1,0:T(8,128)}, f32[2,4,1024]{2,1,0:T(4,128)S(1)}) custom-call(s32[4]{0:T(128)S(1)} %pad_add_fusion.refs_0_, s32[2]{0:T(128)S(1)} %pad_add_fusion.1.refs_1_, f32[3]{0:T(128)S(1)} %bitcast.51, f32[1,5,32,1024]{3,2,1,0:T(8,128)S(1)} %copy-done.1, f32[1,5,32,1024]{3,2,1,0:T(8,128)S(1)} %copy-done.2, ...), custom_call_target="tpu_custom_call" | custom-call | tf_op jit(solution)/shard_map/pallas_call | solution.py:318
  66.2 0.6 reshape.123
  66.9 0.2 reduce_sum.9
  67.1 0.2 copy.18
  67.3 0.8 %scatter_custom_fusion = f32[64,2]{1,0:T(8,128)S(1)} fusion(s32[64]{0:T(128)S(1)} %fusion.12, f32[64,2]{1,0:T(8,128)S(1)} %bitcast.54, f32[]{:T(128)} %constant.111.clone.1), kind=kCustom, calls=%fused_computation.9 | custom fusion | bytes 516 | tf_op jit(solution)/shard_map/scatter | solution.py:340
  68.1 0.1 copy.20
  68.2 1.5 %collective-permute-start.8 = (f32[2,16,2]{1,0,2:T(2,128)S(1)}, f32[2,16,2]{1,0,2:T(2,128)S(1)}, u32[]{:S(2)}, u32[]{:S(2)}) collective-permute-start(f32[2,16,2]{1,0,2:T(2,128)S(1)} %copy.20), channel_id=1, source_target_pairs={{0,16},{8,24},{16,0},{24,8},{1,17},{9,25},{17,1},{25,9},{2,18},{10... | collective-permute-start | bytes 776 | tf_op jit(solution)/shard_map/ppermute | solution.py:350
  69.7 0.1 copy.19
  69.7 2.0 %collective-permute-done.8 = f32[2,16,2]{1,0,2:T(2,128)S(1)} collective-permute-done((f32[2,16,2]{1,0,2:T(2,128)S(1)}, f32[2,16,2]{1,0,2:T(2,128)S(1)}, u32[]{:S(2)}, u32[]{:S(2)}) %collective-permute-start.8) | collective-permute-done | bytes 288 | tf_op jit(solution)/shard_map/ppermute | solution.py:350
  71.8 0.1 collective-permute-start.9
  71.8 1.1 %collective-permute-done.9 = f32[1,16,2]{1,0,2:T(1,128)S(1)} collective-permute-done((f32[1,16,2]{1,0,2:T(1,128)S(1)}, f32[1,16,2]{1,0,2:T(1,128)S(1)}, u32[]{:S(2)}, u32[]{:S(2)}) %collective-permute-start.9) | collective-permute-done | bytes 160 | tf_op jit(solution)/shard_map/ppermute | solution.py:350
  73.0 0.6 fusion.11
  (33 shorter events, 0.1 us)
Async XLA Ops:
  1.3 0.7 copy-start.10
  3.3 49.1 %copy-start = (f32[4,32,1024]{2,1,0:T(8,128)S(1)}, f32[4,32,1024]{2,1,0:T(8,128)}, u32[]{:S(2)}) copy-start(f32[4,32,1024]{2,1,0:T(8,128)} %fusion.1.refs_4_.refs_7_) | copy-start | bytes 1572868
  3.3 49.1 %copy-start.1 = (f32[1,5,32,1024]{3,2,1,0:T(8,128)S(1)}, f32[1,5,32,1024]{3,2,1,0:T(8,128)}, u32[]{:S(2)}) copy-start(f32[1,5,32,1024]{3,2,1,0:T(8,128)} %refs_3_.3) | copy-start | bytes 1966084
  3.3 49.1 %copy-start.2 = (f32[1,5,32,1024]{3,2,1,0:T(8,128)S(1)}, f32[1,5,32,1024]{3,2,1,0:T(8,128)}, u32[]{:S(2)}) copy-start(f32[1,5,32,1024]{3,2,1,0:T(8,128)} %refs_4_.1) | copy-start | bytes 1966084
  3.3 49.2 %copy-start.4 = (f32[32,1024]{1,0:T(8,128)S(1)}, f32[32,1024]{1,0:T(8,128)}, u32[]{:S(2)}) copy-start(f32[32,1024]{1,0:T(8,128)} %refs_6_.1) | copy-start | bytes 393220
  6.9 45.6 %copy-start.3 = (f32[32,1024]{1,0:T(8,128)S(1)}, f32[32,1024]{1,0:T(8,128)}, u32[]{:S(2)}) copy-start(f32[32,1024]{1,0:T(8,128)} %refs_5_.1) | copy-start | bytes 393220
  6.9 15.6 %collective-permute-start.4 = (f32[139,512]{1,0:T(8,128)}, f32[139,512]{1,0:T(8,128)S(1)}, u32[]{:S(2)}, u32[]{:S(2)}) collective-permute-start(f32[139,512]{1,0:T(8,128)} %get-tuple-element.18), channel_id=1, source_target_pairs={{0,3},{2,5},{4,7},{8,11},{10,13},{12,15},{16,19},{18,21},{20,23},{... | collective-permute-start | bytes 854024 | tf_op jit(solution)/shard_map/ppermute | solution.py:99
  12.9 18.4 %collective-permute-start.5 = (f32[139,512]{1,0:T(8,128)}, f32[139,512]{1,0:T(8,128)S(1)}, u32[]{:S(2)}, u32[]{:S(2)}) collective-permute-start(f32[139,512]{1,0:T(8,128)} %get-tuple-element.19), channel_id=1, source_target_pairs={{1,2},{3,4},{5,6},{9,10},{11,12},{13,14},{17,18},{19,20},{21,22},{... | collective-permute-start | bytes 854024 | tf_op jit(solution)/shard_map/ppermute | solution.py:99
  13.6 38.8 %collective-permute-start.2 = (f32[32,4992]{1,0:T(8,128)}, f32[32,4992]{1,0:T(8,128)S(1)}, u32[]{:S(2)}, u32[]{:S(2)}) collective-permute-start(f32[32,4992]{1,0:T(8,128)} %get-tuple-element.16), channel_id=1, source_target_pairs={{0,1},{2,3},{4,5},{6,7},{8,9},{10,11},{12,13},{14,15},{16,17},{18,... | collective-permute-start | bytes 1916936 | tf_op jit(solution)/shard_map/ppermute | solution.py:99
  19.8 32.6 %collective-permute-start.3 = (f32[32,4992]{1,0:T(8,128)}, f32[32,4992]{1,0:T(8,128)S(1)}, u32[]{:S(2)}, u32[]{:S(2)}) collective-permute-start(f32[32,4992]{1,0:T(8,128)} %get-tuple-element.17), channel_id=1, source_target_pairs={{1,0},{3,2},{5,4},{7,6},{9,8},{11,10},{13,12},{15,14},{17,16},{19,... | collective-permute-start | bytes 1916936 | tf_op jit(solution)/shard_map/ppermute | solution.py:99
  21.1 13.7 %collective-permute-start.6 = (f32[139,512]{1,0:T(8,128)}, f32[139,512]{1,0:T(8,128)}, u32[]{:S(2)}, u32[]{:S(2)}) collective-permute-start(f32[139,512]{1,0:T(8,128)} %get-tuple-element.20), channel_id=1, source_target_pairs={{2,1},{4,3},{6,5},{10,9},{12,11},{14,13},{18,17},{20,19},{22,21},{... | collective-permute-start | bytes 854024 | tf_op jit(solution)/shard_map/ppermute | solution.py:99
  22.5 0.7 copy-start.5
  23.2 29.1 %collective-permute-start = (f32[139,1024]{1,0:T(8,128)}, f32[139,1024]{1,0:T(8,128)}, u32[]{:S(2)}, u32[]{:S(2)}) collective-permute-start(f32[139,1024]{1,0:T(8,128)} %get-tuple-element.14), channel_id=1, source_target_pairs={{0,2},{1,3},{2,4},{3,5},{4,6},{5,7},{8,10},{9,11},{10,12},{11,13},... | collective-permute-start | bytes 1708040 | tf_op jit(solution)/shard_map/ppermute | solution.py:99
  31.3 0.7 copy-start.7
  32.1 20.3 %collective-permute-start.1 = (f32[139,1024]{1,0:T(8,128)}, f32[139,1024]{1,0:T(8,128)}, u32[]{:S(2)}, u32[]{:S(2)}) collective-permute-start(f32[139,1024]{1,0:T(8,128)} %get-tuple-element.15), channel_id=1, source_target_pairs={{2,0},{3,1},{4,2},{5,3},{6,4},{7,5},{10,8},{11,9},{12,10},{13,11},... | collective-permute-start | bytes 1708040 | tf_op jit(solution)/shard_map/ppermute | solution.py:99
  34.8 17.6 %collective-permute-start.7 = (f32[139,512]{1,0:T(8,128)}, f32[139,512]{1,0:T(8,128)S(1)}, u32[]{:S(2)}, u32[]{:S(2)}) collective-permute-start(f32[139,512]{1,0:T(8,128)} %get-tuple-element.21), channel_id=1, source_target_pairs={{3,0},{5,2},{7,4},{11,8},{13,10},{15,12},{19,16},{21,18},{23,20},{... | collective-permute-start | bytes 854024 | tf_op jit(solution)/shard_map/ppermute | solution.py:99
  36.1 0.7 copy-start.11
  36.7 15.7 %copy-start.9 = (f32[1,3]{1,0:T(1,128)S(1)}, f32[1,3]{1,0:T(1,128)}, u32[]{:S(2)}) copy-start(f32[1,3]{1,0:T(1,128)} %param.14) | copy-start | bytes 40
  52.5 1.0 %copy-start.6 = (f32[139,512]{1,0:T(8,128)S(1)}, f32[139,512]{1,0:T(8,128)}, u32[]{:S(2)}) copy-start(f32[139,512]{1,0:T(8,128)} %copy-done.5) | copy-start | bytes 854020
  53.4 1.0 %copy-start.8 = (f32[139,512]{1,0:T(8,128)S(1)}, f32[139,512]{1,0:T(8,128)}, u32[]{:S(2)}) copy-start(f32[139,512]{1,0:T(8,128)} %copy-done.7) | copy-start | bytes 854020
  68.2 3.6 %collective-permute-start.8 = (f32[2,16,2]{1,0,2:T(2,128)S(1)}, f32[2,16,2]{1,0,2:T(2,128)S(1)}, u32[]{:S(2)}, u32[]{:S(2)}) collective-permute-start(f32[2,16,2]{1,0,2:T(2,128)S(1)} %copy.20), channel_id=1, source_target_pairs={{0,16},{8,24},{16,0},{24,8},{1,17},{9,25},{17,1},{25,9},{2,18},{10... | collective-permute-start | bytes 776 | tf_op jit(solution)/shard_map/ppermute | solution.py:350
  71.8 1.2 %collective-permute-start.9 = (f32[1,16,2]{1,0,2:T(1,128)S(1)}, f32[1,16,2]{1,0,2:T(1,128)S(1)}, u32[]{:S(2)}, u32[]{:S(2)}) collective-permute-start(f32[1,16,2]{1,0,2:T(1,128)S(1)} %broadcast_select_fusion), channel_id=1, source_target_pairs={{0,8},{8,0},{16,24},{24,16},{1,9},{9,1},{17,25},{25,17},{2,10},{10... | collective-permute-start | bytes 392 | tf_op jit(solution)/shard_map/ppermute | solution.py:350

commit v13 on v12

--- a/solution.py
+++ b/solution.py
@@ -288,8 +288,8 @@
     source = jnp.stack([src_row, src_lane]).astype(jnp.int32)
 
     recs = receiver_cells[0, 0]
-    at_row = (recs // lanes)[:, None] == lax.broadcasted_iota(jnp.int32, (recs.shape[0], ny), 1)
-    at_lane = (recs % lanes)[:, None] == lax.broadcasted_iota(jnp.int32, (recs.shape[0], lanes), 1)
+    at_row = lax.div(recs, lanes)[:, None] == lax.broadcasted_iota(jnp.int32, (recs.shape[0], ny), 1)
+    at_lane = lax.rem(recs, lanes)[:, None] == lax.broadcasted_iota(jnp.int32, (recs.shape[0], lanes), 1)
     weights = jnp.concatenate([jnp.ones((1, recs.shape[0]), jnp.float32), observed[0, :, 0]], axis=0)
     gauge = jnp.einsum(
         "nky,kl->nyl",

time: 73.9 us -> 73.9 us (level)
  no operation moved by 1% of the time
where the time goes in v13:
time: 73.9 us; the launch traced here: 73.5 us
  starting transfers between devices  27.8 us (38%)
  waiting for transfers between devices  18.8 us (25%)
  Pallas kernels  15.4 us (21%)
  local copies, waits for them, and re-layouts  6.4 us (9%)
  between operations  2.18 us (3%)
  other arithmetic  1.62 us (2%)
  matrix products  1.28 us (2%)
    ppermute x8, starting transfers between devices, move(): return lax.ppermute(piece, ('gy', 'gx'), pairs)  26.3 us
    ppermute x8, waiting for transfers between devices, move(): return lax.ppermute(piece, ('gy', 'gx'), pairs)  15.6 us
    pallas_call x1, Pallas kernels, on_device(): pl.pallas_call(lambda *refs: window_kernel(frame, packing, *refs), out_sh...  11.8 us
    unnamed x25, local copies, waits for them, and re-layouts  4.62 us
    pallas_call x1, Pallas kernels, on_device(): pl.pallas_call(lambda *refs: pack_kernel(frame, packing, *refs), out_shap...  3.6 us
    ppermute x2, waiting for transfers between devices, on_device(): lax.ppermute(other, 'shot', [(i, i ^ span) for i in range(shots)])  3.13 us
    ppermute x2, starting transfers between devices, on_device(): lax.ppermute(other, 'shot', [(i, i ^ span) for i in range(shots)])  1.56 us
  transfers between devices with their start and end apart: 10, of which 3 were waited for; matrix products, arithmetic and copies ran while one was open for 0% of the time, Pallas kernels for 0%

profile of v13, /device:TPU:0, one launch (start us, length us, event | category | flops | bytes accessed | tf_op | source)
XLA Modules:
  0.0 73.5 jit_solution(8456263592674082698)
XLA Ops:
  0.6 0.7 compare_select_fusion.2
  1.3 0.7 copy-done.10
  2.0 1.3 %fusion.1.refs_4_.refs_7_ = f32[4,32,1024]{2,1,0:T(8,128)} fusion(s32[128]{0:T(128)S(1)} %get-tuple-element.34, f32[128,32]{0,1:T(8,128)S(1)} %fusion.9, f32[4,128]{1,0:T(4,128)S(1)} %concatenate.3), kind=kOutput, calls=%fused_computation.3 | convolution fusion | flops 201474048 | bytes 543232 | tf_op jit(solution)/shard_map/nky,kl->nyl/dot_general | solution.py:294
  3.3 3.6 %shard_map.121 = (f32[139,1024]{1,0:T(8,128)}, f32[139,1024]{1,0:T(8,128)}, f32[32,4992]{1,0:T(8,128)}, f32[32,4992]{1,0:T(8,128)}, f32[139,512]{1,0:T(8,128)}, ...) custom-call(f32[1,5,32,1024]{3,2,1,0:T(8,128)} %refs_3_.3, f32[1,5,32,1024]{3,2,1,0:T(8,128)} %refs_4_.1, ...), custom_call_target="tpu_custom_call" | custom-call | tf_op jit(solution)/shard_map/pallas_call | solution.py:302
  6.9 6.0 %collective-permute-start.4 = (f32[139,512]{1,0:T(8,128)}, f32[139,512]{1,0:T(8,128)S(1)}, u32[]{:S(2)}, u32[]{:S(2)}) collective-permute-start(f32[139,512]{1,0:T(8,128)} %get-tuple-element.18), channel_id=1, source_target_pairs={{0,3},{2,5},{4,7},{8,11},{10,13},{12,15},{16,19},{18,21},{20,23},{... | collective-permute-start | bytes 854024 | tf_op jit(solution)/shard_map/ppermute | solution.py:99
  12.9 0.7 collective-permute-start.5
  13.6 6.2 %collective-permute-start.2 = (f32[32,4992]{1,0:T(8,128)}, f32[32,4992]{1,0:T(8,128)S(1)}, u32[]{:S(2)}, u32[]{:S(2)}) collective-permute-start(f32[32,4992]{1,0:T(8,128)} %get-tuple-element.16), channel_id=1, source_target_pairs={{0,1},{2,3},{4,5},{6,7},{8,9},{10,11},{12,13},{14,15},{16,17},{18,... | collective-permute-start | bytes 1916936 | tf_op jit(solution)/shard_map/ppermute | solution.py:99
  19.8 1.3 %collective-permute-start.3 = (f32[32,4992]{1,0:T(8,128)}, f32[32,4992]{1,0:T(8,128)S(1)}, u32[]{:S(2)}, u32[]{:S(2)}) collective-permute-start(f32[32,4992]{1,0:T(8,128)} %get-tuple-element.17), channel_id=1, source_target_pairs={{1,0},{3,2},{5,4},{7,6},{9,8},{11,10},{13,12},{15,14},{17,16},{19,... | collective-permute-start | bytes 1916936 | tf_op jit(solution)/shard_map/ppermute | solution.py:99
  21.1 1.4 %collective-permute-start.6 = (f32[139,512]{1,0:T(8,128)}, f32[139,512]{1,0:T(8,128)}, u32[]{:S(2)}, u32[]{:S(2)}) collective-permute-start(f32[139,512]{1,0:T(8,128)} %get-tuple-element.20), channel_id=1, source_target_pairs={{2,1},{4,3},{6,5},{10,9},{12,11},{14,13},{18,17},{20,19},{22,21},{... | collective-permute-start | bytes 854024 | tf_op jit(solution)/shard_map/ppermute | solution.py:99
  22.5 0.7 copy-done.5
  23.2 8.1 %collective-permute-start = (f32[139,1024]{1,0:T(8,128)}, f32[139,1024]{1,0:T(8,128)}, u32[]{:S(2)}, u32[]{:S(2)}) collective-permute-start(f32[139,1024]{1,0:T(8,128)} %get-tuple-element.14), channel_id=1, source_target_pairs={{0,2},{1,3},{2,4},{3,5},{4,6},{5,7},{8,10},{9,11},{10,12},{11,13},... | collective-permute-start | bytes 1708040 | tf_op jit(solution)/shard_map/ppermute | solution.py:99
  31.3 0.7 copy-done.7
  32.1 1.3 %collective-permute-start.1 = (f32[139,1024]{1,0:T(8,128)}, f32[139,1024]{1,0:T(8,128)}, u32[]{:S(2)}, u32[]{:S(2)}) collective-permute-start(f32[139,1024]{1,0:T(8,128)} %get-tuple-element.15), channel_id=1, source_target_pairs={{2,0},{3,1},{4,2},{5,3},{6,4},{7,5},{10,8},{11,9},{12,10},{13,11},... | collective-permute-start | bytes 1708040 | tf_op jit(solution)/shard_map/ppermute | solution.py:99
  34.7 0.1 pad_add_fusion.1.refs_1_
  34.8 1.3 %collective-permute-start.7 = (f32[139,512]{1,0:T(8,128)}, f32[139,512]{1,0:T(8,128)S(1)}, u32[]{:S(2)}, u32[]{:S(2)}) collective-permute-start(f32[139,512]{1,0:T(8,128)} %get-tuple-element.21), channel_id=1, source_target_pairs={{3,0},{5,2},{7,4},{11,8},{13,10},{15,12},{19,16},{21,18},{23,20},{... | collective-permute-start | bytes 854024 | tf_op jit(solution)/shard_map/ppermute | solution.py:99
  36.1 0.1 pad_add_fusion.refs_0_
  36.2 0.6 copy-done.11
  36.8 15.6 %collective-permute-done.7.refs_15_ = f32[139,512]{1,0:T(8,128)S(1)} collective-permute-done((f32[139,512]{1,0:T(8,128)}, f32[139,512]{1,0:T(8,128)S(1)}, u32[]{:S(2)}, u32[]{:S(2)}) %collective-permute-start.7) | collective-permute-done | bytes 284704 | tf_op jit(solution)/shard_map/ppermute | solution.py:99
  52.5 1.0 %copy-done.6 = f32[139,512]{1,0:T(8,128)S(1)} copy-done((f32[139,512]{1,0:T(8,128)S(1)}, f32[139,512]{1,0:T(8,128)}, u32[]{:S(2)}) %copy-start.6) | copy-done | bytes 284696
  53.4 1.0 %copy-done.8 = f32[139,512]{1,0:T(8,128)S(1)} copy-done((f32[139,512]{1,0:T(8,128)S(1)}, f32[139,512]{1,0:T(8,128)}, u32[]{:S(2)}) %copy-start.8) | copy-done | bytes 284696
  54.4 11.8 %shard_map.122 = (f32[1,5,32,1024]{3,2,1,0:T(8,128)}, f32[1,5,32,1024]{3,2,1,0:T(8,128)}, f32[2,4,1024]{2,1,0:T(4,128)S(1)}) custom-call(s32[4]{0:T(128)S(1)} %pad_add_fusion.refs_0_, s32[2]{0:T(128)S(1)} %pad_add_fusion.1.refs_1_, f32[3]{0:T(128)S(1)} %bitcast.44, f32[1,5,32,1024]{3,2,1,0:T(8,128)S(1)} %copy-done.1, f32[1,5,32,1024]{3,2,1,0:T(8,128)S(1)} %copy-done.2, ...), custom_call_target="tpu_custom_call" | custom-call | tf_op jit(solution)/shard_map/pallas_call | solution.py:318
  66.2 0.6 reshape.100
  66.9 0.2 reduce_sum.9
  67.1 0.2 copy.18
  67.3 0.8 %scatter_custom_fusion = f32[64,2]{1,0:T(8,128)S(1)} fusion(s32[64]{0:T(128)S(1)} %fusion.12, f32[64,2]{1,0:T(8,128)S(1)} %bitcast.47, f32[]{:T(128)} %constant.95.clone.1), kind=kCustom, calls=%fused_computation.9 | custom fusion | bytes 516 | tf_op jit(solution)/shard_map/scatter | solution.py:340
  68.1 0.1 copy.20
  68.2 1.5 %collective-permute-start.8 = (f32[2,16,2]{1,0,2:T(2,128)S(1)}, f32[2,16,2]{1,0,2:T(2,128)S(1)}, u32[]{:S(2)}, u32[]{:S(2)}) collective-permute-start(f32[2,16,2]{1,0,2:T(2,128)S(1)} %copy.20), channel_id=1, source_target_pairs={{0,16},{8,24},{16,0},{24,8},{1,17},{9,25},{17,1},{25,9},{2,18},{10... | collective-permute-start | bytes 776 | tf_op jit(solution)/shard_map/ppermute | solution.py:350
  69.7 0.1 copy.19
  69.7 2.0 %collective-permute-done.8 = f32[2,16,2]{1,0,2:T(2,128)S(1)} collective-permute-done((f32[2,16,2]{1,0,2:T(2,128)S(1)}, f32[2,16,2]{1,0,2:T(2,128)S(1)}, u32[]{:S(2)}, u32[]{:S(2)}) %collective-permute-start.8) | collective-permute-done | bytes 288 | tf_op jit(solution)/shard_map/ppermute | solution.py:350
  71.8 0.1 collective-permute-start.9
  71.8 1.1 %collective-permute-done.9 = f32[1,16,2]{1,0,2:T(1,128)S(1)} collective-permute-done((f32[1,16,2]{1,0,2:T(1,128)S(1)}, f32[1,16,2]{1,0,2:T(1,128)S(1)}, u32[]{:S(2)}, u32[]{:S(2)}) %collective-permute-start.9) | collective-permute-done | bytes 160 | tf_op jit(solution)/shard_map/ppermute | solution.py:350
  73.0 0.6 fusion.11
  (33 shorter events, 0.1 us)
Async XLA Ops:
  1.3 0.7 copy-start.10
  3.3 49.1 %copy-start = (f32[4,32,1024]{2,1,0:T(8,128)S(1)}, f32[4,32,1024]{2,1,0:T(8,128)}, u32[]{:S(2)}) copy-start(f32[4,32,1024]{2,1,0:T(8,128)} %fusion.1.refs_4_.refs_7_) | copy-start | bytes 1572868
  3.3 49.1 %copy-start.1 = (f32[1,5,32,1024]{3,2,1,0:T(8,128)S(1)}, f32[1,5,32,1024]{3,2,1,0:T(8,128)}, u32[]{:S(2)}) copy-start(f32[1,5,32,1024]{3,2,1,0:T(8,128)} %refs_3_.3) | copy-start | bytes 1966084
  3.3 49.1 %copy-start.2 = (f32[1,5,32,1024]{3,2,1,0:T(8,128)S(1)}, f32[1,5,32,1024]{3,2,1,0:T(8,128)}, u32[]{:S(2)}) copy-start(f32[1,5,32,1024]{3,2,1,0:T(8,128)} %refs_4_.1) | copy-start | bytes 1966084
  3.3 49.2 %copy-start.4 = (f32[32,1024]{1,0:T(8,128)S(1)}, f32[32,1024]{1,0:T(8,128)}, u32[]{:S(2)}) copy-start(f32[32,1024]{1,0:T(8,128)} %refs_6_.1) | copy-start | bytes 393220
  6.9 45.6 %copy-start.3 = (f32[32,1024]{1,0:T(8,128)S(1)}, f32[32,1024]{1,0:T(8,128)}, u32[]{:S(2)}) copy-start(f32[32,1024]{1,0:T(8,128)} %refs_5_.1) | copy-start | bytes 393220
  6.9 15.6 %collective-permute-start.4 = (f32[139,512]{1,0:T(8,128)}, f32[139,512]{1,0:T(8,128)S(1)}, u32[]{:S(2)}, u32[]{:S(2)}) collective-permute-start(f32[139,512]{1,0:T(8,128)} %get-tuple-element.18), channel_id=1, source_target_pairs={{0,3},{2,5},{4,7},{8,11},{10,13},{12,15},{16,19},{18,21},{20,23},{... | collective-permute-start | bytes 854024 | tf_op jit(solution)/shard_map/ppermute | solution.py:99
  12.9 18.4 %collective-permute-start.5 = (f32[139,512]{1,0:T(8,128)}, f32[139,512]{1,0:T(8,128)S(1)}, u32[]{:S(2)}, u32[]{:S(2)}) collective-permute-start(f32[139,512]{1,0:T(8,128)} %get-tuple-element.19), channel_id=1, source_target_pairs={{1,2},{3,4},{5,6},{9,10},{11,12},{13,14},{17,18},{19,20},{21,22},{... | collective-permute-start | bytes 854024 | tf_op jit(solution)/shard_map/ppermute | solution.py:99
  13.6 38.8 %collective-permute-start.2 = (f32[32,4992]{1,0:T(8,128)}, f32[32,4992]{1,0:T(8,128)S(1)}, u32[]{:S(2)}, u32[]{:S(2)}) collective-permute-start(f32[32,4992]{1,0:T(8,128)} %get-tuple-element.16), channel_id=1, source_target_pairs={{0,1},{2,3},{4,5},{6,7},{8,9},{10,11},{12,13},{14,15},{16,17},{18,... | collective-permute-start | bytes 1916936 | tf_op jit(solution)/shard_map/ppermute | solution.py:99
  19.8 32.6 %collective-permute-start.3 = (f32[32,4992]{1,0:T(8,128)}, f32[32,4992]{1,0:T(8,128)S(1)}, u32[]{:S(2)}, u32[]{:S(2)}) collective-permute-start(f32[32,4992]{1,0:T(8,128)} %get-tuple-element.17), channel_id=1, source_target_pairs={{1,0},{3,2},{5,4},{7,6},{9,8},{11,10},{13,12},{15,14},{17,16},{19,... | collective-permute-start | bytes 1916936 | tf_op jit(solution)/shard_map/ppermute | solution.py:99
  21.1 13.7 %collective-permute-start.6 = (f32[139,512]{1,0:T(8,128)}, f32[139,512]{1,0:T(8,128)}, u32[]{:S(2)}, u32[]{:S(2)}) collective-permute-start(f32[139,512]{1,0:T(8,128)} %get-tuple-element.20), channel_id=1, source_target_pairs={{2,1},{4,3},{6,5},{10,9},{12,11},{14,13},{18,17},{20,19},{22,21},{... | collective-permute-start | bytes 854024 | tf_op jit(solution)/shard_map/ppermute | solution.py:99
  22.5 0.7 copy-start.5
  23.2 29.1 %collective-permute-start = (f32[139,1024]{1,0:T(8,128)}, f32[139,1024]{1,0:T(8,128)}, u32[]{:S(2)}, u32[]{:S(2)}) collective-permute-start(f32[139,1024]{1,0:T(8,128)} %get-tuple-element.14), channel_id=1, source_target_pairs={{0,2},{1,3},{2,4},{3,5},{4,6},{5,7},{8,10},{9,11},{10,12},{11,13},... | collective-permute-start | bytes 1708040 | tf_op jit(solution)/shard_map/ppermute | solution.py:99
  31.3 0.7 copy-start.7
  32.1 20.3 %collective-permute-start.1 = (f32[139,1024]{1,0:T(8,128)}, f32[139,1024]{1,0:T(8,128)}, u32[]{:S(2)}, u32[]{:S(2)}) collective-permute-start(f32[139,1024]{1,0:T(8,128)} %get-tuple-element.15), channel_id=1, source_target_pairs={{2,0},{3,1},{4,2},{5,3},{6,4},{7,5},{10,8},{11,9},{12,10},{13,11},... | collective-permute-start | bytes 1708040 | tf_op jit(solution)/shard_map/ppermute | solution.py:99
  34.8 17.6 %collective-permute-start.7 = (f32[139,512]{1,0:T(8,128)}, f32[139,512]{1,0:T(8,128)S(1)}, u32[]{:S(2)}, u32[]{:S(2)}) collective-permute-start(f32[139,512]{1,0:T(8,128)} %get-tuple-element.21), channel_id=1, source_target_pairs={{3,0},{5,2},{7,4},{11,8},{13,10},{15,12},{19,16},{21,18},{23,20},{... | collective-permute-start | bytes 854024 | tf_op jit(solution)/shard_map/ppermute | solution.py:99
  36.1 0.7 copy-start.11
  36.7 15.7 %copy-start.9 = (f32[1,3]{1,0:T(1,128)S(1)}, f32[1,3]{1,0:T(1,128)}, u32[]{:S(2)}) copy-start(f32[1,3]{1,0:T(1,128)} %param.14) | copy-start | bytes 40
  52.5 1.0 %copy-start.6 = (f32[139,512]{1,0:T(8,128)S(1)}, f32[139,512]{1,0:T(8,128)}, u32[]{:S(2)}) copy-start(f32[139,512]{1,0:T(8,128)} %copy-done.5) | copy-start | bytes 854020
  53.4 1.0 %copy-start.8 = (f32[139,512]{1,0:T(8,128)S(1)}, f32[139,512]{1,0:T(8,128)}, u32[]{:S(2)}) copy-start(f32[139,512]{1,0:T(8,128)} %copy-done.7) | copy-start | bytes 854020
  68.2 3.6 %collective-permute-start.8 = (f32[2,16,2]{1,0,2:T(2,128)S(1)}, f32[2,16,2]{1,0,2:T(2,128)S(1)}, u32[]{:S(2)}, u32[]{:S(2)}) collective-permute-start(f32[2,16,2]{1,0,2:T(2,128)S(1)} %copy.20), channel_id=1, source_target_pairs={{0,16},{8,24},{16,0},{24,8},{1,17},{9,25},{17,1},{25,9},{2,18},{10... | collective-permute-start | bytes 776 | tf_op jit(solution)/shard_map/ppermute | solution.py:350
  71.8 1.2 %collective-permute-start.9 = (f32[1,16,2]{1,0,2:T(1,128)S(1)}, f32[1,16,2]{1,0,2:T(1,128)S(1)}, u32[]{:S(2)}, u32[]{:S(2)}) collective-permute-start(f32[1,16,2]{1,0,2:T(1,128)S(1)} %broadcast_select_fusion), channel_id=1, source_target_pairs={{0,8},{8,0},{16,24},{24,16},{1,9},{9,1},{17,25},{25,17},{2,10},{10... | collective-permute-start | bytes 392 | tf_op jit(solution)/shard_map/ppermute | solution.py:350

commit v14 on v13

--- a/solution.py
+++ b/solution.py
@@ -51,9 +51,21 @@
         self.corner = frame.ox
 
 
-def pack_kernel(frame, packing, fwd_ref, adj_ref, vel_ref, att_ref, gauge_ref, *outs):
-    up, down, east, west, up_east, up_west, down_east, down_west = outs
+def pack_kernel(frame, packing, fwd_ref, adj_ref, vel_ref, att_ref, rec_row_ref, rec_col_ref, weight_ref, *outs):
+    up, down, east, west, up_east, up_west, down_east, down_west, gauge_ref = outs
     ny, lanes, cw = frame.ny, frame.lanes, packing.corner
+    count = rec_row_ref.shape[1]
+    at_row = lax.broadcasted_iota(jnp.int32, (ny, count), 0) == lax.div(rec_row_ref[...], lanes)
+    at_lane = (
+        lax.rem(rec_col_ref[...], lanes) == lax.broadcasted_iota(jnp.int32, (count, lanes), 1)
+    ).astype(jnp.float32)
+    for n in range(1 + STEPS):
+        gauge_ref[n] = jnp.dot(
+            jnp.where(at_row, weight_ref[n : n + 1, :], 0.0),
+            at_lane,
+            precision=lax.Precision.HIGHEST,
+            preferred_element_type=jnp.float32,
+        )
 
     def field(j):
         if j < 5:
@@ -288,15 +300,7 @@
     source = jnp.stack([src_row, src_lane]).astype(jnp.int32)
 
     recs = receiver_cells[0, 0]
-    at_row = lax.div(recs, lanes)[:, None] == lax.broadcasted_iota(jnp.int32, (recs.shape[0], ny), 1)
-    at_lane = lax.rem(recs, lanes)[:, None] == lax.broadcasted_iota(jnp.int32, (recs.shape[0], lanes), 1)
     weights = jnp.concatenate([jnp.ones((1, recs.shape[0]), jnp.float32), observed[0, :, 0]], axis=0)
-    gauge = jnp.einsum(
-        "nky,kl->nyl",
-        weights[:, :, None] * at_row.astype(jnp.float32)[None],
-        at_lane.astype(jnp.float32),
-        precision=lax.Precision.HIGHEST,
-    )
 
     packing = Packing(frame)
     packed = pl.pallas_call(
@@ -307,12 +311,14 @@
                 [(packing.total_rows, lanes)] * 2
                 + [(ny, packing.total_lanes)] * 2
                 + [(packing.total_rows, packing.corner)] * 4
+                + [(1 + STEPS, ny, lanes)]
             )
         ),
-        in_specs=[vmem()] * 5,
-        out_specs=tuple([vmem()] * 8),
-    )(forward_start, adjoint_end, velocity, attenuation, gauge)
-    pieces = send_pieces(packed)
+        in_specs=[vmem()] * 7,
+        out_specs=tuple([vmem()] * 9),
+    )(forward_start, adjoint_end, velocity, attenuation, recs[None], recs[:, None], weights)
+    gauge = packed[8]
+    pieces = send_pieces(packed[:8])
 
     ext_shape = (frame.ey, frame.el)
     forward_end, adjoint_start, row_sums = pl.pallas_call(

time: 73.9 us -> 75 us (1.015)
  local copies, waits for them, and re-layouts: 6.4 us -> 9.32 us
  matrix products: 1.28 us -> 0 us
  Pallas kernels: 15.4 us -> 16.3 us
    unnamed x25 -> x27, local copies, waits for them, and re-layouts: 4.62 us -> 6.23 us
    dot_general x1 -> x0, matrix products: 1.28 us -> none  [on_device(): jnp.einsum('nky,kl->nyl', weights[:, :, None] * at_row.astype(jnp.float32...]
    pallas_call x1, Pallas kernels: 3.6 us -> 4.61 us  [on_device(): pl.pallas_call(lambda *refs: pack_kernel(frame, packing, *refs), out_shap...]
where the time goes in v14:
time: 75 us; the launch traced here: 74.6 us
  starting transfers between devices  27.2 us (36%)
  waiting for transfers between devices  18.6 us (25%)
  Pallas kernels  16.3 us (22%)
  local copies, waits for them, and re-layouts  9.32 us (12%)
  between operations  2.19 us (3%)
  other arithmetic  0.95 us (1%)
    ppermute x8, starting transfers between devices, move(): return lax.ppermute(piece, ('gy', 'gx'), pairs)  25.7 us
    ppermute x8, waiting for transfers between devices, move(): return lax.ppermute(piece, ('gy', 'gx'), pairs)  15.5 us
    pallas_call x1, Pallas kernels, on_device(): pl.pallas_call(lambda *refs: window_kernel(frame, packing, *refs), out_sh...  11.7 us
    unnamed x27, local copies, waits for them, and re-layouts  6.23 us
    pallas_call x1, Pallas kernels, on_device(): pl.pallas_call(lambda *refs: pack_kernel(frame, packing, *refs), out_shap...  4.61 us
    ppermute x2, waiting for transfers between devices, on_device(): lax.ppermute(other, 'shot', [(i, i ^ span) for i in range(shots)])  3.13 us
    ppermute x2, starting transfers between devices, on_device(): lax.ppermute(other, 'shot', [(i, i ^ span) for i in range(shots)])  1.56 us
  transfers between devices with their start and end apart: 10, of which 3 were waited for; matrix products, arithmetic and copies ran while one was open for 0% of the time, Pallas kernels for 0%

profile of v14, /device:TPU:0, one launch (start us, length us, event | category | flops | bytes accessed | tf_op | source)
XLA Modules:
  0.0 74.6 jit_solution(11601760516010390252)
XLA Ops:
  0.6 0.6 copy-done.10
  1.3 0.7 copy.15.refs_5_
  2.0 0.6 concatenate.3.refs_6_
  2.6 4.6 %shard_map.121 = (f32[139,1024]{1,0:T(8,128)}, f32[139,1024]{1,0:T(8,128)}, f32[32,4992]{1,0:T(8,128)}, f32[32,4992]{1,0:T(8,128)}, f32[139,512]{1,0:T(8,128)}, ...) custom-call(f32[1,5,32,1024]{3,2,1,0:T(8,128)} %refs_3_.3, ...), custom_call_target="tpu_custom_call" | custom-call | tf_op jit(solution)/shard_map/pallas_call | solution.py:306
  7.2 6.0 %collective-permute-start.4 = (f32[139,512]{1,0:T(8,128)}, f32[139,512]{1,0:T(8,128)S(1)}, u32[]{:S(2)}, u32[]{:S(2)}) collective-permute-start(f32[139,512]{1,0:T(8,128)} %get-tuple-element.20), channel_id=1, source_target_pairs={{0,3},{2,5},{4,7},{8,11},{10,13},{12,15},{16,19},{18,21},{20,23},{... | collective-permute-start | bytes 854024 | tf_op jit(solution)/shard_map/ppermute | solution.py:111
  13.3 0.7 collective-permute-start.5
  13.9 6.2 %collective-permute-start.2 = (f32[32,4992]{1,0:T(8,128)}, f32[32,4992]{1,0:T(8,128)S(1)}, u32[]{:S(2)}, u32[]{:S(2)}) collective-permute-start(f32[32,4992]{1,0:T(8,128)} %get-tuple-element.18), channel_id=1, source_target_pairs={{0,1},{2,3},{4,5},{6,7},{8,9},{10,11},{12,13},{14,15},{16,17},{18,... | collective-permute-start | bytes 1916936 | tf_op jit(solution)/shard_map/ppermute | solution.py:111
  20.2 1.3 %collective-permute-start.3 = (f32[32,4992]{1,0:T(8,128)}, f32[32,4992]{1,0:T(8,128)S(1)}, u32[]{:S(2)}, u32[]{:S(2)}) collective-permute-start(f32[32,4992]{1,0:T(8,128)} %get-tuple-element.19), channel_id=1, source_target_pairs={{1,0},{3,2},{5,4},{7,6},{9,8},{11,10},{13,12},{15,14},{17,16},{19,... | collective-permute-start | bytes 1916936 | tf_op jit(solution)/shard_map/ppermute | solution.py:111
  21.5 1.4 %collective-permute-start.6 = (f32[139,512]{1,0:T(8,128)}, f32[139,512]{1,0:T(8,128)}, u32[]{:S(2)}, u32[]{:S(2)}) collective-permute-start(f32[139,512]{1,0:T(8,128)} %get-tuple-element.22), channel_id=1, source_target_pairs={{2,1},{4,3},{6,5},{10,9},{12,11},{14,13},{18,17},{20,19},{22,21},{... | collective-permute-start | bytes 854024 | tf_op jit(solution)/shard_map/ppermute | solution.py:111
  22.9 0.7 copy-done.5
  23.6 7.3 %collective-permute-start = (f32[139,1024]{1,0:T(8,128)}, f32[139,1024]{1,0:T(8,128)S(1)}, u32[]{:S(2)}, u32[]{:S(2)}) collective-permute-start(f32[139,1024]{1,0:T(8,128)} %get-tuple-element.16), channel_id=1, source_target_pairs={{0,2},{1,3},{2,4},{3,5},{4,6},{5,7},{8,10},{9,11},{10,12},{11,13},... | collective-permute-start | bytes 1708040 | tf_op jit(solution)/shard_map/ppermute | solution.py:111
  30.9 0.7 copy-done.7
  31.6 1.3 %collective-permute-start.1 = (f32[139,1024]{1,0:T(8,128)}, f32[139,1024]{1,0:T(8,128)}, u32[]{:S(2)}, u32[]{:S(2)}) collective-permute-start(f32[139,1024]{1,0:T(8,128)} %get-tuple-element.17), channel_id=1, source_target_pairs={{2,0},{3,1},{4,2},{5,3},{6,4},{7,5},{10,8},{11,9},{12,10},{13,11},... | collective-permute-start | bytes 1708040 | tf_op jit(solution)/shard_map/ppermute | solution.py:111
  34.4 1.5 %collective-permute-start.7 = (f32[139,512]{1,0:T(8,128)}, f32[139,512]{1,0:T(8,128)S(1)}, u32[]{:S(2)}, u32[]{:S(2)}) collective-permute-start(f32[139,512]{1,0:T(8,128)} %get-tuple-element.23), channel_id=1, source_target_pairs={{3,0},{5,2},{7,4},{11,8},{13,10},{15,12},{19,16},{21,18},{23,20},{... | collective-permute-start | bytes 854024 | tf_op jit(solution)/shard_map/ppermute | solution.py:111
  35.8 0.1 pad_add_fusion.refs_0_
  35.9 0.6 copy-done.12
  36.5 15.4 %collective-permute-done.7.refs_15_ = f32[139,512]{1,0:T(8,128)S(1)} collective-permute-done((f32[139,512]{1,0:T(8,128)}, f32[139,512]{1,0:T(8,128)S(1)}, u32[]{:S(2)}, u32[]{:S(2)}) %collective-permute-start.7) | collective-permute-done | bytes 284704 | tf_op jit(solution)/shard_map/ppermute | solution.py:111
  52.0 0.6 copy-done.9
  52.6 1.0 %copy-done.2 = f32[4,32,1024]{2,1,0:T(8,128)S(1)} copy-done((f32[4,32,1024]{2,1,0:T(8,128)S(1)}, f32[4,32,1024]{2,1,0:T(8,128)}, u32[]{:S(2)}) %copy-start.2) | copy-done | bytes 524312
  53.7 1.0 %copy-done.6 = f32[139,512]{1,0:T(8,128)S(1)} copy-done((f32[139,512]{1,0:T(8,128)S(1)}, f32[139,512]{1,0:T(8,128)}, u32[]{:S(2)}) %copy-start.6) | copy-done | bytes 284696
  54.6 1.0 %copy-done.8 = f32[139,512]{1,0:T(8,128)S(1)} copy-done((f32[139,512]{1,0:T(8,128)S(1)}, f32[139,512]{1,0:T(8,128)}, u32[]{:S(2)}) %copy-start.8) | copy-done | bytes 284696
  55.6 11.7 %shard_map.122 = (f32[1,5,32,1024]{3,2,1,0:T(8,128)}, f32[1,5,32,1024]{3,2,1,0:T(8,128)}, f32[2,4,1024]{2,1,0:T(4,128)S(1)}) custom-call(s32[4]{0:T(128)S(1)} %pad_add_fusion.refs_0_, s32[2]{0:T(128)S(1)} %pad_add_fusion.1.refs_1_, f32[3]{0:T(128)S(1)} %bitcast.35, f32[1,5,32,1024]{3,2,1,0:T(8,128)S(1)} %copy-done, f32[1,5,32,1024]{3,2,1,0:T(8,128)S(1)} %copy-done.1, ...), custom_call_target="tpu_custom_call" | custom-call | tf_op jit(solution)/shard_map/pallas_call | solution.py:324
  67.3 0.6 reshape.56
  67.9 0.2 reduce_sum.9
  68.1 0.2 copy.20
  68.3 0.8 %scatter_custom_fusion = f32[64,2]{1,0:T(8,128)S(1)} fusion(s32[64]{0:T(128)S(1)} %fusion.4, f32[64,2]{1,0:T(8,128)S(1)} %bitcast.38, f32[]{:T(128)} %constant.88.clone.1), kind=kCustom, calls=%fused_computation.2 | custom fusion | bytes 516 | tf_op jit(solution)/shard_map/scatter | solution.py:346
  69.1 0.1 copy.22
  69.2 1.5 %collective-permute-start.8 = (f32[2,16,2]{1,0,2:T(2,128)S(1)}, f32[2,16,2]{1,0,2:T(2,128)S(1)}, u32[]{:S(2)}, u32[]{:S(2)}) collective-permute-start(f32[2,16,2]{1,0,2:T(2,128)S(1)} %copy.22), channel_id=1, source_target_pairs={{0,16},{8,24},{16,0},{24,8},{1,17},{9,25},{17,1},{25,9},{2,18},{10... | collective-permute-start | bytes 776 | tf_op jit(solution)/shard_map/ppermute | solution.py:356
  70.7 0.1 copy.21
  70.8 2.0 %collective-permute-done.8 = f32[2,16,2]{1,0,2:T(2,128)S(1)} collective-permute-done((f32[2,16,2]{1,0,2:T(2,128)S(1)}, f32[2,16,2]{1,0,2:T(2,128)S(1)}, u32[]{:S(2)}, u32[]{:S(2)}) %collective-permute-start.8) | collective-permute-done | bytes 288 | tf_op jit(solution)/shard_map/ppermute | solution.py:356
  72.9 1.1 %collective-permute-done.9 = f32[1,16,2]{1,0,2:T(1,128)S(1)} collective-permute-done((f32[1,16,2]{1,0,2:T(1,128)S(1)}, f32[1,16,2]{1,0,2:T(1,128)S(1)}, u32[]{:S(2)}, u32[]{:S(2)}) %collective-permute-start.9) | collective-permute-done | bytes 160 | tf_op jit(solution)/shard_map/ppermute | solution.py:356
  74.0 0.6 fusion.3
  (33 shorter events, 0.2 us)
Async XLA Ops:
  0.6 0.7 copy-start.10
  1.3 0.7 copy-start.11
  2.6 49.4 %copy-start = (f32[1,5,32,1024]{3,2,1,0:T(8,128)S(1)}, f32[1,5,32,1024]{3,2,1,0:T(8,128)}, u32[]{:S(2)}) copy-start(f32[1,5,32,1024]{3,2,1,0:T(8,128)} %refs_3_.3) | copy-start | bytes 1966084
  2.6 49.4 %copy-start.1 = (f32[1,5,32,1024]{3,2,1,0:T(8,128)S(1)}, f32[1,5,32,1024]{3,2,1,0:T(8,128)}, u32[]{:S(2)}) copy-start(f32[1,5,32,1024]{3,2,1,0:T(8,128)} %refs_4_.1) | copy-start | bytes 1966084
  2.6 49.4 %copy-start.4 = (f32[32,1024]{1,0:T(8,128)S(1)}, f32[32,1024]{1,0:T(8,128)}, u32[]{:S(2)}) copy-start(f32[32,1024]{1,0:T(8,128)} %refs_6_.1) | copy-start | bytes 393220
  7.2 44.8 %copy-start.3 = (f32[32,1024]{1,0:T(8,128)S(1)}, f32[32,1024]{1,0:T(8,128)}, u32[]{:S(2)}) copy-start(f32[32,1024]{1,0:T(8,128)} %refs_5_.1) | copy-start | bytes 393220
  7.2 15.6 %collective-permute-start.4 = (f32[139,512]{1,0:T(8,128)}, f32[139,512]{1,0:T(8,128)S(1)}, u32[]{:S(2)}, u32[]{:S(2)}) collective-permute-start(f32[139,512]{1,0:T(8,128)} %get-tuple-element.20), channel_id=1, source_target_pairs={{0,3},{2,5},{4,7},{8,11},{10,13},{12,15},{16,19},{18,21},{20,23},{... | collective-permute-start | bytes 854024 | tf_op jit(solution)/shard_map/ppermute | solution.py:111
  13.3 17.6 %collective-permute-start.5 = (f32[139,512]{1,0:T(8,128)}, f32[139,512]{1,0:T(8,128)S(1)}, u32[]{:S(2)}, u32[]{:S(2)}) collective-permute-start(f32[139,512]{1,0:T(8,128)} %get-tuple-element.21), channel_id=1, source_target_pairs={{1,2},{3,4},{5,6},{9,10},{11,12},{13,14},{17,18},{19,20},{21,22},{... | collective-permute-start | bytes 854024 | tf_op jit(solution)/shard_map/ppermute | solution.py:111
  13.9 38.0 %collective-permute-start.2 = (f32[32,4992]{1,0:T(8,128)}, f32[32,4992]{1,0:T(8,128)S(1)}, u32[]{:S(2)}, u32[]{:S(2)}) collective-permute-start(f32[32,4992]{1,0:T(8,128)} %get-tuple-element.18), channel_id=1, source_target_pairs={{0,1},{2,3},{4,5},{6,7},{8,9},{10,11},{12,13},{14,15},{16,17},{18,... | collective-permute-start | bytes 1916936 | tf_op jit(solution)/shard_map/ppermute | solution.py:111
  20.2 31.8 %collective-permute-start.3 = (f32[32,4992]{1,0:T(8,128)}, f32[32,4992]{1,0:T(8,128)S(1)}, u32[]{:S(2)}, u32[]{:S(2)}) collective-permute-start(f32[32,4992]{1,0:T(8,128)} %get-tuple-element.19), channel_id=1, source_target_pairs={{1,0},{3,2},{5,4},{7,6},{9,8},{11,10},{13,12},{15,14},{17,16},{19,... | collective-permute-start | bytes 1916936 | tf_op jit(solution)/shard_map/ppermute | solution.py:111
  21.5 12.9 %collective-permute-start.6 = (f32[139,512]{1,0:T(8,128)}, f32[139,512]{1,0:T(8,128)}, u32[]{:S(2)}, u32[]{:S(2)}) collective-permute-start(f32[139,512]{1,0:T(8,128)} %get-tuple-element.22), channel_id=1, source_target_pairs={{2,1},{4,3},{6,5},{10,9},{12,11},{14,13},{18,17},{20,19},{22,21},{... | collective-permute-start | bytes 854024 | tf_op jit(solution)/shard_map/ppermute | solution.py:111
  22.9 0.7 copy-start.5
  23.6 28.4 %collective-permute-start = (f32[139,1024]{1,0:T(8,128)}, f32[139,1024]{1,0:T(8,128)S(1)}, u32[]{:S(2)}, u32[]{:S(2)}) collective-permute-start(f32[139,1024]{1,0:T(8,128)} %get-tuple-element.16), channel_id=1, source_target_pairs={{0,2},{1,3},{2,4},{3,5},{4,6},{5,7},{8,10},{9,11},{10,12},{11,13},... | collective-permute-start | bytes 1708040 | tf_op jit(solution)/shard_map/ppermute | solution.py:111
  30.9 0.7 copy-start.7
  31.6 20.3 %collective-permute-start.1 = (f32[139,1024]{1,0:T(8,128)}, f32[139,1024]{1,0:T(8,128)}, u32[]{:S(2)}, u32[]{:S(2)}) collective-permute-start(f32[139,1024]{1,0:T(8,128)} %get-tuple-element.17), channel_id=1, source_target_pairs={{2,0},{3,1},{4,2},{5,3},{6,4},{7,5},{10,8},{11,9},{12,10},{13,11},... | collective-permute-start | bytes 1708040 | tf_op jit(solution)/shard_map/ppermute | solution.py:111
  34.4 17.6 %collective-permute-start.7 = (f32[139,512]{1,0:T(8,128)}, f32[139,512]{1,0:T(8,128)S(1)}, u32[]{:S(2)}, u32[]{:S(2)}) collective-permute-start(f32[139,512]{1,0:T(8,128)} %get-tuple-element.23), channel_id=1, source_target_pairs={{3,0},{5,2},{7,4},{11,8},{13,10},{15,12},{19,16},{21,18},{23,20},{... | collective-permute-start | bytes 854024 | tf_op jit(solution)/shard_map/ppermute | solution.py:111
  35.8 0.7 copy-start.12
  52.0 0.7 copy-start.9
  52.6 1.0 %copy-start.2 = (f32[4,32,1024]{2,1,0:T(8,128)S(1)}, f32[4,32,1024]{2,1,0:T(8,128)}, u32[]{:S(2)}) copy-start(f32[4,32,1024]{2,1,0:T(8,128)} %get-tuple-element.15.refs_7_) | copy-start | bytes 1572868
  53.7 1.0 %copy-start.6 = (f32[139,512]{1,0:T(8,128)S(1)}, f32[139,512]{1,0:T(8,128)}, u32[]{:S(2)}) copy-start(f32[139,512]{1,0:T(8,128)} %copy-done.5) | copy-start | bytes 854020
  54.6 1.0 %copy-start.8 = (f32[139,512]{1,0:T(8,128)S(1)}, f32[139,512]{1,0:T(8,128)}, u32[]{:S(2)}) copy-start(f32[139,512]{1,0:T(8,128)} %copy-done.7) | copy-start | bytes 854020
  69.2 3.6 %collective-permute-start.8 = (f32[2,16,2]{1,0,2:T(2,128)S(1)}, f32[2,16,2]{1,0,2:T(2,128)S(1)}, u32[]{:S(2)}, u32[]{:S(2)}) collective-permute-start(f32[2,16,2]{1,0,2:T(2,128)S(1)} %copy.22), channel_id=1, source_target_pairs={{0,16},{8,24},{16,0},{24,8},{1,17},{9,25},{17,1},{25,9},{2,18},{10... | collective-permute-start | bytes 776 | tf_op jit(solution)/shard_map/ppermute | solution.py:356
  72.8 1.2 %collective-permute-start.9 = (f32[1,16,2]{1,0,2:T(1,128)S(1)}, f32[1,16,2]{1,0,2:T(1,128)S(1)}, u32[]{:S(2)}, u32[]{:S(2)}) collective-permute-start(f32[1,16,2]{1,0,2:T(1,128)S(1)} %broadcast_select_fusion), channel_id=1, source_target_pairs={{0,8},{8,0},{16,24},{24,16},{1,9},{9,1},{17,25},{25,17},{2,10},{10... | collective-permute-start | bytes 392 | tf_op jit(solution)/shard_map/ppermute | solution.py:356

commit v15 on v12

--- a/solution.py
+++ b/solution.py
@@ -49,6 +49,23 @@
         self.total_rows = sum(self.rows)
         self.total_lanes = sum(self.lanes)
         self.corner = frame.ox
+        shelves = []
+        self.corner_at = [(0, 0)] * len(NEEDS)
+        order = sorted(range(len(NEEDS)), key=lambda j: (-self.lanes[j], -self.rows[j]))
+        for j in order:
+            h, w = self.rows[j], self.lanes[j]
+            if h == 0:
+                continue
+            for shelf in shelves:
+                if shelf[2] + w <= self.corner and shelf[1] >= h:
+                    self.corner_at[j] = (shelf[0], shelf[2])
+                    shelf[2] += w
+                    break
+            else:
+                top = sum(shelf[1] for shelf in shelves)
+                shelves.append([top, h, w])
+                self.corner_at[j] = (top, 0)
+        self.corner_rows = sum(shelf[1] for shelf in shelves)
 
 
 def pack_kernel(frame, packing, fwd_ref, adj_ref, vel_ref, att_ref, gauge_ref, *outs):
@@ -79,10 +96,13 @@
         down[r, :] = src[bottom, :]
         east[:, c] = src[:, lanes - w : lanes]
         west[:, c] = src[:, 0:w]
-        up_east[r, :] = src[top, lanes - cw : lanes]
-        up_west[r, :] = src[top, 0:cw]
-        down_east[r, :] = src[bottom, lanes - cw : lanes]
-        down_west[r, :] = src[bottom, 0:cw]
+        cr, cl = packing.corner_at[j]
+        cr = slice(cr, cr + h)
+        cl = slice(cl, cl + w)
+        up_east[cr, cl] = src[top, lanes - w : lanes]
+        up_west[cr, cl] = src[top, 0:w]
+        down_east[cr, cl] = src[bottom, lanes - w : lanes]
+        down_west[cr, cl] = src[bottom, 0:w]
 
 
 def send_pieces(packed):
@@ -121,10 +141,13 @@
     dst[hi, centre] = above[r, :]
     dst[mid, west] = left[:, c]
     dst[mid, east] = right[:, c]
-    dst[lo, west] = b_l[r, cw - w : cw]
-    dst[lo, east] = b_r[r, 0:w]
-    dst[hi, west] = a_l[r, cw - w : cw]
-    dst[hi, east] = a_r[r, 0:w]
+    cr, cl = packing.corner_at[j]
+    cr = slice(cr, cr + h)
+    cl = slice(cl, cl + w)
+    dst[lo, west] = b_l[cr, cl]
+    dst[lo, east] = b_r[cr, cl]
+    dst[hi, west] = a_l[cr, cl]
+    dst[hi, east] = a_r[cr, cl]
 
 
 def window(frame, depth):
@@ -306,7 +329,7 @@
             for shape in (
                 [(packing.total_rows, lanes)] * 2
                 + [(ny, packing.total_lanes)] * 2
-                + [(packing.total_rows, packing.corner)] * 4
+                + [(packing.corner_rows, packing.corner)] * 4
             )
         ),
         in_specs=[vmem()] * 5,

time: 73.9 us -> 72.9 us (0.986)
  waiting for transfers between devices: 18.8 us -> 17.8 us
    ppermute x8, waiting for transfers between devices: 15.6 us -> 14.7 us  [move(): return lax.ppermute(piece, ('gy', 'gx'), pairs)]
where the time goes in v15:
time: 72.9 us; the launch traced here: 72.5 us
  starting transfers between devices  27.8 us (38%)
  waiting for transfers between devices  17.8 us (24%)
  Pallas kernels  15.4 us (21%)
  local copies, waits for them, and re-layouts  6.4 us (9%)
  between operations  2.17 us (3%)
  other arithmetic  1.62 us (2%)
  matrix products  1.28 us (2%)
    ppermute x8, starting transfers between devices, move(): return lax.ppermute(piece, ('gy', 'gx'), pairs)  26.2 us
    ppermute x8, waiting for transfers between devices, move(): return lax.ppermute(piece, ('gy', 'gx'), pairs)  14.7 us
    pallas_call x1, Pallas kernels, on_device(): pl.pallas_call(lambda *refs: window_kernel(frame, packing, *refs), out_sh...  11.9 us
    unnamed x25, local copies, waits for them, and re-layouts  4.61 us
    pallas_call x1, Pallas kernels, on_device(): pl.pallas_call(lambda *refs: pack_kernel(frame, packing, *refs), out_shap...  3.54 us
    ppermute x2, waiting for transfers between devices, on_device(): lax.ppermute(other, 'shot', [(i, i ^ span) for i in range(shots)])  3.14 us
    ppermute x2, starting transfers between devices, on_device(): lax.ppermute(other, 'shot', [(i, i ^ span) for i in range(shots)])  1.56 us
  transfers between devices with their start and end apart: 10, of which 3 were waited for; matrix products, arithmetic and copies ran while one was open for 0% of the time, Pallas kernels for 0%

profile of v15, /device:TPU:0, one launch (start us, length us, event | category | flops | bytes accessed | tf_op | source)
XLA Modules:
  0.0 72.5 jit_solution(16138777328183739804)
XLA Ops:
  0.6 0.7 and_select_fusion.1
  1.3 0.7 copy-done.10
  2.0 1.3 %fusion.1.refs_4_.refs_7_ = f32[4,32,1024]{2,1,0:T(8,128)} fusion(s32[128]{0:T(128)S(1)} %get-tuple-element.34, f32[128,32]{0,1:T(8,128)S(1)} %fusion.9, f32[4,128]{1,0:T(4,128)S(1)} %concatenate.3), kind=kOutput, calls=%fused_computation.3 | convolution fusion | flops 201474048 | bytes 543232 | tf_op jit(solution)/shard_map/nky,kl->nyl/dot_general | solution.py:317
  3.3 3.5 %shard_map.121 = (f32[139,1024]{1,0:T(8,128)}, f32[139,1024]{1,0:T(8,128)}, f32[32,4992]{1,0:T(8,128)}, f32[32,4992]{1,0:T(8,128)}, f32[118,512]{1,0:T(8,128)}, ...) custom-call(f32[1,5,32,1024]{3,2,1,0:T(8,128)} %refs_3_.3, f32[1,5,32,1024]{3,2,1,0:T(8,128)} %refs_4_.1, ...), custom_call_target="tpu_custom_call" | custom-call | tf_op jit(solution)/shard_map/pallas_call | solution.py:325
  6.8 6.0 %collective-permute-start.4 = (f32[118,512]{1,0:T(8,128)}, f32[118,512]{1,0:T(8,128)S(1)}, u32[]{:S(2)}, u32[]{:S(2)}) collective-permute-start(f32[118,512]{1,0:T(8,128)} %get-tuple-element.18), channel_id=1, source_target_pairs={{0,3},{2,5},{4,7},{8,11},{10,13},{12,15},{16,19},{18,21},{20,23},{... | collective-permute-start | bytes 725000 | tf_op jit(solution)/shard_map/ppermute | solution.py:119
  12.9 0.7 collective-permute-start.5
  13.5 6.2 %collective-permute-start.2 = (f32[32,4992]{1,0:T(8,128)}, f32[32,4992]{1,0:T(8,128)S(1)}, u32[]{:S(2)}, u32[]{:S(2)}) collective-permute-start(f32[32,4992]{1,0:T(8,128)} %get-tuple-element.16), channel_id=1, source_target_pairs={{0,1},{2,3},{4,5},{6,7},{8,9},{10,11},{12,13},{14,15},{16,17},{18,... | collective-permute-start | bytes 1916936 | tf_op jit(solution)/shard_map/ppermute | solution.py:119
  19.8 1.3 %collective-permute-start.3 = (f32[32,4992]{1,0:T(8,128)}, f32[32,4992]{1,0:T(8,128)S(1)}, u32[]{:S(2)}, u32[]{:S(2)}) collective-permute-start(f32[32,4992]{1,0:T(8,128)} %get-tuple-element.17), channel_id=1, source_target_pairs={{1,0},{3,2},{5,4},{7,6},{9,8},{11,10},{13,12},{15,14},{17,16},{19,... | collective-permute-start | bytes 1916936 | tf_op jit(solution)/shard_map/ppermute | solution.py:119
  21.1 1.4 %collective-permute-start.6 = (f32[118,512]{1,0:T(8,128)}, f32[118,512]{1,0:T(8,128)}, u32[]{:S(2)}, u32[]{:S(2)}) collective-permute-start(f32[118,512]{1,0:T(8,128)} %get-tuple-element.20), channel_id=1, source_target_pairs={{2,1},{4,3},{6,5},{10,9},{12,11},{14,13},{18,17},{20,19},{22,21},{... | collective-permute-start | bytes 725000 | tf_op jit(solution)/shard_map/ppermute | solution.py:119
  22.4 0.7 copy-done.5
  23.1 8.1 %collective-permute-start = (f32[139,1024]{1,0:T(8,128)}, f32[139,1024]{1,0:T(8,128)}, u32[]{:S(2)}, u32[]{:S(2)}) collective-permute-start(f32[139,1024]{1,0:T(8,128)} %get-tuple-element.14), channel_id=1, source_target_pairs={{0,2},{1,3},{2,4},{3,5},{4,6},{5,7},{8,10},{9,11},{10,12},{11,13},... | collective-permute-start | bytes 1708040 | tf_op jit(solution)/shard_map/ppermute | solution.py:119
  31.2 0.7 copy-done.7
  31.9 1.3 %collective-permute-start.1 = (f32[139,1024]{1,0:T(8,128)}, f32[139,1024]{1,0:T(8,128)}, u32[]{:S(2)}, u32[]{:S(2)}) collective-permute-start(f32[139,1024]{1,0:T(8,128)} %get-tuple-element.15), channel_id=1, source_target_pairs={{2,0},{3,1},{4,2},{5,3},{6,4},{7,5},{10,8},{11,9},{12,10},{13,11},... | collective-permute-start | bytes 1708040 | tf_op jit(solution)/shard_map/ppermute | solution.py:119
  33.9 0.1 pad_add_fusion.1.refs_1_
  34.0 1.3 %collective-permute-start.7 = (f32[118,512]{1,0:T(8,128)}, f32[118,512]{1,0:T(8,128)}, u32[]{:S(2)}, u32[]{:S(2)}) collective-permute-start(f32[118,512]{1,0:T(8,128)} %get-tuple-element.21), channel_id=1, source_target_pairs={{3,0},{5,2},{7,4},{11,8},{13,10},{15,12},{19,16},{21,18},{23,20},{... | collective-permute-start | bytes 725000 | tf_op jit(solution)/shard_map/ppermute | solution.py:119
  35.3 0.1 pad_add_fusion.refs_0_
  36.0 0.6 copy-done.11
  36.7 14.6 %collective-permute-done.7.refs_15_ = f32[118,512]{1,0:T(8,128)} collective-permute-done((f32[118,512]{1,0:T(8,128)}, f32[118,512]{1,0:T(8,128)}, u32[]{:S(2)}, u32[]{:S(2)}) %collective-permute-start.7) | collective-permute-done | bytes 241696 | tf_op jit(solution)/shard_map/ppermute | solution.py:119
  51.4 0.9 %copy-done.6 = f32[118,512]{1,0:T(8,128)S(1)} copy-done((f32[118,512]{1,0:T(8,128)S(1)}, f32[118,512]{1,0:T(8,128)}, u32[]{:S(2)}) %copy-start.6) | copy-done | bytes 241688
  52.4 0.9 %copy-done.8 = f32[118,512]{1,0:T(8,128)S(1)} copy-done((f32[118,512]{1,0:T(8,128)S(1)}, f32[118,512]{1,0:T(8,128)}, u32[]{:S(2)}) %copy-start.8) | copy-done | bytes 241688
  53.3 11.9 %shard_map.122 = (f32[1,5,32,1024]{3,2,1,0:T(8,128)}, f32[1,5,32,1024]{3,2,1,0:T(8,128)}, f32[2,4,1024]{2,1,0:T(4,128)S(1)}) custom-call(s32[4]{0:T(128)S(1)} %pad_add_fusion.refs_0_, s32[2]{0:T(128)S(1)} %pad_add_fusion.1.refs_1_, f32[3]{0:T(128)S(1)} %bitcast.51, f32[1,5,32,1024]{3,2,1,0:T(8,128)S(1)} %copy-done.1, f32[1,5,32,1024]{3,2,1,0:T(8,128)S(1)} %copy-done.2, ...), custom_call_target="tpu_custom_call" | custom-call | tf_op jit(solution)/shard_map/pallas_call | solution.py:341
  65.2 0.6 reshape.123
  65.8 0.2 reduce_sum.9
  66.1 0.2 copy.18
  66.3 0.8 %scatter_custom_fusion = f32[64,2]{1,0:T(8,128)S(1)} fusion(s32[64]{0:T(128)S(1)} %fusion.12, f32[64,2]{1,0:T(8,128)S(1)} %bitcast.54, f32[]{:T(128)} %constant.111.clone.1), kind=kCustom, calls=%fused_computation.9 | custom fusion | bytes 516 | tf_op jit(solution)/shard_map/scatter | solution.py:363
  67.0 0.1 copy.20
  67.1 1.5 %collective-permute-start.8 = (f32[2,16,2]{1,0,2:T(2,128)S(1)}, f32[2,16,2]{1,0,2:T(2,128)S(1)}, u32[]{:S(2)}, u32[]{:S(2)}) collective-permute-start(f32[2,16,2]{1,0,2:T(2,128)S(1)} %copy.20), channel_id=1, source_target_pairs={{0,16},{8,24},{16,0},{24,8},{1,17},{9,25},{17,1},{25,9},{2,18},{10... | collective-permute-start | bytes 776 | tf_op jit(solution)/shard_map/ppermute | solution.py:373
  68.6 0.1 copy.19
  68.7 2.0 %collective-permute-done.8 = f32[2,16,2]{1,0,2:T(2,128)S(1)} collective-permute-done((f32[2,16,2]{1,0,2:T(2,128)S(1)}, f32[2,16,2]{1,0,2:T(2,128)S(1)}, u32[]{:S(2)}, u32[]{:S(2)}) %collective-permute-start.8) | collective-permute-done | bytes 288 | tf_op jit(solution)/shard_map/ppermute | solution.py:373
  70.7 0.1 collective-permute-start.9
  70.8 1.1 %collective-permute-done.9 = f32[1,16,2]{1,0,2:T(1,128)S(1)} collective-permute-done((f32[1,16,2]{1,0,2:T(1,128)S(1)}, f32[1,16,2]{1,0,2:T(1,128)S(1)}, u32[]{:S(2)}, u32[]{:S(2)}) %collective-permute-start.9) | collective-permute-done | bytes 160 | tf_op jit(solution)/shard_map/ppermute | solution.py:373
  71.9 0.6 fusion.11
  (33 shorter events, 0.1 us)
Async XLA Ops:
  1.3 0.7 copy-start.10
  3.3 48.1 %copy-start = (f32[4,32,1024]{2,1,0:T(8,128)S(1)}, f32[4,32,1024]{2,1,0:T(8,128)}, u32[]{:S(2)}) copy-start(f32[4,32,1024]{2,1,0:T(8,128)} %fusion.1.refs_4_.refs_7_) | copy-start | bytes 1572868
  3.3 48.1 %copy-start.1 = (f32[1,5,32,1024]{3,2,1,0:T(8,128)S(1)}, f32[1,5,32,1024]{3,2,1,0:T(8,128)}, u32[]{:S(2)}) copy-start(f32[1,5,32,1024]{3,2,1,0:T(8,128)} %refs_3_.3) | copy-start | bytes 1966084
  3.3 48.1 %copy-start.2 = (f32[1,5,32,1024]{3,2,1,0:T(8,128)S(1)}, f32[1,5,32,1024]{3,2,1,0:T(8,128)}, u32[]{:S(2)}) copy-start(f32[1,5,32,1024]{3,2,1,0:T(8,128)} %refs_4_.1) | copy-start | bytes 1966084
  3.3 48.1 %copy-start.4 = (f32[32,1024]{1,0:T(8,128)S(1)}, f32[32,1024]{1,0:T(8,128)}, u32[]{:S(2)}) copy-start(f32[32,1024]{1,0:T(8,128)} %refs_6_.1) | copy-start | bytes 393220
  6.8 44.6 %copy-start.3 = (f32[32,1024]{1,0:T(8,128)S(1)}, f32[32,1024]{1,0:T(8,128)}, u32[]{:S(2)}) copy-start(f32[32,1024]{1,0:T(8,128)} %refs_5_.1) | copy-start | bytes 393220
  6.8 15.6 %collective-permute-start.4 = (f32[118,512]{1,0:T(8,128)}, f32[118,512]{1,0:T(8,128)S(1)}, u32[]{:S(2)}, u32[]{:S(2)}) collective-permute-start(f32[118,512]{1,0:T(8,128)} %get-tuple-element.18), channel_id=1, source_target_pairs={{0,3},{2,5},{4,7},{8,11},{10,13},{12,15},{16,19},{18,21},{20,23},{... | collective-permute-start | bytes 725000 | tf_op jit(solution)/shard_map/ppermute | solution.py:119
  12.9 18.4 %collective-permute-start.5 = (f32[118,512]{1,0:T(8,128)}, f32[118,512]{1,0:T(8,128)S(1)}, u32[]{:S(2)}, u32[]{:S(2)}) collective-permute-start(f32[118,512]{1,0:T(8,128)} %get-tuple-element.19), channel_id=1, source_target_pairs={{1,2},{3,4},{5,6},{9,10},{11,12},{13,14},{17,18},{19,20},{21,22},{... | collective-permute-start | bytes 725000 | tf_op jit(solution)/shard_map/ppermute | solution.py:119
  13.5 37.8 %collective-permute-start.2 = (f32[32,4992]{1,0:T(8,128)}, f32[32,4992]{1,0:T(8,128)S(1)}, u32[]{:S(2)}, u32[]{:S(2)}) collective-permute-start(f32[32,4992]{1,0:T(8,128)} %get-tuple-element.16), channel_id=1, source_target_pairs={{0,1},{2,3},{4,5},{6,7},{8,9},{10,11},{12,13},{14,15},{16,17},{18,... | collective-permute-start | bytes 1916936 | tf_op jit(solution)/shard_map/ppermute | solution.py:119
  19.8 31.6 %collective-permute-start.3 = (f32[32,4992]{1,0:T(8,128)}, f32[32,4992]{1,0:T(8,128)S(1)}, u32[]{:S(2)}, u32[]{:S(2)}) collective-permute-start(f32[32,4992]{1,0:T(8,128)} %get-tuple-element.17), channel_id=1, source_target_pairs={{1,0},{3,2},{5,4},{7,6},{9,8},{11,10},{13,12},{15,14},{17,16},{19,... | collective-permute-start | bytes 1916936 | tf_op jit(solution)/shard_map/ppermute | solution.py:119
  21.1 12.9 %collective-permute-start.6 = (f32[118,512]{1,0:T(8,128)}, f32[118,512]{1,0:T(8,128)}, u32[]{:S(2)}, u32[]{:S(2)}) collective-permute-start(f32[118,512]{1,0:T(8,128)} %get-tuple-element.20), channel_id=1, source_target_pairs={{2,1},{4,3},{6,5},{10,9},{12,11},{14,13},{18,17},{20,19},{22,21},{... | collective-permute-start | bytes 725000 | tf_op jit(solution)/shard_map/ppermute | solution.py:119
  22.4 0.7 copy-start.5
  23.1 28.2 %collective-permute-start = (f32[139,1024]{1,0:T(8,128)}, f32[139,1024]{1,0:T(8,128)}, u32[]{:S(2)}, u32[]{:S(2)}) collective-permute-start(f32[139,1024]{1,0:T(8,128)} %get-tuple-element.14), channel_id=1, source_target_pairs={{0,2},{1,3},{2,4},{3,5},{4,6},{5,7},{8,10},{9,11},{10,12},{11,13},... | collective-permute-start | bytes 1708040 | tf_op jit(solution)/shard_map/ppermute | solution.py:119
  31.2 0.7 copy-start.7
  31.9 19.4 %collective-permute-start.1 = (f32[139,1024]{1,0:T(8,128)}, f32[139,1024]{1,0:T(8,128)}, u32[]{:S(2)}, u32[]{:S(2)}) collective-permute-start(f32[139,1024]{1,0:T(8,128)} %get-tuple-element.15), channel_id=1, source_target_pairs={{2,0},{3,1},{4,2},{5,3},{6,4},{7,5},{10,8},{11,9},{12,10},{13,11},... | collective-permute-start | bytes 1708040 | tf_op jit(solution)/shard_map/ppermute | solution.py:119
  34.0 17.3 %collective-permute-start.7 = (f32[118,512]{1,0:T(8,128)}, f32[118,512]{1,0:T(8,128)}, u32[]{:S(2)}, u32[]{:S(2)}) collective-permute-start(f32[118,512]{1,0:T(8,128)} %get-tuple-element.21), channel_id=1, source_target_pairs={{3,0},{5,2},{7,4},{11,8},{13,10},{15,12},{19,16},{21,18},{23,20},{... | collective-permute-start | bytes 725000 | tf_op jit(solution)/shard_map/ppermute | solution.py:119
  36.0 0.7 copy-start.11
  36.7 14.7 %copy-start.9 = (f32[1,3]{1,0:T(1,128)S(1)}, f32[1,3]{1,0:T(1,128)}, u32[]{:S(2)}) copy-start(f32[1,3]{1,0:T(1,128)} %param.14) | copy-start | bytes 40
  51.4 0.9 %copy-start.6 = (f32[118,512]{1,0:T(8,128)S(1)}, f32[118,512]{1,0:T(8,128)}, u32[]{:S(2)}) copy-start(f32[118,512]{1,0:T(8,128)} %copy-done.5) | copy-start | bytes 724996
  52.4 0.9 %copy-start.8 = (f32[118,512]{1,0:T(8,128)S(1)}, f32[118,512]{1,0:T(8,128)}, u32[]{:S(2)}) copy-start(f32[118,512]{1,0:T(8,128)} %copy-done.7) | copy-start | bytes 724996
  67.1 3.6 %collective-permute-start.8 = (f32[2,16,2]{1,0,2:T(2,128)S(1)}, f32[2,16,2]{1,0,2:T(2,128)S(1)}, u32[]{:S(2)}, u32[]{:S(2)}) collective-permute-start(f32[2,16,2]{1,0,2:T(2,128)S(1)} %copy.20), channel_id=1, source_target_pairs={{0,16},{8,24},{16,0},{24,8},{1,17},{9,25},{17,1},{25,9},{2,18},{10... | collective-permute-start | bytes 776 | tf_op jit(solution)/shard_map/ppermute | solution.py:373
  70.7 1.2 %collective-permute-start.9 = (f32[1,16,2]{1,0,2:T(1,128)S(1)}, f32[1,16,2]{1,0,2:T(1,128)S(1)}, u32[]{:S(2)}, u32[]{:S(2)}) collective-permute-start(f32[1,16,2]{1,0,2:T(1,128)S(1)} %broadcast_select_fusion), channel_id=1, source_target_pairs={{0,8},{8,0},{16,24},{24,16},{1,9},{9,1},{17,25},{25,17},{2,10},{10... | collective-permute-start | bytes 392 | tf_op jit(solution)/shard_map/ppermute | solution.py:373

commit v16 on v15

--- a/solution.py
+++ b/solution.py
@@ -45,9 +45,10 @@
         self.rows = [h for h, w in NEEDS]
         self.lanes = [round_up(w * CZ, 128) for h, w in NEEDS]
         self.row_at = [sum(self.rows[:j]) for j in range(len(NEEDS))]
-        self.lane_at = [sum(self.lanes[:j]) for j in range(len(NEEDS))]
+        self.side = [w * CZ for h, w in NEEDS]
+        self.lane_at = [sum(self.side[:j]) for j in range(len(NEEDS))]
         self.total_rows = sum(self.rows)
-        self.total_lanes = sum(self.lanes)
+        self.total_lanes = sum(self.side)
         self.corner = frame.ox
         shelves = []
         self.corner_at = [(0, 0)] * len(NEEDS)
@@ -89,13 +90,14 @@
             continue
         src = field(j)
         r = slice(packing.row_at[j], packing.row_at[j] + h)
-        c = slice(packing.lane_at[j], packing.lane_at[j] + w)
+        ws = packing.side[j]
+        c = slice(packing.lane_at[j], packing.lane_at[j] + ws)
         top = slice(ny - h, ny)
         bottom = slice(0, h)
         up[r, :] = src[top, :]
         down[r, :] = src[bottom, :]
-        east[:, c] = src[:, lanes - w : lanes]
-        west[:, c] = src[:, 0:w]
+        east[:, c] = src[:, lanes - ws : lanes]
+        west[:, c] = src[:, 0:ws]
         cr, cl = packing.corner_at[j]
         cr = slice(cr, cr + h)
         cl = slice(cl, cl + w)
@@ -132,15 +134,16 @@
     if h == 0:
         return
     r = slice(packing.row_at[j], packing.row_at[j] + h)
-    c = slice(packing.lane_at[j], packing.lane_at[j] + w)
+    ws = packing.side[j]
+    c = slice(packing.lane_at[j], packing.lane_at[j] + ws)
     lo = slice(oy - h, oy)
     hi = slice(oy + ny, oy + ny + h)
     west = slice(ox - w, ox)
     east = slice(ox + lanes, ox + lanes + w)
     dst[lo, centre] = below[r, :]
     dst[hi, centre] = above[r, :]
-    dst[mid, west] = left[:, c]
-    dst[mid, east] = right[:, c]
+    dst[mid, ox - ws : ox] = left[:, c]
+    dst[mid, ox + lanes : ox + lanes + ws] = right[:, c]
     cr, cl = packing.corner_at[j]
     cr = slice(cr, cr + h)
     cl = slice(cl, cl + w)

time: 72.9 us -> 69.9 us (0.959)
  starting transfers between devices: 27.8 us -> 24.5 us
  other arithmetic: 1.62 us -> 3.26 us
  local copies, waits for them, and re-layouts: 6.4 us -> 4.88 us
    ppermute x8, starting transfers between devices: 26.2 us -> 23 us  [move(): return lax.ppermute(piece, ('gy', 'gx'), pairs)]
    unnamed x25, local copies, waits for them, and re-layouts: 4.61 us -> 2.97 us
  transfers between devices with their start and end apart: 10 -> 10, of which waited for: 3 -> 4; matrix products, arithmetic and copies ran while one was open for 0% -> 3% of each run, Pallas kernels for 0% -> 0%
where the time goes in v16:
time: 69.9 us; the launch traced here: 69.6 us
  starting transfers between devices  24.5 us (35%)
  waiting for transfers between devices  17.8 us (25%)
  Pallas kernels  15.7 us (22%)
  local copies, waits for them, and re-layouts  4.88 us (7%)
  other arithmetic  3.26 us (5%)
  between operations  2.16 us (3%)
  matrix products  1.28 us (2%)
    ppermute x8, starting transfers between devices, move(): return lax.ppermute(piece, ('gy', 'gx'), pairs)  23 us
    ppermute x8, waiting for transfers between devices, move(): return lax.ppermute(piece, ('gy', 'gx'), pairs)  14.7 us
    pallas_call x1, Pallas kernels, on_device(): pl.pallas_call(lambda *refs: window_kernel(frame, packing, *refs), out_sh...  12 us
    pallas_call x1, Pallas kernels, on_device(): pl.pallas_call(lambda *refs: pack_kernel(frame, packing, *refs), out_shap...  3.65 us
    ppermute x2, waiting for transfers between devices, on_device(): lax.ppermute(other, 'shot', [(i, i ^ span) for i in range(shots)])  3.13 us
    unnamed x25, local copies, waits for them, and re-layouts  2.97 us
    ppermute x2, starting transfers between devices, on_device(): lax.ppermute(other, 'shot', [(i, i ^ span) for i in range(shots)])  1.56 us
  transfers between devices with their start and end apart: 10, of which 4 were waited for; matrix products, arithmetic and copies ran while one was open for 3% of the time, Pallas kernels for 0%

profile of v16, /device:TPU:0, one launch (start us, length us, event | category | flops | bytes accessed | tf_op | source)
XLA Modules:
  0.0 69.6 jit_solution(818493196531204349)
XLA Ops:
  0.6 0.7 and_select_fusion.1
  1.3 0.7 copy-done.10
  2.0 1.3 %fusion.1.refs_4_.refs_7_ = f32[4,32,1024]{2,1,0:T(8,128)} fusion(s32[128]{0:T(128)S(1)} %get-tuple-element.34, f32[128,32]{0,1:T(8,128)S(1)} %fusion.9, f32[4,128]{1,0:T(4,128)S(1)} %concatenate.3), kind=kOutput, calls=%fused_computation.3 | convolution fusion | flops 201474048 | bytes 543232 | tf_op jit(solution)/shard_map/nky,kl->nyl/dot_general | solution.py:320
  3.3 3.6 %shard_map.121 = (f32[139,1024]{1,0:T(8,128)}, f32[139,1024]{1,0:T(8,128)}, f32[32,4448]{1,0:T(8,128)}, f32[32,4448]{1,0:T(8,128)}, f32[118,512]{1,0:T(8,128)}, ...) custom-call(f32[1,5,32,1024]{3,2,1,0:T(8,128)} %refs_3_.3, f32[1,5,32,1024]{3,2,1,0:T(8,128)} %refs_4_.1, ...), custom_call_target="tpu_custom_call" | custom-call | tf_op jit(solution)/shard_map/pallas_call | solution.py:328
  6.9 6.0 %collective-permute-start.4 = (f32[118,512]{1,0:T(8,128)}, f32[118,512]{1,0:T(8,128)S(1)}, u32[]{:S(2)}, u32[]{:S(2)}) collective-permute-start(f32[118,512]{1,0:T(8,128)} %get-tuple-element.18), channel_id=1, source_target_pairs={{0,3},{2,5},{4,7},{8,11},{10,13},{12,15},{16,19},{18,21},{20,23},{... | collective-permute-start | bytes 725000 | tf_op jit(solution)/shard_map/ppermute | solution.py:121
  13.0 0.7 collective-permute-start.5
  13.7 1.4 %collective-permute-start.6 = (f32[118,512]{1,0:T(8,128)}, f32[118,512]{1,0:T(8,128)}, u32[]{:S(2)}, u32[]{:S(2)}) collective-permute-start(f32[118,512]{1,0:T(8,128)} %get-tuple-element.20), channel_id=1, source_target_pairs={{2,1},{4,3},{6,5},{10,9},{12,11},{14,13},{18,17},{20,19},{22,21},{... | collective-permute-start | bytes 725000 | tf_op jit(solution)/shard_map/ppermute | solution.py:121
  15.0 8.9 %collective-permute-start = (f32[139,1024]{1,0:T(8,128)}, f32[139,1024]{1,0:T(8,128)S(1)}, u32[]{:S(2)}, u32[]{:S(2)}) collective-permute-start(f32[139,1024]{1,0:T(8,128)} %get-tuple-element.14), channel_id=1, source_target_pairs={{0,2},{1,3},{2,4},{3,5},{4,6},{5,7},{8,10},{9,11},{10,12},{11,13},... | collective-permute-start | bytes 1708040 | tf_op jit(solution)/shard_map/ppermute | solution.py:121
  23.9 1.3 %collective-permute-start.1 = (f32[139,1024]{1,0:T(8,128)}, f32[139,1024]{1,0:T(8,128)S(1)}, u32[]{:S(2)}, u32[]{:S(2)}) collective-permute-start(f32[139,1024]{1,0:T(8,128)} %get-tuple-element.15), channel_id=1, source_target_pairs={{2,0},{3,1},{4,2},{5,3},{6,4},{7,5},{10,8},{11,9},{12,10},{13,11},... | collective-permute-start | bytes 1708040 | tf_op jit(solution)/shard_map/ppermute | solution.py:121
  25.2 2.1 %collective-permute-start.2 = (f32[32,4448]{1,0:T(8,128)}, f32[32,4448]{1,0:T(8,128)}, u32[]{:S(2)}, u32[]{:S(2)}) collective-permute-start(f32[32,4448]{1,0:T(8,128)} %get-tuple-element.16), channel_id=1, source_target_pairs={{0,1},{2,3},{4,5},{6,7},{8,9},{10,11},{12,13},{14,15},{16,17},{18,... | collective-permute-start | bytes 1708040 | tf_op jit(solution)/shard_map/ppermute | solution.py:121
  27.4 0.7 copy-done.5
  28.1 1.3 %collective-permute-start.3 = (f32[32,4448]{1,0:T(8,128)}, f32[32,4448]{1,0:T(8,128)}, u32[]{:S(2)}, u32[]{:S(2)}) collective-permute-start(f32[32,4448]{1,0:T(8,128)} %get-tuple-element.17), channel_id=1, source_target_pairs={{1,0},{3,2},{5,4},{7,6},{9,8},{11,10},{13,12},{15,14},{17,16},{19,... | collective-permute-start | bytes 1708040 | tf_op jit(solution)/shard_map/ppermute | solution.py:121
  30.0 0.6 pad_add_fusion.1.refs_1_
  30.6 1.3 %collective-permute-start.7 = (f32[118,512]{1,0:T(8,128)}, f32[118,512]{1,0:T(8,128)}, u32[]{:S(2)}, u32[]{:S(2)}) collective-permute-start(f32[118,512]{1,0:T(8,128)} %get-tuple-element.21), channel_id=1, source_target_pairs={{3,0},{5,2},{7,4},{11,8},{13,10},{15,12},{19,16},{21,18},{23,20},{... | collective-permute-start | bytes 725000 | tf_op jit(solution)/shard_map/ppermute | solution.py:121
  31.9 0.7 pad_add_fusion.refs_0_
  33.3 0.6 copy-done.11
  33.9 0.5 fusion.12
  34.4 9.6 %collective-permute-done.7.refs_15_ = f32[118,512]{1,0:T(8,128)} collective-permute-done((f32[118,512]{1,0:T(8,128)}, f32[118,512]{1,0:T(8,128)}, u32[]{:S(2)}, u32[]{:S(2)}) %collective-permute-start.7) | collective-permute-done | bytes 241696 | tf_op jit(solution)/shard_map/ppermute | solution.py:121
  44.0 5.1 %collective-permute-done.3.refs_11_ = f32[32,4448]{1,0:T(8,128)} collective-permute-done((f32[32,4448]{1,0:T(8,128)}, f32[32,4448]{1,0:T(8,128)}, u32[]{:S(2)}, u32[]{:S(2)}) %collective-permute-start.3) | collective-permute-done | bytes 569376 | tf_op jit(solution)/shard_map/ppermute | solution.py:121
  49.2 0.9 %copy-done.6 = f32[118,512]{1,0:T(8,128)S(1)} copy-done((f32[118,512]{1,0:T(8,128)S(1)}, f32[118,512]{1,0:T(8,128)}, u32[]{:S(2)}) %copy-start.6) | copy-done | bytes 241688
  50.1 12.0 %shard_map.122 = (f32[1,5,32,1024]{3,2,1,0:T(8,128)}, f32[1,5,32,1024]{3,2,1,0:T(8,128)}, f32[2,4,1024]{2,1,0:T(4,128)S(1)}) custom-call(s32[4]{0:T(128)S(1)} %copy-done.7, s32[2]{0:T(128)S(1)} %copy-done.9, f32[3]{0:T(128)S(1)} %bitcast.51, f32[1,5,32,1024]{3,2,1,0:T(8,128)S(1)} %copy-done.1, f32[1,5,32,1024]{3,2,1,0:T(8,128)S(1)} %copy-done.2, ...), custom_call_target="tpu_custom_call" | custom-call | tf_op jit(solution)/shard_map/pallas_call | solution.py:344
  62.1 0.6 reshape.123
  62.8 0.2 reduce_sum.9
  63.0 0.2 copy.18
  63.2 0.9 %scatter_custom_fusion = f32[64,2]{1,0:T(8,128)S(1)} fusion(s32[64]{0:T(128)} %fusion.12, f32[64,2]{1,0:T(8,128)S(1)} %bitcast.54, f32[]{:T(128)} %constant.111.clone.1), kind=kCustom, calls=%fused_computation.9 | custom fusion | bytes 1024 | tf_op jit(solution)/shard_map/scatter | solution.py:366
  64.1 0.1 copy.20
  64.2 1.5 %collective-permute-start.8 = (f32[2,16,2]{1,0,2:T(2,128)S(1)}, f32[2,16,2]{1,0,2:T(2,128)S(1)}, u32[]{:S(2)}, u32[]{:S(2)}) collective-permute-start(f32[2,16,2]{1,0,2:T(2,128)S(1)} %copy.20), channel_id=1, source_target_pairs={{0,16},{8,24},{16,0},{24,8},{1,17},{9,25},{17,1},{25,9},{2,18},{10... | collective-permute-start | bytes 776 | tf_op jit(solution)/shard_map/ppermute | solution.py:376
  65.7 0.1 copy.19
  65.8 2.0 %collective-permute-done.8 = f32[2,16,2]{1,0,2:T(2,128)S(1)} collective-permute-done((f32[2,16,2]{1,0,2:T(2,128)S(1)}, f32[2,16,2]{1,0,2:T(2,128)S(1)}, u32[]{:S(2)}, u32[]{:S(2)}) %collective-permute-start.8) | collective-permute-done | bytes 288 | tf_op jit(solution)/shard_map/ppermute | solution.py:376
  67.8 0.1 collective-permute-start.9
  67.9 1.1 %collective-permute-done.9 = f32[1,16,2]{1,0,2:T(1,128)S(1)} collective-permute-done((f32[1,16,2]{1,0,2:T(1,128)S(1)}, f32[1,16,2]{1,0,2:T(1,128)S(1)}, u32[]{:S(2)}, u32[]{:S(2)}) %collective-permute-start.9) | collective-permute-done | bytes 160 | tf_op jit(solution)/shard_map/ppermute | solution.py:376
  69.0 0.6 fusion.11
  (33 shorter events, 0.1 us)
Async XLA Ops:
  1.3 0.7 copy-start.10
  3.3 45.9 %copy-start = (f32[4,32,1024]{2,1,0:T(8,128)S(1)}, f32[4,32,1024]{2,1,0:T(8,128)}, u32[]{:S(2)}) copy-start(f32[4,32,1024]{2,1,0:T(8,128)} %fusion.1.refs_4_.refs_7_) | copy-start | bytes 1572868
  3.3 45.9 %copy-start.1 = (f32[1,5,32,1024]{3,2,1,0:T(8,128)S(1)}, f32[1,5,32,1024]{3,2,1,0:T(8,128)}, u32[]{:S(2)}) copy-start(f32[1,5,32,1024]{3,2,1,0:T(8,128)} %refs_3_.3) | copy-start | bytes 1966084
  3.3 45.9 %copy-start.2 = (f32[1,5,32,1024]{3,2,1,0:T(8,128)S(1)}, f32[1,5,32,1024]{3,2,1,0:T(8,128)}, u32[]{:S(2)}) copy-start(f32[1,5,32,1024]{3,2,1,0:T(8,128)} %refs_4_.1) | copy-start | bytes 1966084
  3.3 45.9 %copy-start.4 = (f32[32,1024]{1,0:T(8,128)S(1)}, f32[32,1024]{1,0:T(8,128)}, u32[]{:S(2)}) copy-start(f32[32,1024]{1,0:T(8,128)} %refs_6_.1) | copy-start | bytes 393220
  6.9 42.2 %copy-start.3 = (f32[32,1024]{1,0:T(8,128)S(1)}, f32[32,1024]{1,0:T(8,128)}, u32[]{:S(2)}) copy-start(f32[32,1024]{1,0:T(8,128)} %refs_5_.1) | copy-start | bytes 393220
  6.9 18.3 %collective-permute-start.4 = (f32[118,512]{1,0:T(8,128)}, f32[118,512]{1,0:T(8,128)S(1)}, u32[]{:S(2)}, u32[]{:S(2)}) collective-permute-start(f32[118,512]{1,0:T(8,128)} %get-tuple-element.18), channel_id=1, source_target_pairs={{0,3},{2,5},{4,7},{8,11},{10,13},{12,15},{16,19},{18,21},{20,23},{... | collective-permute-start | bytes 725000 | tf_op jit(solution)/shard_map/ppermute | solution.py:121
  13.0 14.4 %collective-permute-start.5 = (f32[118,512]{1,0:T(8,128)}, f32[118,512]{1,0:T(8,128)S(1)}, u32[]{:S(2)}, u32[]{:S(2)}) collective-permute-start(f32[118,512]{1,0:T(8,128)} %get-tuple-element.19), channel_id=1, source_target_pairs={{1,2},{3,4},{5,6},{9,10},{11,12},{13,14},{17,18},{19,20},{21,22},{... | collective-permute-start | bytes 725000 | tf_op jit(solution)/shard_map/ppermute | solution.py:121
  13.7 17.0 %collective-permute-start.6 = (f32[118,512]{1,0:T(8,128)}, f32[118,512]{1,0:T(8,128)}, u32[]{:S(2)}, u32[]{:S(2)}) collective-permute-start(f32[118,512]{1,0:T(8,128)} %get-tuple-element.20), channel_id=1, source_target_pairs={{2,1},{4,3},{6,5},{10,9},{12,11},{14,13},{18,17},{20,19},{22,21},{... | collective-permute-start | bytes 725000 | tf_op jit(solution)/shard_map/ppermute | solution.py:121
  15.0 29.0 %collective-permute-start = (f32[139,1024]{1,0:T(8,128)}, f32[139,1024]{1,0:T(8,128)S(1)}, u32[]{:S(2)}, u32[]{:S(2)}) collective-permute-start(f32[139,1024]{1,0:T(8,128)} %get-tuple-element.14), channel_id=1, source_target_pairs={{0,2},{1,3},{2,4},{3,5},{4,6},{5,7},{8,10},{9,11},{10,12},{11,13},... | collective-permute-start | bytes 1708040 | tf_op jit(solution)/shard_map/ppermute | solution.py:121
  23.9 20.1 %collective-permute-start.1 = (f32[139,1024]{1,0:T(8,128)}, f32[139,1024]{1,0:T(8,128)S(1)}, u32[]{:S(2)}, u32[]{:S(2)}) collective-permute-start(f32[139,1024]{1,0:T(8,128)} %get-tuple-element.15), channel_id=1, source_target_pairs={{2,0},{3,1},{4,2},{5,3},{6,4},{7,5},{10,8},{11,9},{12,10},{13,11},... | collective-permute-start | bytes 1708040 | tf_op jit(solution)/shard_map/ppermute | solution.py:121
  25.2 18.8 %collective-permute-start.2 = (f32[32,4448]{1,0:T(8,128)}, f32[32,4448]{1,0:T(8,128)}, u32[]{:S(2)}, u32[]{:S(2)}) collective-permute-start(f32[32,4448]{1,0:T(8,128)} %get-tuple-element.16), channel_id=1, source_target_pairs={{0,1},{2,3},{4,5},{6,7},{8,9},{10,11},{12,13},{14,15},{16,17},{18,... | collective-permute-start | bytes 1708040 | tf_op jit(solution)/shard_map/ppermute | solution.py:121
  27.4 0.7 copy-start.5
  28.1 21.1 %collective-permute-start.3 = (f32[32,4448]{1,0:T(8,128)}, f32[32,4448]{1,0:T(8,128)}, u32[]{:S(2)}, u32[]{:S(2)}) collective-permute-start(f32[32,4448]{1,0:T(8,128)} %get-tuple-element.17), channel_id=1, source_target_pairs={{1,0},{3,2},{5,4},{7,6},{9,8},{11,10},{13,12},{15,14},{17,16},{19,... | collective-permute-start | bytes 1708040 | tf_op jit(solution)/shard_map/ppermute | solution.py:121
  30.6 13.3 %collective-permute-start.7 = (f32[118,512]{1,0:T(8,128)}, f32[118,512]{1,0:T(8,128)}, u32[]{:S(2)}, u32[]{:S(2)}) collective-permute-start(f32[118,512]{1,0:T(8,128)} %get-tuple-element.21), channel_id=1, source_target_pairs={{3,0},{5,2},{7,4},{11,8},{13,10},{15,12},{19,16},{21,18},{23,20},{... | collective-permute-start | bytes 725000 | tf_op jit(solution)/shard_map/ppermute | solution.py:121
  33.3 0.7 copy-start.11
  34.4 14.7 %copy-start.7 = (s32[4]{0:T(128)S(1)}, s32[4]{0:T(128)}, u32[]{:S(2)}) copy-start(s32[4]{0:T(128)} %pad_add_fusion.refs_0_) | copy-start | bytes 52
  34.4 14.7 %copy-start.8 = (f32[1,3]{1,0:T(1,128)S(1)}, f32[1,3]{1,0:T(1,128)}, u32[]{:S(2)}) copy-start(f32[1,3]{1,0:T(1,128)} %param.14) | copy-start | bytes 40
  34.4 14.7 %copy-start.9 = (s32[2]{0:T(128)S(1)}, s32[2]{0:T(128)}, u32[]{:S(2)}) copy-start(s32[2]{0:T(128)} %pad_add_fusion.1.refs_1_) | copy-start | bytes 28
  49.2 0.9 %copy-start.6 = (f32[118,512]{1,0:T(8,128)S(1)}, f32[118,512]{1,0:T(8,128)}, u32[]{:S(2)}) copy-start(f32[118,512]{1,0:T(8,128)} %copy-done.5) | copy-start | bytes 724996
  64.2 3.6 %collective-permute-start.8 = (f32[2,16,2]{1,0,2:T(2,128)S(1)}, f32[2,16,2]{1,0,2:T(2,128)S(1)}, u32[]{:S(2)}, u32[]{:S(2)}) collective-permute-start(f32[2,16,2]{1,0,2:T(2,128)S(1)} %copy.20), channel_id=1, source_target_pairs={{0,16},{8,24},{16,0},{24,8},{1,17},{9,25},{17,1},{25,9},{2,18},{10... | collective-permute-start | bytes 776 | tf_op jit(solution)/shard_map/ppermute | solution.py:376
  67.8 1.2 %collective-permute-start.9 = (f32[1,16,2]{1,0,2:T(1,128)S(1)}, f32[1,16,2]{1,0,2:T(1,128)S(1)}, u32[]{:S(2)}, u32[]{:S(2)}) collective-permute-start(f32[1,16,2]{1,0,2:T(1,128)S(1)} %broadcast_select_fusion), channel_id=1, source_target_pairs={{0,8},{8,0},{16,24},{24,16},{1,9},{9,1},{17,25},{25,17},{2,10},{10... | collective-permute-start | bytes 392 | tf_op jit(solution)/shard_map/ppermute | solution.py:376
